TPU v7x, 32 devices: a whole 2x2x4 slice. The times are simulated.
32 devices in a mesh: seq: 8 (over y, x, core), head: 4 (over z).
Axes of the slice: x: 2, y: 2, z: 4, core: 2. Of those that a mesh axis runs over, the one named last changes fastest.
Arguments:
- x_in: bfloat16 [8, 2048, 2048], P(None, 'seq', 'head'), may hold values from -6 to 6
- b_in: bfloat16 [8, 256, 2048], P(None, 'seq', 'head'), may hold values from -6 to 6
- c_in: bfloat16 [8, 256, 2048], P(None, 'seq', 'head'), may hold values from -6 to 6
- dt_raw: bfloat16 [8, 32, 2048], P(None, 'seq', 'head'), may hold values from -1.4 to 12.9
- cotangent: bfloat16 [8, 2048, 2048], P(None, 'seq', 'head'), may hold values from -6 to 6
- conv_weight: float32 [8, 4, 2560], P('head'), may hold values from -3 to 3
- conv_bias: float32 [8, 2560], P('head'), may hold values from -0.5 to 0.5
- dt_bias: float32 [8, 32], P('head'), may hold values from -7.6 to -3
- a_log: float32 [8, 32], P('head'), may hold values from -3 to 1.39
- d_skip: float32 [8, 32], P('head'), may hold values from 0.5 to 1.5
- doc_lengths: int32 [4], replicated, may hold values from 1 to 896, 2048 in all
Outputs:
- y_out: bfloat16 [8, 2048, 2048], P(None, 'seq', 'head')
- x_grad: bfloat16 [8, 2048, 2048], P(None, 'seq', 'head')
- b_grad: bfloat16 [8, 256, 2048], P(None, 'seq', 'head')
- c_grad: bfloat16 [8, 256, 2048], P(None, 'seq', 'head')
- dt_grad: bfloat16 [8, 32, 2048], P(None, 'seq', 'head')
Inputs may be any that keep to these rules, and one draw needn't show every extreme that they name: `doc_lengths`: 4 document lengths that sum to 2048.
All inputs are finite; a program needn't handle non-finite values.
Results may differ from a plain program's by a relative error of at most 0.0025.
Values may be sent and summed in bfloat16 or wider, within the bound.
No kernel may reach another device: no remote copies, remote signals or barrier semaphores. Data moves between devices by JAX's collectives and lax.ppermute only.
A program may use at most 256 MiB of HBM per device.

v0:
```python
import jax
import jax.numpy as jnp
from jax import lax
from jax.sharding import PartitionSpec as P

HEAD_DIM = 64
STATE = 256
TAPS = 4
SPAN = 128


precise = lax.Precision.HIGHEST


def passed_along(value, axis, steps):
    count = lax.axis_size(axis)
    first, last = (max(0, -steps), min(count, count - steps))
    return lax.ppermute(value, axis, [(source, source + steps) for source in range(first, last)])


def carried_in(array, axis, combine, identity, reverse):
    peers, index = (lax.axis_size(axis), lax.axis_index(axis))
    everything = jax.tree.map(lambda part: lax.all_gather(part, axis), array)
    start = jax.tree.map(
        lambda part, zero: jnp.broadcast_to(jnp.asarray(zero, part.dtype), part.shape),
        array,
        identity,
    )

    def lap(k, before):
        at = peers - 1 - k if reverse else k
        reached = at > index if reverse else at < index
        new = combine(before, jax.tree.map(lambda part: part[at], everything))
        return jax.tree.map(lambda a, b: jnp.where(reached, a, b), new, before)

    return lax.fori_loop(0, peers, lap, start)


def segment_ids(positions, doc_lengths):
    ends = jnp.cumsum(doc_lengths)
    counted = jnp.sum((ends[None, :] <= positions[:, None]).astype(jnp.int32), axis=1)
    return jnp.where(positions >= 0, counted, -1)


def conv_silu(padded, weight, bias, segment_extended, length):
    total = jnp.zeros((padded.shape[0], length), jnp.float32) + bias[:, None]
    for offset in range(TAPS):
        same_doc = (
            segment_extended[offset : offset + length] == segment_extended[TAPS - 1 :]
        ).astype(jnp.float32)
        total = (
            total
            + weight[offset][:, None] * padded[:, offset : offset + length] * same_doc[None, :]
        )
    return jax.nn.silu(total)


def span_terms(x_conv, b_conv, c_conv, step_size, log_decay, seg_tok, seg_before, skip_gain):
    n_heads, length = step_size.shape
    blocks = length // SPAN
    x_four = x_conv.reshape(n_heads, HEAD_DIM, blocks, SPAN)
    b_three = b_conv.reshape(STATE, blocks, SPAN)
    c_three = c_conv.reshape(STATE, blocks, SPAN)
    step_three = step_size.reshape(n_heads, blocks, SPAN)
    seg_two = seg_tok.reshape(blocks, SPAN)
    rows_idx = lax.broadcasted_iota(jnp.int32, (SPAN, SPAN), 0)
    cols_idx = lax.broadcasted_iota(jnp.int32, (SPAN, SPAN), 1)
    lower = (rows_idx >= cols_idx).astype(jnp.float32)
    cumul = jnp.einsum(
        "hcj,ij->hci", log_decay.reshape(n_heads, blocks, SPAN), lower, precision=precise
    )
    mask_doc = lower[None] * (seg_two[:, :, None] == seg_two[:, None, :]).astype(jnp.float32)
    decay = jnp.exp(jnp.minimum(cumul[:, :, :, None] - cumul[:, :, None, :], 0.0)) * mask_doc[None]
    scores = jnp.einsum("nci,ncj->cij", c_three, b_three, precision=precise)
    weighted = x_four * step_three[:, None]
    y_intra = jnp.einsum("hcij,hpcj->hpci", decay * scores[None], weighted, precision=precise)
    y_intra = y_intra + skip_gain[:, None, None, None] * x_four
    last_cum = cumul[:, :, -1:]
    keep_end = jnp.exp(last_cum - cumul) * (seg_two == seg_two[:, -1:]).astype(jnp.float32)[None]
    states = jnp.einsum("hpcj,hcj,ncj->hcpn", weighted, keep_end, b_three, precision=precise)
    prev_seg = jnp.concatenate([seg_before[None], seg_two[:-1, -1]])
    entry = jnp.exp(cumul) * (seg_two == prev_seg[:, None]).astype(jnp.float32)[None]
    carry = jnp.exp(last_cum[:, :, 0]) * (seg_two[:, -1] == prev_seg).astype(jnp.float32)[None]
    return (y_intra, c_three, entry, carry, states)


def group_terms(
    raw_chan, rim_chan, dt_pre, weight, bias, bias_dt, log_rate, skip_gain, segment_extended
):
    n_heads = dt_pre.shape[0]
    length = raw_chan.shape[1]
    padded = jnp.concatenate([rim_chan, raw_chan], axis=1)
    active = conv_silu(padded, weight, bias, segment_extended, length)
    split_at = n_heads * HEAD_DIM
    x_conv = active[:split_at]
    b_conv = active[split_at : split_at + STATE]
    c_conv = active[split_at + STATE :]
    step_size = jax.nn.softplus(dt_pre + bias_dt[:, None])
    log_decay = step_size * (-jnp.exp(log_rate))[:, None]
    return span_terms(
        x_conv,
        b_conv,
        c_conv,
        step_size,
        log_decay,
        segment_extended[TAPS - 1 :],
        segment_extended[TAPS - 2],
        skip_gain,
    )


def span_fold(carry, states, state_start):

    def span_advance(running, pieces):
        factor, piece = pieces
        return (factor[:, None, None] * running + piece, running)

    state_end, starts = lax.scan(span_advance, state_start, (carry.T, jnp.moveaxis(states, 1, 0)))
    return (starts, state_end)


def assemble(y_intra, c_three, entry, carry, states, state_start):
    starts, state_end = span_fold(carry, states, state_start)
    y_full = y_intra + jnp.einsum("nci,hci,chpn->hpci", c_three, entry, starts, precision=precise)
    return (y_full.reshape(y_full.shape[0] * y_full.shape[1], -1), state_end)


def reach(carry):

    def reach_advance(product, factor):
        return (product * factor, product)

    total, before = lax.scan(
        reach_advance, jnp.ones(carry.shape[:-1], jnp.float32), jnp.moveaxis(carry, -1, 0)
    )
    return (jnp.moveaxis(before, 0, -1), total)


def compose_fwd(preceding_states, later):
    return (
        preceding_states[0] * later[0],
        later[0][..., None, None] * preceding_states[1] + later[1],
    )


def compose_back(preceding_states, later):
    return (
        later[0] * preceding_states[0],
        later[1] + later[0][..., None, None] * preceding_states[1],
    )


def shards(
    x_in, b_in, c_in, dt_raw, cotangent, conv_weight, conv_bias, dt_bias, a_log, d_skip, doc_lengths
):
    x_scan, b_scan, c_scan, dt_scan, cot_scan = (
        lax.all_to_all(
            lax.all_to_all(x_in, "head", split_axis=0, concat_axis=2, tiled=True),
            "seq",
            split_axis=2,
            concat_axis=1,
            tiled=True,
        ),
        lax.all_to_all(
            lax.all_to_all(b_in, "head", split_axis=0, concat_axis=2, tiled=True),
            "seq",
            split_axis=2,
            concat_axis=1,
            tiled=True,
        ),
        lax.all_to_all(
            lax.all_to_all(c_in, "head", split_axis=0, concat_axis=2, tiled=True),
            "seq",
            split_axis=2,
            concat_axis=1,
            tiled=True,
        ),
        lax.all_to_all(
            lax.all_to_all(dt_raw, "head", split_axis=0, concat_axis=2, tiled=True),
            "seq",
            split_axis=2,
            concat_axis=1,
            tiled=True,
        ),
        lax.all_to_all(
            lax.all_to_all(cotangent, "head", split_axis=0, concat_axis=2, tiled=True),
            "seq",
            split_axis=2,
            concat_axis=1,
            tiled=True,
        ),
    )
    groups_here = x_scan.shape[0]
    x_width = x_scan.shape[1]
    n_heads = dt_scan.shape[1]
    length = x_scan.shape[2]
    blocks = length // SPAN
    raw_chan = jnp.concatenate([x_scan, b_scan, c_scan], axis=1)
    rim_chan = passed_along(raw_chan[:, :, length - (TAPS - 1) :], "seq", 1)
    rank = lax.axis_index("seq")
    positions = rank * length + jnp.arange(-(TAPS - 1), length, dtype=jnp.int32)
    segment_extended = segment_ids(positions, doc_lengths)

    def local_terms(raw_float, rim_float, dt_float):
        return jax.vmap(group_terms, in_axes=(0, 0, 0, 0, 0, 0, 0, 0, None))(
            raw_float,
            rim_float,
            dt_float,
            conv_weight,
            conv_bias,
            dt_bias,
            a_log,
            d_skip,
            segment_extended,
        )

    terms, pull_terms = jax.vjp(
        local_terms,
        raw_chan.astype(jnp.float32),
        rim_chan.astype(jnp.float32),
        dt_scan.astype(jnp.float32),
    )
    y_intra, c_three, entry, carry, states = terms
    before, total = reach(carry)
    state_zero = jnp.zeros((groups_here, n_heads, HEAD_DIM, STATE), jnp.float32)
    _, summary = jax.vmap(span_fold)(carry, states, state_zero)
    identity = (jnp.ones_like(total), jnp.zeros_like(summary))
    state_in = carried_in((total, summary), "seq", compose_fwd, identity, False)[1]

    def finish(pieces, state_start):
        return jax.vmap(assemble)(
            pieces[0], pieces[1], pieces[2], pieces[3], pieces[4], state_start
        )

    (y_scan, state_out), pull_out = jax.vjp(finish, terms, state_in)
    y_half = y_scan.astype(jnp.bfloat16)
    cot_float = cot_scan.astype(jnp.float32)
    cot_five = cot_float.reshape(groups_here, n_heads, HEAD_DIM, blocks, SPAN)
    local_grad = jnp.einsum(
        "ghpci,ghci,gnci->ghpn", cot_five, entry * before[..., None], c_three, precision=precise
    )
    grad_out = carried_in((total, local_grad), "seq", compose_back, identity, True)[1]
    d_terms, _ = pull_out((cot_float, grad_out))
    d_raw, d_rim, d_dt = pull_terms(d_terms)
    returned = passed_along(d_rim, "seq", -1)
    cut_at = length - (TAPS - 1)
    d_raw = jnp.concatenate([d_raw[:, :, :cut_at], d_raw[:, :, cut_at:] + returned], axis=2)
    grad_x = d_raw[:, :x_width].astype(jnp.bfloat16)
    grad_b = d_raw[:, x_width : x_width + STATE].astype(jnp.bfloat16)
    readout_gradient = d_raw[:, x_width + STATE :].astype(jnp.bfloat16)
    grad_dt = d_dt.astype(jnp.bfloat16)
    y_out, x_grad, b_grad, c_grad, dt_grad = (
        lax.all_to_all(
            lax.all_to_all(y_half, "seq", split_axis=1, concat_axis=2, tiled=True),
            "head",
            split_axis=2,
            concat_axis=0,
            tiled=True,
        ),
        lax.all_to_all(
            lax.all_to_all(grad_x, "seq", split_axis=1, concat_axis=2, tiled=True),
            "head",
            split_axis=2,
            concat_axis=0,
            tiled=True,
        ),
        lax.all_to_all(
            lax.all_to_all(grad_b, "seq", split_axis=1, concat_axis=2, tiled=True),
            "head",
            split_axis=2,
            concat_axis=0,
            tiled=True,
        ),
        lax.all_to_all(
            lax.all_to_all(readout_gradient, "seq", split_axis=1, concat_axis=2, tiled=True),
            "head",
            split_axis=2,
            concat_axis=0,
            tiled=True,
        ),
        lax.all_to_all(
            lax.all_to_all(grad_dt, "seq", split_axis=1, concat_axis=2, tiled=True),
            "head",
            split_axis=2,
            concat_axis=0,
            tiled=True,
        ),
    )
    return (y_out, x_grad, b_grad, c_grad, dt_grad)


def solution(mesh):
    return jax.shard_map(
        shards,
        mesh=mesh,
        in_specs=(
            P(None, "seq", "head"),
            P(None, "seq", "head"),
            P(None, "seq", "head"),
            P(None, "seq", "head"),
            P(None, "seq", "head"),
            P("head", None, None),
            P("head", None),
            P("head", None),
            P("head", None),
            P("head", None),
            P(),
        ),
        out_specs=(
            P(None, "seq", "head"),
            P(None, "seq", "head"),
            P(None, "seq", "head"),
            P(None, "seq", "head"),
            P(None, "seq", "head"),
        ),
        check_vma=False,
    )
```

profile of v0, /device:TPU:0, one launch (start us, length us, event | category | flops | bytes accessed | tf_op | source)
XLA Modules:
  0.0 996.2 jit_solution(4559923408317850390)
XLA Ops:
  7.2 12.0 %all_to_all.348 = bf16[8,4,512]{2,1,0:T(4,128)(2,1)S(1)} all-to-all(bf16[8,4,512]{2,1,0:T(4,128)(2,1)} %param.26), channel_id=1, replica_groups=mesh['seq'=8,'head'=4] {'head'}, dimensions={0} | all-to-all | bytes 65536 | tf_op jit(solution)/shard_map/all_to_all | solution.py:179
  22.1 8.4 all_to_all.349
  30.4 12.4 %all_to_all.350 = bf16[8,32,512]{2,1,0:T(8,128)(2,1)S(1)} all-to-all(bf16[8,32,512]{2,1,0:T(8,128)(2,1)} %param.25), channel_id=1, replica_groups=mesh['seq'=8,'head'=4] {'head'}, dimensions={0} | all-to-all | bytes 524288 | tf_op jit(solution)/shard_map/all_to_all | solution.py:172
  49.1 5.1 all-to-all-done.2
  57.8 6.7 all-to-all-done.5
  78.8 37.1 %all-to-all-done = bf16[8,256,512]{2,1,0:T(8,128)(2,1)S(1)} async-done(((bf16[8,256,512]{2,1,0:T(8,128)(2,1)}), bf16[8,256,512]{2,1,0:T(8,128)(2,1)S(1)}, u32[]{:S(2)}, u32[]{:S(2)}) %all-to-all-start) | async-done | bytes 2097184 | tf_op jit(solution)/shard_map/all_to_all | solution.py:158
  127.2 5.8 copy.404
  152.3 11.4 %all-to-all-done.1 = bf16[2,256,2048]{1,0,2:T(2,128)(2,1)S(1)} async-done(((bf16[2,256,2048]{1,0,2:T(2,128)(2,1)}), bf16[2,256,2048]{1,0,2:T(2,128)(2,1)S(1)}, u32[]{:S(2)}, u32[]{:S(2)}) %all-to-all-start.1) | async-done | bytes 2097184 | tf_op jit(solution)/shard_map/all_to_all | solution.py:157
  174.8 15.3 %fusion.38 = (f32[2,2560,256]{2,1,0:T(8,128)S(1)}, f32[2,2560,256]{2,1,0:T(8,128)}) fusion(f32[2,2560,256]{2,1,0:T(8,128)} %get-tuple-element.739, f32[2,2560]{1,0:T(2,128)S(1)} %copy-done.30, f32[256]{0:T(256)S(1)} %copy-done.47, f32[2,2560,3]{2,1,0:T(8,128)S(1)} %copy.416, f32[2,2560]{1,0:T(2,128)S(1)} %copy-done.28, f32[256]{0:T(256)S(1)} %copy-done.49, ...), kind=kLoop, calls=%fused_computation.73 | loop fusion | flops 23592960 | bytes 15895552 | tf_op jit(solution)/shard_map/jvp(vmap(jit(silu)))/mul | solution.py:55
  193.2 5.8 reshape.212
  199.2 9.0 fusion.63
  212.2 10.8 %while.89 = (s32[]{:T(128)}, f32[2,32,64,256]{3,2,1,0:T(8,128)}, f32[2,2,32]{2,1,0:T(2,128)S(1)}, f32[2,2,32,64,256]{4,3,2,1,0:T(8,128)}, s32[]{:T(128)}, /*index=5*/s32[]{:T(128)}) while((s32[]{:T(128)}, f32[2,32,64,256]{3,2,1,0:T(8,128)}, f32[2,2,32]{2,1,0:T(2,128)S(1)}, f32[2,2,32,64,256]{4,3,2,1,0:T(8,128)}, s32[]{:T(128)}, ...), condition=%wide.region_5.6_spmd.clone, body=%wide.region_4.5_spmd.clone.sunk | while | flops 3145731 | bytes 12583775 | solution.py:118
  217.0 6.0 bitcast_add_fusion.10
  224.6 52.5 %all_to_all.351 = bf16[8,256,512]{2,1,0:T(8,128)(2,1)} all-to-all(bf16[8,256,512]{2,1,0:T(8,128)(2,1)S(1)} %copy-done.11), channel_id=1, replica_groups=mesh['seq'=8,'head'=4] {'head'}, dimensions={0} | all-to-all | bytes 4194304 | tf_op jit(solution)/shard_map/all_to_all | solution.py:186
  279.9 14.0 %copy.452 = bf16[2,256,2048]{1,0,2:T(2,128)(2,1)} copy(bf16[2,256,2048]{1,2,0:T(8,128)(2,1)S(1)} %bitcast.367) | data formatting | bytes 4194304 | tf_op jit(solution)/shard_map/all_to_all | solution.py:186
  298.0 48.8 %all-to-all-done.11 = bf16[2,256,2048]{1,0,2:T(2,128)(2,1)S(1)} async-done(((bf16[2,256,2048]{1,0,2:T(2,128)(2,1)}), bf16[2,256,2048]{1,0,2:T(2,128)(2,1)S(1)}, u32[]{:S(2)}, u32[]{:S(2)}) %all-to-all-start.11) | async-done | bytes 2097184 | tf_op jit(solution)/shard_map/all_to_all | solution.py:185
  354.3 5.0 fusion.70
  364.6 8.0 all-gather.3
  374.0 14.4 %fusion.84 = (f32[2,32,2,128]{3,2,1,0:T(2,128)}, f32[2,32,2,128]{3,2,1,0:T(2,128)}, f32[2,2,128,128]{2,3,1,0:T(8,128)S(1)}) fusion(f32[2,32,2,128]{3,2,1,0:T(2,128)S(1)} %copy.423, f32[2,128,128]{1,2,0:T(8,128)} %compare_select_fusion.4, f32[2,2,128,128]{2,3,1,0:T(8,128)S(1)} %fusion.137, bf16[2,32,64,2,128]{4,3,2,1,0:T(2,128)(2,1)S(1)} %reshape.215, ...), kind=kOutput, calls=%fused_computation.121 | convolution fusion | flops 1643020288 | bytes 7208960 | tf_op jit(solution)/shard_map/transpose(jvp(vmap(hcij,hpcj->hpci)))/dot_general | solution.py:76
  388.3 19.3 %all-gather.7.cloned.1.call-done = f32[16,32,64,256]{3,2,1,0:T(8,128)} async-done(((f32[2,32,64,256]{3,2,1,0:T(8,128)}), f32[16,32,64,256]{3,2,1,0:T(8,128)}) %all-gather.7.cloned.1.call-update) | async-done | bytes 33554448 | tf_op jit(solution)/shard_map/all_gather | solution.py:23
  407.7 48.7 %while.90 = (s32[]{:T(128)}, f32[2,32,64,256]{3,2,1,0:T(8,128)}, s32[]{:T(128)}, f32[8,2,32]{2,1,0:T(2,128)S(1)}, f32[8,2,32,64,256]{4,3,2,1,0:T(8,128)}, /*index=5*/s32[]{:T(128)}, s32[]{:T(128)}) while((s32[]{:T(128)}, f32[2,32,64,256]{3,2,1,0:T(8,128)}, s32[]{:T(128)}, f32[8,2,32]{2,1,0:T(2,128)S(1)}, ...), condition=%wide.region_7.8_spmd.clone, body=%wide.region_6.7_spmd.clone.sunk | while | flops 4194308 | bytes 12583793 | solution.py:36
  412.4 6.6 fusion.158
  419.0 7.2 fusion.158
  426.2 6.0 fusion.158
  432.3 6.0 fusion.158
  438.3 6.0 fusion.158
  444.3 6.0 fusion.158
  450.4 6.0 fusion.158
  460.8 22.4 %while.86 = (s32[]{:T(128)}, f32[2,32,64,256]{3,2,1,0:T(8,128)}, f32[2,2,32,64,256]{4,3,2,1,0:T(8,128)}, f32[2,2,32,1,1]{2,1,4,3,0:T(2,128)S(1)}, f32[2,2,32]{2,...) while((s32[]{:T(128)}, f32[2,32,64,256]{3,2,1,0:T(8,128)}, f32[2,2,32,64,256]{4,3,2,1,0:T(8,128)}, ...), condition=%wide.region_9.10_spmd, body=%wide.region_8.9_spmd.sunk | while | flops 2097154 | bytes 54528924 | solution.py:118
  470.8 5.3 bitcast_dynamic-update-slice_fusion.6
  483.2 9.5 fusion.22
  495.2 9.0 fusion.66
  504.2 7.8 fusion.85
  511.9 58.4 %all-gather.9.cloned.1.call-done = f32[16,32,64,256]{3,2,1,0:T(8,128)} async-done(((f32[2,32,64,256]{3,2,1,0:T(8,128)}), f32[16,32,64,256]{3,2,1,0:T(8,128)}) %all-gather.9.cloned.1.call-update) | async-done | bytes 33554448 | tf_op jit(solution)/shard_map/all_gather | solution.py:23
  570.4 47.4 %while.91 = (s32[]{:T(128)}, f32[2,32,64,256]{3,2,1,0:T(8,128)}, s32[]{:T(128)}, f32[8,2,32,64,256]{4,3,2,1,0:T(8,128)}, f32[8,2,32]{2,1,0:T(2,128)S(1)}, /*index=5*/s32[]{:T(128)}, s32[]{:T(128)}, s32[]{:T(128)}, s32[]{:T(128)}) while((s32[]{:T(128)}, f32[2,32,64,256]{3,2,1,0:T(8,128)}, s32[]{:T(128)}, ...), condition=%wide.region_12.13_spmd.clone, body=%wide.region_11.12_spmd.clone.sunk | while | flops 4194312 | bytes 12583855 | solution.py:36
  575.2 6.1 fusion.159
  581.3 6.1 fusion.159
  587.3 6.1 fusion.159
  593.4 6.1 fusion.159
  599.5 6.1 fusion.159
  605.6 6.1 fusion.159
  611.7 6.1 fusion.159
  626.7 25.9 %while.87 = (s32[]{:T(128)}, f32[2,32,64,256]{3,2,1,0:T(8,128)}, f32[2,2,32]{2,0,1:T(2,128)S(1)}, f32[2,2,32,64,256]{4,3,2,1,0:T(8,128)}, f32[2,2,32,64,256]{4,3...) while((s32[]{:T(128)}, f32[2,32,64,256]{3,2,1,0:T(8,128)}, ...), condition=%wide.region_15.16_spmd, body=%wide.region_13.15_spmd.sunk | while | flops 4194243 | bytes 58721940 | solution.py:118
  632.8 6.6 fusion.157
  645.6 6.6 fusion.157
  652.6 12.4 %fusion.90 = f32[2,256,2,128]{1,3,2,0:T(8,128)S(1)} fusion(f32[2,2,32,64,256]{4,3,2,1,0:T(8,128)} %get-tuple-element.458, f32[2,32,64,2,128]{4,3,2,1,0:T(2,128)} %reshape.212, f32[2,32,2,128]{3,2,1,0:T(2,128)} %copy-done.15, f32[2,32,2,128]{3,2,1,0:T(2,128)S(1)} %get-tuple-element.724), kind=kOutput, calls=%fused_computation.123 | convolution fusion | flops 3223322624 | bytes 13238272 | tf_op jit(solution)/shard_map/transpose(jvp(vmap(hpcj,hcj,ncj->hcpn)))/dot_general | solution.py:80
  665.1 9.0 fusion.45
  674.8 11.8 %fusion.43 = (f32[2,32,2,128]{3,2,1,0:T(2,128)S(1)}, f32[2,32,64,2,128]{4,2,3,1,0:T(8,128)}) fusion(f32[2,32,64,2,128]{4,3,2,1,0:T(2,128)S(1)} %copy-done.4, f32[2,32,2,128]{3,2,1,0:T(2,128)S(1)} %get-tuple-element.724, bf16[2,32,64,2,128]{4,3,2,1,0:T(2,128)(2,1)S(1)} %reshape.215, f32[2,32]{1,0:T(2,128)S(1)} %copy-done.62, ...), kind=kOutput, calls=%fused_computation.80 | convolution fusion | flops 1627373568 | bytes 15335680 | tf_op jit(solution)/shard_map/transpose(jvp(vmap(hcij,hpcj->hpci)))/dot_general | solution.py:76
  687.2 8.1 copy.477
  695.4 6.5 reshape.218
  701.9 8.0 broadcast_multiply_fusion
  714.9 9.1 pad_add_fusion
  762.3 5.9 all-to-all-done.14
  778.5 5.5 all-to-all-start.15
  795.8 13.3 %fusion.46 = bf16[2,32,64,2,128]{4,2,3,1,0:T(8,128)(2,1)S(1)} fusion(f32[2,2,32,64,128]{4,3,2,1,0:T(8,128)} %copy-done.6, f32[2,32,64,2,128]{4,3,2,1,0:T(2,128)} %reshape.212, f32[2,2,128,128]{2,3,1,0:T(8,128)} %copy-done.18, f32[2,128,128]{1,2,0:T(8,128)} %compare_select_fusion.4, f32[2,32,2,128]{3,2,1,0:T(2,128)} %copy-done.39, ...), kind=kOutput, calls=%fused_computation.86 | convolution fusion | flops 1625292800 | bytes 11075840 | tf_op jit(solution)/shard_map/jvp(vmap(hcij,hpcj->hpci))/dot_general | solution.py:76
  812.6 6.8 reshape.246
  826.2 14.0 %copy.480 = bf16[2,2048,256]{2,0,1:T(2,128)(2,1)} copy(bf16[2,2048,256]{2,1,0:T(8,128)(2,1)S(1)} %slice.118) | data formatting | bytes 4194304 | tf_op jit(solution)/shard_map/slice | solution.py:248
  840.2 10.4 %all-to-all-done.8 = bf16[2,2048,256]{2,0,1:T(2,128)(2,1)} async-done(((bf16[2,2048,256]{2,0,1:T(2,128)(2,1)}), bf16[2,2048,256]{2,0,1:T(2,128)(2,1)}, u32[]{:S(2)}, u32[]{:S(2)}) %all-to-all-start.8) | async-done | bytes 2097184 | tf_op jit(solution)/shard_map/all_to_all | solution.py:254
  861.3 5.8 copy.448
  867.1 13.7 %all-to-all-done.12 = bf16[2,2048,256]{2,0,1:T(2,128)(2,1)S(1)} async-done(((bf16[2,2048,256]{2,0,1:T(2,128)(2,1)}), bf16[2,2048,256]{2,0,1:T(2,128)(2,1)S(1)}, u32[]{:S(2)}, u32[]{:S(2)}) %all-to-all-start.12) | async-done | bytes 2097184 | tf_op jit(solution)/shard_map/all_to_all | solution.py:261
  882.1 5.0 all-to-all-start.9
  894.2 5.8 copy.483
  900.0 32.4 %all-to-all-done.9 = bf16[2,256,2048]{1,0,2:T(2,128)(2,1)S(1)} async-done(((bf16[2,256,2048]{1,0,2:T(2,128)(2,1)}), bf16[2,256,2048]{1,0,2:T(2,128)(2,1)S(1)}, u32[]{:S(2)}, u32[]{:S(2)}) %all-to-all-start.9) | async-done | bytes 2097184 | tf_op jit(solution)/shard_map/all_to_all | solution.py:253
  953.5 31.4 %all-to-all-done.13 = bf16[2,256,2048]{1,0,2:T(2,128)(2,1)} async-done(((bf16[2,256,2048]{1,0,2:T(2,128)(2,1)}), bf16[2,256,2048]{1,0,2:T(2,128)(2,1)}, u32[]{:S(2)}, u32[]{:S(2)}) %all-to-all-start.13) | async-done | bytes 2097184 | tf_op jit(solution)/shard_map/all_to_all | solution.py:260
  (325 shorter events, 279.9 us)
Async XLA Ops:
  7.2 50.5 %copy-start.63 = (s32[4]{0:T(128)S(1)}, s32[4]{0:T(128)}, u32[]{:S(2)}) copy-start(s32[4]{0:T(128)} %param.33) | copy-start | bytes 52
  42.8 26.8 %copy-start.61 = (f32[2,32]{1,0:T(2,128)S(1)}, f32[2,32]{1,0:T(2,128)}, u32[]{:S(2)}) copy-start(f32[2,32]{1,0:T(2,128)} %param.31) | copy-start | bytes 772
  42.8 11.4 %all-to-all-start.2 = ((bf16[8,32,512]{2,1,0:T(8,128)(2,1)}), bf16[8,32,512]{2,1,0:T(8,128)(2,1)S(1)}, u32[]{:S(2)}, u32[]{:S(2)}) async-start(bf16[8,32,512]{2,1,0:T(8,128)(2,1)} %param.24), calls=%async_computation.2 | async-start | bytes 524288 | tf_op jit(solution)/shard_map/all_to_all | solution.py:165
  54.2 10.3 %copy-start.14 = (bf16[8,32,512]{2,1,0:T(8,128)(2,1)}, bf16[8,32,512]{2,1,0:T(8,128)(2,1)S(1)}, u32[]{:S(2)}) copy-start(bf16[8,32,512]{2,1,0:T(8,128)(2,1)S(1)} %all-to-all-done.2) | copy-start | bytes 786436
  54.2 10.3 %all-to-all-start.5 = ((bf16[8,2,8192]{2,1,0:T(2,128)(2,1)}), bf16[8,2,8192]{2,1,0:T(2,128)(2,1)S(1)}, u32[]{:S(2)}, u32[]{:S(2)}) async-start(bf16[8,2,8192]{2,1,0:T(2,128)(2,1)} %reshape.249), calls=%async_computation.5 | async-start | bytes 524288 | tf_op jit(solution)/shard_map/all_to_all | solution.py:171
  64.5 51.4 %all-to-all-start = ((bf16[8,256,512]{2,1,0:T(8,128)(2,1)}), bf16[8,256,512]{2,1,0:T(8,128)(2,1)S(1)}, u32[]{:S(2)}, u32[]{:S(2)}) async-start(bf16[8,256,512]{2,1,0:T(8,128)(2,1)} %param.23), calls=%async_computation | async-start | bytes 4194304 | tf_op jit(solution)/shard_map/all_to_all | solution.py:158
  69.7 72.8 %copy-start.51 = (f32[2,32]{1,0:T(2,128)}, f32[2,32]{1,0:T(2,128)S(1)}, u32[]{:S(2)}) copy-start(f32[2,32]{1,0:T(2,128)S(1)} %exponential_negate_fusion) | copy-start | bytes 772
  115.9 17.0 %all-to-all-start.3 = ((bf16[8,2,8192]{2,1,0:T(2,128)(2,1)}), bf16[8,2,8192]{2,1,0:T(2,128)(2,1)}, u32[]{:S(2)}, u32[]{:S(2)}) async-start(bf16[8,2,8192]{2,1,0:T(2,128)(2,1)} %reshape.251), calls=%async_computation.3 | async-start | bytes 524288 | tf_op jit(solution)/shard_map/all_to_all | solution.py:164
  122.5 51.0 %copy-start.42 = (f32[2,128]{1,0:T(2,128)}, f32[2,128]{1,0:T(2,128)S(1)}, u32[]{:S(2)}) copy-start(f32[2,128]{1,0:T(2,128)S(1)} %get-tuple-element.748) | copy-start | bytes 3076
  124.8 12.8 %copy-start.8 = (bf16[2048,2,4]{2,1,0:T(2,128)(2,1)}, bf16[2048,2,4]{2,1,0:T(2,128)(2,1)S(1)}, u32[]{:S(2)}) copy-start(bf16[2048,2,4]{2,1,0:T(2,128)(2,1)S(1)} %reshape.254) | copy-start | bytes 98308
  132.9 10.8 %copy-start.58 = (f32[2]{0:T(128)S(1)}, f32[2]{0:T(128)}, u32[]{:S(2)}) copy-start(f32[2]{0:T(128)} %get-tuple-element.721) | copy-start | bytes 28
  132.9 30.7 %all-to-all-start.1 = ((bf16[2,256,2048]{1,0,2:T(2,128)(2,1)}), bf16[2,256,2048]{1,0,2:T(2,128)(2,1)S(1)}, u32[]{:S(2)}, u32[]{:S(2)}) async-start(bf16[2,256,2048]{1,0,2:T(2,128)(2,1)} %copy.404), calls=%async_computation.1 | async-start | bytes 4194304 | tf_op jit(solution)/shard_map/all_to_all | solution.py:157
  137.0 270.6 %all-gather.7.cloned.1.call-start = ((), (), s32[]{:S(2)}) async-start(), calls=%async_computation.20 | async-start | bytes 37748736 | tf_op jit(solution)/shard_map/all_gather | solution.py:23
  143.7 29.8 %copy-start.35 = (f32[2,32,2]{1,2,0:T(2,128)}, f32[2,32,2]{1,2,0:T(2,128)S(1)}, u32[]{:S(2)}) copy-start(f32[2,32,2]{1,2,0:T(2,128)S(1)} %slice_reduce_fusion) | copy-start | bytes 1540
  168.2 5.3 copy-start.55
  168.2 5.3 copy-start.57
  171.1 3.6 copy-start.41
  172.0 2.1 collective-permute-start
  173.7 25.5 %copy-start.15 = (f32[2,32,2,128]{3,2,1,0:T(2,128)}, f32[2,32,2,128]{3,2,1,0:T(2,128)S(1)}, u32[]{:S(2)}) copy-start(f32[2,32,2,128]{3,2,1,0:T(2,128)S(1)} %copy.433) | copy-start | bytes 196612
  293.9 52.9 %all-to-all-start.11 = ((bf16[2,256,2048]{1,0,2:T(2,128)(2,1)}), bf16[2,256,2048]{1,0,2:T(2,128)(2,1)S(1)}, u32[]{:S(2)}, u32[]{:S(2)}) async-start(bf16[2,256,2048]{1,0,2:T(2,128)(2,1)} %copy.452), calls=%async_computation.11 | async-start | bytes 4194304 | tf_op jit(solution)/shard_map/all_to_all | solution.py:185
  297.5 272.9 %all-gather.9.cloned.1.call-start = ((), (), s32[]{:S(2)}) async-start(), calls=%async_computation.21 | async-start | bytes 37748736 | tf_op jit(solution)/shard_map/all_gather | solution.py:23
  354.3 5.2 copy-start.54
  363.9 9.3 copy-start.39
  456.4 4.4 copy-start.44
  460.8 4.9 copy-start
  470.8 5.3 copy-start
  483.2 9.5 copy-start.22
  492.7 11.5 %slice-start = ((s8[8388608]{0:T(1024)(128)(4,1)}), s8[4194304]{0:T(1024)(128)(4,1)S(1)}, s32[]{:S(2)}) async-start(s8[8388608]{0:T(1024)(128)(4,1)} %bitcast.347), calls=%async_computation.22 | async-start | bytes 8388608
  495.2 9.0 slice-start.1
  626.7 6.2 copy-start.2
  639.4 6.2 copy-start.2
  652.6 12.4 %copy-start.3 = (f32[2,2,32,64,256]{4,3,2,1,0:T(8,128)S(1)}, f32[2,2,32,64,256]{4,3,2,1,0:T(8,128)}, u32[]{:S(2)}) copy-start(f32[2,2,32,64,256]{4,3,2,1,0:T(8,128)} %get-tuple-element.458) | copy-start | bytes 25165828
  652.6 12.4 %copy-start.4 = (f32[2,32,64,2,128]{4,3,2,1,0:T(2,128)S(1)}, f32[2,32,64,2,128]{4,3,2,1,0:T(2,128)}, u32[]{:S(2)}) copy-start(f32[2,32,64,2,128]{4,3,2,1,0:T(2,128)} %reshape.212) | copy-start | bytes 12582916
  665.0 9.6 copy-start.16
  665.1 9.6 copy-start.19
  665.1 9.6 copy-start.34
  665.1 9.6 copy-start.40
  665.1 9.6 copy-start.62
  674.7 12.1 %copy-start.17 = (f32[2,32,2,128]{3,2,1,0:T(2,128)S(1)}, f32[2,32,2,128]{3,2,1,0:T(2,128)}, u32[]{:S(2)}) copy-start(f32[2,32,2,128]{3,2,1,0:T(2,128)} %get-tuple-element.752) | copy-start | bytes 196612
  674.8 12.1 %copy-start.36 = (f32[2,32,2]{1,2,0:T(2,128)S(1)}, f32[2,32,2]{1,2,0:T(2,128)}, u32[]{:S(2)}) copy-start(f32[2,32,2]{1,2,0:T(2,128)} %copy-done.35) | copy-start | bytes 1540
  674.8 12.1 %copy-start.43 = (f32[2,128]{1,0:T(2,128)S(1)}, f32[2,128]{1,0:T(2,128)}, u32[]{:S(2)}) copy-start(f32[2,128]{1,0:T(2,128)} %copy-done.42) | copy-start | bytes 3076
  674.8 12.3 %copy-start.59 = (f32[2]{0:T(128)S(1)}, f32[2]{0:T(128)}, u32[]{:S(2)}) copy-start(f32[2]{0:T(128)} %get-tuple-element.721) | copy-start | bytes 28
  695.4 6.5 copy-start.10
  695.4 6.5 copy-start.31
  701.8 8.1 copy-start.25
  701.8 8.1 copy-start.27
  701.8 8.1 copy-start.29
  701.9 8.1 copy-start.46
  701.9 8.1 copy-start.48
  701.9 8.1 copy-start.50
  728.1 22.3 %collective-permute-start.1 = (f32[2,2560,3]{1,0,2:T(2,128)S(1)}, f32[2,2560,3]{1,0,2:T(2,128)S(1)}, u32[]{:S(2)}, u32[]{:S(2)}) collective-permute-start(f32[2,2560,3]{1,0,2:T(2,128)S(1)} %copy.478), channel_id=1, source_target_pairs={{4,0},{8,4},{12,8},{16,12},{20,16},{24,20},{28,24},{5,1},{9,5},{13... | collective-permute-start | bytes 184328 | tf_op jit(solution)/shard_map/ppermute | solution.py:18
  730.6 9.5 all-to-all-start.18
  745.8 11.9 %all-to-all-start.19 = ((bf16[4,2,2048]{2,1,0:T(2,128)(2,1)}), bf16[4,2,2048]{2,1,0:T(2,128)(2,1)S(1)}, u32[]{:S(2)}, u32[]{:S(2)}) async-start(bf16[4,2,2048]{2,1,0:T(2,128)(2,1)} %reshape.259), calls=%async_computation.19 | async-start | bytes 65536 | tf_op jit(solution)/shard_map/all_to_all | solution.py:281
  757.7 10.5 %all-to-all-start.14 = ((bf16[2,256,256]{2,0,1:T(2,128)(2,1)}), bf16[2,256,256]{2,0,1:T(2,128)(2,1)S(1)}, u32[]{:S(2)}, u32[]{:S(2)}) async-start(bf16[2,256,256]{2,0,1:T(2,128)(2,1)} %copy.486), calls=%async_computation.14 | async-start | bytes 524288 | tf_op jit(solution)/shard_map/all_to_all | solution.py:268
  761.3 34.5 %copy-start.23 = (f32[2,32,2,128]{3,2,1,0:T(2,128)S(1)}, f32[2,32,2,128]{3,2,1,0:T(2,128)}, u32[]{:S(2)}) copy-start(f32[2,32,2,128]{3,2,1,0:T(2,128)} %copy.443) | copy-start | bytes 196612
  768.3 10.3 %all-to-all-start.16 = ((bf16[2,256,256]{2,0,1:T(2,128)(2,1)}), bf16[2,256,256]{2,0,1:T(2,128)(2,1)S(1)}, u32[]{:S(2)}, u32[]{:S(2)}) async-start(bf16[2,256,256]{2,0,1:T(2,128)(2,1)} %copy.492), calls=%async_computation.16 | async-start | bytes 524288 | tf_op jit(solution)/shard_map/all_to_all | solution.py:275
  778.5 13.9 %all-to-all-start.15 = ((bf16[4,2,16384]{2,1,0:T(2,128)(2,1)}), bf16[4,2,16384]{2,1,0:T(2,128)(2,1)S(1)}, u32[]{:S(2)}, u32[]{:S(2)}) async-start(bf16[4,2,16384]{2,1,0:T(2,128)(2,1)} %reshape.255), calls=%async_computation.15 | async-start | bytes 524288 | tf_op jit(solution)/shard_map/all_to_all | solution.py:267
  792.4 27.0 %all-to-all-start.17 = ((bf16[4,2,16384]{2,1,0:T(2,128)(2,1)}), bf16[4,2,16384]{2,1,0:T(2,128)(2,1)S(1)}, u32[]{:S(2)}, u32[]{:S(2)}) async-start(bf16[4,2,16384]{2,1,0:T(2,128)(2,1)} %reshape.257), calls=%async_computation.17 | async-start | bytes 524288 | tf_op jit(solution)/shard_map/all_to_all | solution.py:274
  819.4 6.7 copy-start.13
  819.4 31.2 %all-to-all-start.8 = ((bf16[2,2048,256]{2,0,1:T(2,128)(2,1)}), bf16[2,2048,256]{2,0,1:T(2,128)(2,1)}, u32[]{:S(2)}, u32[]{:S(2)}) async-start(bf16[2,2048,256]{2,0,1:T(2,128)(2,1)} %reshape.246), calls=%async_computation.8 | async-start | bytes 4194304 | tf_op jit(solution)/shard_map/all_to_all | solution.py:254
  850.6 30.2 %all-to-all-start.12 = ((bf16[2,2048,256]{2,0,1:T(2,128)(2,1)}), bf16[2,2048,256]{2,0,1:T(2,128)(2,1)S(1)}, u32[]{:S(2)}, u32[]{:S(2)}) async-start(bf16[2,2048,256]{2,0,1:T(2,128)(2,1)} %copy.480), calls=%async_computation.12 | async-start | bytes 4194304 | tf_op jit(solution)/shard_map/all_to_all | solution.py:261
  882.1 50.4 %all-to-all-start.9 = ((bf16[2,256,2048]{1,0,2:T(2,128)(2,1)}), bf16[2,256,2048]{1,0,2:T(2,128)(2,1)S(1)}, u32[]{:S(2)}, u32[]{:S(2)}) async-start(bf16[2,256,2048]{1,0,2:T(2,128)(2,1)} %copy.448), calls=%async_computation.9 | async-start | bytes 4194304 | tf_op jit(solution)/shard_map/all_to_all | solution.py:253
  894.2 42.9 %copy-start.33 = (bf16[4,2,2048]{2,1,0:T(2,128)(2,1)S(1)}, bf16[4,2,2048]{2,1,0:T(2,128)(2,1)}, u32[]{:S(2)}) copy-start(bf16[4,2,2048]{2,1,0:T(2,128)(2,1)} %copy-done.32) | copy-start | bytes 98308
  932.5 52.4 %all-to-all-start.13 = ((bf16[2,256,2048]{1,0,2:T(2,128)(2,1)}), bf16[2,256,2048]{1,0,2:T(2,128)(2,1)}, u32[]{:S(2)}, u32[]{:S(2)}) async-start(bf16[2,256,2048]{1,0,2:T(2,128)(2,1)} %copy.483), calls=%async_computation.13 | async-start | bytes 4194304 | tf_op jit(solution)/shard_map/all_to_all | solution.py:260
  (25 other events, 64.7 us)
Sparse Core Ops, SparseCore 0:
  223.1 184.4 all-gather.6
  409.5 160.7 all-gather.8
where the time goes:
time: 1010 us; the launch traced here: 996 us
  waiting for transfers between devices  285 us (28%)
  local copies, waits for them, and re-layouts  243 us (24%)
  other arithmetic  184 us (18%)
  matrix products  105 us (10%)
  blocking collectives  93.3 us (9%)
  starting transfers between devices  69.1 us (7%)
  between operations  15.5 us (2%)
    select_n x16, other arithmetic, lap(): return jax.tree.map(lambda a, b: jnp.where(reached, a, b), new, before)  96.1 us
    all_gather x2, waiting for transfers between devices, carried_in(): everything = jax.tree.map(lambda part: lax.all_gather(part, axis), array)  77.8 us
    all_to_all x1, blocking collectives, shards(): lax.all_to_all(cotangent, 'head', split_axis=0, concat_axis=2, tiled=True)  52.5 us
    all_to_all x1, waiting for transfers between devices, shards(): lax.all_to_all(lax.all_to_all(cotangent, 'head', split_axis=0, concat_axi...  48.8 us
    unnamed x142, local copies, waits for them, and re-layouts  41.8 us
    dot_general x3, matrix products, span_terms(): jnp.einsum('hcij,hpcj->hpci', decay * scores[None], weighted, precision=p...  39.4 us
    all_to_all x1, waiting for transfers between devices, shards(): lax.all_to_all(x_in, 'head', split_axis=0, concat_axis=2, tiled=True)  37.1 us
    all_to_all x1, waiting for transfers between devices, shards(): lax.all_to_all(lax.all_to_all(y_half, 'seq', split_axis=1, concat_axis=2,...  32.4 us
  transfers between devices with their start and end apart: 20, of which 16 were waited for; matrix products, arithmetic and copies ran while one was open for 30% of the time, Pallas kernels for 0%

commit v1 on v0

--- a/solution.py
+++ b/solution.py
@@ -153,51 +153,33 @@
 def shards(
     x_in, b_in, c_in, dt_raw, cotangent, conv_weight, conv_bias, dt_bias, a_log, d_skip, doc_lengths
 ):
-    x_scan, b_scan, c_scan, dt_scan, cot_scan = (
-        lax.all_to_all(
-            lax.all_to_all(x_in, "head", split_axis=0, concat_axis=2, tiled=True),
-            "seq",
-            split_axis=2,
-            concat_axis=1,
-            tiled=True,
-        ),
-        lax.all_to_all(
-            lax.all_to_all(b_in, "head", split_axis=0, concat_axis=2, tiled=True),
-            "seq",
-            split_axis=2,
-            concat_axis=1,
-            tiled=True,
-        ),
-        lax.all_to_all(
-            lax.all_to_all(c_in, "head", split_axis=0, concat_axis=2, tiled=True),
-            "seq",
-            split_axis=2,
-            concat_axis=1,
-            tiled=True,
-        ),
-        lax.all_to_all(
-            lax.all_to_all(dt_raw, "head", split_axis=0, concat_axis=2, tiled=True),
-            "seq",
-            split_axis=2,
-            concat_axis=1,
-            tiled=True,
-        ),
-        lax.all_to_all(
-            lax.all_to_all(cotangent, "head", split_axis=0, concat_axis=2, tiled=True),
-            "seq",
-            split_axis=2,
-            concat_axis=1,
-            tiled=True,
-        ),
-    )
-    groups_here = x_scan.shape[0]
-    x_width = x_scan.shape[1]
-    n_heads = dt_scan.shape[1]
-    length = x_scan.shape[2]
+    lane = lax.axis_index("seq")
+    x_width = x_in.shape[1]
+    n_heads = dt_raw.shape[1]
+    length = x_in.shape[2]
     blocks = length // SPAN
-    raw_chan = jnp.concatenate([x_scan, b_scan, c_scan], axis=1)
-    rim_chan = passed_along(raw_chan[:, :, length - (TAPS - 1) :], "seq", 1)
-    rank = lax.axis_index("seq")
+    b_full = lax.all_gather(b_in, "seq", axis=1, tiled=True)
+    c_full = lax.all_gather(c_in, "seq", axis=1, tiled=True)
+    weight_all = lax.all_gather(conv_weight, "head", axis=0, tiled=True)
+    bias_all = lax.all_gather(conv_bias, "head", axis=0, tiled=True)
+    dt_bias_all = lax.all_gather(dt_bias, "head", axis=0, tiled=True)
+    a_log_all = lax.all_gather(a_log, "head", axis=0, tiled=True)
+    d_skip_all = lax.all_gather(d_skip, "head", axis=0, tiled=True)
+    x_total = weight_all.shape[2] - 2 * STATE
+
+    def own_channels(table):
+        mine = lax.dynamic_slice_in_dim(table, lane * x_width, x_width, axis=table.ndim - 1)
+        return jnp.concatenate([mine, table[..., x_total:]], axis=table.ndim - 1)
+
+    weight_here = own_channels(weight_all)
+    bias_here = own_channels(bias_all)
+    dt_bias_here = lax.dynamic_slice_in_dim(dt_bias_all, lane * n_heads, n_heads, axis=1)
+    a_log_here = lax.dynamic_slice_in_dim(a_log_all, lane * n_heads, n_heads, axis=1)
+    d_skip_here = lax.dynamic_slice_in_dim(d_skip_all, lane * n_heads, n_heads, axis=1)
+    groups_here = x_in.shape[0]
+    raw_chan = jnp.concatenate([x_in, b_full, c_full], axis=1)
+    rim_chan = passed_along(raw_chan[:, :, length - (TAPS - 1) :], "head", 1)
+    rank = lax.axis_index("head")
     positions = rank * length + jnp.arange(-(TAPS - 1), length, dtype=jnp.int32)
     segment_extended = segment_ids(positions, doc_lengths)
 
@@ -206,11 +188,11 @@
             raw_float,
             rim_float,
             dt_float,
-            conv_weight,
-            conv_bias,
-            dt_bias,
-            a_log,
-            d_skip,
+            weight_here,
+            bias_here,
+            dt_bias_here,
+            a_log_here,
+            d_skip_here,
             segment_extended,
         )
 
@@ -218,14 +200,14 @@
         local_terms,
         raw_chan.astype(jnp.float32),
         rim_chan.astype(jnp.float32),
-        dt_scan.astype(jnp.float32),
+        dt_raw.astype(jnp.float32),
     )
     y_intra, c_three, entry, carry, states = terms
     before, total = reach(carry)
     state_zero = jnp.zeros((groups_here, n_heads, HEAD_DIM, STATE), jnp.float32)
     _, summary = jax.vmap(span_fold)(carry, states, state_zero)
     identity = (jnp.ones_like(total), jnp.zeros_like(summary))
-    state_in = carried_in((total, summary), "seq", compose_fwd, identity, False)[1]
+    state_in = carried_in((total, summary), "head", compose_fwd, identity, False)[1]
 
     def finish(pieces, state_start):
         return jax.vmap(assemble)(
@@ -233,59 +215,26 @@
         )
 
     (y_scan, state_out), pull_out = jax.vjp(finish, terms, state_in)
-    y_half = y_scan.astype(jnp.bfloat16)
-    cot_float = cot_scan.astype(jnp.float32)
+    y_out = y_scan.astype(jnp.bfloat16)
+    cot_float = cotangent.astype(jnp.float32)
     cot_five = cot_float.reshape(groups_here, n_heads, HEAD_DIM, blocks, SPAN)
     local_grad = jnp.einsum(
         "ghpci,ghci,gnci->ghpn", cot_five, entry * before[..., None], c_three, precision=precise
     )
-    grad_out = carried_in((total, local_grad), "seq", compose_back, identity, True)[1]
+    grad_out = carried_in((total, local_grad), "head", compose_back, identity, True)[1]
     d_terms, _ = pull_out((cot_float, grad_out))
     d_raw, d_rim, d_dt = pull_terms(d_terms)
-    returned = passed_along(d_rim, "seq", -1)
+    returned = passed_along(d_rim, "head", -1)
     cut_at = length - (TAPS - 1)
     d_raw = jnp.concatenate([d_raw[:, :, :cut_at], d_raw[:, :, cut_at:] + returned], axis=2)
-    grad_x = d_raw[:, :x_width].astype(jnp.bfloat16)
-    grad_b = d_raw[:, x_width : x_width + STATE].astype(jnp.bfloat16)
-    readout_gradient = d_raw[:, x_width + STATE :].astype(jnp.bfloat16)
-    grad_dt = d_dt.astype(jnp.bfloat16)
-    y_out, x_grad, b_grad, c_grad, dt_grad = (
-        lax.all_to_all(
-            lax.all_to_all(y_half, "seq", split_axis=1, concat_axis=2, tiled=True),
-            "head",
-            split_axis=2,
-            concat_axis=0,
-            tiled=True,
-        ),
-        lax.all_to_all(
-            lax.all_to_all(grad_x, "seq", split_axis=1, concat_axis=2, tiled=True),
-            "head",
-            split_axis=2,
-            concat_axis=0,
-            tiled=True,
-        ),
-        lax.all_to_all(
-            lax.all_to_all(grad_b, "seq", split_axis=1, concat_axis=2, tiled=True),
-            "head",
-            split_axis=2,
-            concat_axis=0,
-            tiled=True,
-        ),
-        lax.all_to_all(
-            lax.all_to_all(readout_gradient, "seq", split_axis=1, concat_axis=2, tiled=True),
-            "head",
-            split_axis=2,
-            concat_axis=0,
-            tiled=True,
-        ),
-        lax.all_to_all(
-            lax.all_to_all(grad_dt, "seq", split_axis=1, concat_axis=2, tiled=True),
-            "head",
-            split_axis=2,
-            concat_axis=0,
-            tiled=True,
-        ),
-    )
+    x_grad = d_raw[:, :x_width].astype(jnp.bfloat16)
+    b_grad = lax.psum_scatter(
+        d_raw[:, x_width : x_width + STATE], "seq", scatter_dimension=1, tiled=True
+    ).astype(jnp.bfloat16)
+    c_grad = lax.psum_scatter(
+        d_raw[:, x_width + STATE :], "seq", scatter_dimension=1, tiled=True
+    ).astype(jnp.bfloat16)
+    dt_grad = d_dt.astype(jnp.bfloat16)
     return (y_out, x_grad, b_grad, c_grad, dt_grad)
 
 

time: 1010 us -> 782 us (0.77)
  local copies, waits for them, and re-layouts: 243 us -> 138 us
  starting transfers between devices: 69.1 us -> 3.21 us
  waiting for transfers between devices: 285 us -> 234 us
  matrix products: 105 us -> 150 us
  other arithmetic: 184 us -> 161 us
  blocking collectives: 93.3 us -> 74.8 us
    all_to_all x16 -> x0, waiting for transfers between devices: 207 us -> none  [the longest x1 48.8 us: shards(): lax.all_to_all(lax.all_to_all(cotangent, 'head', split_axis=0, concat_axi...]
    all_to_all x34 -> x0, local copies, waits for them, and re-layouts: 88.5 us -> none  [the longest x2 16.8 us: shards(): lax.all_to_all(cotangent, 'head', split_axis=0, concat_axis=2, tiled=True)]
    all_to_all x4 -> x0, blocking collectives: 85.3 us -> none  [the longest x1 52.5 us: shards(): lax.all_to_all(cotangent, 'head', split_axis=0, concat_axis=2, tiled=True)]
    all_gather x2, waiting for transfers between devices: 77.8 us -> 158 us  [carried_in(): everything = jax.tree.map(lambda part: lax.all_gather(part, axis), array)]
    reduce_scatter x0 -> x2, waiting for transfers between devices: none -> 75.1 us  [the longest x1 53.1 us: shards(): lax.psum_scatter(d_raw[:, x_width + STATE:], 'seq', scatter_dimension=1,...]
    select_n x16 -> x8, other arithmetic: 96.1 us -> 24.1 us  [lap(): return jax.tree.map(lambda a, b: jnp.where(reached, a, b), new, before)]
    all_to_all x16 -> x0, starting transfers between devices: 65.3 us -> none  [the longest x1 5.49 us: shards(): lax.all_to_all(lax.all_to_all(grad_b, 'seq', split_axis=1, concat_axis=2,...]
    all_gather x0 -> x5, blocking collectives: none -> 58.3 us  [the longest x1 14.4 us: shards(): weight_all = lax.all_gather(conv_weight, 'head', axis=0, tiled=True)]
  transfers between devices with their start and end apart: 20 -> 8, of which waited for: 16 -> 5; matrix products, arithmetic and copies ran while one was open for 30% -> 25% of each run, Pallas kernels for 0% -> 0%
where the time goes in v1:
time: 782 us; the launch traced here: 777 us
  waiting for transfers between devices  234 us (30%)
  other arithmetic  161 us (21%)
  matrix products  150 us (19%)
  local copies, waits for them, and re-layouts  138 us (18%)
  blocking collectives  74.8 us (10%)
  between operations  15.3 us (2%)
    all_gather x2, waiting for transfers between devices, carried_in(): everything = jax.tree.map(lambda part: lax.all_gather(part, axis), array)  158 us
    reduce_scatter x1, waiting for transfers between devices, shards(): lax.psum_scatter(d_raw[:, x_width + STATE:], 'seq', scatter_dimension=1,...  53.1 us
    dot_general x3, matrix products, assemble(): jnp.einsum('nci,hci,chpn->hpci', c_three, entry, starts, precision=precise)  45.4 us
    dot_general x3, matrix products, span_terms(): jnp.einsum('hcij,hpcj->hpci', decay * scores[None], weighted, precision=p...  38.7 us
    dot_general x3, matrix products, span_terms(): jnp.einsum('hpcj,hcj,ncj->hcpn', weighted, keep_end, b_three, precision=p...  36.6 us
    reshape x4, local copies, waits for them, and re-layouts, span_terms(): x_four = x_conv.reshape(n_heads, HEAD_DIM, blocks, SPAN)  33.9 us
    mul x2, other arithmetic, conv_silu(): weight[offset][:, None] * padded[:, offset:offset + length]  33.8 us
    mul x1, other arithmetic, conv_silu(): return jax.nn.silu(total)  26.7 us
  transfers between devices with their start and end apart: 8, of which 5 were waited for; matrix products, arithmetic and copies ran while one was open for 25% of the time, Pallas kernels for 0%

profile of v1, /device:TPU:0, one launch (start us, length us, event | category | flops | bytes accessed | tf_op | source)
XLA Modules:
  0.0 776.5 jit_solution(3816300401636666235)
XLA Ops:
  13.0 12.8 %all-gather.5 = f32[4,2,32]{2,1,0:T(2,128)S(1)} all-gather(f32[1,2,32]{2,1,0:T(2,128)} %bitcast.277), channel_id=1, replica_groups=mesh['seq'=8,'head'=4] {'head'}, dimensions={0}, use_global_device_ids=true | all-gather | bytes 1280 | tf_op jit(solution)/shard_map/all_gather | solution.py:166
  25.8 7.9 %all-gather.6 = f32[4,2,32]{2,1,0:T(2,128)S(1)} all-gather(f32[1,2,32]{2,1,0:T(2,128)} %bitcast.278), channel_id=1, replica_groups=mesh['seq'=8,'head'=4] {'head'}, dimensions={0}, use_global_device_ids=true | all-gather | bytes 1280 | tf_op jit(solution)/shard_map/all_gather | solution.py:167
  34.4 9.7 %all-gather.4 = f32[4,2,32]{2,1,0:T(2,128)S(1)} all-gather(f32[1,2,32]{2,1,0:T(2,128)} %bitcast.279), channel_id=1, replica_groups=mesh['seq'=8,'head'=4] {'head'}, dimensions={0}, use_global_device_ids=true | all-gather | bytes 1280 | tf_op jit(solution)/shard_map/all_gather | solution.py:165
  46.6 14.4 %all_gather.42 = f32[8,4,2560]{2,1,0:T(4,128)S(1)} all-gather(f32[2,4,2560]{2,1,0:T(4,128)} %param.28), channel_id=1, replica_groups=mesh['seq'=8,'head'=4] {'head'}, dimensions={0}, use_global_device_ids=true | all-gather | bytes 409600 | tf_op jit(solution)/shard_map/all_gather | solution.py:163
  61.0 13.4 %all-gather.3 = f32[4,2,2560]{2,1,0:T(2,128)S(1)} all-gather(f32[1,2,2560]{2,1,0:T(2,128)} %bitcast.272), channel_id=1, replica_groups=mesh['seq'=8,'head'=4] {'head'}, dimensions={0}, use_global_device_ids=true | all-gather | bytes 102400 | tf_op jit(solution)/shard_map/all_gather | solution.py:164
  78.0 4.3 copy.281
  82.3 4.3 copy.282
  86.6 6.7 pad_maximum_fusion.1
  96.4 26.7 %fusion.17 = (f32[8,768,512]{1,2,0:T(8,128)}, f32[8,768,512]{1,2,0:T(8,128)}) fusion(f32[8,768,512]{1,2,0:T(8,128)} %get-tuple-element.735, f32[8,768]{1,0:T(8,128)S(1)} %get-tuple-element.741, f32[512]{0:T(512)S(1)} %get-tuple-element.748, f32[8,768,3]{1,2,0:T(4,128)S(1)} %convert_element_type.70, f32[8,768]{1,0:T(8,128)S(1)} %get-tuple-element.742, ...), kind=kLoop, calls=%fused_computation.48 | loop fusion | flops 56623104 | bytes 37951488 | tf_op jit(solution)/shard_map/jvp(vmap(jit(silu)))/mul | solution.py:55
  123.1 9.7 %fusion.141 = (f32[8,256,512]{1,2,0:T(8,128)}, f32[8,256,512]{1,2,0:T(8,128)}, f32[8,256,512]{1,2,0:T(8,128)}) fusion(f32[8,768,512]{1,2,0:T(8,128)} %get-tuple-element.722), kind=kLoop, calls=%fused_computation.213 | loop fusion | bytes 25165824 | tf_op jit(solution)/shard_map/jvp(vmap())/slice | solution.py:95
  132.8 8.0 %reshape.234 = f32[8,4,64,4,128]{2,1,4,3,0:T(4,128)} reshape(f32[8,256,512]{1,2,0:T(8,128)} %get-tuple-element.731) | data formatting | bytes 8388608 | tf_op jit(solution)/shard_map/jvp(vmap())/reshape | solution.py:61
  140.8 8.6 %copy.287 = f32[8,4,64,4,128]{4,2,3,1,0:T(8,128)} copy(f32[8,4,64,4,128]{2,1,4,3,0:T(4,128)} %reshape.234) | data formatting | bytes 8388608 | tf_op jit(solution)/shard_map/jvp(vmap())/reshape | solution.py:61
  149.4 10.3 %fusion.68 = f32[4,8,4,64,256]{4,3,2,0,1:T(8,128)S(1)} fusion(f32[8,256,4,128,1]{1,3,4,2,0:T(8,128)} %bitcast.260, f32[8,4,64,4,128]{4,2,3,1,0:T(8,128)} %copy.287, f32[8,4,4,128]{3,2,1,0:T(4,128)S(1)} %copy.297, f32[8,4,4,128]{3,2,1,0:T(4,128)S(1)} %copy.286), kind=kOutput, calls=%fused_computation.116 | convolution fusion | flops 3223322624 | bytes 16908288 | tf_op jit(solution)/shard_map/jvp(vmap(hpcj,hcj,ncj->hcpn))/dot_general | solution.py:80
  159.7 3.9 copy.301
  163.6 8.3 %while.89 = (s32[]{:T(128)}, f32[8,4,64,256]{3,2,1,0:T(8,128)S(1)}, f32[4,8,4]{1,2,0:T(4,128)S(1)}, f32[4,8,4,64,256]{4,3,2,1,0:T(8,128)}, s32[]{:T(128)}, /*index=5*/s32[]{:T(128)}) while((s32[]{:T(128)}, f32[8,4,64,256]{3,2,1,0:T(8,128)S(1)}, f32[4,8,4]{1,2,0:T(4,128)S(1)}, f32[4,8,4,64,256]{4,3,2,1,0:T(8,128)}, s32[]{:T(128)}, ...), condition=%wide.region_5.6_spmd.clone, body=%wide.region_4.5_spmd.clone.sunk | while | flops 1572867 | bytes 6292183 | solution.py:118
  176.1 7.8 fusion.90
  184.2 16.5 %all-gather.7 = f32[4,8,4]{1,2,0:T(4,128)S(1)} all-gather(f32[1,8,4]{1,2,0:T(4,128)S(1)} %bitcast.270), channel_id=2, replica_groups=mesh['seq'=8,'head'=4] {'head'}, dimensions={0}, use_global_device_ids=true | all-gather | bytes 640 | tf_op jit(solution)/shard_map/all_gather | solution.py:23
  200.8 7.9 %fusion.142 = f32[8,4,128,128]{2,3,1,0:T(8,128)S(1)} fusion(f32[8,256,4,128]{1,3,2,0:T(8,128)} %bitcast.256, f32[8,256,4,128]{1,3,2,0:T(8,128)} %bitcast.261), kind=kOutput, calls=%fused_computation.214 | convolution fusion | flops 1610612736 | bytes 10485760 | tf_op jit(solution)/shard_map/jvp(vmap(nci,ncj->cij))/dot_general | solution.py:74
  208.8 14.4 %fusion.97 = (f32[8,4,4,128]{3,2,1,0:T(4,128)}, f32[8,4,4,128]{3,2,1,0:T(4,128)}, f32[8,4,128,128]{2,3,1,0:T(8,128)S(1)}) fusion(f32[8,4,4,128]{3,2,1,0:T(4,128)S(1)} %copy.289, f32[4,128,128]{1,2,0:T(8,128)S(1)} %compare_select_fusion, f32[8,4,128,128]{2,3,1,0:T(8,128)S(1)} %fusion.142, bf16[8,4,4,64,128]{4,2,3,1,0:T(4,128)(2,1)S(1)} %bitcast.264, ...), kind=kOutput, calls=%fused_computation.132 | convolution fusion | flops 1642561536 | bytes 11010048 | tf_op jit(solution)/shard_map/transpose(jvp(vmap(hcij,hpcj->hpci)))/dot_general | solution.py:76
  224.6 5.1 fusion.143
  229.7 94.6 %all-gather.17.cloned.1.call-done = f32[32,4,64,256]{3,2,1,0:T(8,128)} async-done(((f32[8,4,64,256]{3,2,1,0:T(8,128)}), f32[32,4,64,256]{3,2,1,0:T(8,128)}) %all-gather.17.cloned.1.call-update) | async-done | bytes 8388624 | tf_op jit(solution)/shard_map/all_gather | solution.py:23
  324.3 16.0 %while.90 = (s32[]{:T(128)}, f32[8,4,64,256]{3,2,1,0:T(8,128)}, s32[]{:T(128)}, f32[4,8,4]{1,2,0:T(4,128)S(1)}, f32[4,8,4,64,256]{4,3,2,1,0:T(8,128)}, /*index=5*/s32[]{:T(128)}, s32[]{:T(128)}) while((s32[]{:T(128)}, f32[8,4,64,256]{3,2,1,0:T(8,128)}, s32[]{:T(128)}, f32[4,8,4]{1,2,0:T(4,128)S(1)}, ...), condition=%wide.region_7.8_spmd.clone, body=%wide.region_6.7_spmd.clone.sunk | while | flops 2097156 | bytes 6292201 | solution.py:36
  324.4 3.2 fusion.162
  327.7 3.9 fusion.162
  331.7 4.5 fusion.162
  336.2 4.1 fusion.162
  340.4 4.4 broadcast.102.clone
  344.8 28.3 %while.86 = (s32[]{:T(128)}, f32[8,4,64,256]{3,2,1,0:T(8,128)}, f32[4,8,4,64,256]{4,3,2,1,0:T(8,128)}, f32[4,8,4,1,1]{1,2,4,3,0:T(4,128)S(1)}, f32[4,8,4]{1,2,0:...) while((s32[]{:T(128)}, f32[8,4,64,256]{3,2,1,0:T(8,128)}, f32[4,8,4,64,256]{4,3,2,1,0:T(8,128)}, ...), condition=%wide.region_9.10_spmd, body=%wide.region_8.9_spmd.sunk | while | flops 1048578 | bytes 10491097 | solution.py:118
  344.9 3.1 bitcast_dynamic-update-slice_fusion.8
  348.0 3.8 bitcast_add_fusion.11
  351.9 3.1 bitcast_dynamic-update-slice_fusion.8
  355.0 3.8 bitcast_add_fusion.11
  359.0 3.1 bitcast_dynamic-update-slice_fusion.8
  362.1 3.8 bitcast_add_fusion.11
  366.0 3.2 bitcast_dynamic-update-slice_fusion.8
  369.2 3.8 bitcast_add_fusion.11
  373.1 11.2 %fusion.36 = f32[8,4,4,64,128]{4,3,2,1,0:T(8,128)S(1)} fusion(f32[8,256,4,128,1]{1,3,4,2,0:T(8,128)} %bitcast.257, f32[4,8,4,64,256]{4,3,2,1,0:T(8,128)} %get-tuple-element.1061), kind=kOutput, calls=%fused_computation.68 | convolution fusion | flops 3221225472 | bytes 16777216 | tf_op jit(solution)/shard_map/jvp(vmap(nci,hci,chpn->hpci))/dot_general | solution.py:124
  389.3 21.4 %fusion.71 = f32[4,8,4,64,256]{4,3,2,0,1:T(8,128)} fusion(f32[8,256,4,128,1]{1,3,4,2,0:T(8,128)S(1)} %bitcast.258, f32[8,4,4,64,128]{4,3,1,2,0:T(8,128)S(1)} %get-tuple-element.739), kind=kOutput, calls=%fused_computation.117 | convolution fusion | flops 3221225472 | bytes 16777216 | tf_op jit(solution)/shard_map/transpose(jvp(vmap(nci,hci,chpn->hpci)))/dot_general | solution.py:124
  410.7 62.9 %all-gather.19.cloned.1.call-done = f32[32,4,64,256]{3,2,1,0:T(8,128)} async-done(((f32[8,4,64,256]{3,2,1,0:T(8,128)}), f32[32,4,64,256]{3,2,1,0:T(8,128)}) %all-gather.19.cloned.1.call-update) | async-done | bytes 8388624 | tf_op jit(solution)/shard_map/all_gather | solution.py:23
  473.7 8.9 %while.91 = (s32[]{:T(128)}, f32[8,4,64,256]{3,2,1,0:T(8,128)S(1)}, s32[]{:T(128)}, f32[4,8,4,64,256]{4,3,2,1,0:T(8,128)}, f32[4,8,4]{1,2,0:T(4,128)S(1)}, /*index=5*/s32[]{:T(128)}, s32[]{:T(128)}, s32[]{:T(128)}, s32[]{:T(128)}) while((s32[]{:T(128)}, f32[8,4,64,256]{3,2,1,0:T(8,128)S(1)}, s32[]{:T(128)}, ...), condition=%wide.region_12.13_spmd.clone, body=%wide.region_11.12_spmd.clone.sunk | while | flops 2097160 | bytes 6292263 | solution.py:36
  482.5 4.3 broadcast.102
  486.8 18.8 %while.87 = (s32[]{:T(128)}, f32[8,4,64,256]{3,2,1,0:T(8,128)S(1)}, f32[4,8,4]{1,0,2:T(4,128)S(1)}, f32[4,8,4,64,256]{4,3,2,1,0:T(8,128)}, f32[4,8,4,64,256]{4,3...) while((s32[]{:T(128)}, f32[8,4,64,256]{3,2,1,0:T(8,128)S(1)}, ...), condition=%wide.region_15.16_spmd, body=%wide.region_13.15_spmd.sunk | while | flops 2097123 | bytes 12584321 | solution.py:118
  488.5 3.0 fusion.161
  493.2 3.0 fusion.161
  497.9 3.0 fusion.161
  502.5 3.0 fusion.161
  505.7 14.6 %fusion.32 = f32[8,4,256,128,1]{2,3,4,1,0:T(8,128)} fusion(f32[4,8,4,64,256]{4,3,2,1,0:T(8,128)} %get-tuple-element.458, f32[8,4,64,4,128]{4,2,3,1,0:T(8,128)} %copy.287, f32[8,4,4,128]{3,2,1,0:T(4,128)S(1)} %copy.297, f32[8,4,4,128]{3,2,1,0:T(4,128)S(1)} %copy.286), kind=kOutput, calls=%fused_computation.64 | convolution fusion | flops 3223322624 | bytes 16908288 | tf_op jit(solution)/shard_map/transpose(jvp(vmap(hpcj,hcj,ncj->hcpn)))/dot_general | solution.py:80
  520.2 11.8 %fusion.47 = (f32[8,4,4,128]{3,2,1,0:T(4,128)S(1)}, f32[8,4,4,64,128]{4,3,1,2,0:T(8,128)}) fusion(f32[8,4,64,4,128]{4,2,3,1,0:T(8,128)S(1)} %copy-done.8, f32[8,4,4,128]{3,2,1,0:T(4,128)S(1)} %copy.286, f32[8,256,4,128,1]{1,3,2,4,0:T(8,128)S(1)} %bitcast.263, f32[4,8,4,64,256]{4,3,2,1,0:T(8,128)} %get-tuple-element.458), kind=kOutput, calls=%fused_computation.90 | convolution fusion | flops 3224354816 | bytes 21102592 | tf_op jit(solution)/shard_map/transpose(jvp(vmap(hpcj,hcj,ncj->hcpn)))/dot_general | solution.py:80
  532.1 12.7 %bitcast_add_fusion.6 = f32[8,4,128,256]{3,2,1,0:T(8,128)} fusion(f32[8,4,128,256]{3,2,1,0:T(8,128)} %fusion.143, f32[4,8,4,64,256]{4,3,2,1,0:T(8,128)S(1)} %bitcast.254, f32[8,4,4,64,128]{4,3,1,2,0:T(8,128)} %copy-done.9), kind=kOutput, calls=%fused_computation.91 | convolution fusion | flops 3222274048 | bytes 20971520 | tf_op jit(solution)/shard_map/transpose(jvp(vmap(nci,hci,chpn->hpci)))/dot_general | solution.py:124
  544.8 7.0 bitcast_add_fusion.5
  551.8 11.8 %fusion.45 = (f32[8,4,4,128]{3,2,1,0:T(4,128)S(1)}, f32[8,4,64,4,128]{4,2,3,1,0:T(8,128)}) fusion(f32[8,4,64,4,128]{4,2,3,1,0:T(8,128)S(1)} %copy-done.8, f32[8,4,4,128]{3,2,1,0:T(4,128)S(1)} %copy.286, bf16[8,4,64,4,128]{4,3,2,1,0:T(4,128)(2,1)S(1)} %copy-done.13, f32[8,4]{1,0:T(8,128)S(1)} %copy-done.53, bf16[8,4,4,64,128]{4,2,3,1,0:T(4,128)(2,1)S(1)} %bitcast.265, ...), kind=kOutput, calls=%fused_computation.86 | convolution fusion | flops 1627373568 | bytes 19398784 | tf_op jit(solution)/shard_map/transpose(jvp(vmap(hcij,hpcj->hpci)))/dot_general | solution.py:76
  563.6 8.3 %copy.386 = f32[8,4,64,4,128]{2,1,4,3,0:T(4,128)} copy(f32[8,4,64,4,128]{4,2,3,1,0:T(8,128)} %get-tuple-element.737) | data formatting | bytes 8388608 | tf_op jit(solution)/shard_map/transpose(jvp(vmap()))/reshape | solution.py:61
  571.9 9.0 %reshape.233 = f32[8,256,512]{1,2,0:T(8,128)} reshape(f32[8,4,64,4,128]{2,1,4,3,0:T(4,128)} %copy.386) | data formatting | bytes 8388608 | tf_op jit(solution)/shard_map/transpose(jvp(vmap()))/reshape | solution.py:61
  580.9 13.8 %broadcast_multiply_fusion = (f32[8,768,512]{1,2,0:T(8,128)S(1)}, f32[8,768,512]{1,2,0:T(8,128)}) fusion(f32[8,768]{1,0:T(8,128)S(1)} %copy-done.32, f32[8,768,512]{1,2,0:T(8,128)} %get-tuple-element.723, f32[8,256,512]{1,2,0:T(8,128)} %reshape.233, f32[8,256,512]{1,2,0:T(8,128)} %bitcast.267, f32[8,256,512]{1,2,0:T(8,128)} %bitcast.266), kind=kLoop, calls=%fused_computation.74 | loop fusion | flops 37748736 | bytes 50356224 | tf_op jit(solution)/shard_map/transpose(jvp(vmap()))/mul | solution.py:53
  594.8 20.0 %multiply_multiply_fusion.2 = (f32[8,768,512]{1,2,0:T(8,128)}, f32[8,768,512]{1,2,0:T(8,128)}, f32[8,768,512]{1,2,0:T(8,128)}) fusion(f32[8,768,512]{1,2,0:T(8,128)} %get-tuple-element.717, f32[512]{0:T(512)S(1)} %copy-done.44, f32[8,768]{1,0:T(8,128)S(1)} %copy-done.28, f32[512]{0:T(512)S(1)} %copy-done.46, f32[8,768]{1,0:T(8,128)S(1)} %copy-done.30, ...), kind=kLoop, calls=%fused_computation.46 | loop fusion | flops 18874368 | bytes 50411520 | tf_op jit(solution)/shard_map/transpose(jvp(vmap()))/mul | solution.py:53
  617.3 19.0 %pad_add_fusion = f32[8,768,515]{1,2,0:T(8,128)} fusion(f32[8,768,512]{1,2,0:T(8,128)} %get-tuple-element.730, f32[8,768,512]{1,2,0:T(8,128)} %get-tuple-element.729, f32[8,768,512]{1,2,0:T(8,128)} %get-tuple-element.728, f32[8,768,512]{1,2,0:T(8,128)S(1)} %get-tuple-element.716), kind=kLoop, calls=%fused_computation.28 | loop fusion | flops 9492480 | bytes 62988288 | tf_op jit(solution)/shard_map/transpose(jvp(vmap()))/add_any | solution.py:53
  636.3 10.5 %slice.128 = f32[8,768,509]{1,2,0:T(8,128)} slice(f32[8,768,515]{1,2,0:T(8,128)} %pad_add_fusion), slice={[0:8], [0:768], [3:512]} | slice | bytes 25018368 | tf_op jit(solution)/shard_map/slice | solution.py:229
  648.1 3.5 copy-done.3
  651.6 3.8 pad_maximum_fusion.2
  655.4 5.5 copy.333
  661.0 5.8 copy.334
  669.1 12.6 %fusion.48 = bf16[8,4,64,4,128]{4,2,3,1,0:T(8,128)(2,1)S(1)} fusion(f32[8,4,4,64,128]{4,3,2,1,0:T(8,128)} %copy-done.14, f32[8,4,64,4,128]{4,2,3,1,0:T(8,128)} %copy.287, f32[8,4,128,128]{2,3,1,0:T(8,128)S(1)} %copy-done.20, f32[4,128,128]{1,2,0:T(8,128)S(1)} %compare_select_fusion, f32[8,4,4,128]{3,2,1,0:T(4,128)S(1)} %copy.289, ...), kind=kOutput, calls=%fused_computation.93 | convolution fusion | flops 1625292800 | bytes 13041792 | tf_op jit(solution)/shard_map/jvp(vmap(hcij,hpcj->hpci))/dot_general | solution.py:76
  690.7 22.1 %reduce-scatter.3.cloned.1.call-done = f32[8,32,512]{2,0,1:T(8,128)} async-done(((f32[8,256,512]{2,0,1:T(8,128)}), f32[8,32,512]{2,0,1:T(8,128)}) %reduce-scatter.3.cloned.1.call-update) | async-done | bytes 524304 | tf_op jit(solution)/shard_map/reduce_scatter | solution.py:231
  714.6 53.1 %reduce-scatter.5.cloned.1.call-done = f32[8,32,512]{2,0,1:T(8,128)} async-done(((f32[8,256,512]{2,0,1:T(8,128)}), f32[8,32,512]{2,0,1:T(8,128)}) %reduce-scatter.5.cloned.1.call-update) | async-done | bytes 524304 | tf_op jit(solution)/shard_map/reduce_scatter | solution.py:234
  (282 shorter events, 69.6 us)
Async XLA Ops:
  7.2 70.4 %copy-start.37 = (bf16[8,4,512]{2,1,0:T(4,128)(2,1)S(1)}, bf16[8,4,512]{2,1,0:T(4,128)(2,1)}, u32[]{:S(2)}) copy-start(bf16[8,4,512]{2,1,0:T(4,128)(2,1)} %param.26) | copy-start | bytes 98308
  7.2 70.8 %all-gather.13.cloned.1.call-start = ((), (), s32[]{:S(2)}) async-start(), calls=%async_computation.2 | async-start | bytes 2359296 | tf_op jit(solution)/shard_map/all_gather | solution.py:161
  9.0 73.2 %all-gather.15.cloned.1.call-start = ((), (), s32[]{:S(2)}) async-start(), calls=%async_computation.3 | async-start | bytes 2359296 | tf_op jit(solution)/shard_map/all_gather | solution.py:162
  10.9 313.4 %all-gather.17.cloned.1.call-start = ((), (), s32[]{:S(2)}) async-start(), calls=%async_computation.6 | async-start | bytes 10485760 | tf_op jit(solution)/shard_map/all_gather | solution.py:23
  34.4 10.9 %copy-start.54 = (f32[8,4]{0,1:T(4,128)}, f32[8,4]{0,1:T(4,128)S(1)}, u32[]{:S(2)}) copy-start(f32[8,4]{0,1:T(4,128)S(1)} %exponential_negate_fusion) | copy-start | bytes 388
  44.3 37.9 %copy-start.49 = (f32[8,4]{0,1:T(4,128)}, f32[8,4]{0,1:T(4,128)S(1)}, u32[]{:S(2)}) copy-start(f32[8,4]{0,1:T(4,128)S(1)} %copy.393) | copy-start | bytes 388
  45.4 138.6 %copy-start.21 = (f32[8,4,4,128]{3,0,2,1:T(8,128)}, f32[8,4,4,128]{3,0,2,1:T(8,128)S(1)}, u32[]{:S(2)}) copy-start(f32[8,4,4,128]{3,0,2,1:T(8,128)S(1)} %fusion.100) | copy-start | bytes 196612
  45.5 36.7 %copy-start.33 = (f32[8,4,4]{0,2,1:T(4,128)}, f32[8,4,4]{0,2,1:T(4,128)S(1)}, u32[]{:S(2)}) copy-start(f32[8,4,4]{0,2,1:T(4,128)S(1)} %slice_reduce_fusion) | copy-start | bytes 1540
  46.3 31.5 %copy-start.51 = (f32[4]{0:T(128)}, f32[4]{0:T(128)S(1)}, u32[]{:S(2)}) copy-start(f32[4]{0:T(128)S(1)} %get-tuple-element.720) | copy-start | bytes 52
  74.5 7.8 %copy-start.35 = (f32[8,2560]{1,0:T(8,128)}, f32[8,2560]{1,0:T(8,128)S(1)}, u32[]{:S(2)}) copy-start(f32[8,2560]{1,0:T(8,128)S(1)} %reshape.208) | copy-start | bytes 245764
  77.5 9.1 %copy-start.39 = (f32[4,128]{1,0:T(4,128)}, f32[4,128]{1,0:T(4,128)S(1)}, u32[]{:S(2)}) copy-start(f32[4,128]{1,0:T(4,128)S(1)} %get-tuple-element.746) | copy-start | bytes 6148
  77.5 9.1 %copy-start.47 = (f32[4,128]{1,0:T(4,128)}, f32[4,128]{1,0:T(4,128)S(1)}, u32[]{:S(2)}) copy-start(f32[4,128]{1,0:T(4,128)S(1)} %get-tuple-element.745) | copy-start | bytes 6148
  77.6 18.8 %copy-start.41 = (f32[512]{0:T(512)}, f32[512]{0:T(512)S(1)}, u32[]{:S(2)}) copy-start(f32[512]{0:T(512)S(1)} %get-tuple-element.747) | copy-start | bytes 6148
  77.6 18.8 %copy-start.43 = (f32[512]{0:T(512)}, f32[512]{0:T(512)S(1)}, u32[]{:S(2)}) copy-start(f32[512]{0:T(512)S(1)} %get-tuple-element.748) | copy-start | bytes 6148
  77.6 18.8 %copy-start.45 = (f32[512]{0:T(512)}, f32[512]{0:T(512)S(1)}, u32[]{:S(2)}) copy-start(f32[512]{0:T(512)S(1)} %get-tuple-element.749) | copy-start | bytes 6148
  77.8 18.6 %copy-start.25 = (f32[8,768]{1,0:T(8,128)}, f32[8,768]{1,0:T(8,128)S(1)}, u32[]{:S(2)}) copy-start(f32[8,768]{1,0:T(8,128)S(1)} %get-tuple-element.740) | copy-start | bytes 73732
  77.8 18.6 %copy-start.27 = (f32[8,768]{1,0:T(8,128)}, f32[8,768]{1,0:T(8,128)S(1)}, u32[]{:S(2)}) copy-start(f32[8,768]{1,0:T(8,128)S(1)} %get-tuple-element.742) | copy-start | bytes 73732
  77.8 18.6 %copy-start.29 = (f32[8,768]{1,0:T(8,128)}, f32[8,768]{1,0:T(8,128)S(1)}, u32[]{:S(2)}) copy-start(f32[8,768]{1,0:T(8,128)S(1)} %get-tuple-element.743) | copy-start | bytes 73732
  77.8 18.6 %copy-start.31 = (f32[8,768]{1,0:T(8,128)}, f32[8,768]{1,0:T(8,128)S(1)}, u32[]{:S(2)}) copy-start(f32[8,768]{1,0:T(8,128)S(1)} %get-tuple-element.741) | copy-start | bytes 73732
  86.6 8.2 %slice-start.2 = ((f32[8,2560]{1,0:T(8,128)}), f32[8,512]{1,0:T(8,128)S(1)}, s32[]{:S(2)}) async-start(f32[8,2560]{1,0:T(8,128)} %copy-done.35), calls=%async_computation.10 | async-start | bytes 32768 | tf_op jit(solution)/shard_map/slice | solution.py:172
  93.3 3.0 collective-permute-start
  171.9 1.3 copy-start.6
  173.2 300.4 %all-gather.19.cloned.1.call-start = ((), (), s32[]{:S(2)}) async-start(), calls=%async_computation.7 | async-start | bytes 10485760 | tf_op jit(solution)/shard_map/all_gather | solution.py:23
  176.1 7.8 %copy-start.10 = (bf16[8,4,64,4,128]{4,3,2,1,0:T(4,128)(2,1)}, bf16[8,4,64,4,128]{4,3,2,1,0:T(4,128)(2,1)S(1)}, u32[]{:S(2)}) copy-start(bf16[8,4,64,4,128]{4,3,2,1,0:T(4,128)(2,1)S(1)} %reshape.197) | copy-start | bytes 6291460
  183.9 528.8 %reduce-scatter.3.cloned.1.call-start = ((), (), s32[]{:S(2)}) async-start(), calls=%async_computation.4 | async-start | bytes 4718592 | tf_op jit(solution)/shard_map/reduce_scatter | solution.py:231
  184.0 200.3 %copy-start.23 = (f32[8,4,4,128]{3,2,1,0:T(4,128)}, f32[8,4,4,128]{3,2,1,0:T(4,128)S(1)}, u32[]{:S(2)}) copy-start(f32[8,4,4,128]{3,2,1,0:T(4,128)S(1)} %copy.307) | copy-start | bytes 196612
  200.8 8.0 %copy-start.7 = (f32[8,4,64,4,128]{4,2,3,1,0:T(8,128)S(1)}, f32[8,4,64,4,128]{4,2,3,1,0:T(8,128)}, u32[]{:S(2)}) copy-start(f32[8,4,64,4,128]{4,2,3,1,0:T(8,128)} %copy.287) | copy-start | bytes 12582916
  200.8 8.0 %copy-start.11 = (bf16[8,4,64,4,128]{4,3,2,1,0:T(4,128)(2,1)S(1)}, bf16[8,4,64,4,128]{4,3,2,1,0:T(4,128)(2,1)}, u32[]{:S(2)}) copy-start(bf16[8,4,64,4,128]{4,3,2,1,0:T(4,128)(2,1)} %copy-done.10) | copy-start | bytes 6291460
  208.8 14.4 %copy-start.18 = (f32[8,4,128,128]{2,3,1,0:T(8,128)}, f32[8,4,128,128]{2,3,1,0:T(8,128)S(1)}, u32[]{:S(2)}) copy-start(f32[8,4,128,128]{2,3,1,0:T(8,128)S(1)} %fusion.142) | copy-start | bytes 6291460
  208.8 15.8 %copy-start.4 = (f32[8,256,512]{1,2,0:T(8,128)S(1)}, f32[8,256,512]{1,2,0:T(8,128)}, u32[]{:S(2)}) copy-start(f32[8,256,512]{1,2,0:T(8,128)} %get-tuple-element.732) | copy-start | bytes 12582916
  223.2 1.4 copy-start.15
  373.1 11.3 %copy-start.12 = (bf16[8,4,64,4,128]{4,3,2,1,0:T(4,128)(2,1)S(1)}, bf16[8,4,64,4,128]{4,3,2,1,0:T(4,128)(2,1)}, u32[]{:S(2)}) copy-start(bf16[8,4,64,4,128]{4,3,2,1,0:T(4,128)(2,1)} %copy-done.10) | copy-start | bytes 6291460
  384.3 2.3 copy-start.14
  384.3 5.0 copy-start.1
  386.7 2.1 copy-start.9
  505.6 14.6 %copy-start.5 = (f32[8,256,512]{1,2,0:T(8,128)S(1)}, f32[8,256,512]{1,2,0:T(8,128)}, u32[]{:S(2)}) copy-start(f32[8,256,512]{1,2,0:T(8,128)} %get-tuple-element.732) | copy-start | bytes 12582916
  505.7 14.6 %copy-start.8 = (f32[8,4,64,4,128]{4,2,3,1,0:T(8,128)S(1)}, f32[8,4,64,4,128]{4,2,3,1,0:T(8,128)}, u32[]{:S(2)}) copy-start(f32[8,4,64,4,128]{4,2,3,1,0:T(8,128)} %copy.287) | copy-start | bytes 12582916
  505.7 26.4 %slice-start = ((s8[8388608]{0:T(1024)(128)(4,1)}), s8[4194304]{0:T(1024)(128)(4,1)S(1)}, s32[]{:S(2)}) async-start(s8[8388608]{0:T(1024)(128)(4,1)} %bitcast.253), calls=%async_computation.8 | async-start | bytes 8388608
  520.2 11.8 %slice-start.1 = ((s8[8388608]{0:T(1024)(128)(4,1)}), s8[4194304]{0:T(1024)(128)(4,1)S(1)}, s32[]{:S(2)}) async-start(s8[8388608]{0:T(1024)(128)(4,1)} %bitcast.253), calls=%async_computation.9 | async-start | bytes 8388608
  532.0 12.7 %copy-start.2 = (f32[8,256,512]{1,2,0:T(8,128)S(1)}, f32[8,256,512]{1,2,0:T(8,128)}, u32[]{:S(2)}) copy-start(f32[8,256,512]{1,2,0:T(8,128)} %get-tuple-element.733) | copy-start | bytes 12582916
  532.1 12.7 %copy-start.16 = (f32[8,4,128,128]{2,3,1,0:T(8,128)S(1)}, f32[8,4,128,128]{2,3,1,0:T(8,128)}, u32[]{:S(2)}) copy-start(f32[8,4,128,128]{2,3,1,0:T(8,128)} %copy-done.15) | copy-start | bytes 6291460
  544.8 7.0 copy-start.13
  544.8 7.0 copy-start.17
  544.8 7.0 copy-start.19
  544.8 7.0 copy-start.53
  571.9 9.0 %copy-start.32 = (f32[8,768]{1,0:T(8,128)S(1)}, f32[8,768]{1,0:T(8,128)}, u32[]{:S(2)}) copy-start(f32[8,768]{1,0:T(8,128)} %copy-done.31) | copy-start | bytes 73732
  580.9 13.9 %copy-start.26 = (f32[8,768]{1,0:T(8,128)S(1)}, f32[8,768]{1,0:T(8,128)}, u32[]{:S(2)}) copy-start(f32[8,768]{1,0:T(8,128)} %copy-done.25) | copy-start | bytes 73732
  580.9 13.9 %copy-start.28 = (f32[8,768]{1,0:T(8,128)S(1)}, f32[8,768]{1,0:T(8,128)}, u32[]{:S(2)}) copy-start(f32[8,768]{1,0:T(8,128)} %copy-done.27) | copy-start | bytes 73732
  580.9 13.9 %copy-start.30 = (f32[8,768]{1,0:T(8,128)S(1)}, f32[8,768]{1,0:T(8,128)}, u32[]{:S(2)}) copy-start(f32[8,768]{1,0:T(8,128)} %copy-done.29) | copy-start | bytes 73732
  580.9 13.9 %copy-start.42 = (f32[512]{0:T(512)S(1)}, f32[512]{0:T(512)}, u32[]{:S(2)}) copy-start(f32[512]{0:T(512)} %copy-done.41) | copy-start | bytes 6148
  580.9 13.9 %copy-start.44 = (f32[512]{0:T(512)S(1)}, f32[512]{0:T(512)}, u32[]{:S(2)}) copy-start(f32[512]{0:T(512)} %copy-done.43) | copy-start | bytes 6148
  580.9 13.9 %copy-start.46 = (f32[512]{0:T(512)S(1)}, f32[512]{0:T(512)}, u32[]{:S(2)}) copy-start(f32[512]{0:T(512)} %copy-done.45) | copy-start | bytes 6148
  594.8 22.5 %copy-start = (f32[8,768,512]{1,2,0:T(8,128)}, f32[8,768,512]{1,2,0:T(8,128)S(1)}, u32[]{:S(2)}) copy-start(f32[8,768,512]{1,2,0:T(8,128)S(1)} %get-tuple-element.716) | copy-start | bytes 37748740
  616.0 30.8 %collective-permute-start.1 = (f32[8,768,3]{1,2,0:T(4,128)S(1)}, f32[8,768,3]{1,2,0:T(4,128)S(1)}, u32[]{:S(2)}, u32[]{:S(2)}) collective-permute-start(f32[8,768,3]{1,2,0:T(4,128)S(1)} %pad_add_fusion.1), channel_id=1, source_target_pairs={{1,0},{2,1},{3,2},{5,4},{6,5},{7,6},{9,8},{10,9},{11,10},{13,12},{... | collective-permute-start | bytes 221192 | tf_op jit(solution)/shard_map/ppermute | solution.py:18
  646.8 4.9 copy-start.3
  660.9 106.7 %reduce-scatter.5.cloned.1.call-start = ((), (), s32[]{:S(2)}) async-start(), calls=%async_computation.5 | async-start | bytes 4718592 | tf_op jit(solution)/shard_map/reduce_scatter | solution.py:234
  666.8 1.3 copy-start.36
  666.8 1.3 copy-start.38
  666.8 1.3 copy-start.48
  666.8 1.3 copy-start.50
  666.8 1.3 copy-start.55
  666.8 1.3 copy-start.56
  666.9 2.2 copy-start.20
  666.9 2.2 copy-start.24
  (5 other events, 4.9 us)
Sparse Core Ops, SparseCore 0:
  10.5 30.6 all-gather.12
  43.6 27.9 all-gather.14
  173.4 150.9 all-gather.16
  325.8 147.8 all-gather.18
  661.1 51.6 reduce-scatter.2
  716.3 51.2 reduce-scatter.4

commit v2 on v1

--- a/solution.py
+++ b/solution.py
@@ -18,22 +18,20 @@
     return lax.ppermute(value, axis, [(source, source + steps) for source in range(first, last)])
 
 
-def carried_in(array, axis, combine, identity, reverse):
+def carried_in(totals, pieces, axis, reverse):
     peers, index = (lax.axis_size(axis), lax.axis_index(axis))
-    everything = jax.tree.map(lambda part: lax.all_gather(part, axis), array)
-    start = jax.tree.map(
-        lambda part, zero: jnp.broadcast_to(jnp.asarray(zero, part.dtype), part.shape),
-        array,
-        identity,
-    )
-
-    def lap(k, before):
-        at = peers - 1 - k if reverse else k
-        reached = at > index if reverse else at < index
-        new = combine(before, jax.tree.map(lambda part: part[at], everything))
-        return jax.tree.map(lambda a, b: jnp.where(reached, a, b), new, before)
-
-    return lax.fori_loop(0, peers, lap, start)
+    every_total = lax.all_gather(totals, axis)
+    every_piece = lax.all_gather(pieces, axis)
+    idx = jnp.arange(peers)
+    if reverse:
+        between = (index < idx[None, :]) & (idx[None, :] < idx[:, None])
+        valid = idx > index
+    else:
+        between = (idx[:, None] < idx[None, :]) & (idx[None, :] < index)
+        valid = idx < index
+    picked = jnp.where(between[:, :, None, None], every_total[None], 1.0)
+    weight = jnp.prod(picked, axis=1) * valid.astype(jnp.float32)[:, None, None]
+    return jnp.sum(weight[..., None, None] * every_piece, axis=0)
 
 
 def segment_ids(positions, doc_lengths):
@@ -109,14 +107,21 @@
     )
 
 
+def weighted_sum(weight, stacked):
+    return jnp.sum(weight[..., None, None] * stacked, axis=-3)
+
+
 def span_fold(carry, states, state_start):
-
-    def span_advance(running, pieces):
-        factor, piece = pieces
-        return (factor[:, None, None] * running + piece, running)
-
-    state_end, starts = lax.scan(span_advance, state_start, (carry.T, jnp.moveaxis(states, 1, 0)))
-    return (starts, state_end)
+    blocks = carry.shape[-1]
+    idx = jnp.arange(blocks)
+    inside = (idx[None, :, None] < idx[None, None, :]) & (idx[None, None, :] < idx[:, None, None])
+    link = jnp.prod(jnp.where(inside[None], carry[:, None, None, :], 1.0), axis=-1)
+    link = link * (idx[None, :] < idx[:, None]).astype(jnp.float32)[None]
+    lead = jnp.prod(jnp.where((idx[None, :] < idx[:, None])[None], carry[:, None, :], 1.0), axis=-1)
+    tail = jnp.prod(jnp.where((idx[None, :] > idx[:, None])[None], carry[:, None, :], 1.0), axis=-1)
+    starts = weighted_sum(link, states[:, None]) + lead[..., None, None] * state_start[:, None]
+    state_end = weighted_sum(tail, states) + jnp.prod(carry, axis=-1)[:, None, None] * state_start
+    return (jnp.moveaxis(starts, 1, 0), state_end)
 
 
 def assemble(y_intra, c_three, entry, carry, states, state_start):
@@ -134,20 +139,6 @@
         reach_advance, jnp.ones(carry.shape[:-1], jnp.float32), jnp.moveaxis(carry, -1, 0)
     )
     return (jnp.moveaxis(before, 0, -1), total)
-
-
-def compose_fwd(preceding_states, later):
-    return (
-        preceding_states[0] * later[0],
-        later[0][..., None, None] * preceding_states[1] + later[1],
-    )
-
-
-def compose_back(preceding_states, later):
-    return (
-        later[0] * preceding_states[0],
-        later[1] + later[0][..., None, None] * preceding_states[1],
-    )
 
 
 def shards(
@@ -160,11 +151,25 @@
     blocks = length // SPAN
     b_full = lax.all_gather(b_in, "seq", axis=1, tiled=True)
     c_full = lax.all_gather(c_in, "seq", axis=1, tiled=True)
-    weight_all = lax.all_gather(conv_weight, "head", axis=0, tiled=True)
-    bias_all = lax.all_gather(conv_bias, "head", axis=0, tiled=True)
-    dt_bias_all = lax.all_gather(dt_bias, "head", axis=0, tiled=True)
-    a_log_all = lax.all_gather(a_log, "head", axis=0, tiled=True)
-    d_skip_all = lax.all_gather(d_skip, "head", axis=0, tiled=True)
+    groups_held = conv_weight.shape[0]
+    packed = jnp.concatenate(
+        [
+            conv_weight.reshape(groups_held, -1),
+            conv_bias,
+            dt_bias,
+            a_log,
+            d_skip,
+        ],
+        axis=1,
+    )
+    packed_all = lax.all_gather(packed, "head", axis=0, tiled=True)
+    cuts = [conv_weight[0].size, conv_bias.shape[1], dt_bias.shape[1], a_log.shape[1]]
+    bounds = [sum(cuts[:k]) for k in range(len(cuts) + 1)]
+    weight_all = packed_all[:, : bounds[1]].reshape((-1,) + conv_weight.shape[1:])
+    bias_all = packed_all[:, bounds[1] : bounds[2]]
+    dt_bias_all = packed_all[:, bounds[2] : bounds[3]]
+    a_log_all = packed_all[:, bounds[3] : bounds[4]]
+    d_skip_all = packed_all[:, bounds[4] :]
     x_total = weight_all.shape[2] - 2 * STATE
 
     def own_channels(table):
@@ -206,8 +211,7 @@
     before, total = reach(carry)
     state_zero = jnp.zeros((groups_here, n_heads, HEAD_DIM, STATE), jnp.float32)
     _, summary = jax.vmap(span_fold)(carry, states, state_zero)
-    identity = (jnp.ones_like(total), jnp.zeros_like(summary))
-    state_in = carried_in((total, summary), "head", compose_fwd, identity, False)[1]
+    state_in = carried_in(total, summary, "head", False)
 
     def finish(pieces, state_start):
         return jax.vmap(assemble)(
@@ -221,7 +225,7 @@
     local_grad = jnp.einsum(
         "ghpci,ghci,gnci->ghpn", cot_five, entry * before[..., None], c_three, precision=precise
     )
-    grad_out = carried_in((total, local_grad), "head", compose_back, identity, True)[1]
+    grad_out = carried_in(total, local_grad, "head", True)
     d_terms, _ = pull_out((cot_float, grad_out))
     d_raw, d_rim, d_dt = pull_terms(d_terms)
     returned = passed_along(d_rim, "head", -1)

time: 782 us -> 684 us (0.87)
  blocking collectives: 74.8 us -> 28.3 us
  matrix products: 150 us -> 121 us
  local copies, waits for them, and re-layouts: 138 us -> 111 us
    all_gather x6 -> x2, blocking collectives: 74.8 us -> 28.3 us  [the longest x1 16.3 us: shards(): packed_all = lax.all_gather(packed, 'head', axis=0, tiled=True)]
    reduce_sum x4 -> x9, other arithmetic: 11.9 us -> 56.2 us  [the longest x2 37.3 us: weighted_sum(): return jnp.sum(weight[..., None, None] * stacked, axis=-3)]
    all_gather x1, waiting for transfers between devices: 0.02 us -> 26.1 us  [shards(): c_full = lax.all_gather(c_in, 'seq', axis=1, tiled=True)]
    select_n x8 -> x2, other arithmetic: 24.1 us -> 0.27 us  [the longest x1 0.2 us: span_fold(): jnp.where(inside[None], carry[:, None, None, :], 1.0)]
    add x8 -> x1, other arithmetic: 23.2 us -> 1.52 us  [span_fold(): weighted_sum(tail, states)]
    dynamic_update_slice x16 -> x0, local copies, waits for them, and re-layouts: 18.8 us -> none  [the longest x12 18.7 us: span_fold(): lax.scan(span_advance, state_start, (carry.T, jnp.moveaxis(states, 1, 0)))]
    all_gather x2, waiting for transfers between devices: 158 us -> 142 us  [carried_in(): every_piece = lax.all_gather(pieces, axis)]
    dot_general x3, matrix products: 45.4 us -> 29.8 us  [assemble(): jnp.einsum('nci,hci,chpn->hpci', c_three, entry, starts, precision=precise)]
  transfers between devices with their start and end apart: 8 -> 8, of which waited for: 5 -> 6; matrix products, arithmetic and copies ran while one was open for 25% -> 34% of each run, Pallas kernels for 0% -> 0%
where the time goes in v2:
time: 684 us; the launch traced here: 674 us
  waiting for transfers between devices  231 us (34%)
  other arithmetic  162 us (24%)
  matrix products  121 us (18%)
  local copies, waits for them, and re-layouts  111 us (16%)
  blocking collectives  28.3 us (4%)
  between operations  15.8 us (2%)
    all_gather x2, waiting for transfers between devices, carried_in(): every_piece = lax.all_gather(pieces, axis)  142 us
    reduce_scatter x1, waiting for transfers between devices, shards(): lax.psum_scatter(d_raw[:, x_width + STATE:], 'seq', scatter_dimension=1,...  53.1 us
    dot_general x3, matrix products, span_terms(): jnp.einsum('hcij,hpcj->hpci', decay * scores[None], weighted, precision=p...  37.4 us
    reduce_sum x2, other arithmetic, weighted_sum(): return jnp.sum(weight[..., None, None] * stacked, axis=-3)  37.3 us
    mul x3, other arithmetic, conv_silu(): weight[offset][:, None] * padded[:, offset:offset + length]  34.5 us
    reshape x4, local copies, waits for them, and re-layouts, span_terms(): x_four = x_conv.reshape(n_heads, HEAD_DIM, blocks, SPAN)  33.7 us
    dot_general x3, matrix products, assemble(): jnp.einsum('nci,hci,chpn->hpci', c_three, entry, starts, precision=precise)  29.8 us
    dot_general x3, matrix products, span_terms(): jnp.einsum('hpcj,hcj,ncj->hcpn', weighted, keep_end, b_three, precision=p...  28.1 us
  transfers between devices with their start and end apart: 8, of which 6 were waited for; matrix products, arithmetic and copies ran while one was open for 34% of the time, Pallas kernels for 0%

profile of v2, /device:TPU:0, one launch (start us, length us, event | category | flops | bytes accessed | tf_op | source)
XLA Modules:
  0.0 674.2 jit_solution(9186715848391437282)
XLA Ops:
  7.2 1.8 copy.344
  9.1 1.8 copy.345
  14.4 16.3 %all-gather.2 = f32[4,2,12896]{2,1,0:T(2,128)S(1)} all-gather(f32[1,2,12896]{2,1,0:T(2,128)S(1)} %bitcast.254), channel_id=1, replica_groups=mesh['seq'=8,'head'=4] {'head'}, dimensions={0}, use_global_device_ids=true | all-gather | bytes 515840 | tf_op jit(solution)/shard_map/all_gather | solution.py:165
  32.4 1.0 fusion.96
  35.2 2.9 copy.346
  39.0 2.1 all-gather.9.cloned.1.call-done
  41.1 4.3 copy.347
  45.4 26.1 %all-gather.11.cloned.1.call-done = bf16[8,256,512]{2,0,1:T(8,128)(2,1)} async-done(((bf16[8,32,512]{2,0,1:T(8,128)(2,1)}), bf16[8,256,512]{2,0,1:T(8,128)(2,1)}) %all-gather.11.cloned.1.call-update) | async-done | bytes 2097168 | tf_op jit(solution)/shard_map/all_gather | solution.py:153
  71.5 4.3 copy.348
  75.8 6.6 pad_maximum_fusion.1
  82.4 3.4 collective-permute-start
  85.9 2.6 reshape.377
  88.5 26.9 %fusion.14 = (f32[8,768,512]{1,2,0:T(8,128)}, f32[8,768,512]{1,2,0:T(8,128)}) fusion(f32[8,768,512]{1,2,0:T(8,128)} %get-tuple-element.119, f32[8,768]{1,0:T(8,128)} %get-tuple-element.134, f32[512]{0:T(512)S(1)} %get-tuple-element.154, f32[8,768,3]{1,2,0:T(4,128)S(1)} %convert_element_type.93, f32[8,768]{1,0:T(8,128)S(1)} %get-tuple-element.135, ...), kind=kLoop, calls=%fused_computation.33 | loop fusion | flops 56623104 | bytes 37951488 | tf_op jit(solution)/shard_map/jvp(vmap(jit(silu)))/mul | solution.py:53
  115.4 9.3 %fusion.157 = (f32[8,256,512]{1,2,0:T(8,128)}, f32[8,256,512]{1,2,0:T(8,128)}, f32[8,256,512]{1,2,0:T(8,128)S(1)}) fusion(f32[8,768,512]{1,2,0:T(8,128)} %get-tuple-element.108), kind=kLoop, calls=%fused_computation.274 | loop fusion | bytes 25165824 | tf_op jit(solution)/shard_map/jvp(vmap())/slice | solution.py:93
  124.7 2.0 copy-done.1
  126.7 5.6 fusion.85
  133.9 11.9 %all-gather.3 = f32[4,8,4]{1,2,0:T(4,128)S(1)} all-gather(f32[1,8,4]{1,2,0:T(4,128)S(1)} %bitcast.256), channel_id=2, replica_groups=mesh['seq'=8,'head'=4] {'head'}, dimensions={0}, use_global_device_ids=true | all-gather | bytes 640 | tf_op jit(solution)/shard_map/all_gather | solution.py:23
  148.4 8.1 %reshape.407 = f32[8,4,64,4,128]{2,1,4,3,0:T(4,128)} reshape(f32[8,256,512]{1,2,0:T(8,128)} %get-tuple-element.115) | data formatting | bytes 8388608 | tf_op jit(solution)/shard_map/jvp(vmap())/reshape | solution.py:59
  156.5 8.6 %copy.353 = f32[8,4,64,4,128]{4,2,3,1,0:T(8,128)} copy(f32[8,4,64,4,128]{2,1,4,3,0:T(4,128)} %reshape.407) | data formatting | bytes 8388608 | tf_op jit(solution)/shard_map/jvp(vmap())/reshape | solution.py:59
  165.1 9.1 %fusion.66 = f32[8,4,4,64,256]{4,3,1,2,0:T(8,128)S(1)} fusion(f32[8,256,4,128,1]{1,3,4,2,0:T(8,128)} %bitcast.235, f32[8,4,4,128]{3,2,1,0:T(4,128)S(1)} %copy.378, bf16[8,4,64,4,128]{4,3,2,1,0:T(4,128)(2,1)S(1)} %reshape.377), kind=kOutput, calls=%fused_computation.107 | convolution fusion | flops 3223322624 | bytes 14745600 | tf_op jit(solution)/shard_map/transpose(jvp(vmap(nci,hci,chpn->hpci)))/dot_general | solution.py:129
  174.2 7.5 %fusion.63 = f32[8,4,4,64,256]{4,3,1,2,0:T(8,128)S(1)} fusion(f32[8,256,4,128,1]{1,3,4,2,0:T(8,128)S(1)} %bitcast.240, f32[8,4,64,4,128]{4,2,3,1,0:T(8,128)S(1)} %copy-done.10, f32[8,4,4,128]{3,2,1,0:T(4,128)S(1)} %copy.366, f32[8,4,4,128]{3,2,1,0:T(4,128)S(1)} %copy.352), kind=kOutput, calls=%fused_computation.106 | convolution fusion | flops 3223322624 | bytes 16908288 | tf_op jit(solution)/shard_map/jvp(vmap(hpcj,hcj,ncj->hcpn))/dot_general | solution.py:78
  181.7 3.2 copy-done.8
  184.9 17.8 %multiply_reduce_fusion = (f32[8,4,4,4]{3,2,1,0:T(4,128)}, f32[8,4,4,64,256]{4,3,2,1,0:T(8,128)}, f32[8,4,4,64,256]{4,3,2,1,0:T(8,128)}) fusion(f32[8,4,4,4]{3,2,1,0:T(4,128)S(1)} %bitcast_multiply_fusion.8, f32[8,4,4,64,256]{4,3,1,2,0:T(8,128)S(1)} %fusion.63, f32[8,4,4,64,256]{4,3,1,2,0:T(8,128)S(1)} %fusion.66), kind=kLoop, calls=%fused_computation.2 | loop fusion | flops 46136832 | bytes 33558528 | tf_op jit(solution)/shard_map/transpose(jvp(vmap()))/reduce_sum | solution.py:111
  202.7 79.1 %all-gather.15.cloned.1.call-done = f32[32,4,64,256]{3,2,1,0:T(8,128)} async-done(((f32[8,4,64,256]{3,2,1,0:T(8,128)}), f32[32,4,64,256]{3,2,1,0:T(8,128)}) %all-gather.15.cloned.1.call-update) | async-done | bytes 8388624 | tf_op jit(solution)/shard_map/all_gather | solution.py:24
  281.8 4.4 multiply_reduce_fusion.5
  286.2 2.1 copy-done.9
  288.3 19.5 %multiply_reduce_fusion.4 = (f32[8,4,4]{1,2,0:T(4,128)}, f32[8,4,64,256]{3,2,1,0:T(8,128)S(1)}, f32[8,4,4,64,256]{4,3,1,2,0:T(8,128)}) fusion(f32[8,4,4,64,256]{4,3,1,2,0:T(8,128)S(1)} %copy-done.9, f32[8,4,64,256]{3,2,1,0:T(8,128)S(1)} %multiply_reduce_fusion.5, f32[8,4,4]{1,2,0:T(4,128)S(1)} %copy.372, f32[8,4,4,64,256]{4,3,2,1,0:T(8,128)} %get-tuple-element.89, ...), kind=kLoop, calls=%fused_computation.52 | loop fusion | flops 12058496 | bytes 29361664 | tf_op jit(solution)/shard_map/transpose(jvp(vmap()))/reduce_sum | solution.py:111
  307.8 1.5 bitcast_add_fusion.6
  310.7 8.0 %fusion.159 = f32[8,4,128,128]{2,3,1,0:T(8,128)S(1)} fusion(f32[8,256,4,128]{1,3,2,0:T(8,128)} %bitcast.236, f32[8,256,4,128]{1,3,2,0:T(8,128)} %bitcast.239), kind=kOutput, calls=%fused_computation.276 | convolution fusion | flops 1610612736 | bytes 10485760 | tf_op jit(solution)/shard_map/jvp(vmap(nci,ncj->cij))/dot_general | solution.py:72
  318.7 13.9 %fusion.92 = (f32[8,4,4,128]{3,2,1,0:T(4,128)}, f32[8,4,4,128]{3,2,1,0:T(4,128)}, f32[8,4,128,128]{2,3,1,0:T(8,128)S(1)}) fusion(f32[8,4,4,128]{3,2,1,0:T(4,128)S(1)} %copy.355, f32[4,128,128]{1,2,0:T(8,128)S(1)} %compare_select_fusion, f32[8,4,128,128]{2,3,1,0:T(8,128)S(1)} %fusion.159, bf16[8,4,4,64,128]{4,2,3,1,0:T(4,128)(2,1)S(1)} %bitcast.245, ...), kind=kOutput, calls=%fused_computation.124 | convolution fusion | flops 1642561536 | bytes 11010048 | tf_op jit(solution)/shard_map/transpose(jvp(vmap(hcij,hpcj->hpci)))/dot_general | solution.py:74
  332.5 5.2 fusion.160
  337.8 7.7 %fusion.42 = (f32[8,4,4,128]{3,2,1,0:T(4,128)S(1)}, f32[8,4,4,64,128]{4,3,1,2,0:T(8,128)S(1)}) fusion(f32[8,4,64,4,128]{4,2,3,1,0:T(8,128)S(1)} %copy-done.11, f32[8,4,4,128]{3,2,1,0:T(4,128)S(1)} %copy.352, f32[8,4,4,64,256]{4,3,1,2,0:T(8,128)S(1)} %bitcast.244, f32[8,256,4,128,1]{1,3,2,4,0:T(8,128)S(1)} %bitcast.242), kind=kOutput, calls=%fused_computation.80 | convolution fusion | flops 3224354816 | bytes 21102592 | tf_op jit(solution)/shard_map/transpose(jvp(vmap(hpcj,hcj,ncj->hcpn)))/dot_general | solution.py:78
  345.5 13.7 %fusion.40 = (f32[8,4,4,128]{3,2,1,0:T(4,128)}, f32[8,4,64,4,128]{4,2,3,1,0:T(8,128)}) fusion(f32[8,4,64,4,128]{4,2,3,1,0:T(8,128)S(1)} %copy-done.11, f32[8,4,4,128]{3,2,1,0:T(4,128)S(1)} %copy.352, bf16[8,4,64,4,128]{4,3,2,1,0:T(4,128)(2,1)S(1)} %reshape.377, f32[8,4]{1,0:T(8,128)S(1)} %copy-done.64, bf16[8,4,4,64,128]{4,2,3,1,0:T(4,128)(2,1)S(1)} %bitcast.246, ...), kind=kOutput, calls=%fused_computation.76 | convolution fusion | flops 1627373568 | bytes 19398784 | tf_op jit(solution)/shard_map/transpose(jvp(vmap(hcij,hpcj->hpci)))/dot_general | solution.py:74
  359.2 8.4 %copy.466 = f32[8,4,64,4,128]{2,1,4,3,0:T(4,128)} copy(f32[8,4,64,4,128]{4,2,3,1,0:T(8,128)} %get-tuple-element.121) | data formatting | bytes 8388608 | tf_op jit(solution)/shard_map/transpose(jvp(vmap()))/reshape | solution.py:59
  367.6 8.6 %reshape.406 = f32[8,256,512]{1,2,0:T(8,128)} reshape(f32[8,4,64,4,128]{2,1,4,3,0:T(4,128)} %copy.466) | data formatting | bytes 8388608 | tf_op jit(solution)/shard_map/transpose(jvp(vmap()))/reshape | solution.py:59
  376.2 12.9 %fusion.27 = f32[8,4,256,128,1]{2,3,4,1,0:T(8,128)S(1)} fusion(f32[8,4,4,64,256]{4,3,1,2,0:T(8,128)} %get-tuple-element.124, f32[8,4,64,4,128]{4,2,3,1,0:T(8,128)} %copy.353, f32[8,4,4,128]{3,2,1,0:T(4,128)S(1)} %copy.366, f32[8,4,4,128]{3,2,1,0:T(4,128)S(1)} %copy.352), kind=kOutput, calls=%fused_computation.49 | convolution fusion | flops 3223322624 | bytes 16908288 | tf_op jit(solution)/shard_map/transpose(jvp(vmap(hpcj,hcj,ncj->hcpn)))/dot_general | solution.py:78
  389.2 5.4 bitcast_add_fusion.2
  394.6 62.8 %all-gather.13.cloned.1.call-done = f32[4,8,4,64,256]{4,3,2,1,0:T(8,128)} async-done(((f32[1,8,4,64,256]{4,3,2,1,0:T(8,128)}), f32[4,8,4,64,256]{4,3,2,1,0:T(8,128)}) %all-gather.13.cloned.1.call-update) | async-done | bytes 8388624 | tf_op jit(solution)/shard_map/all_gather | solution.py:24
  457.4 4.2 multiply_reduce_fusion.6
  461.7 7.6 %multiply_reduce_fusion.3 = (f32[8,4,4]{1,2,0:T(4,128)S(1)}, f32[8,4,4,64,256]{4,3,1,2,0:T(8,128)S(1)}) fusion(f32[8,4,4,64,256]{4,3,1,2,0:T(8,128)} %copy-done.7, f32[8,4,64,256]{3,2,1,0:T(8,128)S(1)} %multiply_reduce_fusion.6, f32[8,4,4]{1,2,0:T(4,128)S(1)} %copy.370, f32[8,4,4,64,256]{4,3,2,1,0:T(8,128)} %get-tuple-element.88), kind=kLoop, calls=%fused_computation.51 | loop fusion | flops 8388480 | bytes 27264000 | tf_op jit(solution)/shard_map/transpose(jvp(vmap()))/reduce_sum | solution.py:122
  469.5 8.9 %bitcast_add_fusion.3 = f32[8,4,128,256]{3,2,1,0:T(8,128)} fusion(f32[8,4,128,256]{3,2,1,0:T(8,128)S(1)} %copy-done.18, f32[8,4,4,64,256]{4,3,1,2,0:T(8,128)S(1)} %get-tuple-element.123, f32[8,4,4,128]{3,2,1,0:T(4,128)S(1)} %copy.378, bf16[8,4,64,4,128]{4,3,2,1,0:T(4,128)(2,1)S(1)} %reshape.377), kind=kOutput, calls=%fused_computation.81 | convolution fusion | flops 3224371200 | bytes 18939904 | tf_op jit(solution)/shard_map/transpose(jvp(vmap(nci,hci,chpn->hpci)))/dot_general | solution.py:129
  478.4 13.8 %broadcast_multiply_fusion = (f32[8,768,512]{1,2,0:T(8,128)S(1)}, f32[8,768,512]{1,2,0:T(8,128)}) fusion(f32[8,768]{1,0:T(8,128)S(1)} %copy-done.39, f32[8,768,512]{1,2,0:T(8,128)} %get-tuple-element.109, f32[8,256,512]{1,2,0:T(8,128)} %reshape.406, f32[8,256,512]{1,2,0:T(8,128)} %bitcast.247, f32[8,256,512]{1,2,0:T(8,128)} %bitcast.248), kind=kLoop, calls=%fused_computation.64 | loop fusion | flops 37748736 | bytes 50356224 | tf_op jit(solution)/shard_map/transpose(jvp(vmap()))/mul | solution.py:51
  492.2 20.1 %multiply_multiply_fusion.2 = (f32[8,768,512]{1,2,0:T(8,128)}, f32[8,768,512]{1,2,0:T(8,128)}, f32[8,768,512]{1,2,0:T(8,128)}) fusion(f32[8,768,512]{1,2,0:T(8,128)} %get-tuple-element.101, f32[512]{0:T(512)S(1)} %get-tuple-element.154, f32[8,768]{1,0:T(8,128)S(1)} %get-tuple-element.135, f32[512]{0:T(512)S(1)} %get-tuple-element.155, ...), kind=kLoop, calls=%fused_computation.31 | loop fusion | flops 18874368 | bytes 50411520 | tf_op jit(solution)/shard_map/transpose(jvp(vmap()))/mul | solution.py:51
  512.3 1.2 pad_add_fusion.2
  513.4 1.3 collective-permute-start.1
  514.7 19.0 %pad_add_fusion = f32[8,768,515]{1,2,0:T(8,128)} fusion(f32[8,768,512]{1,2,0:T(8,128)} %get-tuple-element.114, f32[8,768,512]{1,2,0:T(8,128)} %get-tuple-element.113, f32[8,768,512]{1,2,0:T(8,128)} %get-tuple-element.112, f32[8,768,512]{1,2,0:T(8,128)S(1)} %get-tuple-element.100), kind=kLoop, calls=%fused_computation.13 | loop fusion | flops 9492480 | bytes 62988288 | tf_op jit(solution)/shard_map/transpose(jvp(vmap()))/add_any | solution.py:51
  533.8 10.4 %slice.232 = f32[8,768,509]{1,2,0:T(8,128)} slice(f32[8,768,515]{1,2,0:T(8,128)} %pad_add_fusion), slice={[0:8], [0:768], [3:512]} | slice | bytes 25018368 | tf_op jit(solution)/shard_map/slice | solution.py:233
  544.2 1.3 add_add_fusion
  545.5 3.5 copy-done.3
  549.1 3.8 pad_maximum_fusion.2
  552.8 5.5 copy.406
  558.6 6.1 copy.407
  565.9 2.1 multiply_reduce_fusion.8
  568.7 11.8 %fusion.31 = f32[8,4,4,64,128]{4,3,2,1,0:T(8,128)S(1)} fusion(f32[8,256,4,128,1]{1,3,4,2,0:T(8,128)} %bitcast.237, f32[8,4,4,64,256]{4,3,1,2,0:T(8,128)} %copy-done.6), kind=kOutput, calls=%fused_computation.58 | convolution fusion | flops 3221225472 | bytes 16777216 | tf_op jit(solution)/shard_map/jvp(vmap(nci,hci,chpn->hpci))/dot_general | solution.py:129
  580.6 1.1 fusion.35
  583.9 9.8 %fusion.43 = bf16[8,4,64,4,128]{4,2,3,1,0:T(8,128)(2,1)S(1)} fusion(f32[8,4,4,64,128]{4,3,2,1,0:T(8,128)S(1)} %fusion.31, f32[8,4,64,4,128]{4,2,3,1,0:T(8,128)S(1)} %copy-done.12, f32[8,4,128,128]{2,3,1,0:T(8,128)S(1)} %copy-done.24, f32[4,128,128]{1,2,0:T(8,128)S(1)} %copy-done.38, f32[8,4,4,128]{3,2,1,0:T(4,128)S(1)} %copy-done.48, ...), kind=kOutput, calls=%fused_computation.83 | convolution fusion | flops 1625292800 | bytes 13041792 | tf_op jit(solution)/shard_map/jvp(vmap(hcij,hpcj->hpci))/dot_general | solution.py:74
  593.8 2.0 copy.379
  595.7 2.2 convert_element_type.107
  598.0 2.4 fusion.38
  600.4 2.4 copy.422
  602.8 7.4 %reduce-scatter.3.cloned.1.call-done = f32[8,32,512]{2,0,1:T(8,128)} async-done(((f32[8,256,512]{2,0,1:T(8,128)}), f32[8,32,512]{2,0,1:T(8,128)}) %reduce-scatter.3.cloned.1.call-update) | async-done | bytes 524304 | tf_op jit(solution)/shard_map/reduce_scatter | solution.py:235
  610.2 1.1 convert_element_type.109
  612.0 53.1 %reduce-scatter.5.cloned.1.call-done = f32[8,32,512]{2,0,1:T(8,128)} async-done(((f32[8,256,512]{2,0,1:T(8,128)}), f32[8,32,512]{2,0,1:T(8,128)}) %reduce-scatter.5.cloned.1.call-update) | async-done | bytes 524304 | tf_op jit(solution)/shard_map/reduce_scatter | solution.py:238
  665.1 1.1 convert_element_type.110
  (270 shorter events, 18.9 us)
Async XLA Ops:
  7.2 34.0 %all-gather.9.cloned.1.call-start = ((), (), s32[]{:S(2)}) async-start(), calls=%async_computation.2 | async-start | bytes 2359296 | tf_op jit(solution)/shard_map/all_gather | solution.py:152
  9.0 62.5 %all-gather.11.cloned.1.call-start = ((), (), s32[]{:S(2)}) async-start(), calls=%async_computation.3 | async-start | bytes 2359296 | tf_op jit(solution)/shard_map/all_gather | solution.py:153
  10.9 270.9 %all-gather.15.cloned.1.call-start = ((), (), s32[]{:S(2)}) async-start(), calls=%async_computation.7 | async-start | bytes 10485760 | tf_op jit(solution)/shard_map/all_gather | solution.py:24
  32.0 100.7 %copy-start.59 = (f32[8,4]{0,1:T(4,128)}, f32[8,4]{0,1:T(4,128)S(1)}, u32[]{:S(2)}) copy-start(f32[8,4]{0,1:T(4,128)S(1)} %copy.351) | copy-start | bytes 388
  33.5 276.0 %copy-start.27 = (f32[8,4,4,128]{3,0,2,1:T(8,128)}, f32[8,4,4,128]{3,0,2,1:T(8,128)S(1)}, u32[]{:S(2)}) copy-start(f32[8,4,4,128]{3,0,2,1:T(8,128)S(1)} %fusion.96) | copy-start | bytes 196612
  33.6 42.2 %copy-start.40 = (f32[8,4,4]{0,2,1:T(4,128)}, f32[8,4,4]{0,2,1:T(4,128)S(1)}, u32[]{:S(2)}) copy-start(f32[8,4,4]{0,2,1:T(4,128)S(1)} %slice_reduce_fusion) | copy-start | bytes 1540
  35.2 111.3 %copy-start.29 = (f32[4,8,4]{1,2,0:T(4,128)}, f32[4,8,4]{1,2,0:T(4,128)S(1)}, u32[]{:S(2)}) copy-start(f32[4,8,4]{1,2,0:T(4,128)S(1)} %get-tuple-element.235) | copy-start | bytes 1540
  38.8 43.6 %copy-start.52 = (f32[4,128]{1,0:T(4,128)}, f32[4,128]{1,0:T(4,128)S(1)}, u32[]{:S(2)}) copy-start(f32[4,128]{1,0:T(4,128)S(1)} %get-tuple-element.151) | copy-start | bytes 6148
  38.8 43.6 %copy-start.56 = (f32[4,128]{1,0:T(4,128)}, f32[4,128]{1,0:T(4,128)S(1)}, u32[]{:S(2)}) copy-start(f32[4,128]{1,0:T(4,128)S(1)} %get-tuple-element.152) | copy-start | bytes 6148
  82.4 6.0 collective-permute-start
  88.4 380.9 %copy-start.13 = (bf16[8,4,64,4,128]{4,3,2,1,0:T(4,128)(2,1)}, bf16[8,4,64,4,128]{4,3,2,1,0:T(4,128)(2,1)S(1)}, u32[]{:S(2)}) copy-start(bf16[8,4,64,4,128]{4,3,2,1,0:T(4,128)(2,1)S(1)} %reshape.377) | copy-start | bytes 6291460
  124.7 8.0 %copy-start.50 = (bf16[8,4,512]{2,1,0:T(4,128)(2,1)S(1)}, bf16[8,4,512]{2,1,0:T(4,128)(2,1)}, u32[]{:S(2)}) copy-start(bf16[8,4,512]{2,1,0:T(4,128)(2,1)} %param.16) | copy-start | bytes 98308
  124.7 21.9 %copy-start.61 = (f32[8,4]{0,1:T(4,128)S(1)}, f32[8,4]{0,1:T(4,128)}, u32[]{:S(2)}) copy-start(f32[8,4]{0,1:T(4,128)} %get-tuple-element.102) | copy-start | bytes 388
  132.3 325.1 %all-gather.13.cloned.1.call-start = ((), (), s32[]{:S(2)}) async-start(), calls=%async_computation.4 | async-start | bytes 10485760 | tf_op jit(solution)/shard_map/all_gather | solution.py:24
  133.2 23.3 %copy-start.69 = (pred[4,4]{0,1:T(4,128)(4,1)}, pred[4,4]{0,1:T(4,128)(4,1)S(1)}, u32[]{:S(2)}) copy-start(pred[4,4]{0,1:T(4,128)(4,1)S(1)} %copy.362) | copy-start | bytes 52
  146.3 10.2 %copy-start.33 = (f32[4,8,4,4]{1,3,2,0:T(4,128)}, f32[4,8,4,4]{1,3,2,0:T(4,128)S(1)}, u32[]{:S(2)}) copy-start(f32[4,8,4,4]{1,3,2,0:T(4,128)S(1)} %get-tuple-element.147) | copy-start | bytes 6148
  146.3 163.4 %copy-start.31 = (f32[4,8,4,4]{1,3,2,0:T(4,128)}, f32[4,8,4,4]{1,3,2,0:T(4,128)S(1)}, u32[]{:S(2)}) copy-start(f32[4,8,4,4]{1,3,2,0:T(4,128)S(1)} %get-tuple-element.148) | copy-start | bytes 6148
  146.3 10.2 %copy-start.42 = (f32[2,8,4,4]{1,3,2,0:T(4,128)}, f32[2,8,4,4]{1,3,2,0:T(4,128)S(1)}, u32[]{:S(2)}) copy-start(f32[2,8,4,4]{1,3,2,0:T(4,128)S(1)} %slice_multiply_fusion.4) | copy-start | bytes 3076
  146.4 10.0 %copy-start.67 = (pred[4,4]{0,1:T(4,128)(4,1)}, pred[4,4]{0,1:T(4,128)(4,1)S(1)}, u32[]{:S(2)}) copy-start(pred[4,4]{0,1:T(4,128)(4,1)S(1)} %iota_compare_fusion.2) | copy-start | bytes 52
  146.7 9.7 %copy-start.54 = (f32[4,4]{1,0:T(4,128)}, f32[4,4]{1,0:T(4,128)S(1)}, u32[]{:S(2)}) copy-start(f32[4,4]{1,0:T(4,128)S(1)} %fusion.146) | copy-start | bytes 196
  165.1 9.1 %copy-start.4 = (f32[8,256,512]{1,2,0:T(8,128)S(1)}, f32[8,256,512]{1,2,0:T(8,128)}, u32[]{:S(2)}) copy-start(f32[8,256,512]{1,2,0:T(8,128)} %get-tuple-element.116) | copy-start | bytes 12582916
  165.1 9.1 %copy-start.10 = (f32[8,4,64,4,128]{4,2,3,1,0:T(8,128)S(1)}, f32[8,4,64,4,128]{4,2,3,1,0:T(8,128)}, u32[]{:S(2)}) copy-start(f32[8,4,64,4,128]{4,2,3,1,0:T(8,128)} %copy.353) | copy-start | bytes 12582916
  174.2 7.5 %copy-start.7 = (f32[8,4,4,64,256]{4,3,1,2,0:T(8,128)}, f32[8,4,4,64,256]{4,3,1,2,0:T(8,128)S(1)}, u32[]{:S(2)}) copy-start(f32[8,4,4,64,256]{4,3,1,2,0:T(8,128)S(1)} %fusion.66) | copy-start | bytes 25165828
  281.8 6.5 copy-start.9
  286.2 21.7 %copy-start.15 = (f32[8,4,64,256]{3,2,1,0:T(8,128)}, f32[8,4,64,256]{3,2,1,0:T(8,128)S(1)}, u32[]{:S(2)}) copy-start(f32[8,4,64,256]{3,2,1,0:T(8,128)S(1)} %multiply_reduce_fusion.5) | copy-start | bytes 6291460
  309.4 300.8 %reduce-scatter.3.cloned.1.call-start = ((), (), s32[]{:S(2)}) async-start(), calls=%async_computation.5 | async-start | bytes 4718592 | tf_op jit(solution)/shard_map/reduce_scatter | solution.py:235
  309.5 36.0 %copy-start.47 = (f32[8,4,4,128]{3,2,1,0:T(4,128)}, f32[8,4,4,128]{3,2,1,0:T(4,128)S(1)}, u32[]{:S(2)}) copy-start(f32[8,4,4,128]{3,2,1,0:T(4,128)S(1)} %copy.355) | copy-start | bytes 196612
  310.5 8.1 %copy-start.11 = (f32[8,4,64,4,128]{4,2,3,1,0:T(8,128)S(1)}, f32[8,4,64,4,128]{4,2,3,1,0:T(8,128)}, u32[]{:S(2)}) copy-start(f32[8,4,64,4,128]{4,2,3,1,0:T(8,128)} %copy.353) | copy-start | bytes 12582916
  310.6 21.9 %copy-start.36 = (f32[4,128,128]{1,2,0:T(8,128)}, f32[4,128,128]{1,2,0:T(8,128)S(1)}, u32[]{:S(2)}) copy-start(f32[4,128,128]{1,2,0:T(8,128)S(1)} %compare_select_fusion) | copy-start | bytes 786436
  310.6 27.1 %slice-start = ((s8[8388608]{0:T(1024)(128)(4,1)}), s8[4194304]{0:T(1024)(128)(4,1)S(1)}, s32[]{:S(2)}) async-start(s8[8388608]{0:T(1024)(128)(4,1)} %bitcast.243), calls=%async_computation.8 | async-start | bytes 8388608
  318.6 13.9 %copy-start.23 = (f32[8,4,128,128]{2,3,1,0:T(8,128)}, f32[8,4,128,128]{2,3,1,0:T(8,128)S(1)}, u32[]{:S(2)}) copy-start(f32[8,4,128,128]{2,3,1,0:T(8,128)S(1)} %fusion.159) | copy-start | bytes 6291460
  318.6 13.9 %copy-start.5 = (f32[8,256,512]{1,2,0:T(8,128)S(1)}, f32[8,256,512]{1,2,0:T(8,128)}, u32[]{:S(2)}) copy-start(f32[8,256,512]{1,2,0:T(8,128)} %get-tuple-element.116) | copy-start | bytes 12582916
  318.7 19.1 %slice-start.1 = ((s8[8388608]{0:T(1024)(128)(4,1)}), s8[4194304]{0:T(1024)(128)(4,1)S(1)}, s32[]{:S(2)}) async-start(s8[8388608]{0:T(1024)(128)(4,1)} %bitcast.243), calls=%async_computation.9 | async-start | bytes 8388608
  332.5 13.0 %copy-start.19 = (f32[8,4,128,128]{2,3,1,0:T(8,128)}, f32[8,4,128,128]{2,3,1,0:T(8,128)S(1)}, u32[]{:S(2)}) copy-start(f32[8,4,128,128]{2,3,1,0:T(8,128)S(1)} %get-tuple-element.84) | copy-start | bytes 6291460
  337.8 7.7 %copy-start.37 = (f32[4,128,128]{1,2,0:T(8,128)S(1)}, f32[4,128,128]{1,2,0:T(8,128)}, u32[]{:S(2)}) copy-start(f32[4,128,128]{1,2,0:T(8,128)} %copy-done.36) | copy-start | bytes 786436
  337.8 7.7 %copy-start.64 = (f32[8,4]{1,0:T(8,128)S(1)}, f32[8,4]{1,0:T(8,128)}, u32[]{:S(2)}) copy-start(f32[8,4]{1,0:T(8,128)} %get-tuple-element.165) | copy-start | bytes 388
  376.2 12.9 %copy-start.2 = (f32[8,256,512]{1,2,0:T(8,128)S(1)}, f32[8,256,512]{1,2,0:T(8,128)}, u32[]{:S(2)}) copy-start(f32[8,256,512]{1,2,0:T(8,128)} %copy-done.1) | copy-start | bytes 12582916
  376.2 12.9 %copy-start.20 = (f32[8,4,128,128]{2,3,1,0:T(8,128)S(1)}, f32[8,4,128,128]{2,3,1,0:T(8,128)}, u32[]{:S(2)}) copy-start(f32[8,4,128,128]{2,3,1,0:T(8,128)} %copy-done.19) | copy-start | bytes 6291460
  461.7 7.6 %copy-start.17 = (f32[8,4,64,256]{3,2,1,0:T(8,128)}, f32[8,4,64,256]{3,2,1,0:T(8,128)S(1)}, u32[]{:S(2)}) copy-start(f32[8,4,64,256]{3,2,1,0:T(8,128)S(1)} %multiply_reduce_fusion.6) | copy-start | bytes 6291460
  461.7 7.8 %copy-start.18 = (f32[8,4,128,256]{3,2,1,0:T(8,128)S(1)}, f32[8,4,128,256]{3,2,1,0:T(8,128)}, u32[]{:S(2)}) copy-start(f32[8,4,128,256]{3,2,1,0:T(8,128)} %fusion.160) | copy-start | bytes 12582916
  469.3 9.1 %copy-start.6 = (f32[8,4,4,64,256]{4,3,1,2,0:T(8,128)}, f32[8,4,4,64,256]{4,3,1,2,0:T(8,128)S(1)}, u32[]{:S(2)}) copy-start(f32[8,4,4,64,256]{4,3,1,2,0:T(8,128)S(1)} %get-tuple-element.123) | copy-start | bytes 25165828
  469.5 8.9 %copy-start.39 = (f32[8,768]{1,0:T(8,128)S(1)}, f32[8,768]{1,0:T(8,128)}, u32[]{:S(2)}) copy-start(f32[8,768]{1,0:T(8,128)} %get-tuple-element.134) | copy-start | bytes 73732
  492.2 22.5 %copy-start = (f32[8,768,512]{1,2,0:T(8,128)}, f32[8,768,512]{1,2,0:T(8,128)S(1)}, u32[]{:S(2)}) copy-start(f32[8,768,512]{1,2,0:T(8,128)S(1)} %get-tuple-element.100) | copy-start | bytes 37748740
  513.4 30.8 %collective-permute-start.1 = (f32[8,768,3]{1,2,0:T(4,128)S(1)}, f32[8,768,3]{1,2,0:T(4,128)S(1)}, u32[]{:S(2)}, u32[]{:S(2)}) collective-permute-start(f32[8,768,3]{1,2,0:T(4,128)S(1)} %pad_add_fusion.2), channel_id=1, source_target_pairs={{1,0},{2,1},{3,2},{5,4},{6,5},{7,6},{9,8},{10,9},{11,10},{13,12},{... | collective-permute-start | bytes 221192 | tf_op jit(solution)/shard_map/ppermute | solution.py:18
  558.4 106.7 %reduce-scatter.5.cloned.1.call-start = ((), (), s32[]{:S(2)}) async-start(), calls=%async_computation.6 | async-start | bytes 4718592 | tf_op jit(solution)/shard_map/reduce_scatter | solution.py:238
  558.5 6.3 copy-start.26
  558.5 6.4 copy-start.22
  558.5 6.5 copy-start.58
  558.5 6.9 %copy-start.46 = (f32[8,4,4]{1,2,0:T(4,128)S(1)}, f32[8,4,4]{1,2,0:T(4,128)}, u32[]{:S(2)}) copy-start(f32[8,4,4]{1,2,0:T(4,128)} %get-tuple-element.85) | copy-start | bytes 1540
  558.5 7.0 %copy-start.49 = (f32[8,4,4,128]{3,2,1,0:T(4,128)S(1)}, f32[8,4,4,128]{3,2,1,0:T(4,128)}, u32[]{:S(2)}) copy-start(f32[8,4,4,128]{3,2,1,0:T(4,128)} %get-tuple-element.120) | copy-start | bytes 196612
  558.5 7.0 %copy-start.43 = (f32[2,8,4,4]{1,3,2,0:T(4,128)S(1)}, f32[2,8,4,4]{1,3,2,0:T(4,128)}, u32[]{:S(2)}) copy-start(f32[2,8,4,4]{1,3,2,0:T(4,128)} %copy-done.42) | copy-start | bytes 3076
  558.5 7.0 %copy-start.34 = (f32[4,8,4,4]{1,3,2,0:T(4,128)S(1)}, f32[4,8,4,4]{1,3,2,0:T(4,128)}, u32[]{:S(2)}) copy-start(f32[4,8,4,4]{1,3,2,0:T(4,128)} %copy-done.33) | copy-start | bytes 6148
  558.5 7.0 %copy-start.68 = (pred[4,4]{0,1:T(4,128)(4,1)S(1)}, pred[4,4]{0,1:T(4,128)(4,1)}, u32[]{:S(2)}) copy-start(pred[4,4]{0,1:T(4,128)(4,1)} %copy-done.67) | copy-start | bytes 52
  558.6 7.1 %copy-start.28 = (f32[8,4,4,128]{3,0,2,1:T(8,128)S(1)}, f32[8,4,4,128]{3,0,2,1:T(8,128)}, u32[]{:S(2)}) copy-start(f32[8,4,4,128]{3,0,2,1:T(8,128)} %copy-done.27) | copy-start | bytes 196612
  558.6 7.1 %copy-start.41 = (f32[8,4,4]{0,2,1:T(4,128)S(1)}, f32[8,4,4]{0,2,1:T(4,128)}, u32[]{:S(2)}) copy-start(f32[8,4,4]{0,2,1:T(4,128)} %copy-done.40) | copy-start | bytes 1540
  558.6 7.1 %copy-start.53 = (f32[4,128]{1,0:T(4,128)S(1)}, f32[4,128]{1,0:T(4,128)}, u32[]{:S(2)}) copy-start(f32[4,128]{1,0:T(4,128)} %copy-done.52) | copy-start | bytes 6148
  558.6 7.3 %copy-start.16 = (f32[8,4,64,256]{3,2,1,0:T(8,128)S(1)}, f32[8,4,64,256]{3,2,1,0:T(8,128)}, u32[]{:S(2)}) copy-start(f32[8,4,64,256]{3,2,1,0:T(8,128)} %copy-done.15) | copy-start | bytes 6291460
  568.7 11.9 %copy-start.14 = (bf16[8,4,64,4,128]{4,3,2,1,0:T(4,128)(2,1)S(1)}, bf16[8,4,64,4,128]{4,3,2,1,0:T(4,128)(2,1)}, u32[]{:S(2)}) copy-start(bf16[8,4,64,4,128]{4,3,2,1,0:T(4,128)(2,1)} %copy-done.13) | copy-start | bytes 6291460
  568.7 13.0 %copy-start.51 = (bf16[8,4,512]{2,1,0:T(4,128)(2,1)S(1)}, bf16[8,4,512]{2,1,0:T(4,128)(2,1)}, u32[]{:S(2)}) copy-start(bf16[8,4,512]{2,1,0:T(4,128)(2,1)} %param.16) | copy-start | bytes 98308
  568.7 13.0 %copy-start.57 = (f32[4,128]{1,0:T(4,128)S(1)}, f32[4,128]{1,0:T(4,128)}, u32[]{:S(2)}) copy-start(f32[4,128]{1,0:T(4,128)} %copy-done.56) | copy-start | bytes 6148
  568.7 13.0 %copy-start.60 = (f32[8,4]{0,1:T(4,128)S(1)}, f32[8,4]{0,1:T(4,128)}, u32[]{:S(2)}) copy-start(f32[8,4]{0,1:T(4,128)} %copy-done.59) | copy-start | bytes 388
  568.7 13.0 %copy-start.66 = (f32[8,4]{0,1:T(4,128)S(1)}, f32[8,4]{0,1:T(4,128)}, u32[]{:S(2)}) copy-start(f32[8,4]{0,1:T(4,128)} %copy-done.65) | copy-start | bytes 388
  568.7 13.0 %copy-start.71 = (f32[8,4,4,128]{3,2,1,0:T(4,128)S(1)}, f32[8,4,4,128]{3,2,1,0:T(4,128)}, u32[]{:S(2)}) copy-start(f32[8,4,4,128]{3,2,1,0:T(4,128)} %get-tuple-element.82) | copy-start | bytes 196612
  568.7 13.0 %copy-start.72 = (f32[8,4,4,128]{3,2,1,0:T(4,128)S(1)}, f32[8,4,4,128]{3,2,1,0:T(4,128)}, u32[]{:S(2)}) copy-start(f32[8,4,4,128]{3,2,1,0:T(4,128)} %get-tuple-element.83) | copy-start | bytes 196612
  (19 other events, 64.1 us)
Sparse Core Ops, SparseCore 0:
  10.5 30.6 all-gather.8
  43.6 27.9 all-gather.10
  132.5 149.2 all-gather.14
  309.5 147.8 all-gather.12
  558.5 51.6 reduce-scatter.2
  613.8 51.2 reduce-scatter.4

commit v3 on v2

--- a/solution.py
+++ b/solution.py
@@ -19,19 +19,12 @@
 
 
 def carried_in(totals, pieces, axis, reverse):
-    peers, index = (lax.axis_size(axis), lax.axis_index(axis))
-    every_total = lax.all_gather(totals, axis)
-    every_piece = lax.all_gather(pieces, axis)
-    idx = jnp.arange(peers)
-    if reverse:
-        between = (index < idx[None, :]) & (idx[None, :] < idx[:, None])
-        valid = idx > index
-    else:
-        between = (idx[:, None] < idx[None, :]) & (idx[None, :] < index)
-        valid = idx < index
-    picked = jnp.where(between[:, :, None, None], every_total[None], 1.0)
-    weight = jnp.prod(picked, axis=1) * valid.astype(jnp.float32)[:, None, None]
-    return jnp.sum(weight[..., None, None] * every_piece, axis=0)
+    steps = -1 if reverse else 1
+    factor = totals[..., None, None]
+    received = passed_along(pieces, axis, steps)
+    for _ in range(lax.axis_size(axis) - 2):
+        received = passed_along(factor * received + pieces, axis, steps)
+    return received
 
 
 def segment_ids(positions, doc_lengths):

time: 684 us -> 674 us (0.985)
  starting transfers between devices: 5.19 us -> 25.9 us
  blocking collectives: 28.3 us -> 16.3 us
  waiting for transfers between devices: 231 us -> 223 us
  other arithmetic: 162 us -> 155 us
    all_gather x2 -> x0, waiting for transfers between devices: 142 us -> none  [carried_in(): every_piece = lax.all_gather(pieces, axis)]
    ppermute x2 -> x8, waiting for transfers between devices: 0.01 us -> 135 us  [passed_along(): lax.ppermute(value, axis, [(source, source + steps) for source in range(f...]
    ppermute x2 -> x8, starting transfers between devices: 4.68 us -> 25.7 us  [passed_along(): lax.ppermute(value, axis, [(source, source + steps) for source in range(f...]
    add x0 -> x4, other arithmetic: none -> 12.7 us  [carried_in(): received = passed_along(factor * received + pieces, axis, steps)]
    all_gather x1 -> x0, blocking collectives: 11.9 us -> none  [carried_in(): every_total = lax.all_gather(totals, axis)]
    reduce_sum x2, other arithmetic: 37.3 us -> 25.6 us  [weighted_sum(): return jnp.sum(weight[..., None, None] * stacked, axis=-3)]
    reduce_sum x2 -> x0, other arithmetic: 8.63 us -> none  [carried_in(): return jnp.sum(weight[..., None, None] * every_piece, axis=0)]
    unnamed x159 -> x157, local copies, waits for them, and re-layouts: 26.8 us -> 21.7 us
  transfers between devices with their start and end apart: 8 -> 12, of which waited for: 6 -> 9; matrix products, arithmetic and copies ran while one was open for 34% -> 35% of each run, Pallas kernels for 0% -> 0%
where the time goes in v3:
time: 674 us; the launch traced here: 663 us
  waiting for transfers between devices  223 us (33%)
  other arithmetic  155 us (23%)
  matrix products  122 us (18%)
  local copies, waits for them, and re-layouts  106 us (16%)
  starting transfers between devices  25.9 us (4%)
  blocking collectives  16.3 us (2%)
  between operations  15.4 us (2%)
    ppermute x8, waiting for transfers between devices, passed_along(): lax.ppermute(value, axis, [(source, source + steps) for source in range(f...  135 us
    reduce_scatter x1, waiting for transfers between devices, shards(): lax.psum_scatter(d_raw[:, x_width + STATE:], 'seq', scatter_dimension=1,...  53.1 us
    dot_general x3, matrix products, span_terms(): jnp.einsum('hcij,hpcj->hpci', decay * scores[None], weighted, precision=p...  36.7 us
    mul x3, other arithmetic, conv_silu(): weight[offset][:, None] * padded[:, offset:offset + length]  34.5 us
    reshape x4, local copies, waits for them, and re-layouts, span_terms(): x_four = x_conv.reshape(n_heads, HEAD_DIM, blocks, SPAN)  33.5 us
    dot_general x3, matrix products, span_terms(): jnp.einsum('hpcj,hcj,ncj->hcpn', weighted, keep_end, b_three, precision=p...  33 us
    dot_general x3, matrix products, assemble(): jnp.einsum('nci,hci,chpn->hpci', c_three, entry, starts, precision=precise)  27.9 us
    mul x1, other arithmetic, conv_silu(): return jax.nn.silu(total)  26.8 us
  transfers between devices with their start and end apart: 12, of which 9 were waited for; matrix products, arithmetic and copies ran while one was open for 35% of the time, Pallas kernels for 0%

profile of v3, /device:TPU:0, one launch (start us, length us, event | category | flops | bytes accessed | tf_op | source)
XLA Modules:
  0.0 663.4 jit_solution(2455426625231672013)
XLA Ops:
  7.2 1.8 copy.339
  9.1 1.8 copy.340
  14.4 16.3 %all-gather = f32[4,2,12896]{2,1,0:T(2,128)S(1)} all-gather(f32[1,2,12896]{2,1,0:T(2,128)S(1)} %bitcast.249), channel_id=1, replica_groups=mesh['seq'=8,'head'=4] {'head'}, dimensions={0}, use_global_device_ids=true | all-gather | bytes 515840 | tf_op jit(solution)/shard_map/all_gather | solution.py:158
  34.5 2.9 copy.341
  38.3 2.8 all-gather.4.cloned.1.call-done
  41.1 4.3 copy.342
  45.4 26.1 %all-gather.6.cloned.1.call-done = bf16[8,256,512]{2,0,1:T(8,128)(2,1)} async-done(((bf16[8,32,512]{2,0,1:T(8,128)(2,1)}), bf16[8,256,512]{2,0,1:T(8,128)(2,1)}) %all-gather.6.cloned.1.call-update) | async-done | bytes 2097168 | tf_op jit(solution)/shard_map/all_gather | solution.py:146
  71.5 4.3 copy.343
  75.8 6.7 %pad_maximum_fusion.1 = (bf16[8,768,512]{1,2,0:T(8,128)(2,1)S(1)}, f32[8,768,512]{1,2,0:T(8,128)}) fusion(bf16[8,256,512]{1,2,0:T(8,128)(2,1)} %copy.343, bf16[8,256,512]{1,2,0:T(8,128)(2,1)} %copy.342, bf16[8,256,512]{1,2,0:T(8,128)(2,1)S(1)} %copy.341), kind=kLoop, calls=%fused_computation.58 | loop fusion | flops 22020096 | bytes 25165824 | tf_op jit(solution)/shard_map/concatenate | solution.py:178
  82.5 3.4 collective-permute-start
  85.9 2.6 reshape.294
  88.6 26.8 %fusion.14 = (f32[8,768,512]{1,2,0:T(8,128)}, f32[8,768,512]{1,2,0:T(8,128)}) fusion(f32[8,768,512]{1,2,0:T(8,128)} %get-tuple-element.117, f32[8,768]{1,0:T(8,128)S(1)} %copy-done.36, f32[512]{0:T(512)S(1)} %get-tuple-element.152, f32[8,768,3]{1,2,0:T(4,128)S(1)} %convert_element_type.79, f32[8,768]{1,0:T(8,128)S(1)} %get-tuple-element.133, ...), kind=kLoop, calls=%fused_computation.33 | loop fusion | flops 56623104 | bytes 37951488 | tf_op jit(solution)/shard_map/jvp(vmap(jit(silu)))/mul | solution.py:46
  115.4 9.3 %fusion.160 = (f32[8,256,512]{1,2,0:T(8,128)}, f32[8,256,512]{1,2,0:T(8,128)}, f32[8,256,512]{1,2,0:T(8,128)S(1)}) fusion(f32[8,768,512]{1,2,0:T(8,128)} %get-tuple-element.106), kind=kLoop, calls=%fused_computation.266 | loop fusion | bytes 25165824 | tf_op jit(solution)/shard_map/jvp(vmap())/slice | solution.py:86
  124.7 5.6 fusion.89
  130.3 1.6 collective-permute-start.4
  133.5 46.7 %collective-permute-done.4 = f32[8,4,64,256]{3,2,1,0:T(8,128)} collective-permute-done((f32[8,4,64,256]{3,2,1,0:T(8,128)}, f32[8,4,64,256]{3,2,1,0:T(8,128)}, u32[]{:S(2)}, u32[]{:S(2)}) %collective-permute-start.4) | collective-permute-done | bytes 2097184 | tf_op jit(solution)/shard_map/ppermute | solution.py:18
  180.1 3.8 multiply_add_fusion.1
  187.7 8.0 %reshape.319 = f32[8,4,64,4,128]{2,1,4,3,0:T(4,128)} reshape(f32[8,256,512]{1,2,0:T(8,128)} %get-tuple-element.113) | data formatting | bytes 8388608 | tf_op jit(solution)/shard_map/jvp(vmap())/reshape | solution.py:52
  195.7 8.5 %copy.348 = f32[8,4,64,4,128]{4,2,3,1,0:T(8,128)} copy(f32[8,4,64,4,128]{2,1,4,3,0:T(4,128)} %reshape.319) | data formatting | bytes 8388608 | tf_op jit(solution)/shard_map/jvp(vmap())/reshape | solution.py:52
  204.3 9.7 %fusion.63 = f32[8,4,4,64,256]{4,3,1,2,0:T(8,128)S(1)} fusion(f32[8,256,4,128,1]{1,3,4,2,0:T(8,128)} %bitcast.235, f32[8,4,64,4,128]{4,2,3,1,0:T(8,128)} %copy.348, f32[8,4,4,128]{3,2,1,0:T(4,128)S(1)} %copy.361, f32[8,4,4,128]{3,2,1,0:T(4,128)S(1)} %copy.347), kind=kOutput, calls=%fused_computation.104 | convolution fusion | flops 3223322624 | bytes 16908288 | tf_op jit(solution)/shard_map/jvp(vmap(hpcj,hcj,ncj->hcpn))/dot_general | solution.py:71
  213.9 18.9 %collective-permute-done.5 = f32[8,4,64,256]{3,2,1,0:T(8,128)} collective-permute-done((f32[8,4,64,256]{3,2,1,0:T(8,128)}, f32[8,4,64,256]{3,2,1,0:T(8,128)}, u32[]{:S(2)}, u32[]{:S(2)}) %collective-permute-start.5) | collective-permute-done | bytes 2097184 | tf_op jit(solution)/shard_map/ppermute | solution.py:18
  232.8 2.5 multiply_add_fusion
  235.3 1.7 collective-permute-start.6
  237.0 7.3 %fusion.66 = f32[8,4,4,64,256]{4,3,1,2,0:T(8,128)S(1)} fusion(f32[8,256,4,128,1]{1,3,4,2,0:T(8,128)S(1)} %bitcast.233, f32[8,4,4,128]{3,2,1,0:T(4,128)S(1)} %copy.373, bf16[8,4,64,4,128]{4,3,2,1,0:T(4,128)(2,1)S(1)} %reshape.294), kind=kOutput, calls=%fused_computation.105 | convolution fusion | flops 3223322624 | bytes 14745600 | tf_op jit(solution)/shard_map/transpose(jvp(vmap(nci,hci,chpn->hpci)))/dot_general | solution.py:122
  244.3 17.8 %multiply_reduce_fusion = (f32[8,4,4,4]{3,2,1,0:T(4,128)}, f32[8,4,4,64,256]{4,3,2,1,0:T(8,128)}, f32[8,4,4,64,256]{4,3,2,1,0:T(8,128)}) fusion(f32[8,4,4,4]{3,2,1,0:T(4,128)S(1)} %bitcast_multiply_fusion.8, f32[8,4,4,64,256]{4,3,1,2,0:T(8,128)S(1)} %fusion.63, f32[8,4,4,64,256]{4,3,1,2,0:T(8,128)S(1)} %fusion.66), kind=kLoop, calls=%fused_computation.2 | loop fusion | flops 46136832 | bytes 33558528 | tf_op jit(solution)/shard_map/transpose(jvp(vmap()))/reduce_sum | solution.py:104
  262.1 20.8 %collective-permute-done.6 = f32[8,4,64,256]{3,2,1,0:T(8,128)S(1)} collective-permute-done((f32[8,4,64,256]{3,2,1,0:T(8,128)S(1)}, f32[8,4,64,256]{3,2,1,0:T(8,128)S(1)}, u32[]{:S(2)}, u32[]{:S(2)}) %collective-permute-start.6) | collective-permute-done | bytes 2097184 | tf_op jit(solution)/shard_map/ppermute | solution.py:18
  283.0 7.8 %multiply_reduce_fusion.4 = (f32[8,4,4]{1,2,0:T(4,128)}, f32[8,4,64,256]{3,2,1,0:T(8,128)S(1)}, f32[8,4,4,64,256]{4,3,1,2,0:T(8,128)}) fusion(f32[8,4,4,64,256]{4,3,1,2,0:T(8,128)S(1)} %fusion.63, f32[8,4,64,256]{3,2,1,0:T(8,128)S(1)} %collective-permute-done.6, f32[8,4,4]{1,2,0:T(4,128)S(1)} %copy.367, f32[8,4,4,64,256]{4,3,2,1,0:T(8,128)} %get-tuple-element.89, ...), kind=kLoop, calls=%fused_computation.52 | loop fusion | flops 12058496 | bytes 29361664 | tf_op jit(solution)/shard_map/transpose(jvp(vmap()))/reduce_sum | solution.py:104
  292.1 1.5 broadcast_add_fusion
  293.6 4.9 collective-permute-start.1
  299.5 7.9 %fusion.162 = f32[8,4,128,128]{2,3,1,0:T(8,128)S(1)} fusion(f32[8,256,4,128]{1,3,2,0:T(8,128)} %bitcast.231, f32[8,256,4,128]{1,3,2,0:T(8,128)} %bitcast.236), kind=kOutput, calls=%fused_computation.268 | convolution fusion | flops 1610612736 | bytes 10485760 | tf_op jit(solution)/shard_map/jvp(vmap(nci,ncj->cij))/dot_general | solution.py:65
  307.4 32.2 %collective-permute-done.1 = f32[8,4,64,256]{3,2,1,0:T(8,128)} collective-permute-done((f32[8,4,64,256]{3,2,1,0:T(8,128)}, f32[8,4,64,256]{3,2,1,0:T(8,128)}, u32[]{:S(2)}, u32[]{:S(2)}) %collective-permute-start.1) | collective-permute-done | bytes 2097184 | tf_op jit(solution)/shard_map/ppermute | solution.py:18
  339.6 3.2 multiply_add_fusion.3
  342.9 5.7 collective-permute-start.2
  348.6 13.8 %fusion.96 = (f32[8,4,4,128]{3,2,1,0:T(4,128)}, f32[8,4,4,128]{3,2,1,0:T(4,128)}, f32[8,4,128,128]{2,3,1,0:T(8,128)S(1)}) fusion(f32[8,4,4,128]{3,2,1,0:T(4,128)S(1)} %copy.350, f32[4,128,128]{1,2,0:T(8,128)S(1)} %compare_select_fusion, f32[8,4,128,128]{2,3,1,0:T(8,128)S(1)} %fusion.162, bf16[8,4,4,64,128]{4,2,3,1,0:T(4,128)(2,1)S(1)} %bitcast.241, ...), kind=kOutput, calls=%fused_computation.126 | convolution fusion | flops 1642561536 | bytes 11010048 | tf_op jit(solution)/shard_map/transpose(jvp(vmap(hcij,hpcj->hpci)))/dot_general | solution.py:67
  362.4 5.2 fusion.163
  367.6 5.2 fusion.164
  372.7 16.2 %collective-permute-done.2 = f32[8,4,64,256]{3,2,1,0:T(8,128)} collective-permute-done((f32[8,4,64,256]{3,2,1,0:T(8,128)}, f32[8,4,64,256]{3,2,1,0:T(8,128)}, u32[]{:S(2)}, u32[]{:S(2)}) %collective-permute-start.2) | collective-permute-done | bytes 2097184 | tf_op jit(solution)/shard_map/ppermute | solution.py:18
  389.0 3.2 multiply_add_fusion.2
  392.2 5.9 collective-permute-start.3
  398.1 7.7 %fusion.42 = (f32[8,4,4,128]{3,2,1,0:T(4,128)S(1)}, f32[8,4,4,64,128]{4,3,1,2,0:T(8,128)S(1)}) fusion(f32[8,4,64,4,128]{4,2,3,1,0:T(8,128)S(1)} %copy-done.8, f32[8,4,4,128]{3,2,1,0:T(4,128)S(1)} %copy.347, f32[8,4,4,64,256]{4,3,1,2,0:T(8,128)S(1)} %bitcast.240, f32[8,256,4,128,1]{1,3,2,4,0:T(8,128)S(1)} %bitcast.238), kind=kOutput, calls=%fused_computation.78 | convolution fusion | flops 3224354816 | bytes 21102592 | tf_op jit(solution)/shard_map/transpose(jvp(vmap(hpcj,hcj,ncj->hcpn)))/dot_general | solution.py:71
  405.8 13.1 %fusion.40 = (f32[8,4,4,128]{3,2,1,0:T(4,128)}, f32[8,4,64,4,128]{4,2,3,1,0:T(8,128)}) fusion(f32[8,4,64,4,128]{4,2,3,1,0:T(8,128)S(1)} %copy-done.8, f32[8,4,4,128]{3,2,1,0:T(4,128)S(1)} %copy.347, bf16[8,4,64,4,128]{4,3,2,1,0:T(4,128)(2,1)S(1)} %reshape.294, f32[8,4]{1,0:T(8,128)S(1)} %copy-done.63, bf16[8,4,4,64,128]{4,2,3,1,0:T(4,128)(2,1)S(1)} %bitcast.242, ...), kind=kOutput, calls=%fused_computation.74 | convolution fusion | flops 1627373568 | bytes 19398784 | tf_op jit(solution)/shard_map/transpose(jvp(vmap(hcij,hpcj->hpci)))/dot_general | solution.py:67
  418.9 8.4 %copy.460 = f32[8,4,64,4,128]{2,1,4,3,0:T(4,128)} copy(f32[8,4,64,4,128]{4,2,3,1,0:T(8,128)} %get-tuple-element.119) | data formatting | bytes 8388608 | tf_op jit(solution)/shard_map/transpose(jvp(vmap()))/reshape | solution.py:52
  427.3 8.5 %reshape.318 = f32[8,256,512]{1,2,0:T(8,128)} reshape(f32[8,4,64,4,128]{2,1,4,3,0:T(4,128)} %copy.460) | data formatting | bytes 8388608 | tf_op jit(solution)/shard_map/transpose(jvp(vmap()))/reshape | solution.py:52
  435.8 15.6 %bitcast_add_fusion.2 = f32[8,256,4,128]{1,3,2,0:T(8,128)} fusion(f32[8,4,128,256]{3,2,1,0:T(8,128)} %fusion.164, f32[8,4,4,64,256]{4,3,1,2,0:T(8,128)} %get-tuple-element.122, f32[8,4,64,4,128]{4,2,3,1,0:T(8,128)} %copy.348, f32[8,4,4,128]{3,2,1,0:T(4,128)S(1)} %copy.361, f32[8,4,4,128]{3,2,1,0:T(4,128)S(1)} %copy.347), kind=kOutput, calls=%fused_computation.70 | convolution fusion | flops 3224371200 | bytes 21102592 | tf_op jit(solution)/shard_map/transpose(jvp(vmap(hpcj,hcj,ncj->hcpn)))/dot_general | solution.py:71
  451.4 8.0 %multiply_reduce_fusion.3 = (f32[8,4,4]{1,2,0:T(4,128)S(1)}, f32[8,4,4,64,256]{4,3,1,2,0:T(8,128)S(1)}) fusion(f32[8,4,4,64,256]{4,3,1,2,0:T(8,128)} %copy-done.7, f32[8,4,64,256]{3,2,1,0:T(8,128)} %collective-permute-done.3, f32[8,4,4]{1,2,0:T(4,128)S(1)} %copy.365, f32[8,4,4,64,256]{4,3,2,1,0:T(8,128)} %get-tuple-element.88), kind=kLoop, calls=%fused_computation.51 | loop fusion | flops 8388480 | bytes 27264000 | tf_op jit(solution)/shard_map/transpose(jvp(vmap()))/reduce_sum | solution.py:115
  459.6 9.1 %bitcast_add_fusion.3 = f32[8,4,128,256]{3,2,1,0:T(8,128)} fusion(f32[8,4,128,256]{3,2,1,0:T(8,128)S(1)} %copy-done.16, f32[8,4,4,64,256]{4,3,1,2,0:T(8,128)S(1)} %get-tuple-element.121, f32[8,4,4,128]{3,2,1,0:T(4,128)S(1)} %copy.373, bf16[8,4,64,4,128]{4,3,2,1,0:T(4,128)(2,1)S(1)} %reshape.294), kind=kOutput, calls=%fused_computation.79 | convolution fusion | flops 3224371200 | bytes 18939904 | tf_op jit(solution)/shard_map/transpose(jvp(vmap(nci,hci,chpn->hpci)))/dot_general | solution.py:122
  468.7 13.8 %broadcast_multiply_fusion = (f32[8,768,512]{1,2,0:T(8,128)S(1)}, f32[8,768,512]{1,2,0:T(8,128)}) fusion(f32[8,768]{1,0:T(8,128)S(1)} %copy-done.37, f32[8,768,512]{1,2,0:T(8,128)} %get-tuple-element.107, f32[8,256,512]{1,2,0:T(8,128)} %reshape.318, f32[8,256,512]{1,2,0:T(8,128)} %bitcast.243, f32[8,256,512]{1,2,0:T(8,128)} %bitcast.244), kind=kLoop, calls=%fused_computation.62 | loop fusion | flops 37748736 | bytes 50356224 | tf_op jit(solution)/shard_map/transpose(jvp(vmap()))/mul | solution.py:44
  482.6 20.1 %multiply_multiply_fusion.2 = (f32[8,768,512]{1,2,0:T(8,128)}, f32[8,768,512]{1,2,0:T(8,128)}, f32[8,768,512]{1,2,0:T(8,128)}) fusion(f32[8,768,512]{1,2,0:T(8,128)} %get-tuple-element.99, f32[512]{0:T(512)S(1)} %get-tuple-element.152, f32[8,768]{1,0:T(8,128)S(1)} %get-tuple-element.133, f32[512]{0:T(512)S(1)} %get-tuple-element.153, ...), kind=kLoop, calls=%fused_computation.31 | loop fusion | flops 18874368 | bytes 50411520 | tf_op jit(solution)/shard_map/transpose(jvp(vmap()))/mul | solution.py:44
  505.1 19.1 %pad_add_fusion = f32[8,768,515]{1,2,0:T(8,128)} fusion(f32[8,768,512]{1,2,0:T(8,128)} %get-tuple-element.112, f32[8,768,512]{1,2,0:T(8,128)} %get-tuple-element.111, f32[8,768,512]{1,2,0:T(8,128)} %get-tuple-element.110, f32[8,768,512]{1,2,0:T(8,128)S(1)} %get-tuple-element.98), kind=kLoop, calls=%fused_computation.13 | loop fusion | flops 9492480 | bytes 62988288 | tf_op jit(solution)/shard_map/transpose(jvp(vmap()))/add_any | solution.py:44
  524.1 10.4 %slice.232 = f32[8,768,509]{1,2,0:T(8,128)} slice(f32[8,768,515]{1,2,0:T(8,128)} %pad_add_fusion), slice={[0:8], [0:768], [3:512]} | slice | bytes 25018368 | tf_op jit(solution)/shard_map/slice | solution.py:226
  534.6 1.3 add_add_fusion
  535.9 3.5 copy-done.4
  539.5 3.7 pad_maximum_fusion.2
  543.2 5.5 copy.400
  548.8 5.8 copy.401
  557.0 2.1 multiply_reduce_fusion.6
  559.7 11.6 %fusion.31 = f32[8,4,4,64,128]{4,3,2,1,0:T(8,128)S(1)} fusion(f32[8,256,4,128,1]{1,3,4,2,0:T(8,128)} %bitcast.232, f32[8,4,4,64,256]{4,3,1,2,0:T(8,128)} %copy-done.6), kind=kOutput, calls=%fused_computation.56 | convolution fusion | flops 3221225472 | bytes 16777216 | tf_op jit(solution)/shard_map/jvp(vmap(nci,hci,chpn->hpci))/dot_general | solution.py:122
  574.2 9.8 %fusion.43 = bf16[8,4,64,4,128]{4,2,3,1,0:T(8,128)(2,1)S(1)} fusion(f32[8,4,4,64,128]{4,3,2,1,0:T(8,128)S(1)} %fusion.31, f32[8,4,64,4,128]{4,2,3,1,0:T(8,128)S(1)} %copy-done.9, f32[8,4,128,128]{2,3,1,0:T(8,128)S(1)} %copy-done.20, f32[4,128,128]{1,2,0:T(8,128)S(1)} %copy-done.35, f32[8,4,4,128]{3,2,1,0:T(4,128)S(1)} %copy-done.46, ...), kind=kOutput, calls=%fused_computation.81 | convolution fusion | flops 1625292800 | bytes 13041792 | tf_op jit(solution)/shard_map/jvp(vmap(hcij,hpcj->hpci))/dot_general | solution.py:67
  584.0 2.0 copy.374
  586.0 2.2 convert_element_type.92
  588.2 2.4 fusion.38
  590.6 2.4 copy.416
  593.0 6.6 reduce-scatter.3.cloned.1.call-done
  601.4 53.1 %reduce-scatter.5.cloned.1.call-done = f32[8,32,512]{2,0,1:T(8,128)} async-done(((f32[8,256,512]{2,0,1:T(8,128)}), f32[8,32,512]{2,0,1:T(8,128)}) %reduce-scatter.5.cloned.1.call-update) | async-done | bytes 524304 | tf_op jit(solution)/shard_map/reduce_scatter | solution.py:231
  (268 shorter events, 27.7 us)
Async XLA Ops:
  7.2 25.3 %copy-start.48 = (bf16[8,4,512]{2,1,0:T(4,128)(2,1)S(1)}, bf16[8,4,512]{2,1,0:T(4,128)(2,1)}, u32[]{:S(2)}) copy-start(bf16[8,4,512]{2,1,0:T(4,128)(2,1)} %param.16) | copy-start | bytes 98308
  7.2 34.0 %all-gather.4.cloned.1.call-start = ((), (), s32[]{:S(2)}) async-start(), calls=%async_computation.2 | async-start | bytes 2359296 | tf_op jit(solution)/shard_map/all_gather | solution.py:145
  9.0 62.5 %all-gather.6.cloned.1.call-start = ((), (), s32[]{:S(2)}) async-start(), calls=%async_computation.3 | async-start | bytes 2359296 | tf_op jit(solution)/shard_map/all_gather | solution.py:146
  10.9 588.6 %reduce-scatter.3.cloned.1.call-start = ((), (), s32[]{:S(2)}) async-start(), calls=%async_computation.4 | async-start | bytes 4718592 | tf_op jit(solution)/shard_map/reduce_scatter | solution.py:228
  31.0 14.4 %copy-start.21 = (f32[8,12896]{1,0:T(8,128)}, f32[8,12896]{1,0:T(8,128)S(1)}, u32[]{:S(2)}) copy-start(f32[8,12896]{1,0:T(8,128)S(1)} %reshape.302) | copy-start | bytes 1238020
  31.9 6.3 copy-start.64
  32.0 100.0 %copy-start.58 = (f32[8,4]{0,1:T(4,128)}, f32[8,4]{0,1:T(4,128)S(1)}, u32[]{:S(2)}) copy-start(f32[8,4]{0,1:T(4,128)S(1)} %copy.346) | copy-start | bytes 388
  32.7 265.8 %copy-start.24 = (f32[8,4,4,128]{3,0,2,1:T(8,128)}, f32[8,4,4,128]{3,0,2,1:T(8,128)S(1)}, u32[]{:S(2)}) copy-start(f32[8,4,4,128]{3,0,2,1:T(8,128)S(1)} %fusion.100) | copy-start | bytes 196612
  32.9 12.5 %copy-start.38 = (f32[8,4,4]{0,2,1:T(4,128)}, f32[8,4,4]{0,2,1:T(4,128)S(1)}, u32[]{:S(2)}) copy-start(f32[8,4,4]{0,2,1:T(4,128)S(1)} %slice_reduce_fusion) | copy-start | bytes 1540
  33.6 4.4 copy-start.61
  34.5 150.9 %copy-start.26 = (f32[4,8,4]{1,2,0:T(4,128)}, f32[4,8,4]{1,2,0:T(4,128)S(1)}, u32[]{:S(2)}) copy-start(f32[4,8,4]{1,2,0:T(4,128)S(1)} %get-tuple-element.223) | copy-start | bytes 1540
  38.1 37.7 %copy-start.51 = (f32[4,128]{1,0:T(4,128)}, f32[4,128]{1,0:T(4,128)S(1)}, u32[]{:S(2)}) copy-start(f32[4,128]{1,0:T(4,128)S(1)} %get-tuple-element.149) | copy-start | bytes 6148
  38.1 37.7 %copy-start.55 = (f32[4,128]{1,0:T(4,128)}, f32[4,128]{1,0:T(4,128)S(1)}, u32[]{:S(2)}) copy-start(f32[4,128]{1,0:T(4,128)S(1)} %get-tuple-element.150) | copy-start | bytes 6148
  75.8 10.1 %slice-start.2 = ((f32[8,12896]{1,0:T(8,128)}), f32[8,512]{1,0:T(8,128)S(1)}, s32[]{:S(2)}) async-start(f32[8,12896]{1,0:T(8,128)} %copy-done.21), calls=%async_computation.8 | async-start | bytes 32768 | tf_op jit(solution)/shard_map/slice | solution.py:170
  82.5 6.1 copy-start.36
  82.5 6.0 collective-permute-start
  88.5 370.9 %copy-start.10 = (bf16[8,4,64,4,128]{4,3,2,1,0:T(4,128)(2,1)}, bf16[8,4,64,4,128]{4,3,2,1,0:T(4,128)(2,1)S(1)}, u32[]{:S(2)}) copy-start(bf16[8,4,64,4,128]{4,3,2,1,0:T(4,128)(2,1)S(1)} %reshape.294) | copy-start | bytes 6291460
  124.7 5.6 copy-start.1
  124.7 7.3 %copy-start.49 = (bf16[8,4,512]{2,1,0:T(4,128)(2,1)S(1)}, bf16[8,4,512]{2,1,0:T(4,128)(2,1)}, u32[]{:S(2)}) copy-start(bf16[8,4,512]{2,1,0:T(4,128)(2,1)} %param.16) | copy-start | bytes 98308
  130.3 55.7 %copy-start.60 = (f32[8,4]{0,1:T(4,128)S(1)}, f32[8,4]{0,1:T(4,128)}, u32[]{:S(2)}) copy-start(f32[8,4]{0,1:T(4,128)} %get-tuple-element.100) | copy-start | bytes 388
  130.3 49.8 %collective-permute-start.4 = (f32[8,4,64,256]{3,2,1,0:T(8,128)}, f32[8,4,64,256]{3,2,1,0:T(8,128)}, u32[]{:S(2)}, u32[]{:S(2)}) collective-permute-start(f32[8,4,64,256]{3,2,1,0:T(8,128)} %fusion.89), channel_id=1, source_target_pairs={{1,0},{2,1},{3,2},{5,4},{6,5},{7,6},{9,8},{10,9},{11,10},{13,12},{... | collective-permute-start | bytes 6291464 | tf_op jit(solution)/shard_map/ppermute | solution.py:18
  132.5 63.2 %copy-start.68 = (pred[4,4]{0,1:T(4,128)(4,1)}, pred[4,4]{0,1:T(4,128)(4,1)S(1)}, u32[]{:S(2)}) copy-start(pred[4,4]{0,1:T(4,128)(4,1)S(1)} %copy.357) | copy-start | bytes 52
  133.4 62.3 %copy-start.30 = (f32[4,8,4,4]{1,3,2,0:T(4,128)}, f32[4,8,4,4]{1,3,2,0:T(4,128)S(1)}, u32[]{:S(2)}) copy-start(f32[4,8,4,4]{1,3,2,0:T(4,128)S(1)} %get-tuple-element.145) | copy-start | bytes 6148
  133.4 165.1 %copy-start.28 = (f32[4,8,4,4]{1,3,2,0:T(4,128)}, f32[4,8,4,4]{1,3,2,0:T(4,128)S(1)}, u32[]{:S(2)}) copy-start(f32[4,8,4,4]{1,3,2,0:T(4,128)S(1)} %get-tuple-element.146) | copy-start | bytes 6148
  133.5 62.2 %copy-start.40 = (f32[2,8,4,4]{1,3,2,0:T(4,128)}, f32[2,8,4,4]{1,3,2,0:T(4,128)S(1)}, u32[]{:S(2)}) copy-start(f32[2,8,4,4]{1,3,2,0:T(4,128)S(1)} %slice_multiply_fusion.4) | copy-start | bytes 3076
  183.9 48.9 %collective-permute-start.5 = (f32[8,4,64,256]{3,2,1,0:T(8,128)}, f32[8,4,64,256]{3,2,1,0:T(8,128)}, u32[]{:S(2)}, u32[]{:S(2)}) collective-permute-start(f32[8,4,64,256]{3,2,1,0:T(8,128)} %multiply_add_fusion.1), channel_id=1, source_target_pairs={{1,0},{2,1},{3,2},{5,4},{6,5},{7,6},{9,8},{10,9},{11,10},{13,12},{... | collective-permute-start | bytes 6291464 | tf_op jit(solution)/shard_map/ppermute | solution.py:18
  186.0 9.7 %copy-start.53 = (f32[4,4]{1,0:T(4,128)}, f32[4,4]{1,0:T(4,128)S(1)}, u32[]{:S(2)}) copy-start(f32[4,4]{1,0:T(4,128)S(1)} %fusion.150) | copy-start | bytes 196
  213.9 23.1 %copy-start.2 = (f32[8,256,512]{1,2,0:T(8,128)S(1)}, f32[8,256,512]{1,2,0:T(8,128)}, u32[]{:S(2)}) copy-start(f32[8,256,512]{1,2,0:T(8,128)} %copy-done.1) | copy-start | bytes 12582916
  235.3 47.6 %collective-permute-start.6 = (f32[8,4,64,256]{3,2,1,0:T(8,128)S(1)}, f32[8,4,64,256]{3,2,1,0:T(8,128)S(1)}, u32[]{:S(2)}, u32[]{:S(2)}) collective-permute-start(f32[8,4,64,256]{3,2,1,0:T(8,128)S(1)} %multiply_add_fusion), channel_id=1, source_target_pairs={{1,0},{2,1},{3,2},{5,4},{6,5},{7,6},{9,8},{10,9},{11,10},{13,12},{... | collective-permute-start | bytes 6291464 | tf_op jit(solution)/shard_map/ppermute | solution.py:18
  244.3 17.8 %copy-start.7 = (f32[8,4,4,64,256]{4,3,1,2,0:T(8,128)}, f32[8,4,4,64,256]{4,3,1,2,0:T(8,128)S(1)}, u32[]{:S(2)}) copy-start(f32[8,4,4,64,256]{4,3,1,2,0:T(8,128)S(1)} %fusion.66) | copy-start | bytes 25165828
  282.9 7.8 %copy-start.14 = (f32[8,4,64,256]{3,2,1,0:T(8,128)}, f32[8,4,64,256]{3,2,1,0:T(8,128)S(1)}, u32[]{:S(2)}) copy-start(f32[8,4,64,256]{3,2,1,0:T(8,128)S(1)} %collective-permute-done.6) | copy-start | bytes 6291460
  293.6 46.0 %collective-permute-start.1 = (f32[8,4,64,256]{3,2,1,0:T(8,128)}, f32[8,4,64,256]{3,2,1,0:T(8,128)}, u32[]{:S(2)}, u32[]{:S(2)}) collective-permute-start(f32[8,4,64,256]{3,2,1,0:T(8,128)} %broadcast_add_fusion), channel_id=1, source_target_pairs={{0,1},{1,2},{2,3},{4,5},{5,6},{6,7},{8,9},{9,10},{10,11},{12,13},{... | collective-permute-start | bytes 6291464 | tf_op jit(solution)/shard_map/ppermute | solution.py:18
  298.5 107.3 %copy-start.45 = (f32[8,4,4,128]{3,2,1,0:T(4,128)}, f32[8,4,4,128]{3,2,1,0:T(4,128)S(1)}, u32[]{:S(2)}) copy-start(f32[8,4,4,128]{3,2,1,0:T(4,128)S(1)} %copy.350) | copy-start | bytes 196612
  299.5 49.0 %copy-start.33 = (f32[4,128,128]{1,2,0:T(8,128)}, f32[4,128,128]{1,2,0:T(8,128)S(1)}, u32[]{:S(2)}) copy-start(f32[4,128,128]{1,2,0:T(8,128)S(1)} %compare_select_fusion) | copy-start | bytes 786436
  299.5 40.1 %copy-start.13 = (f32[8,4,64,256]{3,2,1,0:T(8,128)S(1)}, f32[8,4,64,256]{3,2,1,0:T(8,128)}, u32[]{:S(2)}) copy-start(f32[8,4,64,256]{3,2,1,0:T(8,128)} %copy-done.12) | copy-start | bytes 6291460
  307.4 98.4 %copy-start.19 = (f32[8,4,128,128]{2,3,1,0:T(8,128)}, f32[8,4,128,128]{2,3,1,0:T(8,128)S(1)}, u32[]{:S(2)}) copy-start(f32[8,4,128,128]{2,3,1,0:T(8,128)S(1)} %fusion.162) | copy-start | bytes 6291460
  307.4 41.2 %copy-start.8 = (f32[8,4,64,4,128]{4,2,3,1,0:T(8,128)S(1)}, f32[8,4,64,4,128]{4,2,3,1,0:T(8,128)}, u32[]{:S(2)}) copy-start(f32[8,4,64,4,128]{4,2,3,1,0:T(8,128)} %copy.348) | copy-start | bytes 12582916
  342.9 46.1 %collective-permute-start.2 = (f32[8,4,64,256]{3,2,1,0:T(8,128)}, f32[8,4,64,256]{3,2,1,0:T(8,128)}, u32[]{:S(2)}, u32[]{:S(2)}) collective-permute-start(f32[8,4,64,256]{3,2,1,0:T(8,128)} %multiply_add_fusion.3), channel_id=1, source_target_pairs={{0,1},{1,2},{2,3},{4,5},{5,6},{6,7},{8,9},{9,10},{10,11},{12,13},{... | collective-permute-start | bytes 6291464 | tf_op jit(solution)/shard_map/ppermute | solution.py:18
  348.6 13.8 %copy-start.5 = (f32[8,256,512]{1,2,0:T(8,128)S(1)}, f32[8,256,512]{1,2,0:T(8,128)}, u32[]{:S(2)}) copy-start(f32[8,256,512]{1,2,0:T(8,128)} %get-tuple-element.114) | copy-start | bytes 12582916
  362.4 5.2 copy-start.3
  362.4 35.6 %slice-start = ((s8[8388608]{0:T(1024)(128)(4,1)}), s8[4194304]{0:T(1024)(128)(4,1)S(1)}, s32[]{:S(2)}) async-start(s8[8388608]{0:T(1024)(128)(4,1)} %bitcast.239), calls=%async_computation.6 | async-start | bytes 8388608
  367.6 30.5 %slice-start.1 = ((s8[8388608]{0:T(1024)(128)(4,1)}), s8[4194304]{0:T(1024)(128)(4,1)S(1)}, s32[]{:S(2)}) async-start(s8[8388608]{0:T(1024)(128)(4,1)} %bitcast.239), calls=%async_computation.7 | async-start | bytes 8388608
  392.2 59.2 %collective-permute-start.3 = (f32[8,4,64,256]{3,2,1,0:T(8,128)}, f32[8,4,64,256]{3,2,1,0:T(8,128)}, u32[]{:S(2)}, u32[]{:S(2)}) collective-permute-start(f32[8,4,64,256]{3,2,1,0:T(8,128)} %multiply_add_fusion.2), channel_id=1, source_target_pairs={{0,1},{1,2},{2,3},{4,5},{5,6},{6,7},{8,9},{9,10},{10,11},{12,13},{... | collective-permute-start | bytes 6291464 | tf_op jit(solution)/shard_map/ppermute | solution.py:18
  398.1 7.7 %copy-start.34 = (f32[4,128,128]{1,2,0:T(8,128)S(1)}, f32[4,128,128]{1,2,0:T(8,128)}, u32[]{:S(2)}) copy-start(f32[4,128,128]{1,2,0:T(8,128)} %copy-done.33) | copy-start | bytes 786436
  398.1 7.7 %copy-start.63 = (f32[8,4]{1,0:T(8,128)S(1)}, f32[8,4]{1,0:T(8,128)}, u32[]{:S(2)}) copy-start(f32[8,4]{1,0:T(8,128)} %get-tuple-element.159) | copy-start | bytes 388
  451.4 8.2 %copy-start.16 = (f32[8,4,128,256]{3,2,1,0:T(8,128)S(1)}, f32[8,4,128,256]{3,2,1,0:T(8,128)}, u32[]{:S(2)}) copy-start(f32[8,4,128,256]{3,2,1,0:T(8,128)} %fusion.163) | copy-start | bytes 12582916
  459.4 9.3 %copy-start.6 = (f32[8,4,4,64,256]{4,3,1,2,0:T(8,128)}, f32[8,4,4,64,256]{4,3,1,2,0:T(8,128)S(1)}, u32[]{:S(2)}) copy-start(f32[8,4,4,64,256]{4,3,1,2,0:T(8,128)S(1)} %get-tuple-element.121) | copy-start | bytes 25165828
  459.6 9.1 %copy-start.37 = (f32[8,768]{1,0:T(8,128)S(1)}, f32[8,768]{1,0:T(8,128)}, u32[]{:S(2)}) copy-start(f32[8,768]{1,0:T(8,128)} %get-tuple-element.132) | copy-start | bytes 73732
  482.6 22.5 %copy-start = (f32[8,768,512]{1,2,0:T(8,128)}, f32[8,768,512]{1,2,0:T(8,128)S(1)}, u32[]{:S(2)}) copy-start(f32[8,768,512]{1,2,0:T(8,128)S(1)} %get-tuple-element.98) | copy-start | bytes 37748740
  503.8 30.8 %collective-permute-start.7 = (f32[8,768,3]{1,2,0:T(4,128)S(1)}, f32[8,768,3]{1,2,0:T(4,128)S(1)}, u32[]{:S(2)}, u32[]{:S(2)}) collective-permute-start(f32[8,768,3]{1,2,0:T(4,128)S(1)} %pad_add_fusion.2), channel_id=1, source_target_pairs={{1,0},{2,1},{3,2},{5,4},{6,5},{7,6},{9,8},{10,9},{11,10},{13,12},{... | collective-permute-start | bytes 221192 | tf_op jit(solution)/shard_map/ppermute | solution.py:18
  534.6 4.9 copy-start.4
  548.8 105.7 %reduce-scatter.5.cloned.1.call-start = ((), (), s32[]{:S(2)}) async-start(), calls=%async_computation.5 | async-start | bytes 4718592 | tf_op jit(solution)/shard_map/reduce_scatter | solution.py:231
  554.8 4.4 copy-start.43
  554.8 4.4 copy-start.29
  554.8 4.5 copy-start.69
  554.8 4.6 copy-start.62
  559.7 11.6 %copy-start.11 = (bf16[8,4,64,4,128]{4,3,2,1,0:T(4,128)(2,1)S(1)}, bf16[8,4,64,4,128]{4,3,2,1,0:T(4,128)(2,1)}, u32[]{:S(2)}) copy-start(bf16[8,4,64,4,128]{4,3,2,1,0:T(4,128)(2,1)} %copy-done.10) | copy-start | bytes 6291460
  559.7 12.7 %copy-start.50 = (bf16[8,4,512]{2,1,0:T(4,128)(2,1)S(1)}, bf16[8,4,512]{2,1,0:T(4,128)(2,1)}, u32[]{:S(2)}) copy-start(bf16[8,4,512]{2,1,0:T(4,128)(2,1)} %param.16) | copy-start | bytes 98308
  559.7 12.7 %copy-start.56 = (f32[4,128]{1,0:T(4,128)S(1)}, f32[4,128]{1,0:T(4,128)}, u32[]{:S(2)}) copy-start(f32[4,128]{1,0:T(4,128)} %copy-done.55) | copy-start | bytes 6148
  559.7 12.7 %copy-start.59 = (f32[8,4]{0,1:T(4,128)S(1)}, f32[8,4]{0,1:T(4,128)}, u32[]{:S(2)}) copy-start(f32[8,4]{0,1:T(4,128)} %copy-done.58) | copy-start | bytes 388
  559.7 12.8 %copy-start.65 = (f32[8,4]{0,1:T(4,128)S(1)}, f32[8,4]{0,1:T(4,128)}, u32[]{:S(2)}) copy-start(f32[8,4]{0,1:T(4,128)} %copy-done.64) | copy-start | bytes 388
  559.7 12.8 %copy-start.70 = (f32[8,4,4,128]{3,2,1,0:T(4,128)S(1)}, f32[8,4,4,128]{3,2,1,0:T(4,128)}, u32[]{:S(2)}) copy-start(f32[8,4,4,128]{3,2,1,0:T(4,128)} %get-tuple-element.82) | copy-start | bytes 196612
  559.7 12.8 %copy-start.71 = (f32[8,4,4,128]{3,2,1,0:T(4,128)S(1)}, f32[8,4,4,128]{3,2,1,0:T(4,128)}, u32[]{:S(2)}) copy-start(f32[8,4,4,128]{3,2,1,0:T(4,128)} %get-tuple-element.83) | copy-start | bytes 196612
  571.3 2.9 copy-start.20
  (23 other events, 33.7 us)
Sparse Core Ops, SparseCore 0:
  10.5 30.6 all-gather.3
  43.6 27.8 all-gather.5
  548.9 50.6 reduce-scatter.2
  603.2 51.3 reduce-scatter.4

commit v4 on v3

--- a/solution.py
+++ b/solution.py
@@ -18,12 +18,19 @@
     return lax.ppermute(value, axis, [(source, source + steps) for source in range(first, last)])
 
 
-def carried_in(totals, pieces, axis, reverse):
-    steps = -1 if reverse else 1
+def carried_both(totals, ahead, behind, axis):
     factor = totals[..., None, None]
-    received = passed_along(pieces, axis, steps)
+    pair = lax.optimization_barrier((ahead, behind))
+    received = lax.optimization_barrier(
+        (passed_along(pair[0], axis, 1), passed_along(pair[1], axis, -1))
+    )
     for _ in range(lax.axis_size(axis) - 2):
-        received = passed_along(factor * received + pieces, axis, steps)
+        received = lax.optimization_barrier(
+            (
+                passed_along(factor * received[0] + ahead, axis, 1),
+                passed_along(factor * received[1] + behind, axis, -1),
+            )
+        )
     return received
 
 
@@ -204,21 +211,20 @@
     before, total = reach(carry)
     state_zero = jnp.zeros((groups_here, n_heads, HEAD_DIM, STATE), jnp.float32)
     _, summary = jax.vmap(span_fold)(carry, states, state_zero)
-    state_in = carried_in(total, summary, "head", False)
-
-    def finish(pieces, state_start):
-        return jax.vmap(assemble)(
-            pieces[0], pieces[1], pieces[2], pieces[3], pieces[4], state_start
-        )
-
-    (y_scan, state_out), pull_out = jax.vjp(finish, terms, state_in)
-    y_out = y_scan.astype(jnp.bfloat16)
     cot_float = cotangent.astype(jnp.float32)
     cot_five = cot_float.reshape(groups_here, n_heads, HEAD_DIM, blocks, SPAN)
     local_grad = jnp.einsum(
         "ghpci,ghci,gnci->ghpn", cot_five, entry * before[..., None], c_three, precision=precise
     )
-    grad_out = carried_in(total, local_grad, "head", True)
+    state_in, grad_out = carried_both(total, summary, local_grad, "head")
+
+    def finish(pieces, state_start):
+        return jax.vmap(assemble)(
+            pieces[0], pieces[1], pieces[2], pieces[3], pieces[4], state_start
+        )
+
+    (y_scan, state_out), pull_out = jax.vjp(finish, terms, state_in)
+    y_out = y_scan.astype(jnp.bfloat16)
     d_terms, _ = pull_out((cot_float, grad_out))
     d_raw, d_rim, d_dt = pull_terms(d_terms)
     returned = passed_along(d_rim, "head", -1)

time: 674 us -> 608 us (0.902)
  waiting for transfers between devices: 223 us -> 166 us
  starting transfers between devices: 25.9 us -> 18.6 us
    ppermute x8, waiting for transfers between devices: 135 us -> 76.6 us  [passed_along(): lax.ppermute(value, axis, [(source, source + steps) for source in range(f...]
    ppermute x8, starting transfers between devices: 25.7 us -> 18.4 us  [passed_along(): lax.ppermute(value, axis, [(source, source + steps) for source in range(f...]
    unnamed x157 -> x149, local copies, waits for them, and re-layouts: 21.7 us -> 23.7 us
  transfers between devices with their start and end apart: 12 -> 12, of which waited for: 9 -> 10; matrix products, arithmetic and copies ran while one was open for 35% -> 26% of each run, Pallas kernels for 0% -> 0%
where the time goes in v4:
time: 608 us; the launch traced here: 603 us
  waiting for transfers between devices  166 us (27%)
  other arithmetic  151 us (25%)
  matrix products  128 us (21%)
  local copies, waits for them, and re-layouts  108 us (18%)
  starting transfers between devices  18.6 us (3%)
  blocking collectives  16.3 us (3%)
  between operations  15.2 us (2%)
    ppermute x8, waiting for transfers between devices, passed_along(): lax.ppermute(value, axis, [(source, source + steps) for source in range(f...  76.6 us
    reduce_scatter x1, waiting for transfers between devices, shards(): lax.psum_scatter(d_raw[:, x_width + STATE:], 'seq', scatter_dimension=1,...  53.1 us
    dot_general x3, matrix products, span_terms(): jnp.einsum('hcij,hpcj->hpci', decay * scores[None], weighted, precision=p...  38.1 us
    mul x3, other arithmetic, conv_silu(): weight[offset][:, None] * padded[:, offset:offset + length]  33.9 us
    dot_general x3, matrix products, span_terms(): jnp.einsum('hpcj,hcj,ncj->hcpn', weighted, keep_end, b_three, precision=p...  33.8 us
    reshape x4, local copies, waits for them, and re-layouts, span_terms(): x_four = x_conv.reshape(n_heads, HEAD_DIM, blocks, SPAN)  33.6 us
    dot_general x3, matrix products, assemble(): jnp.einsum('nci,hci,chpn->hpci', c_three, entry, starts, precision=precise)  28.7 us
    mul x1, other arithmetic, conv_silu(): return jax.nn.silu(total)  26.8 us
  transfers between devices with their start and end apart: 12, of which 10 were waited for; matrix products, arithmetic and copies ran while one was open for 26% of the time, Pallas kernels for 0%

profile of v4, /device:TPU:0, one launch (start us, length us, event | category | flops | bytes accessed | tf_op | source)
XLA Modules:
  0.0 602.8 jit_solution(4250849041183160703)
XLA Ops:
  7.2 1.8 copy.339
  9.1 1.8 copy.340
  14.8 16.3 %all-gather = f32[4,2,12896]{2,1,0:T(2,128)S(1)} all-gather(f32[1,2,12896]{2,1,0:T(2,128)S(1)} %bitcast.249), channel_id=1, replica_groups=mesh['seq'=8,'head'=4] {'head'}, dimensions={0}, use_global_device_ids=true | all-gather | bytes 515840 | tf_op jit(solution)/shard_map/all_gather | solution.py:165
  33.4 2.9 copy.341
  37.4 3.7 all-gather.4.cloned.1.call-done
  41.2 4.3 copy.342
  45.4 26.1 %all-gather.6.cloned.1.call-done = bf16[8,256,512]{2,0,1:T(8,128)(2,1)} async-done(((bf16[8,32,512]{2,0,1:T(8,128)(2,1)}), bf16[8,256,512]{2,0,1:T(8,128)(2,1)}) %all-gather.6.cloned.1.call-update) | async-done | bytes 2097168 | tf_op jit(solution)/shard_map/all_gather | solution.py:153
  71.5 4.3 copy.343
  75.8 6.6 %pad_maximum_fusion.1 = (bf16[8,768,512]{1,2,0:T(8,128)(2,1)S(1)}, f32[8,768,512]{1,2,0:T(8,128)}) fusion(bf16[8,256,512]{1,2,0:T(8,128)(2,1)} %copy.343, bf16[8,256,512]{1,2,0:T(8,128)(2,1)} %copy.342, bf16[8,256,512]{1,2,0:T(8,128)(2,1)S(1)} %copy.341), kind=kLoop, calls=%fused_computation.58 | loop fusion | flops 22020096 | bytes 25165824 | tf_op jit(solution)/shard_map/concatenate | solution.py:185
  82.5 3.6 collective-permute-start
  86.4 2.6 reshape.296
  89.1 26.8 %fusion.14 = (f32[8,768,512]{1,2,0:T(8,128)}, f32[8,768,512]{1,2,0:T(8,128)}) fusion(f32[8,768,512]{1,2,0:T(8,128)} %get-tuple-element.131, f32[8,768]{1,0:T(8,128)S(1)} %get-tuple-element.147, f32[512]{0:T(512)S(1)} %get-tuple-element.171, f32[8,768,3]{1,2,0:T(4,128)S(1)} %convert_element_type.79, f32[8,768]{1,0:T(8,128)S(1)} %get-tuple-element.148, ...), kind=kLoop, calls=%fused_computation.33 | loop fusion | flops 56623104 | bytes 37951488 | tf_op jit(solution)/shard_map/jvp(vmap(jit(silu)))/mul | solution.py:53
  115.9 9.5 %fusion.160 = (f32[8,256,512]{1,2,0:T(8,128)}, f32[8,256,512]{1,2,0:T(8,128)}, f32[8,256,512]{1,2,0:T(8,128)}) fusion(f32[8,768,512]{1,2,0:T(8,128)} %get-tuple-element.120), kind=kLoop, calls=%fused_computation.266 | loop fusion | bytes 25165824 | tf_op jit(solution)/shard_map/jvp(vmap())/slice | solution.py:93
  125.4 8.0 %reshape.322 = f32[8,4,64,4,128]{2,1,4,3,0:T(4,128)} reshape(f32[8,256,512]{1,2,0:T(8,128)} %get-tuple-element.127) | data formatting | bytes 8388608 | tf_op jit(solution)/shard_map/jvp(vmap())/reshape | solution.py:59
  133.4 8.5 %copy.348 = f32[8,4,64,4,128]{4,2,3,1,0:T(8,128)} copy(f32[8,4,64,4,128]{2,1,4,3,0:T(4,128)} %reshape.322) | data formatting | bytes 8388608 | tf_op jit(solution)/shard_map/jvp(vmap())/reshape | solution.py:59
  142.0 13.9 %multiply_reduce_fusion.5 = (f32[8,4,64,256]{3,2,1,0:T(8,128)S(1)}, f32[8,4,4,64,256]{4,3,1,2,0:T(8,128)}) fusion(f32[8,4,4]{1,2,0:T(4,128)S(1)} %copy.367, f32[8,256,4,128,1]{1,3,4,2,0:T(8,128)} %bitcast.235, f32[8,4,64,4,128]{4,2,3,1,0:T(8,128)} %copy.348, f32[8,4,4,128]{3,2,1,0:T(4,128)S(1)} %copy.361, f32[8,4,4,128]{3,2,1,0:T(4,128)S(1)} %copy.347), kind=kOutput, calls=%fused_computation.53 | convolution fusion | flops 3226992640 | bytes 19005952 | tf_op jit(solution)/shard_map/jvp(vmap(hpcj,hcj,ncj->hcpn))/dot_general | solution.py:78
  155.9 1.5 broadcast_add_fusion
  157.5 2.2 copy-done.1
  159.6 5.6 fusion.89
  165.2 4.8 collective-permute-start.1
  173.6 8.2 %fusion.162 = f32[8,4,128,128]{2,3,1,0:T(8,128)S(1)} fusion(f32[8,256,4,128]{1,3,2,0:T(8,128)} %bitcast.230, f32[8,256,4,128]{1,3,2,0:T(8,128)} %bitcast.236), kind=kOutput, calls=%fused_computation.268 | convolution fusion | flops 1610612736 | bytes 10485760 | tf_op jit(solution)/shard_map/jvp(vmap(nci,ncj->cij))/dot_general | solution.py:72
  181.9 32.1 %collective-permute-done.1 = f32[8,4,64,256]{3,2,1,0:T(8,128)} collective-permute-done((f32[8,4,64,256]{3,2,1,0:T(8,128)}, f32[8,4,64,256]{3,2,1,0:T(8,128)}, u32[]{:S(2)}, u32[]{:S(2)}) %collective-permute-start.1) | collective-permute-done | bytes 2097184 | tf_op jit(solution)/shard_map/ppermute | solution.py:18
  213.9 5.5 collective-permute-done.2
  219.4 5.8 multiply_add_fusion.2
  225.2 3.4 collective-permute-start.3
  229.9 14.3 %fusion.96 = (f32[8,4,4,128]{3,2,1,0:T(4,128)}, f32[8,4,4,128]{3,2,1,0:T(4,128)}, f32[8,4,128,128]{2,3,1,0:T(8,128)S(1)}) fusion(f32[8,4,4,128]{3,2,1,0:T(4,128)S(1)} %copy.350, f32[4,128,128]{1,2,0:T(8,128)S(1)} %compare_select_fusion, f32[8,4,128,128]{2,3,1,0:T(8,128)S(1)} %fusion.162, bf16[8,4,4,64,128]{4,2,3,1,0:T(4,128)(2,1)S(1)} %bitcast.241, ...), kind=kOutput, calls=%fused_computation.126 | convolution fusion | flops 1642561536 | bytes 11010048 | tf_op jit(solution)/shard_map/transpose(jvp(vmap(hcij,hpcj->hpci)))/dot_general | solution.py:74
  244.3 5.4 fusion.163
  249.7 8.3 %fusion.66 = f32[8,4,4,64,256]{4,3,1,2,0:T(8,128)S(1)} fusion(f32[8,256,4,128,1]{1,3,4,2,0:T(8,128)S(1)} %bitcast.233, f32[8,4,4,128]{3,2,1,0:T(4,128)S(1)} %copy.377, bf16[8,4,64,4,128]{4,3,2,1,0:T(4,128)(2,1)S(1)} %reshape.296), kind=kOutput, calls=%fused_computation.105 | convolution fusion | flops 3223322624 | bytes 14745600 | tf_op jit(solution)/shard_map/transpose(jvp(vmap(nci,hci,chpn->hpci)))/dot_general | solution.py:129
  257.9 13.4 %collective-permute-done.3 = f32[8,4,64,256]{3,2,1,0:T(8,128)} collective-permute-done((f32[8,4,64,256]{3,2,1,0:T(8,128)}, f32[8,4,64,256]{3,2,1,0:T(8,128)}, u32[]{:S(2)}, u32[]{:S(2)}) %collective-permute-start.3) | collective-permute-done | bytes 2097184 | tf_op jit(solution)/shard_map/ppermute | solution.py:18
  271.4 5.5 collective-permute-done.4
  276.8 5.8 multiply_add_fusion
  282.6 1.6 collective-permute-start.5
  284.2 1.3 collective-permute-start.6
  285.5 7.5 %fusion.164 = f32[8,4,128,256]{3,2,1,0:T(8,128)} fusion(f32[8,4,128,128]{2,3,1,0:T(8,128)} %copy-done.21, f32[8,256,4,128]{1,3,2,0:T(8,128)S(1)} %bitcast.234), kind=kOutput, calls=%fused_computation.270 | convolution fusion | flops 1610612736 | bytes 10485760 | tf_op jit(solution)/shard_map/transpose(jvp(vmap(nci,ncj->cij)))/dot_general | solution.py:72
  293.0 18.1 %multiply_reduce_fusion = (f32[8,4,4,4]{3,2,1,0:T(4,128)S(1)}, f32[8,4,4,64,256]{4,3,2,1,0:T(8,128)}, f32[8,4,4,64,256]{4,3,2,1,0:T(8,128)}) fusion(f32[8,4,4,4]{3,2,1,0:T(4,128)S(1)} %bitcast_multiply_fusion.8, f32[8,4,4,64,256]{4,3,1,2,0:T(8,128)S(1)} %bitcast.240, f32[8,4,4,64,256]{4,3,1,2,0:T(8,128)S(1)} %fusion.66), kind=kLoop, calls=%fused_computation.2 | loop fusion | flops 46136832 | bytes 33558528 | tf_op jit(solution)/shard_map/transpose(jvp(vmap()))/reduce_sum | solution.py:111
  311.1 16.0 %collective-permute-done.5 = f32[8,4,64,256]{3,2,1,0:T(8,128)S(1)} collective-permute-done((f32[8,4,64,256]{3,2,1,0:T(8,128)}, f32[8,4,64,256]{3,2,1,0:T(8,128)S(1)}, u32[]{:S(2)}, u32[]{:S(2)}) %collective-permute-start.5) | collective-permute-done | bytes 2097184 | tf_op jit(solution)/shard_map/ppermute | solution.py:18
  327.2 4.1 collective-permute-done.6
  331.3 1.3 copy-done.19
  332.6 8.0 %multiply_reduce_fusion.4 = (f32[8,4,4]{1,2,0:T(4,128)S(1)}, f32[8,4,4,64,256]{4,3,1,2,0:T(8,128)S(1)}) fusion(f32[8,4,4,64,256]{4,3,1,2,0:T(8,128)} %get-tuple-element.176, f32[8,4,64,256]{3,2,1,0:T(8,128)} %copy-done.19, f32[8,4,4,64,256]{4,3,2,1,0:T(8,128)} %get-tuple-element.103, f32[8,4,4]{1,2,0:T(4,128)S(1)} %copy.384), kind=kLoop, calls=%fused_computation.52 | loop fusion | flops 8388480 | bytes 27264000 | tf_op jit(solution)/shard_map/transpose(jvp(vmap()))/reduce_sum | solution.py:111
  340.8 9.0 %fusion.42 = (f32[8,4,4,128]{3,2,1,0:T(4,128)S(1)}, f32[8,4,4,64,128]{4,3,1,2,0:T(8,128)}) fusion(f32[8,4,64,4,128]{4,2,3,1,0:T(8,128)S(1)} %copy-done.8, f32[8,4,4,128]{3,2,1,0:T(4,128)S(1)} %copy.347, f32[8,4,4,64,256]{4,3,1,2,0:T(8,128)S(1)} %get-tuple-element.135, f32[8,256,4,128,1]{1,3,2,4,0:T(8,128)S(1)} %bitcast.238), kind=kOutput, calls=%fused_computation.78 | convolution fusion | flops 3224354816 | bytes 21102592 | tf_op jit(solution)/shard_map/transpose(jvp(vmap(hpcj,hcj,ncj->hcpn)))/dot_general | solution.py:78
  349.8 10.9 %bitcast_add_fusion.2 = f32[8,256,4,128]{1,3,2,0:T(8,128)} fusion(f32[8,4,128,256]{3,2,1,0:T(8,128)} %fusion.164, f32[8,4,4,64,256]{4,3,1,2,0:T(8,128)S(1)} %get-tuple-element.135, f32[8,4,64,4,128]{4,2,3,1,0:T(8,128)S(1)} %copy-done.8, f32[8,4,4,128]{3,2,1,0:T(4,128)S(1)} %copy.361, f32[8,4,4,128]{3,2,1,0:T(4,128)S(1)} %copy.347), kind=kOutput, calls=%fused_computation.70 | convolution fusion | flops 3224371200 | bytes 21102592 | tf_op jit(solution)/shard_map/transpose(jvp(vmap(hpcj,hcj,ncj->hcpn)))/dot_general | solution.py:78
  360.7 14.0 %fusion.40 = (f32[8,4,4,128]{3,2,1,0:T(4,128)}, f32[8,4,64,4,128]{4,2,3,1,0:T(8,128)}) fusion(f32[8,4,64,4,128]{4,2,3,1,0:T(8,128)S(1)} %copy-done.8, f32[8,4,4,128]{3,2,1,0:T(4,128)S(1)} %copy.347, bf16[8,4,64,4,128]{4,3,2,1,0:T(4,128)(2,1)} %copy-done.10, f32[8,4]{1,0:T(8,128)S(1)} %get-tuple-element.180, bf16[8,4,4,64,128]{4,2,3,1,0:T(4,128)(2,1)} %bitcast.242, ...), kind=kOutput, calls=%fused_computation.74 | convolution fusion | flops 1627373568 | bytes 19398784 | tf_op jit(solution)/shard_map/transpose(jvp(vmap(hcij,hpcj->hpci)))/dot_general | solution.py:74
  374.7 8.3 %copy.460 = f32[8,4,64,4,128]{2,1,4,3,0:T(4,128)} copy(f32[8,4,64,4,128]{4,2,3,1,0:T(8,128)} %get-tuple-element.133) | data formatting | bytes 8388608 | tf_op jit(solution)/shard_map/transpose(jvp(vmap()))/reshape | solution.py:59
  383.0 8.7 %reshape.321 = f32[8,256,512]{1,2,0:T(8,128)} reshape(f32[8,4,64,4,128]{2,1,4,3,0:T(4,128)} %copy.460) | data formatting | bytes 8388608 | tf_op jit(solution)/shard_map/transpose(jvp(vmap()))/reshape | solution.py:59
  391.7 6.8 %multiply_reduce_fusion.3 = (f32[8,4,4]{1,2,0:T(4,128)S(1)}, f32[8,4,4,64,256]{4,3,1,2,0:T(8,128)S(1)}) fusion(f32[8,4,4,64,256]{4,3,1,2,0:T(8,128)} %copy-done.6, f32[8,4,64,256]{3,2,1,0:T(8,128)S(1)} %copy-done.17, f32[8,4,4]{1,2,0:T(4,128)S(1)} %copy.365, f32[8,4,4,64,256]{4,3,2,1,0:T(8,128)} %get-tuple-element.102), kind=kLoop, calls=%fused_computation.51 | loop fusion | flops 8388480 | bytes 27264000 | tf_op jit(solution)/shard_map/transpose(jvp(vmap()))/reduce_sum | solution.py:122
  399.4 8.9 %bitcast_add_fusion.3 = f32[8,4,128,256]{3,2,1,0:T(8,128)} fusion(f32[8,4,128,256]{3,2,1,0:T(8,128)S(1)} %copy-done.20, f32[8,4,4,64,256]{4,3,1,2,0:T(8,128)S(1)} %get-tuple-element.137, f32[8,4,4,128]{3,2,1,0:T(4,128)S(1)} %copy.377, bf16[8,4,64,4,128]{4,3,2,1,0:T(4,128)(2,1)S(1)} %copy-done.11), kind=kOutput, calls=%fused_computation.79 | convolution fusion | flops 3224371200 | bytes 18939904 | tf_op jit(solution)/shard_map/transpose(jvp(vmap(nci,hci,chpn->hpci)))/dot_general | solution.py:129
  408.3 13.8 %broadcast_multiply_fusion = (f32[8,768,512]{1,2,0:T(8,128)S(1)}, f32[8,768,512]{1,2,0:T(8,128)}) fusion(f32[8,768]{1,0:T(8,128)S(1)} %get-tuple-element.147, f32[8,768,512]{1,2,0:T(8,128)} %get-tuple-element.121, f32[8,256,512]{1,2,0:T(8,128)} %reshape.321, f32[8,256,512]{1,2,0:T(8,128)} %bitcast.243, f32[8,256,512]{1,2,0:T(8,128)} %bitcast.244), kind=kLoop, calls=%fused_computation.62 | loop fusion | flops 37748736 | bytes 50356224 | tf_op jit(solution)/shard_map/transpose(jvp(vmap()))/mul | solution.py:51
  422.1 20.1 %multiply_multiply_fusion.2 = (f32[8,768,512]{1,2,0:T(8,128)}, f32[8,768,512]{1,2,0:T(8,128)}, f32[8,768,512]{1,2,0:T(8,128)}) fusion(f32[8,768,512]{1,2,0:T(8,128)} %get-tuple-element.113, f32[512]{0:T(512)S(1)} %get-tuple-element.171, f32[8,768]{1,0:T(8,128)S(1)} %get-tuple-element.148, f32[512]{0:T(512)S(1)} %get-tuple-element.172, ...), kind=kLoop, calls=%fused_computation.31 | loop fusion | flops 18874368 | bytes 50411520 | tf_op jit(solution)/shard_map/transpose(jvp(vmap()))/mul | solution.py:51
  444.7 19.1 %pad_add_fusion = f32[8,768,515]{1,2,0:T(8,128)} fusion(f32[8,768,512]{1,2,0:T(8,128)} %get-tuple-element.126, f32[8,768,512]{1,2,0:T(8,128)} %get-tuple-element.125, f32[8,768,512]{1,2,0:T(8,128)} %get-tuple-element.124, f32[8,768,512]{1,2,0:T(8,128)S(1)} %get-tuple-element.112), kind=kLoop, calls=%fused_computation.13 | loop fusion | flops 9492480 | bytes 62988288 | tf_op jit(solution)/shard_map/transpose(jvp(vmap()))/add_any | solution.py:51
  463.7 10.4 %slice.232 = f32[8,768,509]{1,2,0:T(8,128)} slice(f32[8,768,515]{1,2,0:T(8,128)} %pad_add_fusion), slice={[0:8], [0:768], [3:512]} | slice | bytes 25018368 | tf_op jit(solution)/shard_map/slice | solution.py:232
  474.2 1.3 add_add_fusion
  475.5 3.5 copy-done.3
  479.0 3.7 pad_maximum_fusion.2
  482.8 5.5 copy.400
  488.4 5.8 copy.401
  496.3 2.1 multiply_reduce_fusion.6
  499.6 11.5 %fusion.31 = f32[8,4,4,64,128]{4,3,2,1,0:T(8,128)S(1)} fusion(f32[8,256,4,128,1]{1,3,4,2,0:T(8,128)} %bitcast.231, f32[8,4,4,64,256]{4,3,1,2,0:T(8,128)} %copy-done.5), kind=kOutput, calls=%fused_computation.56 | convolution fusion | flops 3221225472 | bytes 16777216 | tf_op jit(solution)/shard_map/jvp(vmap(nci,hci,chpn->hpci))/dot_general | solution.py:129
  514.0 9.8 %fusion.43 = bf16[8,4,64,4,128]{4,2,3,1,0:T(8,128)(2,1)S(1)} fusion(f32[8,4,4,64,128]{4,3,2,1,0:T(8,128)S(1)} %fusion.31, f32[8,4,64,4,128]{4,2,3,1,0:T(8,128)S(1)} %copy-done.9, f32[8,4,128,128]{2,3,1,0:T(8,128)S(1)} %copy-done.25, f32[4,128,128]{1,2,0:T(8,128)S(1)} %copy-done.37, f32[8,4,4,128]{3,2,1,0:T(4,128)S(1)} %copy-done.45, ...), kind=kOutput, calls=%fused_computation.81 | convolution fusion | flops 1625292800 | bytes 13041792 | tf_op jit(solution)/shard_map/jvp(vmap(hcij,hpcj->hpci))/dot_general | solution.py:74
  523.8 2.0 copy.378
  525.8 2.2 convert_element_type.92
  528.0 2.4 fusion.38
  530.5 2.4 copy.416
  532.9 6.3 %reduce-scatter.3.cloned.1.call-done = f32[8,32,512]{2,0,1:T(8,128)} async-done(((f32[8,256,512]{2,0,1:T(8,128)}), f32[8,32,512]{2,0,1:T(8,128)}) %reduce-scatter.3.cloned.1.call-update) | async-done | bytes 524304 | tf_op jit(solution)/shard_map/reduce_scatter | solution.py:234
  541.0 53.1 %reduce-scatter.5.cloned.1.call-done = f32[8,32,512]{2,0,1:T(8,128)} async-done(((f32[8,256,512]{2,0,1:T(8,128)}), f32[8,32,512]{2,0,1:T(8,128)}) %reduce-scatter.5.cloned.1.call-update) | async-done | bytes 524304 | tf_op jit(solution)/shard_map/reduce_scatter | solution.py:237
  (257 shorter events, 25.7 us)
Async XLA Ops:
  7.2 24.7 %copy-start.47 = (bf16[8,4,512]{2,1,0:T(4,128)(2,1)S(1)}, bf16[8,4,512]{2,1,0:T(4,128)(2,1)}, u32[]{:S(2)}) copy-start(bf16[8,4,512]{2,1,0:T(4,128)(2,1)} %param.16) | copy-start | bytes 98308
  7.2 34.0 %all-gather.4.cloned.1.call-start = ((), (), s32[]{:S(2)}) async-start(), calls=%async_computation.2 | async-start | bytes 2359296 | tf_op jit(solution)/shard_map/all_gather | solution.py:152
  9.0 62.5 %all-gather.6.cloned.1.call-start = ((), (), s32[]{:S(2)}) async-start(), calls=%async_computation.3 | async-start | bytes 2359296 | tf_op jit(solution)/shard_map/all_gather | solution.py:153
  10.9 528.3 %reduce-scatter.3.cloned.1.call-start = ((), (), s32[]{:S(2)}) async-start(), calls=%async_computation.4 | async-start | bytes 4718592 | tf_op jit(solution)/shard_map/reduce_scatter | solution.py:234
  31.8 13.6 %copy-start.56 = (f32[8,4]{0,1:T(4,128)}, f32[8,4]{0,1:T(4,128)S(1)}, u32[]{:S(2)}) copy-start(f32[8,4]{0,1:T(4,128)S(1)} %copy.346) | copy-start | bytes 388
  32.1 139.9 %copy-start.28 = (f32[8,4,4,128]{3,0,2,1:T(8,128)}, f32[8,4,4,128]{3,0,2,1:T(8,128)S(1)}, u32[]{:S(2)}) copy-start(f32[8,4,4,128]{3,0,2,1:T(8,128)S(1)} %fusion.100) | copy-start | bytes 196612
  32.3 13.1 %copy-start.38 = (f32[8,4,4]{0,2,1:T(4,128)}, f32[8,4,4]{0,2,1:T(4,128)S(1)}, u32[]{:S(2)}) copy-start(f32[8,4,4]{0,2,1:T(4,128)S(1)} %slice_reduce_fusion) | copy-start | bytes 1540
  33.3 138.6 %copy-start.30 = (f32[4,8,4]{1,2,0:T(4,128)}, f32[4,8,4]{1,2,0:T(4,128)S(1)}, u32[]{:S(2)}) copy-start(f32[4,8,4]{1,2,0:T(4,128)S(1)} %get-tuple-element.245) | copy-start | bytes 1540
  36.2 39.6 %copy-start.62 = (pred[4,4]{0,1:T(4,128)(4,1)}, pred[4,4]{0,1:T(4,128)(4,1)S(1)}, u32[]{:S(2)}) copy-start(pred[4,4]{0,1:T(4,128)(4,1)S(1)} %iota_compare_fusion.2) | copy-start | bytes 52
  36.5 39.3 %copy-start.49 = (f32[4,128]{1,0:T(4,128)}, f32[4,128]{1,0:T(4,128)S(1)}, u32[]{:S(2)}) copy-start(f32[4,128]{1,0:T(4,128)S(1)} %get-tuple-element.168) | copy-start | bytes 6148
  36.5 39.3 %copy-start.53 = (f32[4,128]{1,0:T(4,128)}, f32[4,128]{1,0:T(4,128)S(1)}, u32[]{:S(2)}) copy-start(f32[4,128]{1,0:T(4,128)S(1)} %get-tuple-element.169) | copy-start | bytes 6148
  36.7 39.1 %copy-start.34 = (f32[4,8,4,4]{1,3,2,0:T(4,128)}, f32[4,8,4,4]{1,3,2,0:T(4,128)S(1)}, u32[]{:S(2)}) copy-start(f32[4,8,4,4]{1,3,2,0:T(4,128)S(1)} %get-tuple-element.160) | copy-start | bytes 6148
  36.7 135.7 %copy-start.32 = (f32[4,8,4,4]{1,3,2,0:T(4,128)}, f32[4,8,4,4]{1,3,2,0:T(4,128)S(1)}, u32[]{:S(2)}) copy-start(f32[4,8,4,4]{1,3,2,0:T(4,128)S(1)} %get-tuple-element.161) | copy-start | bytes 6148
  82.5 6.6 %collective-permute-start = (bf16[8,768,3]{1,2,0:T(4,128)(2,1)S(1)}, bf16[8,768,3]{1,2,0:T(4,128)(2,1)S(1)}, u32[]{:S(2)}, u32[]{:S(2)}) collective-permute-start(bf16[8,768,3]{1,2,0:T(4,128)(2,1)S(1)} %slice.204), channel_id=1, source_target_pairs={{0,1},{1,2},{2,3},{4,5},{5,6},{6,7},{8,9},{9,10},{10,11},{12,13},{... | collective-permute-start | bytes 110600 | tf_op jit(solution)/shard_map/ppermute | solution.py:18
  89.0 160.7 %copy-start.10 = (bf16[8,4,64,4,128]{4,3,2,1,0:T(4,128)(2,1)}, bf16[8,4,64,4,128]{4,3,2,1,0:T(4,128)(2,1)S(1)}, u32[]{:S(2)}) copy-start(bf16[8,4,64,4,128]{4,3,2,1,0:T(4,128)(2,1)S(1)} %reshape.296) | copy-start | bytes 6291460
  89.1 82.2 %copy-start.64 = (pred[4,4]{0,1:T(4,128)(4,1)}, pred[4,4]{0,1:T(4,128)(4,1)S(1)}, u32[]{:S(2)}) copy-start(pred[4,4]{0,1:T(4,128)(4,1)S(1)} %copy.357) | copy-start | bytes 52
  155.9 9.3 %copy-start.13 = (f32[8,4,64,256]{3,2,1,0:T(8,128)}, f32[8,4,64,256]{3,2,1,0:T(8,128)S(1)}, u32[]{:S(2)}) copy-start(f32[8,4,64,256]{3,2,1,0:T(8,128)S(1)} %get-tuple-element.175) | copy-start | bytes 6291460
  165.2 48.7 %collective-permute-start.1 = (f32[8,4,64,256]{3,2,1,0:T(8,128)}, f32[8,4,64,256]{3,2,1,0:T(8,128)}, u32[]{:S(2)}, u32[]{:S(2)}) collective-permute-start(f32[8,4,64,256]{3,2,1,0:T(8,128)} %broadcast_add_fusion), channel_id=1, source_target_pairs={{0,1},{1,2},{2,3},{4,5},{5,6},{6,7},{8,9},{9,10},{10,11},{12,13},{... | collective-permute-start | bytes 6291464 | tf_op jit(solution)/shard_map/ppermute | solution.py:18
  170.0 49.4 %collective-permute-start.2 = (f32[8,4,64,256]{3,2,1,0:T(8,128)}, f32[8,4,64,256]{3,2,1,0:T(8,128)}, u32[]{:S(2)}, u32[]{:S(2)}) collective-permute-start(f32[8,4,64,256]{3,2,1,0:T(8,128)} %fusion.89), channel_id=1, source_target_pairs={{1,0},{2,1},{3,2},{5,4},{6,5},{7,6},{9,8},{10,9},{11,10},{13,12},{... | collective-permute-start | bytes 6291464 | tf_op jit(solution)/shard_map/ppermute | solution.py:18
  172.1 57.8 %copy-start.44 = (f32[8,4,4,128]{3,2,1,0:T(4,128)}, f32[8,4,4,128]{3,2,1,0:T(4,128)S(1)}, u32[]{:S(2)}) copy-start(f32[8,4,4,128]{3,2,1,0:T(4,128)S(1)} %copy.350) | copy-start | bytes 196612
  172.4 9.4 %copy-start.42 = (f32[2,8,4,4]{1,3,2,0:T(4,128)}, f32[2,8,4,4]{1,3,2,0:T(4,128)S(1)}, u32[]{:S(2)}) copy-start(f32[2,8,4,4]{1,3,2,0:T(4,128)S(1)} %slice_multiply_fusion.7) | copy-start | bytes 3076
  172.7 9.1 %copy-start.51 = (f32[4,4]{1,0:T(4,128)}, f32[4,4]{1,0:T(4,128)S(1)}, u32[]{:S(2)}) copy-start(f32[4,4]{1,0:T(4,128)S(1)} %fusion.150) | copy-start | bytes 196
  173.1 56.7 %copy-start.36 = (f32[4,128,128]{1,2,0:T(8,128)}, f32[4,128,128]{1,2,0:T(8,128)S(1)}, u32[]{:S(2)}) copy-start(f32[4,128,128]{1,2,0:T(8,128)S(1)} %compare_select_fusion) | copy-start | bytes 786436
  173.6 45.8 %copy-start.14 = (f32[8,4,64,256]{3,2,1,0:T(8,128)S(1)}, f32[8,4,64,256]{3,2,1,0:T(8,128)}, u32[]{:S(2)}) copy-start(f32[8,4,64,256]{3,2,1,0:T(8,128)} %copy-done.13) | copy-start | bytes 6291460
  181.8 48.1 %copy-start.24 = (f32[8,4,128,128]{2,3,1,0:T(8,128)}, f32[8,4,128,128]{2,3,1,0:T(8,128)S(1)}, u32[]{:S(2)}) copy-start(f32[8,4,128,128]{2,3,1,0:T(8,128)S(1)} %fusion.162) | copy-start | bytes 6291460
  181.9 48.1 %copy-start.7 = (f32[8,4,64,4,128]{4,2,3,1,0:T(8,128)S(1)}, f32[8,4,64,4,128]{4,2,3,1,0:T(8,128)}, u32[]{:S(2)}) copy-start(f32[8,4,64,4,128]{4,2,3,1,0:T(8,128)} %copy.348) | copy-start | bytes 12582916
  225.2 46.2 %collective-permute-start.3 = (f32[8,4,64,256]{3,2,1,0:T(8,128)}, f32[8,4,64,256]{3,2,1,0:T(8,128)}, u32[]{:S(2)}, u32[]{:S(2)}) collective-permute-start(f32[8,4,64,256]{3,2,1,0:T(8,128)} %get-tuple-element.167), channel_id=1, source_target_pairs={{0,1},{1,2},{2,3},{4,5},{5,6},{6,7},{8,9},{9,10},{10,11},{12,13},{... | collective-permute-start | bytes 6291464 | tf_op jit(solution)/shard_map/ppermute | solution.py:18
  228.6 48.3 %collective-permute-start.4 = (f32[8,4,64,256]{3,2,1,0:T(8,128)}, f32[8,4,64,256]{3,2,1,0:T(8,128)}, u32[]{:S(2)}, u32[]{:S(2)}) collective-permute-start(f32[8,4,64,256]{3,2,1,0:T(8,128)} %get-tuple-element.166), channel_id=1, source_target_pairs={{1,0},{2,1},{3,2},{5,4},{6,5},{7,6},{9,8},{10,9},{11,10},{13,12},{... | collective-permute-start | bytes 6291464 | tf_op jit(solution)/shard_map/ppermute | solution.py:18
  229.9 14.4 %copy-start.4 = (f32[8,256,512]{1,2,0:T(8,128)S(1)}, f32[8,256,512]{1,2,0:T(8,128)}, u32[]{:S(2)}) copy-start(f32[8,256,512]{1,2,0:T(8,128)} %get-tuple-element.128) | copy-start | bytes 12582916
  244.3 5.4 copy-start.21
  244.3 5.4 copy-start.2
  249.6 27.2 %copy-start.15 = (f32[8,4,64,256]{3,2,1,0:T(8,128)S(1)}, f32[8,4,64,256]{3,2,1,0:T(8,128)}, u32[]{:S(2)}) copy-start(f32[8,4,64,256]{3,2,1,0:T(8,128)} %copy-done.13) | copy-start | bytes 6291460
  249.7 43.3 %slice-start = ((s8[8388608]{0:T(1024)(128)(4,1)}), s8[4194304]{0:T(1024)(128)(4,1)S(1)}, s32[]{:S(2)}) async-start(s8[8388608]{0:T(1024)(128)(4,1)} %bitcast.239), calls=%async_computation.6 | async-start | bytes 8388608
  257.9 35.1 %copy-start.6 = (f32[8,4,4,64,256]{4,3,1,2,0:T(8,128)}, f32[8,4,4,64,256]{4,3,1,2,0:T(8,128)S(1)}, u32[]{:S(2)}) copy-start(f32[8,4,4,64,256]{4,3,1,2,0:T(8,128)S(1)} %fusion.66) | copy-start | bytes 25165828
  257.9 35.1 %slice-start.1 = ((s8[8388608]{0:T(1024)(128)(4,1)}), s8[4194304]{0:T(1024)(128)(4,1)S(1)}, s32[]{:S(2)}) async-start(s8[8388608]{0:T(1024)(128)(4,1)} %bitcast.239), calls=%async_computation.7 | async-start | bytes 8388608
  282.6 44.5 %collective-permute-start.5 = (f32[8,4,64,256]{3,2,1,0:T(8,128)}, f32[8,4,64,256]{3,2,1,0:T(8,128)S(1)}, u32[]{:S(2)}, u32[]{:S(2)}) collective-permute-start(f32[8,4,64,256]{3,2,1,0:T(8,128)} %get-tuple-element.165), channel_id=1, source_target_pairs={{0,1},{1,2},{2,3},{4,5},{5,6},{6,7},{8,9},{9,10},{10,11},{12,13},{... | collective-permute-start | bytes 6291464 | tf_op jit(solution)/shard_map/ppermute | solution.py:18
  284.2 47.1 %collective-permute-start.6 = (f32[8,4,64,256]{3,2,1,0:T(8,128)}, f32[8,4,64,256]{3,2,1,0:T(8,128)S(1)}, u32[]{:S(2)}, u32[]{:S(2)}) collective-permute-start(f32[8,4,64,256]{3,2,1,0:T(8,128)} %get-tuple-element.164), channel_id=1, source_target_pairs={{1,0},{2,1},{3,2},{5,4},{6,5},{7,6},{9,8},{10,9},{11,10},{13,12},{... | collective-permute-start | bytes 6291464 | tf_op jit(solution)/shard_map/ppermute | solution.py:18
  332.6 8.2 %copy-start.8 = (f32[8,4,64,4,128]{4,2,3,1,0:T(8,128)S(1)}, f32[8,4,64,4,128]{4,2,3,1,0:T(8,128)}, u32[]{:S(2)}) copy-start(f32[8,4,64,4,128]{4,2,3,1,0:T(8,128)} %copy.348) | copy-start | bytes 12582916
  383.0 8.7 %copy-start.17 = (f32[8,4,64,256]{3,2,1,0:T(8,128)S(1)}, f32[8,4,64,256]{3,2,1,0:T(8,128)}, u32[]{:S(2)}) copy-start(f32[8,4,64,256]{3,2,1,0:T(8,128)} %copy-done.16) | copy-start | bytes 6291460
  391.7 6.8 %copy-start.11 = (bf16[8,4,64,4,128]{4,3,2,1,0:T(4,128)(2,1)S(1)}, bf16[8,4,64,4,128]{4,3,2,1,0:T(4,128)(2,1)}, u32[]{:S(2)}) copy-start(bf16[8,4,64,4,128]{4,3,2,1,0:T(4,128)(2,1)} %copy-done.10) | copy-start | bytes 6291460
  391.7 7.7 %copy-start.20 = (f32[8,4,128,256]{3,2,1,0:T(8,128)S(1)}, f32[8,4,128,256]{3,2,1,0:T(8,128)}, u32[]{:S(2)}) copy-start(f32[8,4,128,256]{3,2,1,0:T(8,128)} %fusion.163) | copy-start | bytes 12582916
  398.5 9.8 %copy-start.5 = (f32[8,4,4,64,256]{4,3,1,2,0:T(8,128)}, f32[8,4,4,64,256]{4,3,1,2,0:T(8,128)S(1)}, u32[]{:S(2)}) copy-start(f32[8,4,4,64,256]{4,3,1,2,0:T(8,128)S(1)} %get-tuple-element.137) | copy-start | bytes 25165828
  422.1 22.5 %copy-start = (f32[8,768,512]{1,2,0:T(8,128)}, f32[8,768,512]{1,2,0:T(8,128)S(1)}, u32[]{:S(2)}) copy-start(f32[8,768,512]{1,2,0:T(8,128)S(1)} %get-tuple-element.112) | copy-start | bytes 37748740
  443.4 30.8 %collective-permute-start.7 = (f32[8,768,3]{1,2,0:T(4,128)S(1)}, f32[8,768,3]{1,2,0:T(4,128)S(1)}, u32[]{:S(2)}, u32[]{:S(2)}) collective-permute-start(f32[8,768,3]{1,2,0:T(4,128)S(1)} %pad_add_fusion.2), channel_id=1, source_target_pairs={{1,0},{2,1},{3,2},{5,4},{6,5},{7,6},{9,8},{10,9},{11,10},{13,12},{... | collective-permute-start | bytes 221192 | tf_op jit(solution)/shard_map/ppermute | solution.py:18
  474.2 4.9 copy-start.3
  488.4 105.8 %reduce-scatter.5.cloned.1.call-start = ((), (), s32[]{:S(2)}) async-start(), calls=%async_computation.5 | async-start | bytes 4718592 | tf_op jit(solution)/shard_map/reduce_scatter | solution.py:237
  494.3 4.4 copy-start.41
  494.3 4.4 copy-start.35
  494.3 4.5 copy-start.63
  494.3 4.6 copy-start.43
  494.3 4.6 copy-start.33
  494.3 4.6 copy-start.65
  494.3 4.7 copy-start.29
  494.3 4.7 copy-start.39
  494.4 4.7 copy-start.50
  494.4 4.9 copy-start.59
  494.4 5.2 copy-start.46
  499.6 11.6 %copy-start.12 = (bf16[8,4,64,4,128]{4,3,2,1,0:T(4,128)(2,1)S(1)}, bf16[8,4,64,4,128]{4,3,2,1,0:T(4,128)(2,1)}, u32[]{:S(2)}) copy-start(bf16[8,4,64,4,128]{4,3,2,1,0:T(4,128)(2,1)} %copy-done.10) | copy-start | bytes 6291460
  499.6 12.7 %copy-start.48 = (bf16[8,4,512]{2,1,0:T(4,128)(2,1)S(1)}, bf16[8,4,512]{2,1,0:T(4,128)(2,1)}, u32[]{:S(2)}) copy-start(bf16[8,4,512]{2,1,0:T(4,128)(2,1)} %param.16) | copy-start | bytes 98308
  499.6 12.7 %copy-start.54 = (f32[4,128]{1,0:T(4,128)S(1)}, f32[4,128]{1,0:T(4,128)}, u32[]{:S(2)}) copy-start(f32[4,128]{1,0:T(4,128)} %copy-done.53) | copy-start | bytes 6148
  499.6 12.7 %copy-start.57 = (f32[8,4]{0,1:T(4,128)S(1)}, f32[8,4]{0,1:T(4,128)}, u32[]{:S(2)}) copy-start(f32[8,4]{0,1:T(4,128)} %copy-done.56) | copy-start | bytes 388
  499.6 12.7 %copy-start.61 = (f32[8,4]{0,1:T(4,128)S(1)}, f32[8,4]{0,1:T(4,128)}, u32[]{:S(2)}) copy-start(f32[8,4]{0,1:T(4,128)} %copy-done.60) | copy-start | bytes 388
  499.6 12.7 %copy-start.66 = (f32[8,4,4,128]{3,2,1,0:T(4,128)S(1)}, f32[8,4,4,128]{3,2,1,0:T(4,128)}, u32[]{:S(2)}) copy-start(f32[8,4,4,128]{3,2,1,0:T(4,128)} %get-tuple-element.98) | copy-start | bytes 196612
  499.6 12.7 %copy-start.67 = (f32[8,4,4,128]{3,2,1,0:T(4,128)S(1)}, f32[8,4,4,128]{3,2,1,0:T(4,128)}, u32[]{:S(2)}) copy-start(f32[8,4,4,128]{3,2,1,0:T(4,128)} %get-tuple-element.99) | copy-start | bytes 196612
  (18 other events, 33.3 us)
Sparse Core Ops, SparseCore 0:
  10.5 30.6 all-gather.3
  43.6 27.8 all-gather.5
  488.5 50.6 reduce-scatter.2
  542.8 51.3 reduce-scatter.4

commit v5 on v4

--- a/solution.py
+++ b/solution.py
@@ -107,6 +107,26 @@
     )
 
 
+def conv_part(raw_chan, rim_chan, weight, bias, segment_extended):
+    padded = jnp.concatenate([rim_chan, raw_chan], axis=1)
+    return conv_silu(padded, weight, bias, segment_extended, raw_chan.shape[1])
+
+
+def scan_part(x_conv, b_conv, c_conv, dt_pre, bias_dt, log_rate, skip_gain, segment_extended):
+    step_size = jax.nn.softplus(dt_pre + bias_dt[:, None])
+    log_decay = step_size * (-jnp.exp(log_rate))[:, None]
+    return span_terms(
+        x_conv,
+        b_conv,
+        c_conv,
+        step_size,
+        log_decay,
+        segment_extended[TAPS - 1 :],
+        segment_extended[TAPS - 2],
+        skip_gain,
+    )
+
+
 def weighted_sum(weight, stacked):
     return jnp.sum(weight[..., None, None] * stacked, axis=-3)
 
@@ -149,8 +169,6 @@
     n_heads = dt_raw.shape[1]
     length = x_in.shape[2]
     blocks = length // SPAN
-    b_full = lax.all_gather(b_in, "seq", axis=1, tiled=True)
-    c_full = lax.all_gather(c_in, "seq", axis=1, tiled=True)
     groups_held = conv_weight.shape[0]
     packed = jnp.concatenate(
         [
@@ -172,41 +190,59 @@
     d_skip_all = packed_all[:, bounds[4] :]
     x_total = weight_all.shape[2] - 2 * STATE
 
+    b_width = b_in.shape[1]
+
     def own_channels(table):
-        mine = lax.dynamic_slice_in_dim(table, lane * x_width, x_width, axis=table.ndim - 1)
-        return jnp.concatenate([mine, table[..., x_total:]], axis=table.ndim - 1)
-
-    weight_here = own_channels(weight_all)
-    bias_here = own_channels(bias_all)
+        pieces = [
+            lax.dynamic_slice_in_dim(table, start + lane * width, width, axis=table.ndim - 1)
+            for start, width in ((0, x_width), (x_total, b_width), (x_total + STATE, b_width))
+        ]
+        return (pieces[0], jnp.concatenate(pieces[1:], axis=table.ndim - 1))
+
+    weight_x, weight_bc = own_channels(weight_all)
+    bias_x, bias_bc = own_channels(bias_all)
     dt_bias_here = lax.dynamic_slice_in_dim(dt_bias_all, lane * n_heads, n_heads, axis=1)
     a_log_here = lax.dynamic_slice_in_dim(a_log_all, lane * n_heads, n_heads, axis=1)
     d_skip_here = lax.dynamic_slice_in_dim(d_skip_all, lane * n_heads, n_heads, axis=1)
     groups_here = x_in.shape[0]
-    raw_chan = jnp.concatenate([x_in, b_full, c_full], axis=1)
+    raw_chan = jnp.concatenate([x_in, b_in, c_in], axis=1)
     rim_chan = passed_along(raw_chan[:, :, length - (TAPS - 1) :], "head", 1)
     rank = lax.axis_index("head")
     positions = rank * length + jnp.arange(-(TAPS - 1), length, dtype=jnp.int32)
     segment_extended = segment_ids(positions, doc_lengths)
-
-    def local_terms(raw_float, rim_float, dt_float):
-        return jax.vmap(group_terms, in_axes=(0, 0, 0, 0, 0, 0, 0, 0, None))(
-            raw_float,
-            rim_float,
+    each_group = (0, 0, 0, 0, None)
+
+    def own_conv(x_float, bc_float, rim_float):
+        x_conv = jax.vmap(conv_part, in_axes=each_group)(
+            x_float, rim_float[:, :x_width], weight_x, bias_x, segment_extended
+        )
+        bc_conv = jax.vmap(conv_part, in_axes=each_group)(
+            bc_float, rim_float[:, x_width:], weight_bc, bias_bc, segment_extended
+        )
+        return (x_conv, bc_conv)
+
+    (x_conv, bc_conv), pull_conv = jax.vjp(
+        own_conv,
+        x_in.astype(jnp.float32),
+        jnp.concatenate([b_in, c_in], axis=1).astype(jnp.float32),
+        rim_chan.astype(jnp.float32),
+    )
+    b_conv = lax.all_gather(bc_conv[:, :b_width], "seq", axis=1, tiled=True)
+    c_conv = lax.all_gather(bc_conv[:, b_width:], "seq", axis=1, tiled=True)
+
+    def local_terms(x_float, b_float, c_float, dt_float):
+        return jax.vmap(scan_part, in_axes=(0, 0, 0, 0, 0, 0, 0, None))(
+            x_float,
+            b_float,
+            c_float,
             dt_float,
-            weight_here,
-            bias_here,
             dt_bias_here,
             a_log_here,
             d_skip_here,
             segment_extended,
         )
 
-    terms, pull_terms = jax.vjp(
-        local_terms,
-        raw_chan.astype(jnp.float32),
-        rim_chan.astype(jnp.float32),
-        dt_raw.astype(jnp.float32),
-    )
+    terms, pull_terms = jax.vjp(local_terms, x_conv, b_conv, c_conv, dt_raw.astype(jnp.float32))
     y_intra, c_three, entry, carry, states = terms
     before, total = reach(carry)
     state_zero = jnp.zeros((groups_here, n_heads, HEAD_DIM, STATE), jnp.float32)
@@ -226,17 +262,22 @@
     (y_scan, state_out), pull_out = jax.vjp(finish, terms, state_in)
     y_out = y_scan.astype(jnp.bfloat16)
     d_terms, _ = pull_out((cot_float, grad_out))
-    d_raw, d_rim, d_dt = pull_terms(d_terms)
+    d_x_conv, d_b_conv, d_c_conv, d_dt = pull_terms(d_terms)
+    d_bc_conv = jnp.concatenate(
+        [
+            lax.psum_scatter(d_b_conv, "seq", scatter_dimension=1, tiled=True),
+            lax.psum_scatter(d_c_conv, "seq", scatter_dimension=1, tiled=True),
+        ],
+        axis=1,
+    )
+    d_x, d_bc, d_rim = pull_conv((d_x_conv, d_bc_conv))
+    d_raw = jnp.concatenate([d_x, d_bc], axis=1)
     returned = passed_along(d_rim, "head", -1)
     cut_at = length - (TAPS - 1)
     d_raw = jnp.concatenate([d_raw[:, :, :cut_at], d_raw[:, :, cut_at:] + returned], axis=2)
     x_grad = d_raw[:, :x_width].astype(jnp.bfloat16)
-    b_grad = lax.psum_scatter(
-        d_raw[:, x_width : x_width + STATE], "seq", scatter_dimension=1, tiled=True
-    ).astype(jnp.bfloat16)
-    c_grad = lax.psum_scatter(
-        d_raw[:, x_width + STATE :], "seq", scatter_dimension=1, tiled=True
-    ).astype(jnp.bfloat16)
+    b_grad = d_raw[:, x_width : x_width + b_width].astype(jnp.bfloat16)
+    c_grad = d_raw[:, x_width + b_width :].astype(jnp.bfloat16)
     dt_grad = d_dt.astype(jnp.bfloat16)
     return (y_out, x_grad, b_grad, c_grad, dt_grad)
 

time: 608 us -> 488 us (0.80)
  waiting for transfers between devices: 166 us -> 101 us
  other arithmetic: 151 us -> 102 us
  local copies, waits for them, and re-layouts: 108 us -> 83.2 us
  matrix products: 128 us -> 142 us
    reduce_scatter x2, waiting for transfers between devices: 59.4 us -> 0.04 us  [the longest x1 0.02 us: shards(): lax.psum_scatter(d_b_conv, 'seq', scatter_dimension=1, tiled=True)]
    mul x3 -> x5, other arithmetic: 33.9 us -> 6.35 us  [conv_silu(): weight[offset][:, None] * padded[:, offset:offset + length]]
    slice x8 -> x10, local copies, waits for them, and re-layouts: 32 us -> 6.77 us  [the longest x1 1.79 us: shards(): d_raw[:, :, cut_at:] + returned]
    reshape x4 -> x2, local copies, waits for them, and re-layouts: 33.6 us -> 10.8 us  [span_terms(): x_four = x_conv.reshape(n_heads, HEAD_DIM, blocks, SPAN)]
    add_any x1 -> x2, other arithmetic: 19.1 us -> 5.72 us  [conv_silu(): padded[:, offset:offset + length]]
    mul x1 -> x2, other arithmetic: 26.8 us -> 14.5 us  [conv_silu(): return jax.nn.silu(total)]
    reshape x0 -> x2, local copies, waits for them, and re-layouts: none -> 11.1 us  [the longest x1 5.58 us: span_terms(): c_three = c_conv.reshape(STATE, blocks, SPAN)]
    all_gather x2, waiting for transfers between devices: 29.8 us -> 19.4 us  [the longest x1 17.3 us: shards(): c_conv = lax.all_gather(bc_conv[:, b_width:], 'seq', axis=1, tiled=True)]
  transfers between devices with their start and end apart: 12 -> 12, of which waited for: 10 -> 8; matrix products, arithmetic and copies ran while one was open for 26% -> 51% of each run, Pallas kernels for 0% -> 0%
where the time goes in v5:
time: 488 us; the launch traced here: 483 us
  matrix products  142 us (29%)
  other arithmetic  102 us (21%)
  waiting for transfers between devices  101 us (21%)
  local copies, waits for them, and re-layouts  83.2 us (17%)
  starting transfers between devices  23.1 us (5%)
  between operations  15.6 us (3%)
  blocking collectives  15.4 us (3%)
    ppermute x8, waiting for transfers between devices, passed_along(): lax.ppermute(value, axis, [(source, source + steps) for source in range(f...  81.8 us
    dot_general x3, matrix products, span_terms(): jnp.einsum('hcij,hpcj->hpci', decay * scores[None], weighted, precision=p...  41.3 us
    dot_general x3, matrix products, span_terms(): jnp.einsum('hpcj,hcj,ncj->hcpn', weighted, keep_end, b_three, precision=p...  41.1 us
    dot_general x3, matrix products, assemble(): jnp.einsum('nci,hci,chpn->hpci', c_three, entry, starts, precision=precise)  32.7 us
    reduce_sum x2, other arithmetic, weighted_sum(): return jnp.sum(weight[..., None, None] * stacked, axis=-3)  26.9 us
    ppermute x8, starting transfers between devices, passed_along(): lax.ppermute(value, axis, [(source, source + steps) for source in range(f...  22.3 us
    dot_general x3, matrix products, span_terms(): scores = jnp.einsum('nci,ncj->cij', c_three, b_three, precision=precise)  19.2 us
    all_gather x1, waiting for transfers between devices, shards(): c_conv = lax.all_gather(bc_conv[:, b_width:], 'seq', axis=1, tiled=True)  17.3 us
  transfers between devices with their start and end apart: 12, of which 8 were waited for; matrix products, arithmetic and copies ran while one was open for 51% of the time, Pallas kernels for 0%

profile of v5, /device:TPU:0, one launch (start us, length us, event | category | flops | bytes accessed | tf_op | source)
XLA Modules:
  0.0 482.6 jit_solution(5604599219815571334)
XLA Ops:
  7.2 3.4 copy.347
  10.7 1.8 copy.348
  12.4 1.7 copy.349
  14.9 4.9 %collective-permute-start = (bf16[8,320,3]{1,0,2:T(8,128)(2,1)S(1)}, bf16[8,320,3]{1,0,2:T(8,128)(2,1)S(1)}, u32[]{:S(2)}, u32[]{:S(2)}) collective-permute-start(bf16[8,320,3]{1,0,2:T(8,128)(2,1)S(1)} %pad_maximum_fusion.3), channel_id=1, source_target_pairs={{0,1},{1,2},{2,3},{4,5},{5,6},{6,7},{8,9},{9,10},{10,11},{12,13},{... | collective-permute-start | bytes 46088 | tf_op jit(solution)/shard_map/ppermute | solution.py:18
  20.1 15.4 %all-gather = f32[4,2,12896]{2,1,0:T(2,128)S(1)} all-gather(f32[1,2,12896]{2,1,0:T(2,128)S(1)} %bitcast.253), channel_id=1, replica_groups=mesh['seq'=8,'head'=4] {'head'}, dimensions={0}, use_global_device_ids=true | all-gather | bytes 515840 | tf_op jit(solution)/shard_map/all_gather | solution.py:183
  38.4 2.4 fusion.102
  44.1 2.6 convert_element_type.83
  52.0 2.6 reshape.301
  55.2 1.3 constant_dynamic-slice_fusion.6
  57.8 12.1 %fusion.50 = (f32[8,256,512]{2,1,0:T(8,128)}, f32[8,256,512]{2,1,0:T(8,128)}) fusion(f32[8,256,512]{2,1,0:T(8,128)} %convert_element_type.83, f32[8,256]{1,0:T(8,128)S(1)} %get-tuple-element.150, f32[512]{0:T(512)} %copy-done.61, f32[8,256,3]{2,1,0:T(8,128)S(1)} %copy.350, f32[8,256]{1,0:T(8,128)S(1)} %get-tuple-element.148, f32[512]{0:T(512)} %copy-done.63, ...), kind=kLoop, calls=%fused_computation.88 | loop fusion | flops 18874368 | bytes 12654592 | tf_op jit(solution)/shard_map/jvp(vmap(jit(silu)))/mul | solution.py:53
  69.9 5.3 %reshape.297 = f32[8,4,64,4,128]{4,3,2,1,0:T(4,128)} reshape(f32[8,256,512]{2,1,0:T(8,128)} %get-tuple-element.122) | data formatting | bytes 8388608 | tf_op jit(solution)/shard_map/jvp(vmap())/reshape | solution.py:59
  75.2 2.1 all-gather.6.cloned.1.call-done
  77.3 5.3 %copy.363 = f32[8,256,512]{1,2,0:T(8,128)} copy(f32[8,256,512]{2,0,1:T(8,128)} %all-gather.6.cloned.1.call-done) | data formatting | bytes 8388608 | tf_op jit(solution)/shard_map/all_gather | solution.py:230
  82.6 13.8 %multiply_reduce_fusion.5 = (f32[8,4,64,256]{3,2,1,0:T(8,128)S(1)}, f32[8,4,4,64,256]{4,3,1,2,0:T(8,128)}) fusion(f32[8,4,4]{1,2,0:T(4,128)S(1)} %copy-done.56, f32[8,256,4,128,1]{1,3,4,2,0:T(8,128)} %bitcast.239, f32[8,4,64,4,128]{4,3,2,1,0:T(4,128)} %reshape.297, f32[8,4,4,128]{3,2,1,0:T(4,128)S(1)} %copy.372, f32[8,4,4,128]{3,2,1,0:T(4,128)S(1)} %copy.353), kind=kOutput, calls=%fused_computation.25 | convolution fusion | flops 3226992640 | bytes 19005952 | tf_op jit(solution)/shard_map/jvp(vmap(hpcj,hcj,ncj->hcpn))/dot_general | solution.py:78
  97.6 1.5 broadcast_add_fusion
  99.2 17.3 %all-gather.4.cloned.1.call-done = f32[8,256,512]{2,0,1:T(8,128)} async-done(((f32[8,32,512]{2,0,1:T(8,128)}), f32[8,256,512]{2,0,1:T(8,128)}) %all-gather.4.cloned.1.call-update) | async-done | bytes 4194320 | tf_op jit(solution)/shard_map/all_gather | solution.py:231
  116.5 5.3 %copy.361 = f32[8,256,512]{1,2,0:T(8,128)} copy(f32[8,256,512]{2,0,1:T(8,128)} %all-gather.4.cloned.1.call-done) | data formatting | bytes 8388608 | tf_op jit(solution)/shard_map/all_gather | solution.py:231
  121.8 7.0 %fusion.82 = f32[8,4,64,256]{3,2,1,0:T(8,128)} fusion(f32[8,256,4,128,1]{1,3,2,4,0:T(8,128)} %bitcast.234, f32[8,4,4,128]{3,2,1,0:T(4,128)S(1)} %copy.382, bf16[8,4,64,4,128]{4,3,2,1,0:T(4,128)(2,1)S(1)} %reshape.301), kind=kOutput, calls=%fused_computation.113 | convolution fusion | flops 3223322624 | bytes 8454144 | tf_op jit(solution)/shard_map/ghpci,ghci,gnci->ghpn/dot_general | solution.py:252
  128.8 3.5 collective-permute-start.1
  138.8 39.0 %collective-permute-done.1 = f32[8,4,64,256]{3,2,1,0:T(8,128)S(1)} collective-permute-done((f32[8,4,64,256]{3,2,1,0:T(8,128)}, f32[8,4,64,256]{3,2,1,0:T(8,128)S(1)}, u32[]{:S(2)}, u32[]{:S(2)}) %collective-permute-start.1) | collective-permute-done | bytes 2097184 | tf_op jit(solution)/shard_map/ppermute | solution.py:18
  177.8 4.2 collective-permute-done.2
  182.1 5.7 %multiply_add_fusion.2 = (f32[8,4,64,256]{3,2,1,0:T(8,128)}, f32[8,4,64,256]{3,2,1,0:T(8,128)}) fusion(f32[8,4,64,256]{3,2,1,0:T(8,128)} %fusion.82, f32[8,4,64,256]{3,2,1,0:T(8,128)} %collective-permute-done.2, f32[8,4]{1,0:T(8,128)S(1)} %copy.377, f32[8,4,64,256]{3,2,1,0:T(8,128)S(1)} %collective-permute-done.1, f32[8,4,64,256]{3,2,1,0:T(8,128)} %copy-done.14, ...), kind=kLoop, calls=%fused_computation.103 | loop fusion | flops 2621440 | bytes 12583168 | tf_op jit(solution)/shard_map/add | solution.py:31
  187.8 4.6 collective-permute-start.3
  192.4 1.7 collective-permute-start.4
  194.1 5.8 %fusion.171 = f32[8,4,128,128]{2,3,1,0:T(8,128)} fusion(f32[8,256,4,128]{1,3,2,0:T(8,128)S(1)} %bitcast.236, f32[8,256,4,128]{1,3,2,0:T(8,128)S(1)} %bitcast.242), kind=kOutput, calls=%fused_computation.304 | convolution fusion | flops 1610612736 | bytes 10485760 | tf_op jit(solution)/shard_map/jvp(vmap(nci,ncj->cij))/dot_general | solution.py:72
  199.9 7.5 %fusion.60 = f32[8,4,4,64,256]{4,3,1,2,0:T(8,128)S(1)} fusion(f32[8,256,4,128,1]{1,3,4,2,0:T(8,128)S(1)} %bitcast.237, f32[8,4,4,128]{3,2,1,0:T(4,128)S(1)} %copy-done.30, bf16[8,4,64,4,128]{4,3,2,1,0:T(4,128)(2,1)S(1)} %copy-done.7), kind=kOutput, calls=%fused_computation.97 | convolution fusion | flops 3223322624 | bytes 14745600 | tf_op jit(solution)/shard_map/transpose(jvp(vmap(nci,hci,chpn->hpci)))/dot_general | solution.py:149
  207.5 17.9 %fusion.104 = (f32[8,4,4,128]{3,2,1,0:T(4,128)}, f32[8,4,4,128]{3,2,1,0:T(4,128)}, f32[8,4,128,128]{2,3,1,0:T(8,128)}) fusion(f32[8,4,4,128]{3,2,1,0:T(4,128)} %copy.356, f32[4,128,128]{1,2,0:T(8,128)} %compare_select_fusion, f32[8,4,128,128]{2,3,1,0:T(8,128)} %fusion.171, bf16[8,4,4,64,128]{4,2,3,1,0:T(4,128)(2,1)} %bitcast.245, ...), kind=kOutput, calls=%fused_computation.149 | convolution fusion | flops 1642561536 | bytes 11010048 | tf_op jit(solution)/shard_map/transpose(jvp(vmap(hcij,hpcj->hpci)))/dot_general | solution.py:74
  225.4 10.1 %collective-permute-done.3 = f32[8,4,64,256]{3,2,1,0:T(8,128)} collective-permute-done((f32[8,4,64,256]{3,2,1,0:T(8,128)}, f32[8,4,64,256]{3,2,1,0:T(8,128)}, u32[]{:S(2)}, u32[]{:S(2)}) %collective-permute-start.3) | collective-permute-done | bytes 2097184 | tf_op jit(solution)/shard_map/ppermute | solution.py:18
  235.5 5.4 %collective-permute-done.4 = f32[8,4,64,256]{3,2,1,0:T(8,128)} collective-permute-done((f32[8,4,64,256]{3,2,1,0:T(8,128)}, f32[8,4,64,256]{3,2,1,0:T(8,128)}, u32[]{:S(2)}, u32[]{:S(2)}) %collective-permute-start.4) | collective-permute-done | bytes 2097184 | tf_op jit(solution)/shard_map/ppermute | solution.py:18
  240.9 6.3 %multiply_add_fusion = (f32[8,4,64,256]{3,2,1,0:T(8,128)}, f32[8,4,64,256]{3,2,1,0:T(8,128)}) fusion(f32[8,4,64,256]{3,2,1,0:T(8,128)} %fusion.82, f32[8,4,64,256]{3,2,1,0:T(8,128)} %collective-permute-done.4, f32[8,4]{1,0:T(8,128)S(1)} %copy-done.68, f32[8,4,64,256]{3,2,1,0:T(8,128)} %collective-permute-done.3, f32[8,4,64,256]{3,2,1,0:T(8,128)} %copy-done.14, ...), kind=kLoop, calls=%fused_computation.101 | loop fusion | flops 2621440 | bytes 12583168 | tf_op jit(solution)/shard_map/add | solution.py:31
  247.3 3.4 collective-permute-start.5
  252.0 5.1 %fusion.172 = f32[8,4,128,256]{3,2,1,0:T(8,128)} fusion(f32[8,4,128,128]{2,3,1,0:T(8,128)S(1)} %copy-done.18, f32[8,256,4,128]{1,3,2,0:T(8,128)S(1)} %bitcast.238), kind=kOutput, calls=%fused_computation.305 | convolution fusion | flops 1610612736 | bytes 10485760 | tf_op jit(solution)/shard_map/transpose(jvp(vmap(nci,ncj->cij)))/dot_general | solution.py:72
  257.2 17.9 %multiply_reduce_fusion = (f32[8,4,4,4]{3,2,1,0:T(4,128)}, f32[8,4,4,64,256]{4,3,2,1,0:T(8,128)}, f32[8,4,4,64,256]{4,3,2,1,0:T(8,128)}) fusion(f32[8,4,4,4]{3,2,1,0:T(4,128)S(1)} %bitcast_multiply_fusion.8, f32[8,4,4,64,256]{4,3,1,2,0:T(8,128)S(1)} %bitcast.244, f32[8,4,4,64,256]{4,3,1,2,0:T(8,128)S(1)} %fusion.60), kind=kLoop, calls=%fused_computation.2 | loop fusion | flops 46136832 | bytes 33558528 | tf_op jit(solution)/shard_map/transpose(jvp(vmap()))/reduce_sum | solution.py:131
  275.1 17.6 %collective-permute-done.5 = f32[8,4,64,256]{3,2,1,0:T(8,128)} collective-permute-done((f32[8,4,64,256]{3,2,1,0:T(8,128)}, f32[8,4,64,256]{3,2,1,0:T(8,128)}, u32[]{:S(2)}, u32[]{:S(2)}) %collective-permute-start.5) | collective-permute-done | bytes 2097184 | tf_op jit(solution)/shard_map/ppermute | solution.py:18
  292.7 5.4 %collective-permute-done.6 = f32[8,4,64,256]{3,2,1,0:T(8,128)} collective-permute-done((f32[8,4,64,256]{3,2,1,0:T(8,128)}, f32[8,4,64,256]{3,2,1,0:T(8,128)}, u32[]{:S(2)}, u32[]{:S(2)}) %collective-permute-start.6) | collective-permute-done | bytes 2097184 | tf_op jit(solution)/shard_map/ppermute | solution.py:18
  298.1 9.1 %multiply_reduce_fusion.4 = (f32[8,4,4]{1,2,0:T(4,128)}, f32[8,4,4,64,256]{4,3,1,2,0:T(8,128)S(1)}) fusion(f32[8,4,4,64,256]{4,3,1,2,0:T(8,128)} %get-tuple-element.188, f32[8,4,64,256]{3,2,1,0:T(8,128)} %collective-permute-done.6, f32[8,4,4,64,256]{4,3,2,1,0:T(8,128)} %get-tuple-element.103, f32[8,4,4]{1,2,0:T(4,128)S(1)} %copy-done.53), kind=kLoop, calls=%fused_computation.24 | loop fusion | flops 8388480 | bytes 27264000 | tf_op jit(solution)/shard_map/transpose(jvp(vmap()))/reduce_sum | solution.py:131
  307.1 12.4 %bitcast_add_fusion.2 = f32[8,256,4,128]{1,3,2,0:T(8,128)} fusion(f32[8,4,128,256]{3,2,1,0:T(8,128)} %fusion.172, f32[8,4,4,64,256]{4,3,1,2,0:T(8,128)S(1)} %get-tuple-element.134, f32[8,4,64,4,128]{4,3,2,1,0:T(4,128)S(1)} %copy-done.4, f32[8,4,4,128]{3,2,1,0:T(4,128)} %copy-done.28, f32[8,4,4,128]{3,2,1,0:T(4,128)S(1)} %copy.353), kind=kOutput, calls=%fused_computation.59 | convolution fusion | flops 3224371200 | bytes 21102592 | tf_op jit(solution)/shard_map/transpose(jvp(vmap(hpcj,hcj,ncj->hcpn)))/dot_general | solution.py:78
  319.6 5.6 %copy.406 = f32[8,256,512]{2,0,1:T(8,128)} copy(f32[8,256,512]{1,2,0:T(8,128)} %bitcast.247) | data formatting | bytes 8388608 | tf_op jit(solution)/shard_map/transpose(jvp(vmap()))/reshape | solution.py:60
  326.8 8.2 %fusion.173 = f32[8,4,128,256]{3,2,1,0:T(8,128)} fusion(f32[8,4,128,128]{2,3,1,0:T(8,128)S(1)} %copy-done.19, f32[8,256,4,128]{1,3,2,0:T(8,128)} %bitcast.240), kind=kOutput, calls=%fused_computation.306 | convolution fusion | flops 1610612736 | bytes 10485760 | tf_op jit(solution)/shard_map/transpose(jvp(vmap(nci,ncj->cij)))/dot_general | solution.py:72
  335.0 2.7 multiply_reduce_fusion.6
  337.9 11.5 %multiply_reduce_fusion.3 = (f32[8,4,4]{1,2,0:T(4,128)S(1)}, f32[8,4,4,64,256]{4,3,1,2,0:T(8,128)}) fusion(f32[8,4,4,64,256]{4,3,1,2,0:T(8,128)} %copy-done.2, f32[8,4,64,256]{3,2,1,0:T(8,128)} %collective-permute-done.5, f32[8,4,4]{1,2,0:T(4,128)S(1)} %copy.376, f32[8,4,4,64,256]{4,3,2,1,0:T(8,128)} %get-tuple-element.102), kind=kLoop, calls=%fused_computation.23 | loop fusion | flops 8388480 | bytes 27264000 | tf_op jit(solution)/shard_map/transpose(jvp(vmap()))/reduce_sum | solution.py:142
  349.5 13.9 %bitcast_add_fusion.3 = f32[8,4,128,256]{3,2,1,0:T(8,128)} fusion(f32[8,4,128,256]{3,2,1,0:T(8,128)} %fusion.173, f32[8,4,4,64,256]{4,3,1,2,0:T(8,128)} %get-tuple-element.136, f32[8,4,4,128]{3,2,1,0:T(4,128)S(1)} %copy-done.31, bf16[8,4,64,4,128]{4,3,2,1,0:T(4,128)(2,1)S(1)} %copy-done.8), kind=kOutput, calls=%fused_computation.60 | convolution fusion | flops 3224371200 | bytes 18939904 | tf_op jit(solution)/shard_map/transpose(jvp(vmap(nci,hci,chpn->hpci)))/dot_general | solution.py:149
  363.5 5.6 %copy.411 = f32[8,256,512]{2,0,1:T(8,128)} copy(f32[8,256,512]{1,2,0:T(8,128)} %bitcast.248) | data formatting | bytes 8388608 | tf_op jit(solution)/shard_map/transpose(jvp(vmap()))/reshape | solution.py:61
  369.2 14.9 %fusion.38 = (f32[8,4,4,128]{3,2,1,0:T(4,128)S(1)}, f32[8,4,4,64,128]{4,3,1,2,0:T(8,128)}) fusion(f32[8,4,64,4,128]{4,3,2,1,0:T(4,128)} %reshape.297, f32[8,4,4,128]{3,2,1,0:T(4,128)S(1)} %copy.353, f32[8,4,4,64,256]{4,3,1,2,0:T(8,128)} %copy-done.3, f32[8,256,4,128,1]{1,3,2,4,0:T(8,128)} %bitcast.241), kind=kOutput, calls=%fused_computation.68 | convolution fusion | flops 3224354816 | bytes 21102592 | tf_op jit(solution)/shard_map/transpose(jvp(vmap(hpcj,hcj,ncj->hcpn)))/dot_general | solution.py:78
  385.2 13.6 %fusion.36 = (f32[8,4,4,128]{3,2,1,0:T(4,128)S(1)}, f32[8,4,64,4,128]{4,2,3,1,0:T(8,128)}) fusion(f32[8,4,64,4,128]{4,3,2,1,0:T(4,128)} %reshape.297, f32[8,4,4,128]{3,2,1,0:T(4,128)S(1)} %copy.353, bf16[8,4,64,4,128]{4,3,2,1,0:T(4,128)(2,1)S(1)} %copy-done.8, f32[8,4]{1,0:T(8,128)S(1)} %copy-done.89, bf16[8,4,4,64,128]{4,2,3,1,0:T(4,128)(2,1)S(1)} %bitcast.246, ...), kind=kOutput, calls=%fused_computation.64 | convolution fusion | flops 1627373568 | bytes 19398784 | tf_op jit(solution)/shard_map/transpose(jvp(vmap(hcij,hpcj->hpci)))/dot_general | solution.py:74
  398.9 11.3 %fusion.16 = f32[8,4,4,64,128]{4,3,2,1,0:T(8,128)S(1)} fusion(f32[8,256,4,128,1]{1,3,4,2,0:T(8,128)} %bitcast.235, f32[8,4,4,64,256]{4,3,1,2,0:T(8,128)} %get-tuple-element.136), kind=kOutput, calls=%fused_computation.28 | convolution fusion | flops 3221225472 | bytes 16777216 | tf_op jit(solution)/shard_map/jvp(vmap(nci,hci,chpn->hpci))/dot_general | solution.py:149
  414.0 5.7 %copy.401 = f32[8,4,64,4,128]{4,3,2,1,0:T(4,128)} copy(f32[8,4,64,4,128]{4,2,3,1,0:T(8,128)S(1)} %copy-done.22) | data formatting | bytes 8388608 | tf_op jit(solution)/shard_map/transpose(jvp(vmap()))/add_any | solution.py:73
  419.7 5.6 %reshape.304 = f32[8,256,512]{2,1,0:T(8,128)} reshape(f32[8,4,64,4,128]{4,3,2,1,0:T(4,128)} %copy.401) | data formatting | bytes 8388608 | tf_op jit(solution)/shard_map/transpose(jvp(vmap()))/reshape | solution.py:59
  425.3 4.3 broadcast_multiply_fusion
  431.6 4.6 pad_add_fusion
  436.3 3.3 split.16
  439.6 1.7 copy-done.16
  441.3 9.7 %fusion.39 = bf16[8,4,64,4,128]{4,2,3,1,0:T(8,128)(2,1)S(1)} fusion(f32[8,4,4,64,128]{4,3,2,1,0:T(8,128)S(1)} %copy-done.16, f32[8,4,64,4,128]{4,3,2,1,0:T(4,128)S(1)} %copy-done.5, f32[8,4,128,128]{2,3,1,0:T(8,128)S(1)} %copy-done.23, f32[4,128,128]{1,2,0:T(8,128)S(1)} %copy-done.37, f32[8,4,4,128]{3,2,1,0:T(4,128)S(1)} %copy-done.55, ...), kind=kOutput, calls=%fused_computation.70 | convolution fusion | flops 1625292800 | bytes 13041792 | tf_op jit(solution)/shard_map/jvp(vmap(hcij,hpcj->hpci))/dot_general | solution.py:74
  451.0 2.0 copy.389
  453.0 2.2 convert_element_type.96
  455.2 2.6 pad_add_fusion.3
  457.9 1.4 copy_dynamic-update-slice_fusion.1
  459.3 1.4 copy_dynamic-update-slice_fusion
  462.7 1.3 split.17
  464.6 1.6 collective-permute-start.7
  466.2 2.9 slice_maximum_fusion
  469.1 1.5 pad_maximum_fusion.1
  470.5 1.8 copy.415
  474.1 1.5 slice.267
  (344 shorter events, 36.4 us)
Async XLA Ops:
  7.2 70.1 %all-gather.6.cloned.1.call-start = ((), (), s32[]{:S(2)}) async-start(), calls=%async_computation.3 | async-start | bytes 4718592 | tf_op jit(solution)/shard_map/all_gather | solution.py:230
  10.6 9.2 %copy-start.39 = (f32[2,4,2560]{2,1,0:T(4,128)S(1)}, f32[2,4,2560]{2,1,0:T(4,128)}, u32[]{:S(2)}) copy-start(f32[2,4,2560]{2,1,0:T(4,128)} %param.18) | copy-start | bytes 245764
  10.6 9.3 %copy-start.77 = (f32[2,2560]{1,0:T(2,128)S(1)}, f32[2,2560]{1,0:T(2,128)}, u32[]{:S(2)}) copy-start(f32[2,2560]{1,0:T(2,128)} %param.19) | copy-start | bytes 61444
  10.6 9.3 %copy-start.97 = (f32[2,32]{1,0:T(2,128)S(1)}, f32[2,32]{1,0:T(2,128)}, u32[]{:S(2)}) copy-start(f32[2,32]{1,0:T(2,128)} %param.20) | copy-start | bytes 772
  10.6 9.3 %copy-start.98 = (f32[2,32]{1,0:T(2,128)S(1)}, f32[2,32]{1,0:T(2,128)}, u32[]{:S(2)}) copy-start(f32[2,32]{1,0:T(2,128)} %param.21) | copy-start | bytes 772
  10.6 9.3 %copy-start.99 = (f32[2,32]{1,0:T(2,128)S(1)}, f32[2,32]{1,0:T(2,128)}, u32[]{:S(2)}) copy-start(f32[2,32]{1,0:T(2,128)} %param.22) | copy-start | bytes 772
  14.1 23.2 %copy-start.101 = (s32[4]{0:T(128)S(1)}, s32[4]{0:T(128)}, u32[]{:S(2)}) copy-start(s32[4]{0:T(128)} %param.23) | copy-start | bytes 52
  14.9 22.9 %collective-permute-start = (bf16[8,320,3]{1,0,2:T(8,128)(2,1)S(1)}, bf16[8,320,3]{1,0,2:T(8,128)(2,1)S(1)}, u32[]{:S(2)}, u32[]{:S(2)}) collective-permute-start(bf16[8,320,3]{1,0,2:T(8,128)(2,1)S(1)} %pad_maximum_fusion.3), channel_id=1, source_target_pairs={{0,1},{1,2},{2,3},{4,5},{5,6},{6,7},{8,9},{9,10},{10,11},{12,13},{... | collective-permute-start | bytes 46088 | tf_op jit(solution)/shard_map/ppermute | solution.py:18
  37.6 5.5 %copy-start.63 = (f32[512]{0:T(512)}, f32[512]{0:T(512)S(1)}, u32[]{:S(2)}) copy-start(f32[512]{0:T(512)S(1)} %get-tuple-element.184) | copy-start | bytes 6148
  38.4 5.7 %copy-start.20 = (bf16[8,256,512]{2,1,0:T(8,128)(2,1)S(1)}, bf16[8,256,512]{2,1,0:T(8,128)(2,1)}, u32[]{:S(2)}) copy-start(bf16[8,256,512]{2,1,0:T(8,128)(2,1)} %param.13) | copy-start | bytes 6291460
  42.0 7.0 %copy-start.75 = (bf16[8,4,512]{2,1,0:T(4,128)(2,1)S(1)}, bf16[8,4,512]{2,1,0:T(4,128)(2,1)}, u32[]{:S(2)}) copy-start(bf16[8,4,512]{2,1,0:T(4,128)(2,1)} %param.16) | copy-start | bytes 98308
  42.0 74.5 %all-gather.4.cloned.1.call-start = ((), (), s32[]{:S(2)}) async-start(), calls=%async_computation.2 | async-start | bytes 4718592 | tf_op jit(solution)/shard_map/all_gather | solution.py:231
  43.2 414.6 %reduce-scatter.3.cloned.1.call-start = ((), (), s32[]{:S(2)}) async-start(), calls=%async_computation.4 | async-start | bytes 4718592 | tf_op jit(solution)/shard_map/reduce_scatter | solution.py:268
  46.7 10.6 %copy-start.49 = (bf16[8,320,3]{1,0,2:T(8,128)(2,1)S(1)}, bf16[8,320,3]{1,0,2:T(8,128)(2,1)}, u32[]{:S(2)}) copy-start(bf16[8,320,3]{1,0,2:T(8,128)(2,1)} %copy-done.48) | copy-start | bytes 46084
  48.5 8.0 %copy-start.85 = (f32[8,4]{0,1:T(4,128)}, f32[8,4]{0,1:T(4,128)S(1)}, u32[]{:S(2)}) copy-start(f32[8,4]{0,1:T(4,128)S(1)} %copy.352) | copy-start | bytes 388
  48.6 8.8 %copy-start.57 = (s32[4,128]{1,0:T(4,128)}, s32[4,128]{1,0:T(4,128)S(1)}, u32[]{:S(2)}) copy-start(s32[4,128]{1,0:T(4,128)S(1)} %slice_bitcast_fusion) | copy-start | bytes 6148
  49.2 84.5 %copy-start.25 = (f32[8,4,4,128]{3,0,2,1:T(8,128)}, f32[8,4,4,128]{3,0,2,1:T(8,128)S(1)}, u32[]{:S(2)}) copy-start(f32[8,4,4,128]{3,0,2,1:T(8,128)S(1)} %fusion.108) | copy-start | bytes 196612
  50.8 5.8 %copy-start.78 = (f32[4,128]{1,0:T(4,128)}, f32[4,128]{1,0:T(4,128)S(1)}, u32[]{:S(2)}) copy-start(f32[4,128]{1,0:T(4,128)S(1)} %get-tuple-element.180) | copy-start | bytes 6148
  50.8 5.8 %copy-start.82 = (f32[4,128]{1,0:T(4,128)}, f32[4,128]{1,0:T(4,128)S(1)}, u32[]{:S(2)}) copy-start(f32[4,128]{1,0:T(4,128)S(1)} %get-tuple-element.181) | copy-start | bytes 6148
  50.9 31.6 %copy-start.28 = (f32[8,4,4,128]{3,2,1,0:T(4,128)}, f32[8,4,4,128]{3,2,1,0:T(4,128)S(1)}, u32[]{:S(2)}) copy-start(f32[8,4,4,128]{3,2,1,0:T(4,128)S(1)} %copy.372) | copy-start | bytes 196612
  51.0 5.6 %copy-start.93 = (pred[4,4]{0,1:T(4,128)(4,1)}, pred[4,4]{0,1:T(4,128)(4,1)S(1)}, u32[]{:S(2)}) copy-start(pred[4,4]{0,1:T(4,128)(4,1)S(1)} %iota_compare_fusion.2) | copy-start | bytes 52
  52.0 44.3 %copy-start.50 = (f32[8,4]{1,0:T(8,128)}, f32[8,4]{1,0:T(8,128)S(1)}, u32[]{:S(2)}) copy-start(f32[8,4]{1,0:T(8,128)S(1)} %copy.380) | copy-start | bytes 388
  54.6 67.2 %copy-start.6 = (bf16[8,4,64,4,128]{4,3,2,1,0:T(4,128)(2,1)}, bf16[8,4,64,4,128]{4,3,2,1,0:T(4,128)(2,1)S(1)}, u32[]{:S(2)}) copy-start(bf16[8,4,64,4,128]{4,3,2,1,0:T(4,128)(2,1)S(1)} %reshape.301) | copy-start | bytes 6291460
  57.3 12.5 %copy-start.40 = (f32[8,256]{1,0:T(8,128)}, f32[8,256]{1,0:T(8,128)S(1)}, u32[]{:S(2)}) copy-start(f32[8,256]{1,0:T(8,128)S(1)} %get-tuple-element.147) | copy-start | bytes 24580
  57.4 12.5 %copy-start.42 = (f32[8,256]{1,0:T(8,128)}, f32[8,256]{1,0:T(8,128)S(1)}, u32[]{:S(2)}) copy-start(f32[8,256]{1,0:T(8,128)S(1)} %get-tuple-element.148) | copy-start | bytes 24580
  57.4 12.5 %copy-start.44 = (f32[8,256]{1,0:T(8,128)}, f32[8,256]{1,0:T(8,128)S(1)}, u32[]{:S(2)}) copy-start(f32[8,256]{1,0:T(8,128)S(1)} %get-tuple-element.149) | copy-start | bytes 24580
  57.4 12.5 %copy-start.46 = (f32[8,256]{1,0:T(8,128)}, f32[8,256]{1,0:T(8,128)S(1)}, u32[]{:S(2)}) copy-start(f32[8,256]{1,0:T(8,128)S(1)} %get-tuple-element.150) | copy-start | bytes 24580
  75.2 7.4 %copy-start.56 = (f32[8,4,4]{1,2,0:T(4,128)S(1)}, f32[8,4,4]{1,2,0:T(4,128)}, u32[]{:S(2)}) copy-start(f32[8,4,4]{1,2,0:T(4,128)} %copy.378) | copy-start | bytes 1540
  121.8 13.4 %copy-start.90 = (pred[4,4]{1,0:T(4,128)(4,1)S(1)}, pred[4,4]{1,0:T(4,128)(4,1)}, u32[]{:S(2)}) copy-start(pred[4,4]{1,0:T(4,128)(4,1)} %get-tuple-element.194) | copy-start | bytes 52
  121.8 14.4 %copy-start.100 = (pred[4,4]{1,0:T(4,128)(4,1)S(1)}, pred[4,4]{1,0:T(4,128)(4,1)}, u32[]{:S(2)}) copy-start(pred[4,4]{1,0:T(4,128)(4,1)} %get-tuple-element.193) | copy-start | bytes 52
  121.8 16.2 %copy-start.58 = (s32[4,128]{1,0:T(4,128)S(1)}, s32[4,128]{1,0:T(4,128)}, u32[]{:S(2)}) copy-start(s32[4,128]{1,0:T(4,128)} %copy-done.57) | copy-start | bytes 6148
  121.8 60.3 %copy-start.51 = (f32[8,4]{1,0:T(8,128)S(1)}, f32[8,4]{1,0:T(8,128)}, u32[]{:S(2)}) copy-start(f32[8,4]{1,0:T(8,128)} %copy-done.50) | copy-start | bytes 388
  128.8 49.0 %collective-permute-start.1 = (f32[8,4,64,256]{3,2,1,0:T(8,128)}, f32[8,4,64,256]{3,2,1,0:T(8,128)S(1)}, u32[]{:S(2)}, u32[]{:S(2)}) collective-permute-start(f32[8,4,64,256]{3,2,1,0:T(8,128)} %broadcast_add_fusion), channel_id=1, source_target_pairs={{0,1},{1,2},{2,3},{4,5},{5,6},{6,7},{8,9},{9,10},{10,11},{12,13},{... | collective-permute-start | bytes 6291464 | tf_op jit(solution)/shard_map/ppermute | solution.py:18
  132.4 49.7 %collective-permute-start.2 = (f32[8,4,64,256]{3,2,1,0:T(8,128)}, f32[8,4,64,256]{3,2,1,0:T(8,128)}, u32[]{:S(2)}, u32[]{:S(2)}) collective-permute-start(f32[8,4,64,256]{3,2,1,0:T(8,128)} %fusion.82), channel_id=1, source_target_pairs={{1,0},{2,1},{3,2},{5,4},{6,5},{7,6},{9,8},{10,9},{11,10},{13,12},{... | collective-permute-start | bytes 6291464 | tf_op jit(solution)/shard_map/ppermute | solution.py:18
  134.5 53.3 %copy-start.67 = (f32[8,4]{1,0:T(8,128)}, f32[8,4]{1,0:T(8,128)S(1)}, u32[]{:S(2)}) copy-start(f32[8,4]{1,0:T(8,128)S(1)} %copy.377) | copy-start | bytes 388
  136.8 50.9 %copy-start.34 = (f32[4,8,4,4]{1,3,2,0:T(4,128)}, f32[4,8,4,4]{1,3,2,0:T(4,128)S(1)}, u32[]{:S(2)}) copy-start(f32[4,8,4,4]{1,3,2,0:T(4,128)S(1)} %get-tuple-element.172) | copy-start | bytes 6148
  137.7 50.1 %copy-start.80 = (f32[4,4]{1,0:T(4,128)}, f32[4,4]{1,0:T(4,128)S(1)}, u32[]{:S(2)}) copy-start(f32[4,4]{1,0:T(4,128)S(1)} %fusion.158) | copy-start | bytes 196
  138.8 55.3 %copy-start = (f32[8,256,512]{1,2,0:T(8,128)S(1)}, f32[8,256,512]{1,2,0:T(8,128)}, u32[]{:S(2)}) copy-start(f32[8,256,512]{1,2,0:T(8,128)} %copy.361) | copy-start | bytes 12582916
  138.8 55.3 %copy-start.1 = (f32[8,256,512]{1,2,0:T(8,128)S(1)}, f32[8,256,512]{1,2,0:T(8,128)}, u32[]{:S(2)}) copy-start(f32[8,256,512]{1,2,0:T(8,128)} %copy.363) | copy-start | bytes 12582916
  187.8 47.7 %collective-permute-start.3 = (f32[8,4,64,256]{3,2,1,0:T(8,128)}, f32[8,4,64,256]{3,2,1,0:T(8,128)}, u32[]{:S(2)}, u32[]{:S(2)}) collective-permute-start(f32[8,4,64,256]{3,2,1,0:T(8,128)} %get-tuple-element.179), channel_id=1, source_target_pairs={{0,1},{1,2},{2,3},{4,5},{5,6},{6,7},{8,9},{9,10},{10,11},{12,13},{... | collective-permute-start | bytes 6291464 | tf_op jit(solution)/shard_map/ppermute | solution.py:18
  192.4 48.6 %collective-permute-start.4 = (f32[8,4,64,256]{3,2,1,0:T(8,128)}, f32[8,4,64,256]{3,2,1,0:T(8,128)}, u32[]{:S(2)}, u32[]{:S(2)}) collective-permute-start(f32[8,4,64,256]{3,2,1,0:T(8,128)} %get-tuple-element.178), channel_id=1, source_target_pairs={{1,0},{2,1},{3,2},{5,4},{6,5},{7,6},{9,8},{10,9},{11,10},{13,12},{... | collective-permute-start | bytes 6291464 | tf_op jit(solution)/shard_map/ppermute | solution.py:18
  194.1 5.8 %copy-start.7 = (bf16[8,4,64,4,128]{4,3,2,1,0:T(4,128)(2,1)S(1)}, bf16[8,4,64,4,128]{4,3,2,1,0:T(4,128)(2,1)}, u32[]{:S(2)}) copy-start(bf16[8,4,64,4,128]{4,3,2,1,0:T(4,128)(2,1)} %copy-done.6) | copy-start | bytes 6291460
  194.1 5.8 %copy-start.30 = (f32[8,4,4,128]{3,2,1,0:T(4,128)S(1)}, f32[8,4,4,128]{3,2,1,0:T(4,128)}, u32[]{:S(2)}) copy-start(f32[8,4,4,128]{3,2,1,0:T(4,128)} %copy.388) | copy-start | bytes 196612
  199.9 7.5 %copy-start.4 = (f32[8,4,64,4,128]{4,3,2,1,0:T(4,128)S(1)}, f32[8,4,64,4,128]{4,3,2,1,0:T(4,128)}, u32[]{:S(2)}) copy-start(f32[8,4,64,4,128]{4,3,2,1,0:T(4,128)} %reshape.297) | copy-start | bytes 12582916
  199.9 57.2 %slice-start = ((s8[8388608]{0:T(1024)(128)(4,1)}), s8[4194304]{0:T(1024)(128)(4,1)S(1)}, s32[]{:S(2)}) async-start(s8[8388608]{0:T(1024)(128)(4,1)} %bitcast.243), calls=%async_computation.6 | async-start | bytes 8388608
  207.4 49.7 %copy-start.2 = (f32[8,4,4,64,256]{4,3,1,2,0:T(8,128)}, f32[8,4,4,64,256]{4,3,1,2,0:T(8,128)S(1)}, u32[]{:S(2)}) copy-start(f32[8,4,4,64,256]{4,3,1,2,0:T(8,128)S(1)} %fusion.60) | copy-start | bytes 25165828
  207.5 33.5 %copy-start.52 = (f32[8,4]{1,0:T(8,128)S(1)}, f32[8,4]{1,0:T(8,128)}, u32[]{:S(2)}) copy-start(f32[8,4]{1,0:T(8,128)} %copy-done.50) | copy-start | bytes 388
  207.5 33.5 %copy-start.68 = (f32[8,4]{1,0:T(8,128)S(1)}, f32[8,4]{1,0:T(8,128)}, u32[]{:S(2)}) copy-start(f32[8,4]{1,0:T(8,128)} %copy-done.67) | copy-start | bytes 388
  207.5 49.7 %slice-start.1 = ((s8[8388608]{0:T(1024)(128)(4,1)}), s8[4194304]{0:T(1024)(128)(4,1)S(1)}, s32[]{:S(2)}) async-start(s8[8388608]{0:T(1024)(128)(4,1)} %bitcast.243), calls=%async_computation.7 | async-start | bytes 8388608
  225.4 26.6 %copy-start.18 = (f32[8,4,128,128]{2,3,1,0:T(8,128)S(1)}, f32[8,4,128,128]{2,3,1,0:T(8,128)}, u32[]{:S(2)}) copy-start(f32[8,4,128,128]{2,3,1,0:T(8,128)} %get-tuple-element.100) | copy-start | bytes 6291460
  247.3 45.4 %collective-permute-start.5 = (f32[8,4,64,256]{3,2,1,0:T(8,128)}, f32[8,4,64,256]{3,2,1,0:T(8,128)}, u32[]{:S(2)}, u32[]{:S(2)}) collective-permute-start(f32[8,4,64,256]{3,2,1,0:T(8,128)} %get-tuple-element.177), channel_id=1, source_target_pairs={{0,1},{1,2},{2,3},{4,5},{5,6},{6,7},{8,9},{9,10},{10,11},{12,13},{... | collective-permute-start | bytes 6291464 | tf_op jit(solution)/shard_map/ppermute | solution.py:18
  250.7 47.4 %collective-permute-start.6 = (f32[8,4,64,256]{3,2,1,0:T(8,128)}, f32[8,4,64,256]{3,2,1,0:T(8,128)}, u32[]{:S(2)}, u32[]{:S(2)}) collective-permute-start(f32[8,4,64,256]{3,2,1,0:T(8,128)} %get-tuple-element.176), channel_id=1, source_target_pairs={{1,0},{2,1},{3,2},{5,4},{6,5},{7,6},{9,8},{10,9},{11,10},{13,12},{... | collective-permute-start | bytes 6291464 | tf_op jit(solution)/shard_map/ppermute | solution.py:18
  257.2 40.9 %copy-start.53 = (f32[8,4,4]{1,2,0:T(4,128)S(1)}, f32[8,4,4]{1,2,0:T(4,128)}, u32[]{:S(2)}) copy-start(f32[8,4,4]{1,2,0:T(4,128)} %copy.391) | copy-start | bytes 1540
  307.1 12.4 %copy-start.3 = (f32[8,4,4,64,256]{4,3,1,2,0:T(8,128)}, f32[8,4,4,64,256]{4,3,1,2,0:T(8,128)S(1)}, u32[]{:S(2)}) copy-start(f32[8,4,4,64,256]{4,3,1,2,0:T(8,128)S(1)} %get-tuple-element.134) | copy-start | bytes 25165828
  325.2 134.1 %reduce-scatter.5.cloned.1.call-start = ((), (), s32[]{:S(2)}) async-start(), calls=%async_computation.5 | async-start | bytes 4718592 | tf_op jit(solution)/shard_map/reduce_scatter | solution.py:269
  337.9 11.7 %copy-start.8 = (bf16[8,4,64,4,128]{4,3,2,1,0:T(4,128)(2,1)S(1)}, bf16[8,4,64,4,128]{4,3,2,1,0:T(4,128)(2,1)}, u32[]{:S(2)}) copy-start(bf16[8,4,64,4,128]{4,3,2,1,0:T(4,128)(2,1)} %copy-done.6) | copy-start | bytes 6291460
  337.9 11.7 %copy-start.31 = (f32[8,4,4,128]{3,2,1,0:T(4,128)S(1)}, f32[8,4,4,128]{3,2,1,0:T(4,128)}, u32[]{:S(2)}) copy-start(f32[8,4,4,128]{3,2,1,0:T(4,128)} %copy.388) | copy-start | bytes 196612
  363.5 5.6 %copy-start.35 = (f32[4,8,4,4]{1,3,2,0:T(4,128)S(1)}, f32[4,8,4,4]{1,3,2,0:T(4,128)}, u32[]{:S(2)}) copy-start(f32[4,8,4,4]{1,3,2,0:T(4,128)} %copy-done.34) | copy-start | bytes 6148
  363.5 5.6 %copy-start.94 = (pred[4,4]{0,1:T(4,128)(4,1)S(1)}, pred[4,4]{0,1:T(4,128)(4,1)}, u32[]{:S(2)}) copy-start(pred[4,4]{0,1:T(4,128)(4,1)} %copy-done.93) | copy-start | bytes 52
  369.2 15.0 %copy-start.26 = (f32[8,4,4,128]{3,0,2,1:T(8,128)S(1)}, f32[8,4,4,128]{3,0,2,1:T(8,128)}, u32[]{:S(2)}) copy-start(f32[8,4,4,128]{3,0,2,1:T(8,128)} %copy-done.25) | copy-start | bytes 196612
  369.2 15.0 %copy-start.79 = (f32[4,128]{1,0:T(4,128)S(1)}, f32[4,128]{1,0:T(4,128)}, u32[]{:S(2)}) copy-start(f32[4,128]{1,0:T(4,128)} %copy-done.78) | copy-start | bytes 6148
  419.7 5.6 %copy-start.47 = (f32[8,256]{1,0:T(8,128)S(1)}, f32[8,256]{1,0:T(8,128)}, u32[]{:S(2)}) copy-start(f32[8,256]{1,0:T(8,128)} %copy-done.46) | copy-start | bytes 24580
  431.6 8.0 %copy-start.23 = (f32[8,4,128,128]{2,3,1,0:T(8,128)S(1)}, f32[8,4,128,128]{2,3,1,0:T(8,128)}, u32[]{:S(2)}) copy-start(f32[8,4,128,128]{2,3,1,0:T(8,128)} %fusion.171) | copy-start | bytes 6291460
  464.6 7.7 %collective-permute-start.7 = (f32[8,320,3]{1,0,2:T(8,128)S(1)}, f32[8,320,3]{1,0,2:T(8,128)S(1)}, u32[]{:S(2)}, u32[]{:S(2)}) collective-permute-start(f32[8,320,3]{1,0,2:T(8,128)S(1)} %copy.414), channel_id=1, source_target_pairs={{1,0},{2,1},{3,2},{5,4},{6,5},{7,6},{9,8},{10,9},{11,10},{13,12},{... | collective-permute-start | bytes 92168 | tf_op jit(solution)/shard_map/ppermute | solution.py:18
  (54 other events, 165.7 us)
Sparse Core Ops, SparseCore 0:
  42.1 35.0 all-gather.5
  79.7 36.7 all-gather.3
  325.3 48.5 reduce-scatter.2
  384.6 48.7 reduce-scatter.4

commit v6 on v5

--- a/solution.py
+++ b/solution.py
@@ -18,20 +18,28 @@
     return lax.ppermute(value, axis, [(source, source + steps) for source in range(first, last)])
 
 
-def carried_both(totals, ahead, behind, axis):
-    factor = totals[..., None, None]
-    pair = lax.optimization_barrier((ahead, behind))
-    received = lax.optimization_barrier(
-        (passed_along(pair[0], axis, 1), passed_along(pair[1], axis, -1))
-    )
-    for _ in range(lax.axis_size(axis) - 2):
-        received = lax.optimization_barrier(
-            (
-                passed_along(factor * received[0] + ahead, axis, 1),
-                passed_along(factor * received[1] + behind, axis, -1),
-            )
-        )
-    return received
+def carried_both(totals, ahead, behind, axis, chunks=2):
+    hops = lax.axis_size(axis) - 1
+    size = totals.shape[0] // chunks
+    part = lambda value, c: value[c * size : (c + 1) * size]
+    factor = [part(totals, c)[..., None, None] for c in range(chunks)]
+    ahead, behind = lax.optimization_barrier((ahead, behind))
+    own = [(part(ahead, c), part(behind, c)) for c in range(chunks)]
+    received = [None] * chunks
+    for step in range(hops + chunks - 1):
+        sent = {}
+        for c in range(chunks):
+            hop = step - c
+            if 0 <= hop < hops:
+                if hop == 0:
+                    values = own[c]
+                else:
+                    values = tuple(factor[c] * r + o for r, o in zip(received[c], own[c]))
+                sent[c] = (passed_along(values[0], axis, 1), passed_along(values[1], axis, -1))
+        sent = lax.optimization_barrier(sent)
+        for c, values in sent.items():
+            received[c] = values
+    return tuple(jnp.concatenate([received[c][k] for c in range(chunks)], axis=0) for k in range(2))
 
 
 def segment_ids(positions, doc_lengths):

time: 488 us -> 499 us (1.023)
  starting transfers between devices: 23.1 us -> 39.7 us
  matrix products: 142 us -> 129 us
  local copies, waits for them, and re-layouts: 83.2 us -> 94.7 us
    ppermute x8 -> x14, starting transfers between devices: 22.3 us -> 38.9 us  [passed_along(): lax.ppermute(value, axis, [(source, source + steps) for source in range(f...]
    add x2, other arithmetic: 12 us -> 6.02 us  [carried_both(): values = tuple((factor[c] * r + o for r, o in zip(received[c], own[c])))]
    dot_general x3, matrix products: 32.7 us -> 27.5 us  [assemble(): jnp.einsum('nci,hci,chpn->hpci', c_three, entry, starts, precision=precise)]
    ppermute x8 -> x14, waiting for transfers between devices: 81.8 us -> 79.9 us  [passed_along(): lax.ppermute(value, axis, [(source, source + steps) for source in range(f...]
    unnamed x219 -> x217, local copies, waits for them, and re-layouts: 16.5 us -> 17.2 us
  transfers between devices with their start and end apart: 12 -> 18, of which waited for: 8 -> 11; matrix products, arithmetic and copies ran while one was open for 51% -> 50% of each run, Pallas kernels for 0% -> 0%
where the time goes in v6:
time: 499 us; the launch traced here: 493 us
  matrix products  129 us (26%)
  other arithmetic  103 us (21%)
  waiting for transfers between devices  96.5 us (19%)
  local copies, waits for them, and re-layouts  94.7 us (19%)
  starting transfers between devices  39.7 us (8%)
  between operations  15.6 us (3%)
  blocking collectives  15.2 us (3%)
    ppermute x14, waiting for transfers between devices, passed_along(): lax.ppermute(value, axis, [(source, source + steps) for source in range(f...  79.9 us
    ppermute x14, starting transfers between devices, passed_along(): lax.ppermute(value, axis, [(source, source + steps) for source in range(f...  38.9 us
    dot_general x3, matrix products, span_terms(): jnp.einsum('hpcj,hcj,ncj->hcpn', weighted, keep_end, b_three, precision=p...  38.2 us
    dot_general x3, matrix products, span_terms(): jnp.einsum('hcij,hpcj->hpci', decay * scores[None], weighted, precision=p...  37.7 us
    dot_general x3, matrix products, assemble(): jnp.einsum('nci,hci,chpn->hpci', c_three, entry, starts, precision=precise)  27.5 us
    reduce_sum x2, other arithmetic, weighted_sum(): return jnp.sum(weight[..., None, None] * stacked, axis=-3)  25.9 us
    dot_general x3, matrix products, span_terms(): scores = jnp.einsum('nci,ncj->cij', c_three, b_three, precision=precise)  18.9 us
    unnamed x217, local copies, waits for them, and re-layouts  17.2 us
  transfers between devices with their start and end apart: 18, of which 11 were waited for; matrix products, arithmetic and copies ran while one was open for 50% of the time, Pallas kernels for 0%

profile of v6, /device:TPU:0, one launch (start us, length us, event | category | flops | bytes accessed | tf_op | source)
XLA Modules:
  0.0 493.3 jit_solution(7720536201914128465)
XLA Ops:
  7.2 1.7 copy.354
  8.9 2.6 copy.353
  11.6 3.4 copy.352
  16.4 5.5 %collective-permute-start = (bf16[8,320,3]{1,0,2:T(8,128)(2,1)}, bf16[8,320,3]{1,0,2:T(8,128)(2,1)}, u32[]{:S(2)}, u32[]{:S(2)}) collective-permute-start(bf16[8,320,3]{1,0,2:T(8,128)(2,1)} %pad_maximum_fusion.3), channel_id=1, source_target_pairs={{0,1},{1,2},{2,3},{4,5},{5,6},{6,7},{8,9},{9,10},{10,11},{12,13},{... | collective-permute-start | bytes 46088 | tf_op jit(solution)/shard_map/ppermute | solution.py:18
  22.3 15.2 %all-gather = f32[4,2,12896]{2,1,0:T(2,128)S(1)} all-gather(f32[1,2,12896]{2,1,0:T(2,128)S(1)} %bitcast.253), channel_id=1, replica_groups=mesh['seq'=8,'head'=4] {'head'}, dimensions={0}, use_global_device_ids=true | all-gather | bytes 515840 | tf_op jit(solution)/shard_map/all_gather | solution.py:191
  48.3 3.2 fusion.98
  53.4 2.6 convert_element_type.83
  61.6 2.5 reshape.302
  71.6 12.4 %fusion.50 = (f32[8,256,512]{2,1,0:T(8,128)}, f32[8,256,512]{2,1,0:T(8,128)}) fusion(f32[8,256,512]{2,1,0:T(8,128)} %convert_element_type.83, f32[8,256]{1,0:T(8,128)S(1)} %get-tuple-element.170, f32[512]{0:T(512)} %get-tuple-element.201, f32[8,256,3]{2,1,0:T(8,128)S(1)} %copy.355, f32[8,256]{1,0:T(8,128)S(1)} %get-tuple-element.168, ...), kind=kLoop, calls=%fused_computation.88 | loop fusion | flops 18874368 | bytes 12654592 | tf_op jit(solution)/shard_map/jvp(vmap(jit(silu)))/mul | solution.py:61
  84.1 5.3 %reshape.298 = f32[8,4,64,4,128]{4,3,2,1,0:T(4,128)} reshape(f32[8,256,512]{2,1,0:T(8,128)} %get-tuple-element.134) | data formatting | bytes 8388608 | tf_op jit(solution)/shard_map/jvp(vmap())/reshape | solution.py:67
  89.4 5.3 %copy.368 = f32[8,256,512]{1,2,0:T(8,128)} copy(f32[8,256,512]{2,0,1:T(8,128)} %all-gather.6.cloned.1.call-done) | data formatting | bytes 8388608 | tf_op jit(solution)/shard_map/all_gather | solution.py:238
  94.7 13.9 %multiply_reduce_fusion.5 = (f32[8,4,64,256]{3,2,1,0:T(8,128)S(1)}, f32[8,4,4,64,256]{4,3,1,2,0:T(8,128)}) fusion(f32[8,4,4]{1,2,0:T(4,128)S(1)} %copy-done.60, f32[8,256,4,128,1]{1,3,4,2,0:T(8,128)} %bitcast.239, f32[8,4,64,4,128]{4,3,2,1,0:T(4,128)} %reshape.298, f32[8,4,4,128]{3,2,1,0:T(4,128)S(1)} %copy.377, f32[8,4,4,128]{3,2,1,0:T(4,128)S(1)} %copy.358), kind=kOutput, calls=%fused_computation.25 | convolution fusion | flops 3226992640 | bytes 19005952 | tf_op jit(solution)/shard_map/jvp(vmap(hpcj,hcj,ncj->hcpn))/dot_general | solution.py:86
  110.1 16.5 %all-gather.4.cloned.1.call-done = f32[8,256,512]{2,0,1:T(8,128)} async-done(((f32[8,32,512]{2,0,1:T(8,128)}), f32[8,256,512]{2,0,1:T(8,128)}) %all-gather.4.cloned.1.call-update) | async-done | bytes 4194320 | tf_op jit(solution)/shard_map/all_gather | solution.py:239
  126.6 5.2 %copy.366 = f32[8,256,512]{1,2,0:T(8,128)} copy(f32[8,256,512]{2,0,1:T(8,128)} %all-gather.4.cloned.1.call-done) | data formatting | bytes 8388608 | tf_op jit(solution)/shard_map/all_gather | solution.py:239
  131.9 6.2 %fusion.78 = f32[8,4,64,256]{3,2,1,0:T(8,128)S(1)} fusion(f32[8,256,4,128,1]{1,3,2,4,0:T(8,128)} %bitcast.234, f32[8,4,4,128]{3,2,1,0:T(4,128)S(1)} %copy.387, bf16[8,4,64,4,128]{4,3,2,1,0:T(4,128)(2,1)S(1)} %reshape.302), kind=kOutput, calls=%fused_computation.109 | convolution fusion | flops 3223322624 | bytes 8454144 | tf_op jit(solution)/shard_map/ghpci,ghci,gnci->ghpn/dot_general | solution.py:260
  139.2 4.5 collective-permute-start.1
  147.3 18.6 %collective-permute-done.1 = f32[4,4,64,256]{3,2,1,0:T(8,128)} collective-permute-done((f32[4,4,64,256]{3,2,1,0:T(8,128)}, f32[4,4,64,256]{3,2,1,0:T(8,128)}, u32[]{:S(2)}, u32[]{:S(2)}) %collective-permute-start.1) | collective-permute-done | bytes 1048608 | tf_op jit(solution)/shard_map/ppermute | solution.py:18
  165.9 6.2 %collective-permute-done.2 = f32[4,4,64,256]{3,2,1,0:T(8,128)} collective-permute-done((f32[4,4,64,256]{3,2,1,0:T(8,128)}, f32[4,4,64,256]{3,2,1,0:T(8,128)}, u32[]{:S(2)}, u32[]{:S(2)}) %collective-permute-start.2) | collective-permute-done | bytes 1048608 | tf_op jit(solution)/shard_map/ppermute | solution.py:18
  173.7 2.7 collective-permute-start.3
  176.5 2.5 fusion.165
  180.3 4.6 collective-permute-start.5
  187.1 7.3 %fusion.60 = f32[8,4,4,64,256]{4,3,1,2,0:T(8,128)S(1)} fusion(f32[8,256,4,128,1]{1,3,4,2,0:T(8,128)S(1)} %bitcast.236, f32[8,4,4,128]{3,2,1,0:T(4,128)S(1)} %copy.394, bf16[8,4,64,4,128]{4,3,2,1,0:T(4,128)(2,1)S(1)} %copy-done.8), kind=kOutput, calls=%fused_computation.97 | convolution fusion | flops 3223322624 | bytes 14745600 | tf_op jit(solution)/shard_map/transpose(jvp(vmap(nci,hci,chpn->hpci)))/dot_general | solution.py:157
  194.4 5.6 %collective-permute-done.3 = f32[4,4,64,256]{3,2,1,0:T(8,128)S(1)} collective-permute-done((f32[4,4,64,256]{3,2,1,0:T(8,128)S(1)}, f32[4,4,64,256]{3,2,1,0:T(8,128)S(1)}, u32[]{:S(2)}, u32[]{:S(2)}) %collective-permute-start.3) | collective-permute-done | bytes 1048608 | tf_op jit(solution)/shard_map/ppermute | solution.py:18
  200.0 7.2 %collective-permute-done.4 = f32[4,4,64,256]{3,2,1,0:T(8,128)S(1)} collective-permute-done((f32[4,4,64,256]{3,2,1,0:T(8,128)}, f32[4,4,64,256]{3,2,1,0:T(8,128)S(1)}, u32[]{:S(2)}, u32[]{:S(2)}) %collective-permute-start.4) | collective-permute-done | bytes 1048608 | tf_op jit(solution)/shard_map/ppermute | solution.py:18
  207.2 13.4 %collective-permute-done.5 = f32[4,4,64,256]{3,2,1,0:T(8,128)S(1)} collective-permute-done((f32[4,4,64,256]{3,2,1,0:T(8,128)S(1)}, f32[4,4,64,256]{3,2,1,0:T(8,128)S(1)}, u32[]{:S(2)}, u32[]{:S(2)}) %collective-permute-start.5) | collective-permute-done | bytes 1048608 | tf_op jit(solution)/shard_map/ppermute | solution.py:18
  221.6 6.0 %collective-permute-done.6 = f32[4,4,64,256]{3,2,1,0:T(8,128)} collective-permute-done((f32[4,4,64,256]{3,2,1,0:T(8,128)S(1)}, f32[4,4,64,256]{3,2,1,0:T(8,128)}, u32[]{:S(2)}, u32[]{:S(2)}) %collective-permute-start.6) | collective-permute-done | bytes 1048608 | tf_op jit(solution)/shard_map/ppermute | solution.py:18
  227.6 4.1 multiply_add_fusion.3
  231.6 3.4 collective-permute-start.7
  236.3 5.6 %collective-permute-start.9 = (f32[4,4,64,256]{3,2,1,0:T(8,128)}, f32[4,4,64,256]{3,2,1,0:T(8,128)}, u32[]{:S(2)}, u32[]{:S(2)}) collective-permute-start(f32[4,4,64,256]{3,2,1,0:T(8,128)} %get-tuple-element.151), channel_id=1, source_target_pairs={{0,1},{1,2},{2,3},{4,5},{5,6},{6,7},{8,9},{9,10},{10,11},{12,13},{... | collective-permute-start | bytes 3145736 | tf_op jit(solution)/shard_map/ppermute | solution.py:18
  243.4 17.7 %multiply_reduce_fusion = (f32[8,4,4,4]{3,2,1,0:T(4,128)S(1)}, f32[8,4,4,64,256]{4,3,2,1,0:T(8,128)}, f32[8,4,4,64,256]{4,3,2,1,0:T(8,128)}) fusion(f32[8,4,4,4]{3,2,1,0:T(4,128)S(1)} %bitcast_multiply_fusion.8, f32[8,4,4,64,256]{4,3,1,2,0:T(8,128)S(1)} %bitcast.244, f32[8,4,4,64,256]{4,3,1,2,0:T(8,128)S(1)} %fusion.60), kind=kLoop, calls=%fused_computation.2 | loop fusion | flops 46136832 | bytes 33558528 | tf_op jit(solution)/shard_map/transpose(jvp(vmap()))/reduce_sum | solution.py:139
  261.1 4.5 fusion.170
  265.7 12.6 %collective-permute-done.9 = f32[4,4,64,256]{3,2,1,0:T(8,128)} collective-permute-done((f32[4,4,64,256]{3,2,1,0:T(8,128)}, f32[4,4,64,256]{3,2,1,0:T(8,128)}, u32[]{:S(2)}, u32[]{:S(2)}) %collective-permute-start.9) | collective-permute-done | bytes 1048608 | tf_op jit(solution)/shard_map/ppermute | solution.py:18
  278.2 4.2 collective-permute-done.10
  282.4 2.0 multiply_add_fusion
  284.4 2.5 collective-permute-start.11
  286.9 1.7 collective-permute-start.12
  288.6 14.5 %fusion.100 = (f32[8,4,4,128]{3,2,1,0:T(4,128)}, f32[8,4,4,128]{3,2,1,0:T(4,128)}, f32[8,4,128,128]{2,3,1,0:T(8,128)}) fusion(f32[8,4,4,128]{3,2,1,0:T(4,128)S(1)} %copy.361, f32[4,128,128]{1,2,0:T(8,128)S(1)} %copy-done.43, f32[8,4,128,128]{2,3,1,0:T(8,128)S(1)} %fusion.170, bf16[8,4,4,64,128]{4,2,3,1,0:T(4,128)(2,1)S(1)} %bitcast.245, ...), kind=kOutput, calls=%fused_computation.153 | convolution fusion | flops 1642561536 | bytes 11010048 | tf_op jit(solution)/shard_map/transpose(jvp(vmap(hcij,hpcj->hpci)))/dot_general | solution.py:82
  304.4 2.0 collective-permute-done.11
  306.4 4.2 collective-permute-done.12
  310.6 8.2 %multiply_reduce_fusion.4 = (f32[8,4,4]{1,2,0:T(4,128)}, f32[8,4,4,64,256]{4,3,1,2,0:T(8,128)S(1)}) fusion(f32[8,4,4,64,256]{4,3,1,2,0:T(8,128)} %get-tuple-element.210, f32[8,4,64,256]{3,2,1,0:T(8,128)S(1)} %constant_dynamic-update-slice_fusion.2, f32[8,4,4,64,256]{4,3,2,1,0:T(8,128)} %get-tuple-element.115, f32[8,4,4]{1,2,0:T(4,128)S(1)} %copy.397), kind=kLoop, calls=%fused_computation.24 | loop fusion | flops 8388480 | bytes 27264000 | tf_op jit(solution)/shard_map/transpose(jvp(vmap()))/reduce_sum | solution.py:139
  318.8 9.2 %fusion.12 = f32[8,4,256,128,1]{2,3,4,1,0:T(8,128)} fusion(f32[8,4,4,64,256]{4,3,1,2,0:T(8,128)S(1)} %get-tuple-element.146, f32[8,4,64,4,128]{4,3,2,1,0:T(4,128)S(1)} %copy-done.5, f32[8,4,4,128]{3,2,1,0:T(4,128)S(1)} %copy.377, f32[8,4,4,128]{3,2,1,0:T(4,128)S(1)} %copy.358), kind=kOutput, calls=%fused_computation.21 | convolution fusion | flops 3223322624 | bytes 16908288 | tf_op jit(solution)/shard_map/transpose(jvp(vmap(hpcj,hcj,ncj->hcpn)))/dot_general | solution.py:86
  328.0 8.6 %bitcast_add_fusion.2 = f32[8,256,4,128]{1,3,2,0:T(8,128)} fusion(f32[8,4,256,128,1]{2,3,4,1,0:T(8,128)} %fusion.12, f32[8,4,128,128]{2,3,1,0:T(8,128)} %get-tuple-element.112, f32[8,256,4,128]{1,3,2,0:T(8,128)S(1)} %bitcast.238), kind=kOutput, calls=%fused_computation.59 | convolution fusion | flops 1611661312 | bytes 14680064 | tf_op jit(solution)/shard_map/transpose(jvp(vmap(nci,ncj->cij)))/dot_general | solution.py:80
  336.6 5.6 %copy.412 = f32[8,256,512]{2,0,1:T(8,128)} copy(f32[8,256,512]{1,2,0:T(8,128)} %bitcast.247) | data formatting | bytes 8388608 | tf_op jit(solution)/shard_map/transpose(jvp(vmap()))/reshape | solution.py:68
  344.3 5.8 %fusion.171 = f32[8,4,128,256]{3,2,1,0:T(8,128)S(1)} fusion(f32[8,4,128,128]{2,3,1,0:T(8,128)S(1)} %copy-done.28, f32[8,256,4,128]{1,3,2,0:T(8,128)} %bitcast.240), kind=kOutput, calls=%fused_computation.316 | convolution fusion | flops 1610612736 | bytes 10485760 | tf_op jit(solution)/shard_map/transpose(jvp(vmap(nci,ncj->cij)))/dot_general | solution.py:80
  350.3 8.1 %multiply_reduce_fusion.3 = (f32[8,4,4]{1,2,0:T(4,128)S(1)}, f32[8,4,4,64,256]{4,3,1,2,0:T(8,128)S(1)}) fusion(f32[8,4,4,64,256]{4,3,1,2,0:T(8,128)} %copy-done.2, f32[8,4,64,256]{3,2,1,0:T(8,128)S(1)} %constant_dynamic-update-slice_fusion, f32[8,4,4]{1,2,0:T(4,128)S(1)} %copy.381, f32[8,4,4,64,256]{4,3,2,1,0:T(8,128)} %get-tuple-element.114), kind=kLoop, calls=%fused_computation.23 | loop fusion | flops 8388480 | bytes 27264000 | tf_op jit(solution)/shard_map/transpose(jvp(vmap()))/reduce_sum | solution.py:150
  358.4 9.0 %bitcast_add_fusion.3 = f32[8,4,128,256]{3,2,1,0:T(8,128)} fusion(f32[8,4,128,256]{3,2,1,0:T(8,128)S(1)} %fusion.171, f32[8,4,4,64,256]{4,3,1,2,0:T(8,128)S(1)} %get-tuple-element.148, f32[8,4,4,128]{3,2,1,0:T(4,128)S(1)} %copy.394, bf16[8,4,64,4,128]{4,3,2,1,0:T(4,128)(2,1)S(1)} %copy-done.10), kind=kOutput, calls=%fused_computation.60 | convolution fusion | flops 3224371200 | bytes 18939904 | tf_op jit(solution)/shard_map/transpose(jvp(vmap(nci,hci,chpn->hpci)))/dot_general | solution.py:157
  367.4 5.6 %copy.417 = f32[8,256,512]{2,0,1:T(8,128)} copy(f32[8,256,512]{1,2,0:T(8,128)} %bitcast.248) | data formatting | bytes 8388608 | tf_op jit(solution)/shard_map/transpose(jvp(vmap()))/reshape | solution.py:69
  373.0 11.3 %fusion.16 = f32[8,4,4,64,128]{4,3,2,1,0:T(8,128)S(1)} fusion(f32[8,256,4,128,1]{1,3,4,2,0:T(8,128)} %bitcast.235, f32[8,4,4,64,256]{4,3,1,2,0:T(8,128)} %copy-done.4), kind=kOutput, calls=%fused_computation.28 | convolution fusion | flops 3221225472 | bytes 16777216 | tf_op jit(solution)/shard_map/jvp(vmap(nci,hci,chpn->hpci))/dot_general | solution.py:157
  384.3 2.1 copy-done.26
  386.4 10.9 %fusion.39 = bf16[8,4,64,4,128]{4,2,3,1,0:T(8,128)(2,1)} fusion(f32[8,4,4,64,128]{4,3,2,1,0:T(8,128)S(1)} %fusion.16, f32[8,4,64,4,128]{4,3,2,1,0:T(4,128)S(1)} %copy-done.6, f32[8,4,128,128]{2,3,1,0:T(8,128)S(1)} %copy-done.32, f32[4,128,128]{1,2,0:T(8,128)S(1)} %copy-done.44, f32[8,4,4,128]{3,2,1,0:T(4,128)S(1)} %copy-done.59, ...), kind=kOutput, calls=%fused_computation.70 | convolution fusion | flops 1625292800 | bytes 13041792 | tf_op jit(solution)/shard_map/jvp(vmap(hcij,hpcj->hpci))/dot_general | solution.py:82
  397.4 15.1 %fusion.38 = (f32[8,4,4,128]{3,2,1,0:T(4,128)S(1)}, f32[8,4,4,64,128]{4,3,1,2,0:T(8,128)}) fusion(f32[8,4,64,4,128]{4,3,2,1,0:T(4,128)} %reshape.298, f32[8,4,4,128]{3,2,1,0:T(4,128)S(1)} %copy.358, f32[8,4,4,64,256]{4,3,1,2,0:T(8,128)} %copy-done.3, f32[8,256,4,128,1]{1,3,2,4,0:T(8,128)} %bitcast.241), kind=kOutput, calls=%fused_computation.68 | convolution fusion | flops 3224354816 | bytes 21102592 | tf_op jit(solution)/shard_map/transpose(jvp(vmap(hpcj,hcj,ncj->hcpn)))/dot_general | solution.py:86
  412.5 3.3 copy.395
  415.7 4.5 convert_element_type.96
  420.2 12.3 %fusion.36 = (f32[8,4,4,128]{3,2,1,0:T(4,128)S(1)}, f32[8,4,64,4,128]{4,2,3,1,0:T(8,128)S(1)}) fusion(f32[8,4,64,4,128]{4,3,2,1,0:T(4,128)} %reshape.298, f32[8,4,4,128]{3,2,1,0:T(4,128)S(1)} %copy.358, bf16[8,4,64,4,128]{4,3,2,1,0:T(4,128)(2,1)S(1)} %copy-done.10, f32[8,4]{1,0:T(8,128)S(1)} %copy-done.90, bf16[8,4,4,64,128]{4,2,3,1,0:T(4,128)(2,1)S(1)} %bitcast.246, ...), kind=kOutput, calls=%fused_computation.64 | convolution fusion | flops 1627373568 | bytes 19398784 | tf_op jit(solution)/shard_map/transpose(jvp(vmap(hcij,hpcj->hpci)))/dot_general | solution.py:82
  432.5 5.6 %copy.407 = f32[8,4,64,4,128]{4,3,2,1,0:T(4,128)} copy(f32[8,4,64,4,128]{4,2,3,1,0:T(8,128)S(1)} %get-tuple-element.139) | data formatting | bytes 8388608 | tf_op jit(solution)/shard_map/transpose(jvp(vmap()))/add_any | solution.py:81
  438.1 5.5 %reshape.305 = f32[8,256,512]{2,1,0:T(8,128)} reshape(f32[8,4,64,4,128]{4,3,2,1,0:T(4,128)} %copy.407) | data formatting | bytes 8388608 | tf_op jit(solution)/shard_map/transpose(jvp(vmap()))/reshape | solution.py:67
  443.7 4.4 broadcast_multiply_fusion
  450.1 4.8 pad_add_fusion
  455.0 3.2 split.16
  458.5 2.5 multiply_reduce_fusion.6
  461.9 3.3 fusion.30
  466.2 2.6 pad_add_fusion.3
  477.1 2.9 slice_maximum_fusion
  481.5 1.8 copy.421
  (362 shorter events, 63.1 us)
Async XLA Ops:
  7.2 82.2 %all-gather.6.cloned.1.call-start = ((), (), s32[]{:S(2)}) async-start(), calls=%async_computation.3 | async-start | bytes 4718592 | tf_op jit(solution)/shard_map/all_gather | solution.py:238
  11.6 10.4 %copy-start.39 = (bf16[8,32,512]{2,1,0:T(8,128)(2,1)S(1)}, bf16[8,32,512]{2,1,0:T(8,128)(2,1)}, u32[]{:S(2)}) copy-start(bf16[8,32,512]{2,1,0:T(8,128)(2,1)} %param.15) | copy-start | bytes 786436
  11.6 10.5 %copy-start.48 = (f32[2,4,2560]{2,1,0:T(4,128)S(1)}, f32[2,4,2560]{2,1,0:T(4,128)}, u32[]{:S(2)}) copy-start(f32[2,4,2560]{2,1,0:T(4,128)} %param.18) | copy-start | bytes 245764
  11.6 10.6 %copy-start.75 = (f32[2,2560]{1,0:T(2,128)S(1)}, f32[2,2560]{1,0:T(2,128)}, u32[]{:S(2)}) copy-start(f32[2,2560]{1,0:T(2,128)} %param.19) | copy-start | bytes 61444
  11.6 10.6 %copy-start.97 = (f32[2,32]{1,0:T(2,128)S(1)}, f32[2,32]{1,0:T(2,128)}, u32[]{:S(2)}) copy-start(f32[2,32]{1,0:T(2,128)} %param.20) | copy-start | bytes 772
  11.6 10.6 %copy-start.98 = (f32[2,32]{1,0:T(2,128)S(1)}, f32[2,32]{1,0:T(2,128)}, u32[]{:S(2)}) copy-start(f32[2,32]{1,0:T(2,128)} %param.21) | copy-start | bytes 772
  11.6 10.6 %copy-start.99 = (f32[2,32]{1,0:T(2,128)S(1)}, f32[2,32]{1,0:T(2,128)}, u32[]{:S(2)}) copy-start(f32[2,32]{1,0:T(2,128)} %param.22) | copy-start | bytes 772
  16.4 29.8 %collective-permute-start = (bf16[8,320,3]{1,0,2:T(8,128)(2,1)}, bf16[8,320,3]{1,0,2:T(8,128)(2,1)}, u32[]{:S(2)}, u32[]{:S(2)}) collective-permute-start(bf16[8,320,3]{1,0,2:T(8,128)(2,1)} %pad_maximum_fusion.3), channel_id=1, source_target_pairs={{0,1},{1,2},{2,3},{4,5},{5,6},{6,7},{8,9},{9,10},{10,11},{12,13},{... | collective-permute-start | bytes 46088 | tf_op jit(solution)/shard_map/ppermute | solution.py:18
  38.5 14.9 %copy-start.29 = (bf16[8,256,512]{2,1,0:T(8,128)(2,1)S(1)}, bf16[8,256,512]{2,1,0:T(8,128)(2,1)}, u32[]{:S(2)}) copy-start(bf16[8,256,512]{2,1,0:T(8,128)(2,1)} %param.13) | copy-start | bytes 6291460
  40.7 15.3 %copy-start.47 = (f32[8,2560]{1,0:T(8,128)}, f32[8,2560]{1,0:T(8,128)S(1)}, u32[]{:S(2)}) copy-start(f32[8,2560]{1,0:T(8,128)S(1)} %slice.253) | copy-start | bytes 245764
  52.7 73.9 %all-gather.4.cloned.1.call-start = ((), (), s32[]{:S(2)}) async-start(), calls=%async_computation.2 | async-start | bytes 4718592 | tf_op jit(solution)/shard_map/all_gather | solution.py:239
  57.7 13.9 %copy-start.63 = (f32[512]{0:T(512)S(1)}, f32[512]{0:T(512)}, u32[]{:S(2)}) copy-start(f32[512]{0:T(512)} %get-tuple-element.200) | copy-start | bytes 6148
  58.8 410.0 %reduce-scatter.3.cloned.1.call-start = ((), (), s32[]{:S(2)}) async-start(), calls=%async_computation.4 | async-start | bytes 4718592 | tf_op jit(solution)/shard_map/reduce_scatter | solution.py:276
  59.5 11.0 %copy-start.83 = (f32[8,4]{0,1:T(4,128)}, f32[8,4]{0,1:T(4,128)S(1)}, u32[]{:S(2)}) copy-start(f32[8,4]{0,1:T(4,128)S(1)} %copy.357) | copy-start | bytes 388
  60.4 23.7 %copy-start.45 = (f32[8,4,4]{0,2,1:T(4,128)}, f32[8,4,4]{0,2,1:T(4,128)S(1)}, u32[]{:S(2)}) copy-start(f32[8,4,4]{0,2,1:T(4,128)S(1)} %slice_reduce_fusion) | copy-start | bytes 1540
  64.2 67.7 %copy-start.7 = (bf16[8,4,64,4,128]{4,3,2,1,0:T(4,128)(2,1)}, bf16[8,4,64,4,128]{4,3,2,1,0:T(4,128)(2,1)S(1)}, u32[]{:S(2)}) copy-start(bf16[8,4,64,4,128]{4,3,2,1,0:T(4,128)(2,1)S(1)} %reshape.302) | copy-start | bytes 6291460
  69.1 14.9 %copy-start.49 = (f32[8,256]{1,0:T(8,128)}, f32[8,256]{1,0:T(8,128)S(1)}, u32[]{:S(2)}) copy-start(f32[8,256]{1,0:T(8,128)S(1)} %get-tuple-element.168) | copy-start | bytes 24580
  69.1 14.9 %copy-start.51 = (f32[8,256]{1,0:T(8,128)}, f32[8,256]{1,0:T(8,128)S(1)}, u32[]{:S(2)}) copy-start(f32[8,256]{1,0:T(8,128)S(1)} %get-tuple-element.169) | copy-start | bytes 24580
  69.1 14.9 %copy-start.53 = (f32[8,256]{1,0:T(8,128)}, f32[8,256]{1,0:T(8,128)S(1)}, u32[]{:S(2)}) copy-start(f32[8,256]{1,0:T(8,128)S(1)} %get-tuple-element.170) | copy-start | bytes 24580
  94.7 14.0 %copy-start.78 = (f32[8,4]{1,0:T(8,128)S(1)}, f32[8,4]{1,0:T(8,128)}, u32[]{:S(2)}) copy-start(f32[8,4]{1,0:T(8,128)} %copy.385) | copy-start | bytes 388
  138.1 8.4 %copy-start.87 = (f32[4,4]{0,1:T(4,128)S(1)}, f32[4,4]{0,1:T(4,128)}, u32[]{:S(2)}) copy-start(f32[4,4]{0,1:T(4,128)} %get-tuple-element.206) | copy-start | bytes 196
  138.1 8.5 %copy-start.86 = (f32[4,4]{0,1:T(4,128)S(1)}, f32[4,4]{0,1:T(4,128)}, u32[]{:S(2)}) copy-start(f32[4,4]{0,1:T(4,128)} %get-tuple-element.205) | copy-start | bytes 196
  138.1 8.5 %copy-start.85 = (pred[4,4,4]{1,0,2:T(4,128)(4,1)S(1)}, pred[4,4,4]{1,0,2:T(4,128)(4,1)}, u32[]{:S(2)}) copy-start(pred[4,4,4]{1,0,2:T(4,128)(4,1)} %get-tuple-element.208) | copy-start | bytes 196
  138.1 33.9 %copy-start.18 = (f32[8,4,64,256]{3,2,1,0:T(8,128)S(1)}, f32[8,4,64,256]{3,2,1,0:T(8,128)}, u32[]{:S(2)}) copy-start(f32[8,4,64,256]{3,2,1,0:T(8,128)} %broadcast_add_fusion) | copy-start | bytes 6291460
  139.2 26.7 %collective-permute-start.1 = (f32[4,4,64,256]{3,2,1,0:T(8,128)}, f32[4,4,64,256]{3,2,1,0:T(8,128)}, u32[]{:S(2)}, u32[]{:S(2)}) collective-permute-start(f32[4,4,64,256]{3,2,1,0:T(8,128)} %slice.235), channel_id=1, source_target_pairs={{0,1},{1,2},{2,3},{4,5},{5,6},{6,7},{8,9},{9,10},{10,11},{12,13},{... | collective-permute-start | bytes 3145736 | tf_op jit(solution)/shard_map/ppermute | solution.py:18
  144.8 27.2 %collective-permute-start.2 = (f32[4,4,64,256]{3,2,1,0:T(8,128)}, f32[4,4,64,256]{3,2,1,0:T(8,128)}, u32[]{:S(2)}, u32[]{:S(2)}) collective-permute-start(f32[4,4,64,256]{3,2,1,0:T(8,128)} %slice.236), channel_id=1, source_target_pairs={{1,0},{2,1},{3,2},{5,4},{6,5},{7,6},{9,8},{10,9},{11,10},{13,12},{... | collective-permute-start | bytes 3145736 | tf_op jit(solution)/shard_map/ppermute | solution.py:18
  146.4 142.2 %copy-start.58 = (f32[8,4,4,128]{3,2,1,0:T(4,128)}, f32[8,4,4,128]{3,2,1,0:T(4,128)S(1)}, u32[]{:S(2)}) copy-start(f32[8,4,4,128]{3,2,1,0:T(4,128)S(1)} %copy.361) | copy-start | bytes 196612
  147.0 29.4 %copy-start.22 = (f32[8,4,64,256]{3,2,1,0:T(8,128)S(1)}, f32[8,4,64,256]{3,2,1,0:T(8,128)}, u32[]{:S(2)}) copy-start(f32[8,4,64,256]{3,2,1,0:T(8,128)} %copy-done.21) | copy-start | bytes 6291460
  147.3 38.9 %copy-start.62 = (s32[4,128]{1,0:T(4,128)S(1)}, s32[4,128]{1,0:T(4,128)}, u32[]{:S(2)}) copy-start(s32[4,128]{1,0:T(4,128)} %copy-done.61) | copy-start | bytes 6148
  172.1 15.0 %copy-start.8 = (bf16[8,4,64,4,128]{4,3,2,1,0:T(4,128)(2,1)S(1)}, bf16[8,4,64,4,128]{4,3,2,1,0:T(4,128)(2,1)}, u32[]{:S(2)}) copy-start(bf16[8,4,64,4,128]{4,3,2,1,0:T(4,128)(2,1)} %copy-done.7) | copy-start | bytes 6291460
  173.7 13.4 %copy-start = (f32[8,256,512]{1,2,0:T(8,128)S(1)}, f32[8,256,512]{1,2,0:T(8,128)}, u32[]{:S(2)}) copy-start(f32[8,256,512]{1,2,0:T(8,128)} %copy.366) | copy-start | bytes 12582916
  173.7 26.3 %collective-permute-start.3 = (f32[4,4,64,256]{3,2,1,0:T(8,128)S(1)}, f32[4,4,64,256]{3,2,1,0:T(8,128)S(1)}, u32[]{:S(2)}, u32[]{:S(2)}) collective-permute-start(f32[4,4,64,256]{3,2,1,0:T(8,128)S(1)} %get-tuple-element.156), channel_id=1, source_target_pairs={{0,1},{1,2},{2,3},{4,5},{5,6},{6,7},{8,9},{9,10},{10,11},{12,13},{... | collective-permute-start | bytes 3145736 | tf_op jit(solution)/shard_map/ppermute | solution.py:18
  179.0 28.2 %collective-permute-start.4 = (f32[4,4,64,256]{3,2,1,0:T(8,128)}, f32[4,4,64,256]{3,2,1,0:T(8,128)S(1)}, u32[]{:S(2)}, u32[]{:S(2)}) collective-permute-start(f32[4,4,64,256]{3,2,1,0:T(8,128)} %get-tuple-element.154), channel_id=1, source_target_pairs={{1,0},{2,1},{3,2},{5,4},{6,5},{7,6},{9,8},{10,9},{11,10},{13,12},{... | collective-permute-start | bytes 3145736 | tf_op jit(solution)/shard_map/ppermute | solution.py:18
  180.3 40.3 %collective-permute-start.5 = (f32[4,4,64,256]{3,2,1,0:T(8,128)S(1)}, f32[4,4,64,256]{3,2,1,0:T(8,128)S(1)}, u32[]{:S(2)}, u32[]{:S(2)}) collective-permute-start(f32[4,4,64,256]{3,2,1,0:T(8,128)S(1)} %get-tuple-element.155), channel_id=1, source_target_pairs={{0,1},{1,2},{2,3},{4,5},{5,6},{6,7},{8,9},{9,10},{10,11},{12,13},{... | collective-permute-start | bytes 3145736 | tf_op jit(solution)/shard_map/ppermute | solution.py:18
  184.9 42.7 %collective-permute-start.6 = (f32[4,4,64,256]{3,2,1,0:T(8,128)S(1)}, f32[4,4,64,256]{3,2,1,0:T(8,128)}, u32[]{:S(2)}, u32[]{:S(2)}) collective-permute-start(f32[4,4,64,256]{3,2,1,0:T(8,128)S(1)} %get-tuple-element.153), channel_id=1, source_target_pairs={{1,0},{2,1},{3,2},{5,4},{6,5},{7,6},{9,8},{10,9},{11,10},{13,12},{... | collective-permute-start | bytes 3145736 | tf_op jit(solution)/shard_map/ppermute | solution.py:18
  187.1 56.3 %slice-start = ((s8[8388608]{0:T(1024)(128)(4,1)}), s8[4194304]{0:T(1024)(128)(4,1)S(1)}, s32[]{:S(2)}) async-start(s8[8388608]{0:T(1024)(128)(4,1)} %bitcast.243), calls=%async_computation.6 | async-start | bytes 8388608
  187.1 40.5 %copy-start.19 = (f32[8,4,64,256]{3,2,1,0:T(8,128)S(1)}, f32[8,4,64,256]{3,2,1,0:T(8,128)}, u32[]{:S(2)}) copy-start(f32[8,4,64,256]{3,2,1,0:T(8,128)} %broadcast_add_fusion) | copy-start | bytes 6291460
  187.1 56.3 %slice-start.1 = ((s8[8388608]{0:T(1024)(128)(4,1)}), s8[4194304]{0:T(1024)(128)(4,1)S(1)}, s32[]{:S(2)}) async-start(s8[8388608]{0:T(1024)(128)(4,1)} %bitcast.243), calls=%async_computation.7 | async-start | bytes 8388608
  194.4 49.0 %copy-start.2 = (f32[8,4,4,64,256]{4,3,1,2,0:T(8,128)}, f32[8,4,4,64,256]{4,3,1,2,0:T(8,128)S(1)}, u32[]{:S(2)}) copy-start(f32[8,4,4,64,256]{4,3,1,2,0:T(8,128)S(1)} %fusion.60) | copy-start | bytes 25165828
  231.6 34.0 %collective-permute-start.7 = (f32[4,4,64,256]{3,2,1,0:T(8,128)}, f32[4,4,64,256]{3,2,1,0:T(8,128)S(1)}, u32[]{:S(2)}, u32[]{:S(2)}) collective-permute-start(f32[4,4,64,256]{3,2,1,0:T(8,128)} %get-tuple-element.152), channel_id=1, source_target_pairs={{0,1},{1,2},{2,3},{4,5},{5,6},{6,7},{8,9},{9,10},{10,11},{12,13},{... | collective-permute-start | bytes 3145736 | tf_op jit(solution)/shard_map/ppermute | solution.py:18
  235.0 30.6 %collective-permute-start.8 = (f32[4,4,64,256]{3,2,1,0:T(8,128)}, f32[4,4,64,256]{3,2,1,0:T(8,128)}, u32[]{:S(2)}, u32[]{:S(2)}) collective-permute-start(f32[4,4,64,256]{3,2,1,0:T(8,128)} %get-tuple-element.196), channel_id=1, source_target_pairs={{1,0},{2,1},{3,2},{5,4},{6,5},{7,6},{9,8},{10,9},{11,10},{13,12},{... | collective-permute-start | bytes 3145736 | tf_op jit(solution)/shard_map/ppermute | solution.py:18
  236.3 41.9 %collective-permute-start.9 = (f32[4,4,64,256]{3,2,1,0:T(8,128)}, f32[4,4,64,256]{3,2,1,0:T(8,128)}, u32[]{:S(2)}, u32[]{:S(2)}) collective-permute-start(f32[4,4,64,256]{3,2,1,0:T(8,128)} %get-tuple-element.151), channel_id=1, source_target_pairs={{0,1},{1,2},{2,3},{4,5},{5,6},{6,7},{8,9},{9,10},{10,11},{12,13},{... | collective-permute-start | bytes 3145736 | tf_op jit(solution)/shard_map/ppermute | solution.py:18
  241.9 40.5 %collective-permute-start.10 = (f32[4,4,64,256]{3,2,1,0:T(8,128)}, f32[4,4,64,256]{3,2,1,0:T(8,128)}, u32[]{:S(2)}, u32[]{:S(2)}) collective-permute-start(f32[4,4,64,256]{3,2,1,0:T(8,128)} %get-tuple-element.197), channel_id=1, source_target_pairs={{1,0},{2,1},{3,2},{5,4},{6,5},{7,6},{9,8},{10,9},{11,10},{13,12},{... | collective-permute-start | bytes 3145736 | tf_op jit(solution)/shard_map/ppermute | solution.py:18
  243.4 17.7 %copy-start.1 = (f32[8,256,512]{1,2,0:T(8,128)S(1)}, f32[8,256,512]{1,2,0:T(8,128)}, u32[]{:S(2)}) copy-start(f32[8,256,512]{1,2,0:T(8,128)} %copy.368) | copy-start | bytes 12582916
  261.1 21.3 %copy-start.20 = (f32[8,4,64,256]{3,2,1,0:T(8,128)S(1)}, f32[8,4,64,256]{3,2,1,0:T(8,128)}, u32[]{:S(2)}) copy-start(f32[8,4,64,256]{3,2,1,0:T(8,128)} %broadcast_add_fusion) | copy-start | bytes 6291460
  261.1 21.3 %copy-start.23 = (f32[8,4,64,256]{3,2,1,0:T(8,128)S(1)}, f32[8,4,64,256]{3,2,1,0:T(8,128)}, u32[]{:S(2)}) copy-start(f32[8,4,64,256]{3,2,1,0:T(8,128)} %copy-done.21) | copy-start | bytes 6291460
  261.1 27.5 %copy-start.43 = (f32[4,128,128]{1,2,0:T(8,128)S(1)}, f32[4,128,128]{1,2,0:T(8,128)}, u32[]{:S(2)}) copy-start(f32[4,128,128]{1,2,0:T(8,128)} %compare_select_fusion) | copy-start | bytes 786436
  265.6 23.0 %copy-start.31 = (f32[8,4,128,128]{2,3,1,0:T(8,128)}, f32[8,4,128,128]{2,3,1,0:T(8,128)S(1)}, u32[]{:S(2)}) copy-start(f32[8,4,128,128]{2,3,1,0:T(8,128)S(1)} %fusion.170) | copy-start | bytes 6291460
  265.6 23.0 %copy-start.5 = (f32[8,4,64,4,128]{4,3,2,1,0:T(4,128)S(1)}, f32[8,4,64,4,128]{4,3,2,1,0:T(4,128)}, u32[]{:S(2)}) copy-start(f32[8,4,64,4,128]{4,3,2,1,0:T(4,128)} %reshape.298) | copy-start | bytes 12582916
  265.6 23.0 %copy-start.9 = (bf16[8,4,64,4,128]{4,3,2,1,0:T(4,128)(2,1)S(1)}, bf16[8,4,64,4,128]{4,3,2,1,0:T(4,128)(2,1)}, u32[]{:S(2)}) copy-start(bf16[8,4,64,4,128]{4,3,2,1,0:T(4,128)(2,1)} %copy-done.7) | copy-start | bytes 6291460
  265.7 37.5 %copy-start.35 = (f32[4,4,64,256]{3,2,1,0:T(8,128)}, f32[4,4,64,256]{3,2,1,0:T(8,128)S(1)}, u32[]{:S(2)}) copy-start(f32[4,4,64,256]{3,2,1,0:T(8,128)S(1)} %collective-permute-done.7) | copy-start | bytes 3145732
  284.4 22.0 %collective-permute-start.11 = (f32[4,4,64,256]{3,2,1,0:T(8,128)S(1)}, f32[4,4,64,256]{3,2,1,0:T(8,128)S(1)}, u32[]{:S(2)}, u32[]{:S(2)}) collective-permute-start(f32[4,4,64,256]{3,2,1,0:T(8,128)S(1)} %get-tuple-element.204), channel_id=1, source_target_pairs={{0,1},{1,2},{2,3},{4,5},{5,6},{6,7},{8,9},{9,10},{10,11},{12,13},{... | collective-permute-start | bytes 3145736 | tf_op jit(solution)/shard_map/ppermute | solution.py:18
  286.9 23.7 %collective-permute-start.12 = (f32[4,4,64,256]{3,2,1,0:T(8,128)S(1)}, f32[4,4,64,256]{3,2,1,0:T(8,128)S(1)}, u32[]{:S(2)}, u32[]{:S(2)}) collective-permute-start(f32[4,4,64,256]{3,2,1,0:T(8,128)S(1)} %get-tuple-element.203), channel_id=1, source_target_pairs={{1,0},{2,1},{3,2},{5,4},{6,5},{7,6},{9,8},{10,9},{11,10},{13,12},{... | collective-permute-start | bytes 3145736 | tf_op jit(solution)/shard_map/ppermute | solution.py:18
  306.4 12.4 %copy-start.37 = (f32[4,4,64,256]{3,2,1,0:T(8,128)}, f32[4,4,64,256]{3,2,1,0:T(8,128)S(1)}, u32[]{:S(2)}) copy-start(f32[4,4,64,256]{3,2,1,0:T(8,128)S(1)} %collective-permute-done.11) | copy-start | bytes 3145732
  318.8 9.2 %copy-start.3 = (f32[8,4,4,64,256]{4,3,1,2,0:T(8,128)}, f32[8,4,4,64,256]{4,3,1,2,0:T(8,128)S(1)}, u32[]{:S(2)}) copy-start(f32[8,4,4,64,256]{4,3,1,2,0:T(8,128)S(1)} %get-tuple-element.146) | copy-start | bytes 25165828
  342.2 128.0 %reduce-scatter.5.cloned.1.call-start = ((), (), s32[]{:S(2)}) async-start(), calls=%async_computation.5 | async-start | bytes 4718592 | tf_op jit(solution)/shard_map/reduce_scatter | solution.py:277
  358.4 9.0 %copy-start.4 = (f32[8,4,4,64,256]{4,3,1,2,0:T(8,128)}, f32[8,4,4,64,256]{4,3,1,2,0:T(8,128)S(1)}, u32[]{:S(2)}) copy-start(f32[8,4,4,64,256]{4,3,1,2,0:T(8,128)S(1)} %get-tuple-element.148) | copy-start | bytes 25165828
  373.0 13.4 %copy-start.6 = (f32[8,4,64,4,128]{4,3,2,1,0:T(4,128)S(1)}, f32[8,4,64,4,128]{4,3,2,1,0:T(4,128)}, u32[]{:S(2)}) copy-start(f32[8,4,64,4,128]{4,3,2,1,0:T(4,128)} %reshape.298) | copy-start | bytes 12582916
  373.0 13.4 %copy-start.32 = (f32[8,4,128,128]{2,3,1,0:T(8,128)S(1)}, f32[8,4,128,128]{2,3,1,0:T(8,128)}, u32[]{:S(2)}) copy-start(f32[8,4,128,128]{2,3,1,0:T(8,128)} %copy-done.31) | copy-start | bytes 6291460
  373.0 13.4 %copy-start.44 = (f32[4,128,128]{1,2,0:T(8,128)S(1)}, f32[4,128,128]{1,2,0:T(8,128)}, u32[]{:S(2)}) copy-start(f32[4,128,128]{1,2,0:T(8,128)} %compare_select_fusion) | copy-start | bytes 786436
  373.0 13.4 %copy-start.59 = (f32[8,4,4,128]{3,2,1,0:T(4,128)S(1)}, f32[8,4,4,128]{3,2,1,0:T(4,128)}, u32[]{:S(2)}) copy-start(f32[8,4,4,128]{3,2,1,0:T(4,128)} %copy-done.58) | copy-start | bytes 196612
  373.0 13.4 %copy-start.90 = (f32[8,4]{1,0:T(8,128)S(1)}, f32[8,4]{1,0:T(8,128)}, u32[]{:S(2)}) copy-start(f32[8,4]{1,0:T(8,128)} %get-tuple-element.214) | copy-start | bytes 388
  397.3 15.1 %copy-start.33 = (bf16[8,4,64,4,128]{4,2,3,1,0:T(8,128)(2,1)S(1)}, bf16[8,4,64,4,128]{4,2,3,1,0:T(8,128)(2,1)}, u32[]{:S(2)}) copy-start(bf16[8,4,64,4,128]{4,2,3,1,0:T(8,128)(2,1)} %fusion.39) | copy-start | bytes 6291460
  475.6 7.7 %collective-permute-start.13 = (f32[8,320,3]{1,0,2:T(8,128)S(1)}, f32[8,320,3]{1,0,2:T(8,128)S(1)}, u32[]{:S(2)}, u32[]{:S(2)}) collective-permute-start(f32[8,320,3]{1,0,2:T(8,128)S(1)} %copy.420), channel_id=1, source_target_pairs={{1,0},{2,1},{3,2},{5,4},{6,5},{7,6},{9,8},{10,9},{11,10},{13,12},{... | collective-permute-start | bytes 92168 | tf_op jit(solution)/shard_map/ppermute | solution.py:18
  (58 other events, 243.2 us)
Sparse Core Ops, SparseCore 0:
  52.9 35.0 all-gather.5
  89.9 36.7 all-gather.3
  342.3 48.5 reduce-scatter.2
  397.5 48.9 reduce-scatter.4

commit v7 on v5

--- a/solution.py
+++ b/solution.py
@@ -180,7 +180,9 @@
         ],
         axis=1,
     )
-    packed_all = lax.all_gather(packed, "head", axis=0, tiled=True)
+    slots = jnp.zeros((lax.axis_size("head") * groups_held, packed.shape[1]), packed.dtype)
+    slots = lax.dynamic_update_slice_in_dim(slots, packed, lax.axis_index("head") * groups_held, 0)
+    packed_all = lax.psum(slots, "head")
     cuts = [conv_weight[0].size, conv_bias.shape[1], dt_bias.shape[1], a_log.shape[1]]
     bounds = [sum(cuts[:k]) for k in range(len(cuts) + 1)]
     weight_all = packed_all[:, : bounds[1]].reshape((-1,) + conv_weight.shape[1:])

time: 488 us -> 504 us (1.033)
  waiting for transfers between devices: 101 us -> 130 us
  blocking collectives: 15.4 us -> 0 us
    psum x0 -> x1, waiting for transfers between devices: none -> 26.5 us  [shards(): packed_all = lax.psum(slots, 'head')]
    all_gather x1 -> x0, blocking collectives: 15.4 us -> none  [shards(): packed_all = lax.all_gather(packed, 'head', axis=0, tiled=True)]
    unnamed x219 -> x198, local copies, waits for them, and re-layouts: 16.5 us -> 17 us
  transfers between devices with their start and end apart: 12 -> 13, of which waited for: 8 -> 9; matrix products, arithmetic and copies ran while one was open for 51% -> 51% of each run, Pallas kernels for 0% -> 0%
where the time goes in v7:
time: 504 us; the launch traced here: 499 us
  matrix products  142 us (28%)
  waiting for transfers between devices  130 us (26%)
  other arithmetic  103 us (20%)
  local copies, waits for them, and re-layouts  84.8 us (17%)
  starting transfers between devices  23.1 us (5%)
  between operations  15.6 us (3%)
    ppermute x8, waiting for transfers between devices, passed_along(): lax.ppermute(value, axis, [(source, source + steps) for source in range(f...  81.8 us
    dot_general x3, matrix products, span_terms(): jnp.einsum('hcij,hpcj->hpci', decay * scores[None], weighted, precision=p...  41.3 us
    dot_general x3, matrix products, span_terms(): jnp.einsum('hpcj,hcj,ncj->hcpn', weighted, keep_end, b_three, precision=p...  41.2 us
    dot_general x3, matrix products, assemble(): jnp.einsum('nci,hci,chpn->hpci', c_three, entry, starts, precision=precise)  32.7 us
    reduce_sum x2, other arithmetic, weighted_sum(): return jnp.sum(weight[..., None, None] * stacked, axis=-3)  26.7 us
    psum x1, waiting for transfers between devices, shards(): packed_all = lax.psum(slots, 'head')  26.5 us
    ppermute x8, starting transfers between devices, passed_along(): lax.ppermute(value, axis, [(source, source + steps) for source in range(f...  22.3 us
    dot_general x3, matrix products, span_terms(): scores = jnp.einsum('nci,ncj->cij', c_three, b_three, precision=precise)  19.3 us
  transfers between devices with their start and end apart: 13, of which 9 were waited for; matrix products, arithmetic and copies ran while one was open for 51% of the time, Pallas kernels for 0%

profile of v7, /device:TPU:0, one launch (start us, length us, event | category | flops | bytes accessed | tf_op | source)
XLA Modules:
  0.0 498.7 jit_solution(15676975901025980586)
XLA Ops:
  10.0 3.3 copy.347
  13.3 1.7 copy.348
  15.1 1.7 copy.349
  17.5 4.9 collective-permute-start
  24.1 26.5 %all-reduce.29.cloned.1.call-done = f32[8,12896]{1,0:T(8,128)} async-done(((f32[8,12896]{1,0:T(8,128)}), f32[8,12896]{1,0:T(8,128)}) %all-reduce.29.cloned.1.call-update) | async-done | bytes 412688 | tf_op jit(solution)/shard_map/psum | solution.py:185
  52.9 2.4 fusion.102
  58.6 2.6 convert_element_type.83
  61.1 2.6 reshape.301
  70.7 12.6 %fusion.50 = (f32[8,256,512]{2,1,0:T(8,128)}, f32[8,256,512]{2,1,0:T(8,128)}) fusion(f32[8,256,512]{2,1,0:T(8,128)} %convert_element_type.83, f32[8,256]{1,0:T(8,128)S(1)} %get-tuple-element.150, f32[512]{0:T(512)S(1)} %get-tuple-element.183, f32[8,256,3]{2,1,0:T(8,128)S(1)} %copy.350, f32[8,256]{1,0:T(8,128)S(1)} %get-tuple-element.148, ...), kind=kLoop, calls=%fused_computation.88 | loop fusion | flops 18874368 | bytes 12654592 | tf_op jit(solution)/shard_map/jvp(vmap(jit(silu)))/mul | solution.py:53
  83.4 5.4 %reshape.297 = f32[8,4,64,4,128]{4,3,2,1,0:T(4,128)} reshape(f32[8,256,512]{2,1,0:T(8,128)} %get-tuple-element.122) | data formatting | bytes 8388608 | tf_op jit(solution)/shard_map/jvp(vmap())/reshape | solution.py:59
  89.3 3.8 all-gather.5.cloned.1.call-done
  93.1 5.3 %copy.363 = f32[8,256,512]{1,2,0:T(8,128)} copy(f32[8,256,512]{2,0,1:T(8,128)} %all-gather.5.cloned.1.call-done) | data formatting | bytes 8388608 | tf_op jit(solution)/shard_map/all_gather | solution.py:232
  98.4 13.8 %multiply_reduce_fusion.5 = (f32[8,4,64,256]{3,2,1,0:T(8,128)S(1)}, f32[8,4,4,64,256]{4,3,1,2,0:T(8,128)}) fusion(f32[8,4,4]{1,2,0:T(4,128)S(1)} %copy.378, f32[8,256,4,128,1]{1,3,4,2,0:T(8,128)} %bitcast.238, f32[8,4,64,4,128]{4,3,2,1,0:T(4,128)} %reshape.297, f32[8,4,4,128]{3,2,1,0:T(4,128)S(1)} %copy.372, f32[8,4,4,128]{3,2,1,0:T(4,128)S(1)} %copy.353), kind=kOutput, calls=%fused_computation.25 | convolution fusion | flops 3226992640 | bytes 19005952 | tf_op jit(solution)/shard_map/jvp(vmap(hpcj,hcj,ncj->hcpn))/dot_general | solution.py:78
  112.2 1.3 copy-done.14
  113.5 1.5 broadcast_add_fusion
  115.0 17.5 %all-gather.3.cloned.1.call-done = f32[8,256,512]{2,0,1:T(8,128)} async-done(((f32[8,32,512]{2,0,1:T(8,128)}), f32[8,256,512]{2,0,1:T(8,128)}) %all-gather.3.cloned.1.call-update) | async-done | bytes 4194320 | tf_op jit(solution)/shard_map/all_gather | solution.py:233
  132.5 5.3 %copy.361 = f32[8,256,512]{1,2,0:T(8,128)} copy(f32[8,256,512]{2,0,1:T(8,128)} %all-gather.3.cloned.1.call-done) | data formatting | bytes 8388608 | tf_op jit(solution)/shard_map/all_gather | solution.py:233
  137.8 7.0 %fusion.82 = f32[8,4,64,256]{3,2,1,0:T(8,128)} fusion(f32[8,256,4,128,1]{1,3,2,4,0:T(8,128)} %bitcast.233, f32[8,4,4,128]{3,2,1,0:T(4,128)S(1)} %copy.382, bf16[8,4,64,4,128]{4,3,2,1,0:T(4,128)(2,1)S(1)} %reshape.301), kind=kOutput, calls=%fused_computation.113 | convolution fusion | flops 3223322624 | bytes 8454144 | tf_op jit(solution)/shard_map/ghpci,ghci,gnci->ghpn/dot_general | solution.py:254
  144.9 3.5 collective-permute-start.1
  154.9 39.0 %collective-permute-done.1 = f32[8,4,64,256]{3,2,1,0:T(8,128)S(1)} collective-permute-done((f32[8,4,64,256]{3,2,1,0:T(8,128)}, f32[8,4,64,256]{3,2,1,0:T(8,128)S(1)}, u32[]{:S(2)}, u32[]{:S(2)}) %collective-permute-start.1) | collective-permute-done | bytes 2097184 | tf_op jit(solution)/shard_map/ppermute | solution.py:18
  193.9 4.2 collective-permute-done.2
  198.1 5.7 %multiply_add_fusion.2 = (f32[8,4,64,256]{3,2,1,0:T(8,128)}, f32[8,4,64,256]{3,2,1,0:T(8,128)}) fusion(f32[8,4,64,256]{3,2,1,0:T(8,128)} %fusion.82, f32[8,4,64,256]{3,2,1,0:T(8,128)} %collective-permute-done.2, f32[8,4]{1,0:T(8,128)S(1)} %copy.377, f32[8,4,64,256]{3,2,1,0:T(8,128)S(1)} %collective-permute-done.1, f32[8,4,64,256]{3,2,1,0:T(8,128)} %copy-done.14, ...), kind=kLoop, calls=%fused_computation.103 | loop fusion | flops 2621440 | bytes 12583168 | tf_op jit(solution)/shard_map/add | solution.py:31
  203.8 4.6 collective-permute-start.3
  208.4 1.7 collective-permute-start.4
  210.2 5.8 %fusion.171 = f32[8,4,128,128]{2,3,1,0:T(8,128)} fusion(f32[8,256,4,128]{1,3,2,0:T(8,128)S(1)} %bitcast.235, f32[8,256,4,128]{1,3,2,0:T(8,128)S(1)} %bitcast.241), kind=kOutput, calls=%fused_computation.305 | convolution fusion | flops 1610612736 | bytes 10485760 | tf_op jit(solution)/shard_map/jvp(vmap(nci,ncj->cij))/dot_general | solution.py:72
  216.1 7.5 %fusion.60 = f32[8,4,4,64,256]{4,3,1,2,0:T(8,128)S(1)} fusion(f32[8,256,4,128,1]{1,3,4,2,0:T(8,128)S(1)} %bitcast.236, f32[8,4,4,128]{3,2,1,0:T(4,128)S(1)} %copy-done.30, bf16[8,4,64,4,128]{4,3,2,1,0:T(4,128)(2,1)S(1)} %copy-done.7), kind=kOutput, calls=%fused_computation.97 | convolution fusion | flops 3223322624 | bytes 14745600 | tf_op jit(solution)/shard_map/transpose(jvp(vmap(nci,hci,chpn->hpci)))/dot_general | solution.py:149
  223.6 17.9 %fusion.104 = (f32[8,4,4,128]{3,2,1,0:T(4,128)}, f32[8,4,4,128]{3,2,1,0:T(4,128)}, f32[8,4,128,128]{2,3,1,0:T(8,128)}) fusion(f32[8,4,4,128]{3,2,1,0:T(4,128)} %copy.356, f32[4,128,128]{1,2,0:T(8,128)} %compare_select_fusion, f32[8,4,128,128]{2,3,1,0:T(8,128)} %fusion.171, bf16[8,4,4,64,128]{4,2,3,1,0:T(4,128)(2,1)} %bitcast.244, ...), kind=kOutput, calls=%fused_computation.149 | convolution fusion | flops 1642561536 | bytes 11010048 | tf_op jit(solution)/shard_map/transpose(jvp(vmap(hcij,hpcj->hpci)))/dot_general | solution.py:74
  241.5 10.1 %collective-permute-done.3 = f32[8,4,64,256]{3,2,1,0:T(8,128)} collective-permute-done((f32[8,4,64,256]{3,2,1,0:T(8,128)}, f32[8,4,64,256]{3,2,1,0:T(8,128)}, u32[]{:S(2)}, u32[]{:S(2)}) %collective-permute-start.3) | collective-permute-done | bytes 2097184 | tf_op jit(solution)/shard_map/ppermute | solution.py:18
  251.6 5.4 %collective-permute-done.4 = f32[8,4,64,256]{3,2,1,0:T(8,128)} collective-permute-done((f32[8,4,64,256]{3,2,1,0:T(8,128)}, f32[8,4,64,256]{3,2,1,0:T(8,128)}, u32[]{:S(2)}, u32[]{:S(2)}) %collective-permute-start.4) | collective-permute-done | bytes 2097184 | tf_op jit(solution)/shard_map/ppermute | solution.py:18
  257.0 6.4 %multiply_add_fusion = (f32[8,4,64,256]{3,2,1,0:T(8,128)}, f32[8,4,64,256]{3,2,1,0:T(8,128)}) fusion(f32[8,4,64,256]{3,2,1,0:T(8,128)} %fusion.82, f32[8,4,64,256]{3,2,1,0:T(8,128)} %collective-permute-done.4, f32[8,4]{1,0:T(8,128)S(1)} %copy-done.61, f32[8,4,64,256]{3,2,1,0:T(8,128)} %collective-permute-done.3, f32[8,4,64,256]{3,2,1,0:T(8,128)} %copy-done.14, ...), kind=kLoop, calls=%fused_computation.101 | loop fusion | flops 2621440 | bytes 12583168 | tf_op jit(solution)/shard_map/add | solution.py:31
  263.4 3.4 collective-permute-start.5
  268.1 5.2 %fusion.172 = f32[8,4,128,256]{3,2,1,0:T(8,128)} fusion(f32[8,4,128,128]{2,3,1,0:T(8,128)S(1)} %copy-done.18, f32[8,256,4,128]{1,3,2,0:T(8,128)S(1)} %bitcast.237), kind=kOutput, calls=%fused_computation.306 | convolution fusion | flops 1610612736 | bytes 10485760 | tf_op jit(solution)/shard_map/transpose(jvp(vmap(nci,ncj->cij)))/dot_general | solution.py:72
  273.3 17.8 %multiply_reduce_fusion = (f32[8,4,4,4]{3,2,1,0:T(4,128)}, f32[8,4,4,64,256]{4,3,2,1,0:T(8,128)}, f32[8,4,4,64,256]{4,3,2,1,0:T(8,128)}) fusion(f32[8,4,4,4]{3,2,1,0:T(4,128)S(1)} %bitcast_multiply_fusion.8, f32[8,4,4,64,256]{4,3,1,2,0:T(8,128)S(1)} %bitcast.243, f32[8,4,4,64,256]{4,3,1,2,0:T(8,128)S(1)} %fusion.60), kind=kLoop, calls=%fused_computation.2 | loop fusion | flops 46136832 | bytes 33558528 | tf_op jit(solution)/shard_map/transpose(jvp(vmap()))/reduce_sum | solution.py:131
  291.1 17.7 %collective-permute-done.5 = f32[8,4,64,256]{3,2,1,0:T(8,128)} collective-permute-done((f32[8,4,64,256]{3,2,1,0:T(8,128)}, f32[8,4,64,256]{3,2,1,0:T(8,128)}, u32[]{:S(2)}, u32[]{:S(2)}) %collective-permute-start.5) | collective-permute-done | bytes 2097184 | tf_op jit(solution)/shard_map/ppermute | solution.py:18
  308.7 5.4 %collective-permute-done.6 = f32[8,4,64,256]{3,2,1,0:T(8,128)} collective-permute-done((f32[8,4,64,256]{3,2,1,0:T(8,128)}, f32[8,4,64,256]{3,2,1,0:T(8,128)}, u32[]{:S(2)}, u32[]{:S(2)}) %collective-permute-start.6) | collective-permute-done | bytes 2097184 | tf_op jit(solution)/shard_map/ppermute | solution.py:18
  314.1 8.9 %multiply_reduce_fusion.4 = (f32[8,4,4]{1,2,0:T(4,128)}, f32[8,4,4,64,256]{4,3,1,2,0:T(8,128)S(1)}) fusion(f32[8,4,4,64,256]{4,3,1,2,0:T(8,128)} %get-tuple-element.188, f32[8,4,64,256]{3,2,1,0:T(8,128)} %collective-permute-done.6, f32[8,4,4,64,256]{4,3,2,1,0:T(8,128)} %get-tuple-element.103, f32[8,4,4]{1,2,0:T(4,128)S(1)} %copy-done.49), kind=kLoop, calls=%fused_computation.24 | loop fusion | flops 8388480 | bytes 27264000 | tf_op jit(solution)/shard_map/transpose(jvp(vmap()))/reduce_sum | solution.py:131
  323.0 12.5 %bitcast_add_fusion.2 = f32[8,256,4,128]{1,3,2,0:T(8,128)} fusion(f32[8,4,128,256]{3,2,1,0:T(8,128)} %fusion.172, f32[8,4,4,64,256]{4,3,1,2,0:T(8,128)S(1)} %get-tuple-element.134, f32[8,4,64,4,128]{4,3,2,1,0:T(4,128)S(1)} %copy-done.4, f32[8,4,4,128]{3,2,1,0:T(4,128)} %copy-done.28, f32[8,4,4,128]{3,2,1,0:T(4,128)S(1)} %copy.353), kind=kOutput, calls=%fused_computation.59 | convolution fusion | flops 3224371200 | bytes 21102592 | tf_op jit(solution)/shard_map/transpose(jvp(vmap(hpcj,hcj,ncj->hcpn)))/dot_general | solution.py:78
  335.5 5.6 %copy.406 = f32[8,256,512]{2,0,1:T(8,128)} copy(f32[8,256,512]{1,2,0:T(8,128)} %bitcast.246) | data formatting | bytes 8388608 | tf_op jit(solution)/shard_map/transpose(jvp(vmap()))/reshape | solution.py:60
  342.7 8.3 %fusion.173 = f32[8,4,128,256]{3,2,1,0:T(8,128)} fusion(f32[8,4,128,128]{2,3,1,0:T(8,128)S(1)} %copy-done.19, f32[8,256,4,128]{1,3,2,0:T(8,128)} %bitcast.239), kind=kOutput, calls=%fused_computation.307 | convolution fusion | flops 1610612736 | bytes 10485760 | tf_op jit(solution)/shard_map/transpose(jvp(vmap(nci,ncj->cij)))/dot_general | solution.py:72
  351.0 2.7 multiply_reduce_fusion.6
  353.8 11.5 %multiply_reduce_fusion.3 = (f32[8,4,4]{1,2,0:T(4,128)S(1)}, f32[8,4,4,64,256]{4,3,1,2,0:T(8,128)}) fusion(f32[8,4,4,64,256]{4,3,1,2,0:T(8,128)} %copy-done.2, f32[8,4,64,256]{3,2,1,0:T(8,128)} %collective-permute-done.5, f32[8,4,4]{1,2,0:T(4,128)S(1)} %copy.376, f32[8,4,4,64,256]{4,3,2,1,0:T(8,128)} %get-tuple-element.102), kind=kLoop, calls=%fused_computation.23 | loop fusion | flops 8388480 | bytes 27264000 | tf_op jit(solution)/shard_map/transpose(jvp(vmap()))/reduce_sum | solution.py:142
  365.5 14.0 %bitcast_add_fusion.3 = f32[8,4,128,256]{3,2,1,0:T(8,128)} fusion(f32[8,4,128,256]{3,2,1,0:T(8,128)} %fusion.173, f32[8,4,4,64,256]{4,3,1,2,0:T(8,128)} %get-tuple-element.136, f32[8,4,4,128]{3,2,1,0:T(4,128)S(1)} %copy-done.31, bf16[8,4,64,4,128]{4,3,2,1,0:T(4,128)(2,1)S(1)} %copy-done.8), kind=kOutput, calls=%fused_computation.60 | convolution fusion | flops 3224371200 | bytes 18939904 | tf_op jit(solution)/shard_map/transpose(jvp(vmap(nci,hci,chpn->hpci)))/dot_general | solution.py:149
  379.4 5.6 %copy.411 = f32[8,256,512]{2,0,1:T(8,128)} copy(f32[8,256,512]{1,2,0:T(8,128)} %bitcast.247) | data formatting | bytes 8388608 | tf_op jit(solution)/shard_map/transpose(jvp(vmap()))/reshape | solution.py:61
  385.2 15.0 %fusion.38 = (f32[8,4,4,128]{3,2,1,0:T(4,128)S(1)}, f32[8,4,4,64,128]{4,3,1,2,0:T(8,128)}) fusion(f32[8,4,64,4,128]{4,3,2,1,0:T(4,128)} %reshape.297, f32[8,4,4,128]{3,2,1,0:T(4,128)S(1)} %copy.353, f32[8,4,4,64,256]{4,3,1,2,0:T(8,128)} %copy-done.3, f32[8,256,4,128,1]{1,3,2,4,0:T(8,128)} %bitcast.240), kind=kOutput, calls=%fused_computation.68 | convolution fusion | flops 3224354816 | bytes 21102592 | tf_op jit(solution)/shard_map/transpose(jvp(vmap(hpcj,hcj,ncj->hcpn)))/dot_general | solution.py:78
  401.2 13.7 %fusion.36 = (f32[8,4,4,128]{3,2,1,0:T(4,128)S(1)}, f32[8,4,64,4,128]{4,2,3,1,0:T(8,128)}) fusion(f32[8,4,64,4,128]{4,3,2,1,0:T(4,128)} %reshape.297, f32[8,4,4,128]{3,2,1,0:T(4,128)S(1)} %copy.353, bf16[8,4,64,4,128]{4,3,2,1,0:T(4,128)(2,1)S(1)} %copy-done.8, f32[8,4]{1,0:T(8,128)S(1)} %copy-done.82, bf16[8,4,4,64,128]{4,2,3,1,0:T(4,128)(2,1)S(1)} %bitcast.245, ...), kind=kOutput, calls=%fused_computation.64 | convolution fusion | flops 1627373568 | bytes 19398784 | tf_op jit(solution)/shard_map/transpose(jvp(vmap(hcij,hpcj->hpci)))/dot_general | solution.py:74
  415.0 11.3 %fusion.16 = f32[8,4,4,64,128]{4,3,2,1,0:T(8,128)S(1)} fusion(f32[8,256,4,128,1]{1,3,4,2,0:T(8,128)} %bitcast.234, f32[8,4,4,64,256]{4,3,1,2,0:T(8,128)} %get-tuple-element.136), kind=kOutput, calls=%fused_computation.28 | convolution fusion | flops 3221225472 | bytes 16777216 | tf_op jit(solution)/shard_map/jvp(vmap(nci,hci,chpn->hpci))/dot_general | solution.py:149
  430.1 5.7 %copy.401 = f32[8,4,64,4,128]{4,3,2,1,0:T(4,128)} copy(f32[8,4,64,4,128]{4,2,3,1,0:T(8,128)S(1)} %copy-done.22) | data formatting | bytes 8388608 | tf_op jit(solution)/shard_map/transpose(jvp(vmap()))/add_any | solution.py:73
  435.8 5.6 %reshape.304 = f32[8,256,512]{2,1,0:T(8,128)} reshape(f32[8,4,64,4,128]{4,3,2,1,0:T(4,128)} %copy.401) | data formatting | bytes 8388608 | tf_op jit(solution)/shard_map/transpose(jvp(vmap()))/reshape | solution.py:59
  441.4 4.3 broadcast_multiply_fusion
  447.7 4.6 pad_add_fusion
  452.4 3.3 split.16
  455.7 1.7 copy-done.16
  457.4 9.7 %fusion.39 = bf16[8,4,64,4,128]{4,2,3,1,0:T(8,128)(2,1)S(1)} fusion(f32[8,4,4,64,128]{4,3,2,1,0:T(8,128)S(1)} %copy-done.16, f32[8,4,64,4,128]{4,3,2,1,0:T(4,128)S(1)} %copy-done.5, f32[8,4,128,128]{2,3,1,0:T(8,128)S(1)} %copy-done.23, f32[4,128,128]{1,2,0:T(8,128)S(1)} %copy-done.38, f32[8,4,4,128]{3,2,1,0:T(4,128)S(1)} %copy-done.51, ...), kind=kOutput, calls=%fused_computation.70 | convolution fusion | flops 1625292800 | bytes 13041792 | tf_op jit(solution)/shard_map/jvp(vmap(hcij,hpcj->hpci))/dot_general | solution.py:74
  467.1 2.0 copy.389
  469.1 2.2 convert_element_type.96
  471.3 2.6 pad_add_fusion.3
  473.9 1.4 copy_dynamic-update-slice_fusion.1
  475.3 1.4 copy_dynamic-update-slice_fusion
  478.8 1.3 split.17
  480.7 1.6 collective-permute-start.7
  482.2 2.9 slice_maximum_fusion
  485.1 1.5 pad_maximum_fusion.1
  486.6 1.8 copy.415
  490.2 1.5 slice.267
  (327 shorter events, 38.9 us)
Async XLA Ops:
  7.2 7.9 %copy-start.27 = (bf16[8,32,512]{2,1,0:T(8,128)(2,1)S(1)}, bf16[8,32,512]{2,1,0:T(8,128)(2,1)}, u32[]{:S(2)}) copy-start(bf16[8,32,512]{2,1,0:T(8,128)(2,1)} %param.15) | copy-start | bytes 786436
  7.2 43.5 %all-reduce.29.cloned.1.call-start = ((), (), s32[]{:S(2)}) async-start(), calls=%async_computation.2 | async-start | bytes 827392 | tf_op jit(solution)/shard_map/psum | solution.py:185
  9.9 83.2 %all-gather.5.cloned.1.call-start = ((), (), s32[]{:S(2)}) async-start(), calls=%async_computation.4 | async-start | bytes 4718592 | tf_op jit(solution)/shard_map/all_gather | solution.py:232
  13.3 9.2 %copy-start.91 = (s32[4]{0:T(128)S(1)}, s32[4]{0:T(128)}, u32[]{:S(2)}) copy-start(s32[4]{0:T(128)} %param.23) | copy-start | bytes 52
  17.5 6.4 %collective-permute-start = (bf16[8,320,3]{1,0,2:T(8,128)(2,1)S(1)}, bf16[8,320,3]{1,0,2:T(8,128)(2,1)S(1)}, u32[]{:S(2)}, u32[]{:S(2)}) collective-permute-start(bf16[8,320,3]{1,0,2:T(8,128)(2,1)S(1)} %pad_maximum_fusion.3), channel_id=1, source_target_pairs={{0,1},{1,2},{2,3},{4,5},{5,6},{6,7},{8,9},{9,10},{10,11},{12,13},{... | collective-permute-start | bytes 46088 | tf_op jit(solution)/shard_map/ppermute | solution.py:18
  22.8 47.9 %copy-start.52 = (f32[512]{0:T(512)}, f32[512]{0:T(512)S(1)}, u32[]{:S(2)}) copy-start(f32[512]{0:T(512)S(1)} %get-tuple-element.182) | copy-start | bytes 6148
  22.8 47.9 %copy-start.54 = (f32[512]{0:T(512)}, f32[512]{0:T(512)S(1)}, u32[]{:S(2)}) copy-start(f32[512]{0:T(512)S(1)} %get-tuple-element.183) | copy-start | bytes 6148
  22.8 47.9 %copy-start.56 = (f32[512]{0:T(512)}, f32[512]{0:T(512)S(1)}, u32[]{:S(2)}) copy-start(f32[512]{0:T(512)S(1)} %get-tuple-element.184) | copy-start | bytes 6148
  52.9 5.7 %copy-start.20 = (bf16[8,256,512]{2,1,0:T(8,128)(2,1)S(1)}, bf16[8,256,512]{2,1,0:T(8,128)(2,1)}, u32[]{:S(2)}) copy-start(bf16[8,256,512]{2,1,0:T(8,128)(2,1)} %param.13) | copy-start | bytes 6291460
  56.5 76.0 %all-gather.3.cloned.1.call-start = ((), (), s32[]{:S(2)}) async-start(), calls=%async_computation.3 | async-start | bytes 4718592 | tf_op jit(solution)/shard_map/all_gather | solution.py:233
  57.7 416.2 %reduce-scatter.3.cloned.1.call-start = ((), (), s32[]{:S(2)}) async-start(), calls=%async_computation.5 | async-start | bytes 4718592 | tf_op jit(solution)/shard_map/reduce_scatter | solution.py:270
  61.1 7.2 %copy-start.68 = (bf16[8,4,512]{2,1,0:T(4,128)(2,1)S(1)}, bf16[8,4,512]{2,1,0:T(4,128)(2,1)}, u32[]{:S(2)}) copy-start(bf16[8,4,512]{2,1,0:T(4,128)(2,1)} %param.16) | copy-start | bytes 98308
  63.7 74.1 %copy-start.6 = (bf16[8,4,64,4,128]{4,3,2,1,0:T(4,128)(2,1)}, bf16[8,4,64,4,128]{4,3,2,1,0:T(4,128)(2,1)S(1)}, u32[]{:S(2)}) copy-start(bf16[8,4,64,4,128]{4,3,2,1,0:T(4,128)(2,1)S(1)} %reshape.301) | copy-start | bytes 6291460
  68.4 20.7 %copy-start.78 = (f32[8,4]{0,1:T(4,128)}, f32[8,4]{0,1:T(4,128)S(1)}, u32[]{:S(2)}) copy-start(f32[8,4]{0,1:T(4,128)S(1)} %copy.352) | copy-start | bytes 388
  68.6 83.1 %copy-start.25 = (f32[8,4,4,128]{3,0,2,1:T(8,128)}, f32[8,4,4,128]{3,0,2,1:T(8,128)S(1)}, u32[]{:S(2)}) copy-start(f32[8,4,4,128]{3,0,2,1:T(8,128)S(1)} %fusion.108) | copy-start | bytes 196612
  69.9 28.5 %copy-start.28 = (f32[8,4,4,128]{3,2,1,0:T(4,128)}, f32[8,4,4,128]{3,2,1,0:T(4,128)S(1)}, u32[]{:S(2)}) copy-start(f32[8,4,4,128]{3,2,1,0:T(4,128)S(1)} %copy.372) | copy-start | bytes 196612
  70.7 12.7 %copy-start.39 = (f32[8,256]{1,0:T(8,128)}, f32[8,256]{1,0:T(8,128)S(1)}, u32[]{:S(2)}) copy-start(f32[8,256]{1,0:T(8,128)S(1)} %get-tuple-element.147) | copy-start | bytes 24580
  70.7 12.7 %copy-start.41 = (f32[8,256]{1,0:T(8,128)}, f32[8,256]{1,0:T(8,128)S(1)}, u32[]{:S(2)}) copy-start(f32[8,256]{1,0:T(8,128)S(1)} %get-tuple-element.148) | copy-start | bytes 24580
  70.7 12.7 %copy-start.43 = (f32[8,256]{1,0:T(8,128)}, f32[8,256]{1,0:T(8,128)S(1)}, u32[]{:S(2)}) copy-start(f32[8,256]{1,0:T(8,128)S(1)} %get-tuple-element.149) | copy-start | bytes 24580
  70.7 12.7 %copy-start.45 = (f32[8,256]{1,0:T(8,128)}, f32[8,256]{1,0:T(8,128)S(1)}, u32[]{:S(2)}) copy-start(f32[8,256]{1,0:T(8,128)S(1)} %get-tuple-element.150) | copy-start | bytes 24580
  83.4 5.4 %copy-start.86 = (pred[4,4]{0,1:T(4,128)(4,1)S(1)}, pred[4,4]{0,1:T(4,128)(4,1)}, u32[]{:S(2)}) copy-start(pred[4,4]{0,1:T(4,128)(4,1)} %iota_compare_fusion.2) | copy-start | bytes 52
  83.4 5.6 %copy-start.69 = (bf16[8,4,512]{2,1,0:T(4,128)(2,1)S(1)}, bf16[8,4,512]{2,1,0:T(4,128)(2,1)}, u32[]{:S(2)}) copy-start(bf16[8,4,512]{2,1,0:T(4,128)(2,1)} %param.16) | copy-start | bytes 98308
  83.4 5.9 %copy-start.37 = (f32[8,4,4,128]{3,0,2,1:T(8,128)S(1)}, f32[8,4,4,128]{3,0,2,1:T(8,128)}, u32[]{:S(2)}) copy-start(f32[8,4,4,128]{3,0,2,1:T(8,128)} %get-tuple-element.116) | copy-start | bytes 196612
  89.3 108.8 %copy-start.47 = (f32[8,4]{1,0:T(8,128)}, f32[8,4]{1,0:T(8,128)S(1)}, u32[]{:S(2)}) copy-start(f32[8,4]{1,0:T(8,128)S(1)} %copy.380) | copy-start | bytes 388
  137.8 11.9 %copy-start.83 = (pred[4,4]{1,0:T(4,128)(4,1)S(1)}, pred[4,4]{1,0:T(4,128)(4,1)}, u32[]{:S(2)}) copy-start(pred[4,4]{1,0:T(4,128)(4,1)} %get-tuple-element.194) | copy-start | bytes 52
  137.8 15.3 %copy-start.90 = (pred[4,4]{1,0:T(4,128)(4,1)S(1)}, pred[4,4]{1,0:T(4,128)(4,1)}, u32[]{:S(2)}) copy-start(pred[4,4]{1,0:T(4,128)(4,1)} %get-tuple-element.193) | copy-start | bytes 52
  144.9 49.0 %collective-permute-start.1 = (f32[8,4,64,256]{3,2,1,0:T(8,128)}, f32[8,4,64,256]{3,2,1,0:T(8,128)S(1)}, u32[]{:S(2)}, u32[]{:S(2)}) collective-permute-start(f32[8,4,64,256]{3,2,1,0:T(8,128)} %broadcast_add_fusion), channel_id=1, source_target_pairs={{0,1},{1,2},{2,3},{4,5},{5,6},{6,7},{8,9},{9,10},{10,11},{12,13},{... | collective-permute-start | bytes 6291464 | tf_op jit(solution)/shard_map/ppermute | solution.py:18
  148.4 49.7 %collective-permute-start.2 = (f32[8,4,64,256]{3,2,1,0:T(8,128)}, f32[8,4,64,256]{3,2,1,0:T(8,128)}, u32[]{:S(2)}, u32[]{:S(2)}) collective-permute-start(f32[8,4,64,256]{3,2,1,0:T(8,128)} %fusion.82), channel_id=1, source_target_pairs={{1,0},{2,1},{3,2},{5,4},{6,5},{7,6},{9,8},{10,9},{11,10},{13,12},{... | collective-permute-start | bytes 6291464 | tf_op jit(solution)/shard_map/ppermute | solution.py:18
  149.9 53.9 %copy-start.88 = (pred[4,4]{0,1:T(4,128)(4,1)}, pred[4,4]{0,1:T(4,128)(4,1)S(1)}, u32[]{:S(2)}) copy-start(pred[4,4]{0,1:T(4,128)(4,1)S(1)} %copy.368) | copy-start | bytes 52
  150.8 53.0 %copy-start.73 = (f32[4,4]{1,0:T(4,128)}, f32[4,4]{1,0:T(4,128)S(1)}, u32[]{:S(2)}) copy-start(f32[4,4]{1,0:T(4,128)S(1)} %fusion.158) | copy-start | bytes 196
  152.5 51.3 %copy-start.60 = (f32[8,4]{1,0:T(8,128)}, f32[8,4]{1,0:T(8,128)S(1)}, u32[]{:S(2)}) copy-start(f32[8,4]{1,0:T(8,128)S(1)} %copy.377) | copy-start | bytes 388
  153.8 50.0 %copy-start.34 = (f32[4,8,4,4]{1,3,2,0:T(4,128)}, f32[4,8,4,4]{1,3,2,0:T(4,128)S(1)}, u32[]{:S(2)}) copy-start(f32[4,8,4,4]{1,3,2,0:T(4,128)S(1)} %get-tuple-element.172) | copy-start | bytes 6148
  154.8 55.3 %copy-start = (f32[8,256,512]{1,2,0:T(8,128)S(1)}, f32[8,256,512]{1,2,0:T(8,128)}, u32[]{:S(2)}) copy-start(f32[8,256,512]{1,2,0:T(8,128)} %copy.361) | copy-start | bytes 12582916
  154.9 55.3 %copy-start.1 = (f32[8,256,512]{1,2,0:T(8,128)S(1)}, f32[8,256,512]{1,2,0:T(8,128)}, u32[]{:S(2)}) copy-start(f32[8,256,512]{1,2,0:T(8,128)} %copy.363) | copy-start | bytes 12582916
  203.8 47.7 %collective-permute-start.3 = (f32[8,4,64,256]{3,2,1,0:T(8,128)}, f32[8,4,64,256]{3,2,1,0:T(8,128)}, u32[]{:S(2)}, u32[]{:S(2)}) collective-permute-start(f32[8,4,64,256]{3,2,1,0:T(8,128)} %get-tuple-element.179), channel_id=1, source_target_pairs={{0,1},{1,2},{2,3},{4,5},{5,6},{6,7},{8,9},{9,10},{10,11},{12,13},{... | collective-permute-start | bytes 6291464 | tf_op jit(solution)/shard_map/ppermute | solution.py:18
  208.4 48.6 %collective-permute-start.4 = (f32[8,4,64,256]{3,2,1,0:T(8,128)}, f32[8,4,64,256]{3,2,1,0:T(8,128)}, u32[]{:S(2)}, u32[]{:S(2)}) collective-permute-start(f32[8,4,64,256]{3,2,1,0:T(8,128)} %get-tuple-element.178), channel_id=1, source_target_pairs={{1,0},{2,1},{3,2},{5,4},{6,5},{7,6},{9,8},{10,9},{11,10},{13,12},{... | collective-permute-start | bytes 6291464 | tf_op jit(solution)/shard_map/ppermute | solution.py:18
  210.2 5.8 %copy-start.7 = (bf16[8,4,64,4,128]{4,3,2,1,0:T(4,128)(2,1)S(1)}, bf16[8,4,64,4,128]{4,3,2,1,0:T(4,128)(2,1)}, u32[]{:S(2)}) copy-start(bf16[8,4,64,4,128]{4,3,2,1,0:T(4,128)(2,1)} %copy-done.6) | copy-start | bytes 6291460
  210.2 5.8 %copy-start.30 = (f32[8,4,4,128]{3,2,1,0:T(4,128)S(1)}, f32[8,4,4,128]{3,2,1,0:T(4,128)}, u32[]{:S(2)}) copy-start(f32[8,4,4,128]{3,2,1,0:T(4,128)} %copy.388) | copy-start | bytes 196612
  216.0 7.5 %copy-start.4 = (f32[8,4,64,4,128]{4,3,2,1,0:T(4,128)S(1)}, f32[8,4,64,4,128]{4,3,2,1,0:T(4,128)}, u32[]{:S(2)}) copy-start(f32[8,4,64,4,128]{4,3,2,1,0:T(4,128)} %reshape.297) | copy-start | bytes 12582916
  216.0 57.2 %slice-start = ((s8[8388608]{0:T(1024)(128)(4,1)}), s8[4194304]{0:T(1024)(128)(4,1)S(1)}, s32[]{:S(2)}) async-start(s8[8388608]{0:T(1024)(128)(4,1)} %bitcast.242), calls=%async_computation.7 | async-start | bytes 8388608
  223.6 49.7 %copy-start.2 = (f32[8,4,4,64,256]{4,3,1,2,0:T(8,128)}, f32[8,4,4,64,256]{4,3,1,2,0:T(8,128)S(1)}, u32[]{:S(2)}) copy-start(f32[8,4,4,64,256]{4,3,1,2,0:T(8,128)S(1)} %fusion.60) | copy-start | bytes 25165828
  223.6 33.4 %copy-start.48 = (f32[8,4]{1,0:T(8,128)S(1)}, f32[8,4]{1,0:T(8,128)}, u32[]{:S(2)}) copy-start(f32[8,4]{1,0:T(8,128)} %copy-done.47) | copy-start | bytes 388
  223.6 33.4 %copy-start.61 = (f32[8,4]{1,0:T(8,128)S(1)}, f32[8,4]{1,0:T(8,128)}, u32[]{:S(2)}) copy-start(f32[8,4]{1,0:T(8,128)} %copy-done.60) | copy-start | bytes 388
  223.6 49.6 %slice-start.1 = ((s8[8388608]{0:T(1024)(128)(4,1)}), s8[4194304]{0:T(1024)(128)(4,1)S(1)}, s32[]{:S(2)}) async-start(s8[8388608]{0:T(1024)(128)(4,1)} %bitcast.242), calls=%async_computation.8 | async-start | bytes 8388608
  241.5 26.6 %copy-start.18 = (f32[8,4,128,128]{2,3,1,0:T(8,128)S(1)}, f32[8,4,128,128]{2,3,1,0:T(8,128)}, u32[]{:S(2)}) copy-start(f32[8,4,128,128]{2,3,1,0:T(8,128)} %get-tuple-element.100) | copy-start | bytes 6291460
  263.4 45.4 %collective-permute-start.5 = (f32[8,4,64,256]{3,2,1,0:T(8,128)}, f32[8,4,64,256]{3,2,1,0:T(8,128)}, u32[]{:S(2)}, u32[]{:S(2)}) collective-permute-start(f32[8,4,64,256]{3,2,1,0:T(8,128)} %get-tuple-element.177), channel_id=1, source_target_pairs={{0,1},{1,2},{2,3},{4,5},{5,6},{6,7},{8,9},{9,10},{10,11},{12,13},{... | collective-permute-start | bytes 6291464 | tf_op jit(solution)/shard_map/ppermute | solution.py:18
  266.8 47.4 %collective-permute-start.6 = (f32[8,4,64,256]{3,2,1,0:T(8,128)}, f32[8,4,64,256]{3,2,1,0:T(8,128)}, u32[]{:S(2)}, u32[]{:S(2)}) collective-permute-start(f32[8,4,64,256]{3,2,1,0:T(8,128)} %get-tuple-element.176), channel_id=1, source_target_pairs={{1,0},{2,1},{3,2},{5,4},{6,5},{7,6},{9,8},{10,9},{11,10},{13,12},{... | collective-permute-start | bytes 6291464 | tf_op jit(solution)/shard_map/ppermute | solution.py:18
  273.3 40.9 %copy-start.49 = (f32[8,4,4]{1,2,0:T(4,128)S(1)}, f32[8,4,4]{1,2,0:T(4,128)}, u32[]{:S(2)}) copy-start(f32[8,4,4]{1,2,0:T(4,128)} %copy.391) | copy-start | bytes 1540
  323.0 12.5 %copy-start.3 = (f32[8,4,4,64,256]{4,3,1,2,0:T(8,128)}, f32[8,4,4,64,256]{4,3,1,2,0:T(8,128)S(1)}, u32[]{:S(2)}) copy-start(f32[8,4,4,64,256]{4,3,1,2,0:T(8,128)S(1)} %get-tuple-element.134) | copy-start | bytes 25165828
  341.1 134.2 %reduce-scatter.5.cloned.1.call-start = ((), (), s32[]{:S(2)}) async-start(), calls=%async_computation.6 | async-start | bytes 4718592 | tf_op jit(solution)/shard_map/reduce_scatter | solution.py:271
  353.8 11.6 %copy-start.8 = (bf16[8,4,64,4,128]{4,3,2,1,0:T(4,128)(2,1)S(1)}, bf16[8,4,64,4,128]{4,3,2,1,0:T(4,128)(2,1)}, u32[]{:S(2)}) copy-start(bf16[8,4,64,4,128]{4,3,2,1,0:T(4,128)(2,1)} %copy-done.6) | copy-start | bytes 6291460
  353.8 11.6 %copy-start.31 = (f32[8,4,4,128]{3,2,1,0:T(4,128)S(1)}, f32[8,4,4,128]{3,2,1,0:T(4,128)}, u32[]{:S(2)}) copy-start(f32[8,4,4,128]{3,2,1,0:T(4,128)} %copy.388) | copy-start | bytes 196612
  379.4 5.6 %copy-start.35 = (f32[4,8,4,4]{1,3,2,0:T(4,128)S(1)}, f32[4,8,4,4]{1,3,2,0:T(4,128)}, u32[]{:S(2)}) copy-start(f32[4,8,4,4]{1,3,2,0:T(4,128)} %copy-done.34) | copy-start | bytes 6148
  379.4 5.6 %copy-start.87 = (pred[4,4]{0,1:T(4,128)(4,1)S(1)}, pred[4,4]{0,1:T(4,128)(4,1)}, u32[]{:S(2)}) copy-start(pred[4,4]{0,1:T(4,128)(4,1)} %iota_compare_fusion.2) | copy-start | bytes 52
  385.2 15.1 %copy-start.26 = (f32[8,4,4,128]{3,0,2,1:T(8,128)S(1)}, f32[8,4,4,128]{3,0,2,1:T(8,128)}, u32[]{:S(2)}) copy-start(f32[8,4,4,128]{3,0,2,1:T(8,128)} %copy-done.25) | copy-start | bytes 196612
  385.2 15.1 %copy-start.72 = (f32[4,128]{1,0:T(4,128)S(1)}, f32[4,128]{1,0:T(4,128)}, u32[]{:S(2)}) copy-start(f32[4,128]{1,0:T(4,128)} %copy-done.71) | copy-start | bytes 6148
  435.8 5.6 %copy-start.46 = (f32[8,256]{1,0:T(8,128)S(1)}, f32[8,256]{1,0:T(8,128)}, u32[]{:S(2)}) copy-start(f32[8,256]{1,0:T(8,128)} %copy-done.45) | copy-start | bytes 24580
  447.0 5.4 %copy-start.11 = (f32[8,256,512]{2,1,0:T(8,128)}, f32[8,256,512]{2,1,0:T(8,128)S(1)}, u32[]{:S(2)}) copy-start(f32[8,256,512]{2,1,0:T(8,128)S(1)} %get-tuple-element.128) | copy-start | bytes 12582916
  447.0 5.4 %copy-start.12 = (f32[8,256,512]{2,1,0:T(8,128)}, f32[8,256,512]{2,1,0:T(8,128)S(1)}, u32[]{:S(2)}) copy-start(f32[8,256,512]{2,1,0:T(8,128)S(1)} %get-tuple-element.129) | copy-start | bytes 12582916
  447.0 5.4 %copy-start.13 = (f32[8,256,512]{2,1,0:T(8,128)}, f32[8,256,512]{2,1,0:T(8,128)S(1)}, u32[]{:S(2)}) copy-start(f32[8,256,512]{2,1,0:T(8,128)S(1)} %get-tuple-element.130) | copy-start | bytes 12582916
  447.7 8.0 %copy-start.23 = (f32[8,4,128,128]{2,3,1,0:T(8,128)S(1)}, f32[8,4,128,128]{2,3,1,0:T(8,128)}, u32[]{:S(2)}) copy-start(f32[8,4,128,128]{2,3,1,0:T(8,128)} %fusion.171) | copy-start | bytes 6291460
  471.3 5.4 %copy-start.21 = (f32[8,64,512]{2,1,0:T(8,128)S(1)}, f32[8,64,512]{2,1,0:T(8,128)}, u32[]{:S(2)}) copy-start(f32[8,64,512]{2,1,0:T(8,128)} %get-tuple-element.125) | copy-start | bytes 3145732
  471.3 5.4 %copy-start.59 = (f32[8,64]{1,0:T(8,128)S(1)}, f32[8,64]{1,0:T(8,128)}, u32[]{:S(2)}) copy-start(f32[8,64]{1,0:T(8,128)} %copy-done.58) | copy-start | bytes 6148
  480.7 7.7 %collective-permute-start.7 = (f32[8,320,3]{1,0,2:T(8,128)S(1)}, f32[8,320,3]{1,0,2:T(8,128)S(1)}, u32[]{:S(2)}, u32[]{:S(2)}) collective-permute-start(f32[8,320,3]{1,0,2:T(8,128)S(1)} %copy.414), channel_id=1, source_target_pairs={{1,0},{2,1},{3,2},{5,4},{6,5},{7,6},{9,8},{10,9},{11,10},{13,12},{... | collective-permute-start | bytes 92168 | tf_op jit(solution)/shard_map/ppermute | solution.py:18
  (45 other events, 122.1 us)
Sparse Core Ops, SparseCore 0:
  10.9 39.6 all-reduce.28
  56.6 36.4 all-gather.4
  95.7 36.7 all-gather.2
  341.2 48.5 reduce-scatter.2
  400.6 48.6 reduce-scatter.4

commit v8 on v5

--- a/solution.py
+++ b/solution.py
@@ -18,11 +18,11 @@
     return lax.ppermute(value, axis, [(source, source + steps) for source in range(first, last)])
 
 
-def carried_both(totals, ahead, behind, axis):
+def carried_both(totals, ahead, behind, axis, beside):
     factor = totals[..., None, None]
     pair = lax.optimization_barrier((ahead, behind))
-    received = lax.optimization_barrier(
-        (passed_along(pair[0], axis, 1), passed_along(pair[1], axis, -1))
+    received, beside = lax.optimization_barrier(
+        ((passed_along(pair[0], axis, 1), passed_along(pair[1], axis, -1)), beside)
     )
     for _ in range(lax.axis_size(axis) - 2):
         received = lax.optimization_barrier(
@@ -31,7 +31,7 @@
                 passed_along(factor * received[1] + behind, axis, -1),
             )
         )
-    return received
+    return received + (beside,)
 
 
 def segment_ids(positions, doc_lengths):
@@ -242,8 +242,11 @@
             segment_extended,
         )
 
-    terms, pull_terms = jax.vjp(local_terms, x_conv, b_conv, c_conv, dt_raw.astype(jnp.float32))
-    y_intra, c_three, entry, carry, states = terms
+    operands = (x_conv, b_conv, c_conv, dt_raw.astype(jnp.float32))
+    y_intra, pull_intra = jax.vjp(lambda *a: local_terms(*a)[0], *operands)
+    cross, pull_cross = jax.vjp(lambda *a: local_terms(*a)[1:], *operands)
+    terms = (y_intra,) + tuple(cross)
+    c_three, entry, carry, states = cross
     before, total = reach(carry)
     state_zero = jnp.zeros((groups_here, n_heads, HEAD_DIM, STATE), jnp.float32)
     _, summary = jax.vmap(span_fold)(carry, states, state_zero)
@@ -252,7 +255,8 @@
     local_grad = jnp.einsum(
         "ghpci,ghci,gnci->ghpn", cot_five, entry * before[..., None], c_three, precision=precise
     )
-    state_in, grad_out = carried_both(total, summary, local_grad, "head")
+    d_intra = pull_intra(cot_float.reshape(y_intra.shape))
+    state_in, grad_out, d_intra = carried_both(total, summary, local_grad, "head", d_intra)
 
     def finish(pieces, state_start):
         return jax.vmap(assemble)(
@@ -262,7 +266,9 @@
     (y_scan, state_out), pull_out = jax.vjp(finish, terms, state_in)
     y_out = y_scan.astype(jnp.bfloat16)
     d_terms, _ = pull_out((cot_float, grad_out))
-    d_x_conv, d_b_conv, d_c_conv, d_dt = pull_terms(d_terms)
+    d_x_conv, d_b_conv, d_c_conv, d_dt = (
+        a + b for a, b in zip(pull_cross(tuple(d_terms[1:])), d_intra)
+    )
     d_bc_conv = jnp.concatenate(
         [
             lax.psum_scatter(d_b_conv, "seq", scatter_dimension=1, tiled=True),

time: 488 us -> 515 us (1.055)
  local copies, waits for them, and re-layouts: 83.2 us -> 106 us
  other arithmetic: 102 us -> 119 us
  matrix products: 142 us -> 128 us
    all_gather x1, waiting for transfers between devices: 2.09 us -> 33.9 us  [shards(): b_conv = lax.all_gather(bc_conv[:, :b_width], 'seq', axis=1, tiled=True)]
    ppermute x8, waiting for transfers between devices: 81.8 us -> 64.9 us  [passed_along(): lax.ppermute(value, axis, [(source, source + steps) for source in range(f...]
    all_gather x1, waiting for transfers between devices: 17.3 us -> 2.26 us  [shards(): c_conv = lax.all_gather(bc_conv[:, b_width:], 'seq', axis=1, tiled=True)]
    add x0 -> x2, other arithmetic: none -> 12.9 us  [shards(): a + b]
    optimization_barrier x0 -> x2, local copies, waits for them, and re-layouts: none -> 11.4 us  [carried_both(): lax.optimization_barrier(((passed_along(pair[0], axis, 1), passed_along(p...]
    unnamed x3 -> x4, other arithmetic: 1.1 us -> 8.22 us
    dot_general x3, matrix products: 41.3 us -> 34.7 us  [span_terms(): jnp.einsum('hcij,hpcj->hpci', decay * scores[None], weighted, precision=p...]
    dot_general x3, matrix products: 41.1 us -> 35.2 us  [span_terms(): jnp.einsum('hpcj,hcj,ncj->hcpn', weighted, keep_end, b_three, precision=p...]
  transfers between devices with their start and end apart: 12 -> 12, of which waited for: 8 -> 8; matrix products, arithmetic and copies ran while one was open for 51% -> 48% of each run, Pallas kernels for 0% -> 0%
where the time goes in v8:
time: 515 us; the launch traced here: 507 us
  matrix products  128 us (25%)
  other arithmetic  119 us (23%)
  local copies, waits for them, and re-layouts  106 us (21%)
  waiting for transfers between devices  101 us (20%)
  starting transfers between devices  22 us (4%)
  between operations  15.5 us (3%)
  blocking collectives  15.4 us (3%)
    ppermute x8, waiting for transfers between devices, passed_along(): lax.ppermute(value, axis, [(source, source + steps) for source in range(f...  64.9 us
    dot_general x3, matrix products, span_terms(): jnp.einsum('hpcj,hcj,ncj->hcpn', weighted, keep_end, b_three, precision=p...  35.2 us
    dot_general x3, matrix products, span_terms(): jnp.einsum('hcij,hpcj->hpci', decay * scores[None], weighted, precision=p...  34.7 us
    all_gather x1, waiting for transfers between devices, shards(): b_conv = lax.all_gather(bc_conv[:, :b_width], 'seq', axis=1, tiled=True)  33.9 us
    dot_general x3, matrix products, assemble(): jnp.einsum('nci,hci,chpn->hpci', c_three, entry, starts, precision=precise)  29.4 us
    reduce_sum x2, other arithmetic, weighted_sum(): return jnp.sum(weight[..., None, None] * stacked, axis=-3)  25.9 us
    dot_general x3, matrix products, span_terms(): scores = jnp.einsum('nci,ncj->cij', c_three, b_three, precision=precise)  22 us
    ppermute x8, starting transfers between devices, passed_along(): lax.ppermute(value, axis, [(source, source + steps) for source in range(f...  21.9 us
  transfers between devices with their start and end apart: 12, of which 8 were waited for; matrix products, arithmetic and copies ran while one was open for 48% of the time, Pallas kernels for 0%

profile of v8, /device:TPU:0, one launch (start us, length us, event | category | flops | bytes accessed | tf_op | source)
XLA Modules:
  0.0 507.5 jit_solution(13823467967460826510)
XLA Ops:
  7.2 1.7 copy.363
  8.9 2.6 copy.362
  11.6 3.4 copy.361
  16.4 4.9 collective-permute-start
  21.8 15.4 %all-gather = f32[4,2,12896]{2,1,0:T(2,128)S(1)} all-gather(f32[1,2,12896]{2,1,0:T(2,128)S(1)} %bitcast.272), channel_id=1, replica_groups=mesh['seq'=8,'head'=4] {'head'}, dimensions={0}, use_global_device_ids=true | all-gather | bytes 515840 | tf_op jit(solution)/shard_map/all_gather | solution.py:183
  39.0 3.2 fusion.94
  45.3 2.6 convert_element_type.84
  52.2 2.6 reshape.326
  59.2 12.0 %fusion.50 = (f32[8,256,512]{2,1,0:T(8,128)}, f32[8,256,512]{2,1,0:T(8,128)}) fusion(f32[8,256,512]{2,1,0:T(8,128)} %convert_element_type.84, f32[8,256]{1,0:T(8,128)S(1)} %get-tuple-element.165, f32[512]{0:T(512)S(1)} %get-tuple-element.198, f32[8,256,3]{2,1,0:T(8,128)S(1)} %copy.364, f32[8,256]{1,0:T(8,128)S(1)} %get-tuple-element.163, ...), kind=kLoop, calls=%fused_computation.88 | loop fusion | flops 18874368 | bytes 12654592 | tf_op jit(solution)/shard_map/jvp(vmap(jit(silu)))/mul | solution.py:53
  71.2 5.3 %reshape.322 = f32[8,4,64,4,128]{4,3,2,1,0:T(4,128)} reshape(f32[8,256,512]{2,1,0:T(8,128)} %get-tuple-element.134) | data formatting | bytes 8388608 | tf_op jit(solution)/shard_map/jvp(vmap())/reshape | solution.py:59
  76.5 2.3 all-gather.4.cloned.1.call-done
  78.7 5.3 %copy.375 = f32[8,256,512]{1,2,0:T(8,128)} copy(f32[8,256,512]{2,0,1:T(8,128)} %all-gather.4.cloned.1.call-done) | data formatting | bytes 8388608 | tf_op jit(solution)/shard_map/all_gather | solution.py:231
  84.0 33.9 %all-gather.6.cloned.1.call-done = f32[8,256,512]{2,0,1:T(8,128)} async-done(((f32[8,32,512]{2,0,1:T(8,128)}), f32[8,256,512]{2,0,1:T(8,128)}) %all-gather.6.cloned.1.call-update) | async-done | bytes 4194320 | tf_op jit(solution)/shard_map/all_gather | solution.py:230
  117.9 5.4 %copy.377 = f32[8,256,512]{1,2,0:T(8,128)} copy(f32[8,256,512]{2,0,1:T(8,128)} %all-gather.6.cloned.1.call-done) | data formatting | bytes 8388608 | tf_op jit(solution)/shard_map/all_gather | solution.py:230
  123.4 7.9 %fusion.166 = f32[8,4,128,128]{2,3,1,0:T(8,128)S(1)} fusion(f32[8,256,4,128]{1,3,2,0:T(8,128)} %bitcast.251, f32[8,256,4,128]{1,3,2,0:T(8,128)} %bitcast.256), kind=kOutput, calls=%fused_computation.306 | convolution fusion | flops 1610612736 | bytes 10485760 | tf_op jit(solution)/shard_map/jvp(vmap(nci,ncj->cij))/dot_general | solution.py:72
  131.3 5.6 %fusion.72 = f32[8,4,64,256]{3,2,1,0:T(8,128)} fusion(f32[8,256,4,128,1]{1,3,2,4,0:T(8,128)S(1)} %bitcast.253, f32[8,4,4,128]{3,2,1,0:T(4,128)S(1)} %copy.396, bf16[8,4,64,4,128]{4,3,2,1,0:T(4,128)(2,1)S(1)} %reshape.326), kind=kOutput, calls=%fused_computation.113 | convolution fusion | flops 3223322624 | bytes 8454144 | tf_op jit(solution)/shard_map/ghpci,ghci,gnci->ghpn/dot_general | solution.py:255
  136.9 9.6 %fusion.39 = (f32[8,4,4,128]{3,2,1,0:T(4,128)S(1)}, f32[8,4,4,128,64]{3,4,2,1,0:T(8,128)S(1)}, f32[8,4,64,4,128]{4,2,3,1,0:T(8,128)S(1)}) fusion(f32[8,4,64,4,128]{4,3,2,1,0:T(4,128)S(1)} %copy-done.10, f32[8,4,4,128]{3,2,1,0:T(4,128)S(1)} %copy.386, f32[8,4,4,128]{3,2,1,0:T(4,128)S(1)} %copy.367, bf16[8,4,64,4,128]{4,3,2,1,0:T(4,128)(2,1)S(1)} %reshape.326, ...), kind=kOutput, calls=%fused_computation.71 | convolution fusion | flops 1627373568 | bytes 19398784 | tf_op jit(solution)/shard_map/transpose(jvp(vmap(hcij,hpcj->hpci)))/dot_general | solution.py:74
  146.5 9.7 %multiply_reduce_fusion.5 = (f32[8,4,64,256]{3,2,1,0:T(8,128)S(1)}, f32[8,4,4,64,256]{4,3,1,2,0:T(8,128)}) fusion(f32[8,4,4]{1,2,0:T(4,128)S(1)} %copy.392, f32[8,256,4,128,1]{1,3,4,2,0:T(8,128)S(1)} %bitcast.258, f32[8,4,4,128,64]{3,4,2,1,0:T(8,128)S(1)} %get-tuple-element.144), kind=kOutput, calls=%fused_computation.25 | convolution fusion | flops 3224895488 | bytes 18874880 | tf_op jit(solution)/shard_map/jvp(vmap(hpcj,hcj,ncj->hcpn))/dot_general | solution.py:78
  156.2 1.7 broadcast_add_fusion
  157.9 4.7 collective-permute-start.1
  163.9 14.9 %fusion.96 = (f32[8,4,4,128]{3,2,1,0:T(4,128)S(1)}, f32[8,4,4,128]{3,2,1,0:T(4,128)S(1)}, f32[8,4,128,128]{2,3,1,0:T(8,128)}) fusion(f32[8,4,4,128]{3,2,1,0:T(4,128)S(1)} %copy-done.37, f32[4,128,128]{1,2,0:T(8,128)S(1)} %copy-done.33, f32[8,4,128,128]{2,3,1,0:T(8,128)S(1)} %fusion.166, bf16[8,4,4,64,128]{4,2,3,1,0:T(4,128)(2,1)S(1)} %bitcast.263, ...), kind=kOutput, calls=%fused_computation.152 | convolution fusion | flops 1642561536 | bytes 11010048 | tf_op jit(solution)/shard_map/transpose(jvp(vmap(hcij,hpcj->hpci)))/dot_general | solution.py:74
  178.8 5.7 %copy.402 = f32[8,4,64,4,128]{4,3,2,1,0:T(4,128)} copy(f32[8,4,64,4,128]{4,2,3,1,0:T(8,128)S(1)} %get-tuple-element.145) | data formatting | bytes 8388608 | tf_op jit(solution)/shard_map/transpose(jvp(vmap()))/add_any | solution.py:73
  184.5 5.5 %reshape.329 = f32[8,256,512]{2,1,0:T(8,128)} reshape(f32[8,4,64,4,128]{4,3,2,1,0:T(4,128)} %copy.402) | data formatting | bytes 8388608 | tf_op jit(solution)/shard_map/transpose(jvp(vmap()))/reshape | solution.py:59
  190.9 8.7 %fusion.167 = f32[8,4,128,256]{3,2,1,0:T(8,128)} fusion(f32[8,4,128,128]{2,3,1,0:T(8,128)} %get-tuple-element.112, f32[8,256,4,128]{1,3,2,0:T(8,128)} %bitcast.252), kind=kOutput, calls=%fused_computation.307 | convolution fusion | flops 1610612736 | bytes 10485760 | tf_op jit(solution)/shard_map/transpose(jvp(vmap(nci,ncj->cij)))/dot_general | solution.py:72
  199.6 5.4 %fusion.168 = f32[8,4,128,256]{3,2,1,0:T(8,128)} fusion(f32[8,4,128,128]{2,3,1,0:T(8,128)S(1)} %copy-done.22, f32[8,256,4,128]{1,3,2,0:T(8,128)S(1)} %bitcast.259), kind=kOutput, calls=%fused_computation.308 | convolution fusion | flops 1610612736 | bytes 10485760 | tf_op jit(solution)/shard_map/transpose(jvp(vmap(nci,ncj->cij)))/dot_general | solution.py:72
  205.0 1.9 collective-permute-done.1
  206.9 5.4 %collective-permute-done.2 = f32[8,4,64,256]{3,2,1,0:T(8,128)} collective-permute-done((f32[8,4,64,256]{3,2,1,0:T(8,128)}, f32[8,4,64,256]{3,2,1,0:T(8,128)}, u32[]{:S(2)}, u32[]{:S(2)}) %collective-permute-start.2) | collective-permute-done | bytes 2097184 | tf_op jit(solution)/shard_map/ppermute | solution.py:18
  212.3 5.8 %multiply_add_fusion.2 = (f32[8,4,64,256]{3,2,1,0:T(8,128)}, f32[8,4,64,256]{3,2,1,0:T(8,128)}) fusion(f32[8,4,64,256]{3,2,1,0:T(8,128)} %fusion.72, f32[8,4,64,256]{3,2,1,0:T(8,128)} %collective-permute-done.2, f32[8,4]{1,0:T(8,128)S(1)} %copy.391, f32[8,4,64,256]{3,2,1,0:T(8,128)} %collective-permute-done.1, f32[8,4,64,256]{3,2,1,0:T(8,128)S(1)} %copy-done.17, ...), kind=kLoop, calls=%fused_computation.103 | loop fusion | flops 2621440 | bytes 12583168 | tf_op jit(solution)/shard_map/add | solution.py:31
  218.2 3.4 collective-permute-start.3
  223.9 40.8 %collective-permute-done.3 = f32[8,4,64,256]{3,2,1,0:T(8,128)} collective-permute-done((f32[8,4,64,256]{3,2,1,0:T(8,128)}, f32[8,4,64,256]{3,2,1,0:T(8,128)}, u32[]{:S(2)}, u32[]{:S(2)}) %collective-permute-start.3) | collective-permute-done | bytes 2097184 | tf_op jit(solution)/shard_map/ppermute | solution.py:18
  264.7 5.4 %collective-permute-done.4 = f32[8,4,64,256]{3,2,1,0:T(8,128)} collective-permute-done((f32[8,4,64,256]{3,2,1,0:T(8,128)}, f32[8,4,64,256]{3,2,1,0:T(8,128)}, u32[]{:S(2)}, u32[]{:S(2)}) %collective-permute-start.4) | collective-permute-done | bytes 2097184 | tf_op jit(solution)/shard_map/ppermute | solution.py:18
  270.2 6.5 %multiply_add_fusion = (f32[8,4,64,256]{3,2,1,0:T(8,128)}, f32[8,4,64,256]{3,2,1,0:T(8,128)}) fusion(f32[8,4,64,256]{3,2,1,0:T(8,128)} %fusion.72, f32[8,4,64,256]{3,2,1,0:T(8,128)} %collective-permute-done.4, f32[8,4]{1,0:T(8,128)S(1)} %copy.391, f32[8,4,64,256]{3,2,1,0:T(8,128)} %collective-permute-done.3, f32[8,4,64,256]{3,2,1,0:T(8,128)} %copy-done.16, ...), kind=kLoop, calls=%fused_computation.101 | loop fusion | flops 2621440 | bytes 12583168 | tf_op jit(solution)/shard_map/add | solution.py:31
  276.6 3.4 collective-permute-start.5
  281.4 8.0 %fusion.60 = f32[8,4,4,64,256]{4,3,1,2,0:T(8,128)S(1)} fusion(f32[8,256,4,128,1]{1,3,4,2,0:T(8,128)S(1)} %bitcast.254, f32[8,4,4,128]{3,2,1,0:T(4,128)S(1)} %copy.413, bf16[8,4,64,4,128]{4,3,2,1,0:T(4,128)(2,1)S(1)} %reshape.326), kind=kOutput, calls=%fused_computation.97 | convolution fusion | flops 3223322624 | bytes 14745600 | tf_op jit(solution)/shard_map/transpose(jvp(vmap(nci,hci,chpn->hpci)))/dot_general | solution.py:149
  289.4 3.3 copy-done.6
  292.7 17.9 %multiply_reduce_fusion = (f32[8,4,4,4]{3,2,1,0:T(4,128)S(1)}, f32[8,4,4,64,256]{4,3,2,1,0:T(8,128)}, f32[8,4,4,64,256]{4,3,2,1,0:T(8,128)}) fusion(f32[8,4,4,4]{3,2,1,0:T(4,128)S(1)} %bitcast_multiply_fusion.10, f32[8,4,4,64,256]{4,3,1,2,0:T(8,128)S(1)} %bitcast.261, f32[8,4,4,64,256]{4,3,1,2,0:T(8,128)S(1)} %fusion.60), kind=kLoop, calls=%fused_computation.2 | loop fusion | flops 46136832 | bytes 33558528 | tf_op jit(solution)/shard_map/transpose(jvp(vmap()))/reduce_sum | solution.py:131
  310.6 5.5 %copy.427 = f32[8,256,512]{2,0,1:T(8,128)} copy(f32[8,256,512]{1,2,0:T(8,128)} %bitcast.266) | data formatting | bytes 8388608 | tf_op jit(solution)/shard_map/optimization_barrier | solution.py:24
  316.2 5.8 %collective-permute-done.5 = f32[8,4,64,256]{3,2,1,0:T(8,128)} collective-permute-done((f32[8,4,64,256]{3,2,1,0:T(8,128)}, f32[8,4,64,256]{3,2,1,0:T(8,128)}, u32[]{:S(2)}, u32[]{:S(2)}) %collective-permute-start.5) | collective-permute-done | bytes 2097184 | tf_op jit(solution)/shard_map/ppermute | solution.py:18
  322.0 5.4 %collective-permute-done.6 = f32[8,4,64,256]{3,2,1,0:T(8,128)} collective-permute-done((f32[8,4,64,256]{3,2,1,0:T(8,128)}, f32[8,4,64,256]{3,2,1,0:T(8,128)}, u32[]{:S(2)}, u32[]{:S(2)}) %collective-permute-start.6) | collective-permute-done | bytes 2097184 | tf_op jit(solution)/shard_map/ppermute | solution.py:18
  327.4 8.0 %multiply_reduce_fusion.4 = (f32[8,4,4]{1,2,0:T(4,128)S(1)}, f32[8,4,4,64,256]{4,3,1,2,0:T(8,128)S(1)}) fusion(f32[8,4,4,64,256]{4,3,1,2,0:T(8,128)} %get-tuple-element.203, f32[8,4,64,256]{3,2,1,0:T(8,128)} %collective-permute-done.6, f32[8,4,4,64,256]{4,3,2,1,0:T(8,128)} %get-tuple-element.115, f32[8,4,4]{1,2,0:T(4,128)S(1)} %copy.415), kind=kLoop, calls=%fused_computation.24 | loop fusion | flops 8388480 | bytes 27264000 | tf_op jit(solution)/shard_map/transpose(jvp(vmap()))/reduce_sum | solution.py:131
  335.7 9.4 %fusion.12 = f32[8,4,256,128,1]{2,3,4,1,0:T(8,128)} fusion(f32[8,4,4,64,256]{4,3,1,2,0:T(8,128)S(1)} %get-tuple-element.149, f32[8,4,4,128,64]{3,4,2,1,0:T(8,128)S(1)} %copy-done.20), kind=kOutput, calls=%fused_computation.21 | convolution fusion | flops 3221225472 | bytes 16777216 | tf_op jit(solution)/shard_map/transpose(jvp(vmap(hpcj,hcj,ncj->hcpn)))/dot_general | solution.py:78
  345.1 5.6 %copy.426 = f32[8,256,512]{2,0,1:T(8,128)} copy(f32[8,256,512]{1,2,0:T(8,128)} %bitcast.267) | data formatting | bytes 8388608 | tf_op jit(solution)/shard_map/transpose(jvp(vmap()))/reshape | solution.py:60
  350.7 6.4 %add.240 = f32[8,256,512]{2,0,1:T(8,128)} add(f32[8,256,512]{2,0,1:T(8,128)} %copy.426, f32[8,256,512]{2,0,1:T(8,128)} %copy.427) | non-fusion elementwise | flops 1048576 | bytes 12582912 | tf_op jit(solution)/shard_map/add | solution.py:270
  357.9 5.9 %copy.431 = f32[8,256,512]{2,0,1:T(8,128)} copy(f32[8,256,512]{1,2,0:T(8,128)} %bitcast.265) | data formatting | bytes 8388608 | tf_op jit(solution)/shard_map/optimization_barrier | solution.py:24
  363.8 9.0 %multiply_reduce_fusion.3 = (f32[8,4,4]{1,2,0:T(4,128)S(1)}, f32[8,4,4,64,256]{4,3,1,2,0:T(8,128)S(1)}) fusion(f32[8,4,4,64,256]{4,3,1,2,0:T(8,128)} %copy-done.6, f32[8,4,64,256]{3,2,1,0:T(8,128)} %collective-permute-done.5, f32[8,4,4]{1,2,0:T(4,128)S(1)} %copy.390, f32[8,4,4,64,256]{4,3,2,1,0:T(8,128)} %get-tuple-element.114), kind=kLoop, calls=%fused_computation.23 | loop fusion | flops 8388480 | bytes 27264000 | tf_op jit(solution)/shard_map/transpose(jvp(vmap()))/reduce_sum | solution.py:142
  373.1 8.5 %fusion.16 = f32[8,4,4,64,128]{4,3,2,1,0:T(8,128)S(1)} fusion(f32[8,256,4,128,1]{1,3,4,2,0:T(8,128)S(1)} %bitcast.255, f32[8,4,4,64,256]{4,3,1,2,0:T(8,128)S(1)} %get-tuple-element.151), kind=kOutput, calls=%fused_computation.28 | convolution fusion | flops 3221225472 | bytes 16777216 | tf_op jit(solution)/shard_map/jvp(vmap(nci,hci,chpn->hpci))/dot_general | solution.py:149
  381.6 10.2 %fusion.37 = bf16[8,4,64,4,128]{4,2,3,1,0:T(8,128)(2,1)S(1)} fusion(f32[8,4,4,64,128]{4,3,2,1,0:T(8,128)S(1)} %fusion.16, f32[8,4,64,4,128]{4,3,2,1,0:T(4,128)S(1)} %copy-done.11, f32[8,4,128,128]{2,3,1,0:T(8,128)S(1)} %copy-done.26, f32[4,128,128]{1,2,0:T(8,128)S(1)} %copy-done.33, f32[8,4,4,128]{3,2,1,0:T(4,128)S(1)} %copy-done.38, ...), kind=kOutput, calls=%fused_computation.66 | convolution fusion | flops 1625292800 | bytes 13041792 | tf_op jit(solution)/shard_map/jvp(vmap(hcij,hpcj->hpci))/dot_general | solution.py:74
  391.8 3.3 copy.414
  395.1 4.2 convert_element_type.97
  399.3 12.8 %fusion.14 = f32[8,4,128,256,1]{3,2,4,1,0:T(8,128)} fusion(f32[8,4,4,64,256]{4,3,1,2,0:T(8,128)} %copy-done.7, f32[8,4,4,128]{3,2,1,0:T(4,128)S(1)} %copy.413, bf16[8,4,64,4,128]{4,3,2,1,0:T(4,128)(2,1)S(1)} %reshape.326), kind=kOutput, calls=%fused_computation.26 | convolution fusion | flops 3223322624 | bytes 14745600 | tf_op jit(solution)/shard_map/transpose(jvp(vmap(nci,hci,chpn->hpci)))/dot_general | solution.py:149
  412.2 5.5 %copy.430 = f32[8,256,512]{2,0,1:T(8,128)} copy(f32[8,256,512]{1,2,0:T(8,128)} %bitcast.264) | data formatting | bytes 8388608 | tf_op jit(solution)/shard_map/transpose(jvp(vmap()))/reshape | solution.py:61
  417.7 6.5 %add.241 = f32[8,256,512]{2,0,1:T(8,128)} add(f32[8,256,512]{2,0,1:T(8,128)} %copy.430, f32[8,256,512]{2,0,1:T(8,128)} %copy.431) | non-fusion elementwise | flops 1048576 | bytes 12582912 | tf_op jit(solution)/shard_map/add | solution.py:270
  424.2 16.1 %fusion.35 = (f32[8,4,4,128]{3,2,1,0:T(4,128)S(1)}, f32[8,4,64,4,128]{4,2,3,1,0:T(8,128)S(1)}, f32[8,4,4,64,128]{4,3,1,2,0:T(8,128)}) fusion(f32[8,4,64,4,128]{4,3,2,1,0:T(4,128)} %reshape.322, f32[8,4,4,128]{3,2,1,0:T(4,128)S(1)} %copy.386, f32[8,4,4,128]{3,2,1,0:T(4,128)S(1)} %copy.367, f32[8,4,4,64,256]{4,3,1,2,0:T(8,128)} %copy-done.5, ...), kind=kOutput, calls=%fused_computation.61 | convolution fusion | flops 3225403392 | bytes 25362432 | tf_op jit(solution)/shard_map/transpose(jvp(vmap(hpcj,hcj,ncj->hcpn)))/dot_general | solution.py:78
  440.3 5.6 %copy.423 = f32[8,4,64,4,128]{4,3,2,1,0:T(4,128)} copy(f32[8,4,64,4,128]{4,2,3,1,0:T(8,128)S(1)} %get-tuple-element.139) | data formatting | bytes 8388608 | tf_op jit(solution)/shard_map/transpose(jvp(vmap()))/mul | solution.py:73
  445.9 5.5 %reshape.334 = f32[8,256,512]{2,1,0:T(8,128)} reshape(f32[8,4,64,4,128]{4,3,2,1,0:T(4,128)} %copy.423) | data formatting | bytes 8388608 | tf_op jit(solution)/shard_map/transpose(jvp(vmap()))/reshape | solution.py:59
  451.4 5.6 %broadcast_multiply_fusion = (f32[8,256,512]{2,1,0:T(8,128)S(1)}, f32[8,256,512]{2,1,0:T(8,128)S(1)}) fusion(f32[8,256]{1,0:T(8,128)S(1)} %get-tuple-element.165, f32[8,256,512]{2,1,0:T(8,128)} %get-tuple-element.135, f32[8,256,512]{2,1,0:T(8,128)} %reshape.334, f32[8,256,512]{2,1,0:T(8,128)} %reshape.329), kind=kLoop, calls=%fused_computation.108 | loop fusion | flops 11534336 | bytes 20979712 | tf_op jit(solution)/shard_map/transpose(jvp(vmap()))/mul | solution.py:51
  459.1 4.9 pad_add_fusion
  464.0 3.2 split.16
  467.4 2.5 multiply_reduce_fusion.6
  470.3 4.9 fusion.36
  475.8 3.3 fusion.30
  480.1 2.6 pad_add_fusion.3
  491.0 2.9 slice_maximum_fusion
  495.4 1.8 copy.435
  (289 shorter events, 39.3 us)
Async XLA Ops:
  7.2 71.5 %all-gather.4.cloned.1.call-start = ((), (), s32[]{:S(2)}) async-start(), calls=%async_computation.2 | async-start | bytes 4718592 | tf_op jit(solution)/shard_map/all_gather | solution.py:231
  11.6 9.8 %copy-start.30 = (bf16[8,32,512]{2,1,0:T(8,128)(2,1)S(1)}, bf16[8,32,512]{2,1,0:T(8,128)(2,1)}, u32[]{:S(2)}) copy-start(bf16[8,32,512]{2,1,0:T(8,128)(2,1)} %param.16) | copy-start | bytes 786436
  11.6 9.9 %copy-start.36 = (f32[2,4,2560]{2,1,0:T(4,128)S(1)}, f32[2,4,2560]{2,1,0:T(4,128)}, u32[]{:S(2)}) copy-start(f32[2,4,2560]{2,1,0:T(4,128)} %param.19) | copy-start | bytes 245764
  11.6 10.0 %copy-start.50 = (f32[2,2560]{1,0:T(2,128)S(1)}, f32[2,2560]{1,0:T(2,128)}, u32[]{:S(2)}) copy-start(f32[2,2560]{1,0:T(2,128)} %param.20) | copy-start | bytes 61444
  11.6 10.0 %copy-start.67 = (f32[2,32]{1,0:T(2,128)S(1)}, f32[2,32]{1,0:T(2,128)}, u32[]{:S(2)}) copy-start(f32[2,32]{1,0:T(2,128)} %param.21) | copy-start | bytes 772
  11.6 10.0 %copy-start.68 = (f32[2,32]{1,0:T(2,128)S(1)}, f32[2,32]{1,0:T(2,128)}, u32[]{:S(2)}) copy-start(f32[2,32]{1,0:T(2,128)} %param.22) | copy-start | bytes 772
  11.6 10.0 %copy-start.69 = (f32[2,32]{1,0:T(2,128)S(1)}, f32[2,32]{1,0:T(2,128)}, u32[]{:S(2)}) copy-start(f32[2,32]{1,0:T(2,128)} %param.23) | copy-start | bytes 772
  15.0 6.4 %copy-start.31 = (bf16[8,32,512]{2,1,0:T(8,128)(2,1)S(1)}, bf16[8,32,512]{2,1,0:T(8,128)(2,1)}, u32[]{:S(2)}) copy-start(bf16[8,32,512]{2,1,0:T(8,128)(2,1)} %param.15) | copy-start | bytes 786436
  15.0 22.5 %copy-start.70 = (s32[4]{0:T(128)S(1)}, s32[4]{0:T(128)}, u32[]{:S(2)}) copy-start(s32[4]{0:T(128)} %param.24) | copy-start | bytes 52
  16.4 22.4 %collective-permute-start = (bf16[8,320,3]{1,0,2:T(8,128)(2,1)}, bf16[8,320,3]{1,0,2:T(8,128)(2,1)S(1)}, u32[]{:S(2)}, u32[]{:S(2)}) collective-permute-start(bf16[8,320,3]{1,0,2:T(8,128)(2,1)} %pad_maximum_fusion.3), channel_id=1, source_target_pairs={{0,1},{1,2},{2,3},{4,5},{5,6},{6,7},{8,9},{9,10},{10,11},{12,13},{... | collective-permute-start | bytes 46088 | tf_op jit(solution)/shard_map/ppermute | solution.py:18
  38.1 6.5 %copy-start.40 = (f32[8,64]{1,0:T(8,128)}, f32[8,64]{1,0:T(8,128)S(1)}, u32[]{:S(2)}) copy-start(f32[8,64]{1,0:T(8,128)S(1)} %get-tuple-element.179) | copy-start | bytes 6148
  38.1 6.5 %copy-start.42 = (f32[8,64]{1,0:T(8,128)}, f32[8,64]{1,0:T(8,128)S(1)}, u32[]{:S(2)}) copy-start(f32[8,64]{1,0:T(8,128)S(1)} %get-tuple-element.177) | copy-start | bytes 6148
  38.1 6.5 %copy-start.44 = (f32[8,64]{1,0:T(8,128)}, f32[8,64]{1,0:T(8,128)S(1)}, u32[]{:S(2)}) copy-start(f32[8,64]{1,0:T(8,128)S(1)} %get-tuple-element.178) | copy-start | bytes 6148
  38.1 6.5 %copy-start.46 = (f32[8,64]{1,0:T(8,128)}, f32[8,64]{1,0:T(8,128)S(1)}, u32[]{:S(2)}) copy-start(f32[8,64]{1,0:T(8,128)S(1)} %get-tuple-element.180) | copy-start | bytes 6148
  39.0 6.3 %copy-start.23 = (bf16[8,256,512]{2,1,0:T(8,128)(2,1)S(1)}, bf16[8,256,512]{2,1,0:T(8,128)(2,1)}, u32[]{:S(2)}) copy-start(bf16[8,256,512]{2,1,0:T(8,128)(2,1)} %param.14) | copy-start | bytes 6291460
  43.4 6.2 %copy-start.48 = (bf16[8,4,512]{2,1,0:T(4,128)(2,1)S(1)}, bf16[8,4,512]{2,1,0:T(4,128)(2,1)}, u32[]{:S(2)}) copy-start(bf16[8,4,512]{2,1,0:T(4,128)(2,1)} %param.17) | copy-start | bytes 98308
  43.4 74.5 %all-gather.6.cloned.1.call-start = ((), (), s32[]{:S(2)}) async-start(), calls=%async_computation.3 | async-start | bytes 4718592 | tf_op jit(solution)/shard_map/all_gather | solution.py:230
  44.6 438.1 %reduce-scatter.3.cloned.1.call-start = ((), (), s32[]{:S(2)}) async-start(), calls=%async_computation.4 | async-start | bytes 4718592 | tf_op jit(solution)/shard_map/reduce_scatter | solution.py:274
  49.6 6.7 %copy-start.55 = (f32[8,4]{0,1:T(4,128)}, f32[8,4]{0,1:T(4,128)S(1)}, u32[]{:S(2)}) copy-start(f32[8,4]{0,1:T(4,128)S(1)} %copy.366) | copy-start | bytes 388
  49.9 8.9 %copy-start.28 = (f32[8,4,4,128]{3,0,2,1:T(8,128)}, f32[8,4,4,128]{3,0,2,1:T(8,128)S(1)}, u32[]{:S(2)}) copy-start(f32[8,4,4,128]{3,0,2,1:T(8,128)S(1)} %fusion.100) | copy-start | bytes 196612
  51.2 5.2 %copy-start.34 = (f32[8,4,4]{0,2,1:T(4,128)}, f32[8,4,4]{0,2,1:T(4,128)S(1)}, u32[]{:S(2)}) copy-start(f32[8,4,4]{0,2,1:T(4,128)S(1)} %slice_reduce_fusion) | copy-start | bytes 1540
  123.4 7.9 %copy-start = (f32[8,256,512]{1,2,0:T(8,128)S(1)}, f32[8,256,512]{1,2,0:T(8,128)}, u32[]{:S(2)}) copy-start(f32[8,256,512]{1,2,0:T(8,128)} %copy.375) | copy-start | bytes 12582916
  131.2 32.7 %copy-start.25 = (f32[8,4,128,128]{2,3,1,0:T(8,128)}, f32[8,4,128,128]{2,3,1,0:T(8,128)S(1)}, u32[]{:S(2)}) copy-start(f32[8,4,128,128]{2,3,1,0:T(8,128)S(1)} %fusion.166) | copy-start | bytes 6291460
  131.3 5.6 %copy-start.10 = (f32[8,4,64,4,128]{4,3,2,1,0:T(4,128)S(1)}, f32[8,4,64,4,128]{4,3,2,1,0:T(4,128)}, u32[]{:S(2)}) copy-start(f32[8,4,64,4,128]{4,3,2,1,0:T(4,128)} %reshape.322) | copy-start | bytes 12582916
  131.3 5.6 %copy-start.33 = (f32[4,128,128]{1,2,0:T(8,128)S(1)}, f32[4,128,128]{1,2,0:T(8,128)}, u32[]{:S(2)}) copy-start(f32[4,128,128]{1,2,0:T(8,128)} %compare_select_fusion) | copy-start | bytes 786436
  131.3 5.6 %copy-start.37 = (f32[8,4,4,128]{3,2,1,0:T(4,128)S(1)}, f32[8,4,4,128]{3,2,1,0:T(4,128)}, u32[]{:S(2)}) copy-start(f32[8,4,4,128]{3,2,1,0:T(4,128)} %copy.370) | copy-start | bytes 196612
  131.3 5.6 %copy-start.60 = (f32[8,4]{1,0:T(8,128)S(1)}, f32[8,4]{1,0:T(8,128)}, u32[]{:S(2)}) copy-start(f32[8,4]{1,0:T(8,128)} %get-tuple-element.206) | copy-start | bytes 388
  136.9 9.6 %copy-start.3 = (f32[8,256,512]{1,2,0:T(8,128)S(1)}, f32[8,256,512]{1,2,0:T(8,128)}, u32[]{:S(2)}) copy-start(f32[8,256,512]{1,2,0:T(8,128)} %copy.377) | copy-start | bytes 12582916
  146.5 9.7 %copy-start.19 = (f32[8,4,4,128,64]{3,4,2,1,0:T(8,128)}, f32[8,4,4,128,64]{3,4,2,1,0:T(8,128)S(1)}, u32[]{:S(2)}) copy-start(f32[8,4,4,128,64]{3,4,2,1,0:T(8,128)S(1)} %get-tuple-element.144) | copy-start | bytes 12582916
  156.2 22.6 %copy-start.16 = (f32[8,4,64,256]{3,2,1,0:T(8,128)}, f32[8,4,64,256]{3,2,1,0:T(8,128)S(1)}, u32[]{:S(2)}) copy-start(f32[8,4,64,256]{3,2,1,0:T(8,128)S(1)} %get-tuple-element.202) | copy-start | bytes 6291460
  157.9 49.0 %collective-permute-start.1 = (f32[8,4,64,256]{3,2,1,0:T(8,128)}, f32[8,4,64,256]{3,2,1,0:T(8,128)}, u32[]{:S(2)}, u32[]{:S(2)}) collective-permute-start(f32[8,4,64,256]{3,2,1,0:T(8,128)} %broadcast_add_fusion), channel_id=1, source_target_pairs={{0,1},{1,2},{2,3},{4,5},{5,6},{6,7},{8,9},{9,10},{10,11},{12,13},{... | collective-permute-start | bytes 6291464 | tf_op jit(solution)/shard_map/ppermute | solution.py:18
  162.6 49.7 %collective-permute-start.2 = (f32[8,4,64,256]{3,2,1,0:T(8,128)}, f32[8,4,64,256]{3,2,1,0:T(8,128)}, u32[]{:S(2)}, u32[]{:S(2)}) collective-permute-start(f32[8,4,64,256]{3,2,1,0:T(8,128)} %fusion.72), channel_id=1, source_target_pairs={{1,0},{2,1},{3,2},{5,4},{6,5},{7,6},{9,8},{10,9},{11,10},{13,12},{... | collective-permute-start | bytes 6291464 | tf_op jit(solution)/shard_map/ppermute | solution.py:18
  184.5 5.5 %copy-start.49 = (bf16[8,4,512]{2,1,0:T(4,128)(2,1)S(1)}, bf16[8,4,512]{2,1,0:T(4,128)(2,1)}, u32[]{:S(2)}) copy-start(bf16[8,4,512]{2,1,0:T(4,128)(2,1)} %param.17) | copy-start | bytes 98308
  184.5 5.6 %copy-start.56 = (f32[8,4]{0,1:T(4,128)S(1)}, f32[8,4]{0,1:T(4,128)}, u32[]{:S(2)}) copy-start(f32[8,4]{0,1:T(4,128)} %copy-done.55) | copy-start | bytes 388
  184.5 5.6 %copy-start.63 = (f32[8,4]{0,1:T(4,128)S(1)}, f32[8,4]{0,1:T(4,128)}, u32[]{:S(2)}) copy-start(f32[8,4]{0,1:T(4,128)} %copy-done.62) | copy-start | bytes 388
  190.9 8.7 %copy-start.4 = (f32[8,256,512]{1,2,0:T(8,128)S(1)}, f32[8,256,512]{1,2,0:T(8,128)}, u32[]{:S(2)}) copy-start(f32[8,256,512]{1,2,0:T(8,128)} %copy.377) | copy-start | bytes 12582916
  190.9 8.7 %copy-start.22 = (f32[8,4,128,128]{2,3,1,0:T(8,128)S(1)}, f32[8,4,128,128]{2,3,1,0:T(8,128)}, u32[]{:S(2)}) copy-start(f32[8,4,128,128]{2,3,1,0:T(8,128)} %get-tuple-element.112) | copy-start | bytes 6291460
  199.6 12.7 %copy-start.17 = (f32[8,4,64,256]{3,2,1,0:T(8,128)S(1)}, f32[8,4,64,256]{3,2,1,0:T(8,128)}, u32[]{:S(2)}) copy-start(f32[8,4,64,256]{3,2,1,0:T(8,128)} %copy-done.16) | copy-start | bytes 6291460
  218.2 46.6 %collective-permute-start.3 = (f32[8,4,64,256]{3,2,1,0:T(8,128)}, f32[8,4,64,256]{3,2,1,0:T(8,128)}, u32[]{:S(2)}, u32[]{:S(2)}) collective-permute-start(f32[8,4,64,256]{3,2,1,0:T(8,128)} %get-tuple-element.194), channel_id=1, source_target_pairs={{0,1},{1,2},{2,3},{4,5},{5,6},{6,7},{8,9},{9,10},{10,11},{12,13},{... | collective-permute-start | bytes 6291464 | tf_op jit(solution)/shard_map/ppermute | solution.py:18
  221.6 48.6 %collective-permute-start.4 = (f32[8,4,64,256]{3,2,1,0:T(8,128)}, f32[8,4,64,256]{3,2,1,0:T(8,128)}, u32[]{:S(2)}, u32[]{:S(2)}) collective-permute-start(f32[8,4,64,256]{3,2,1,0:T(8,128)} %get-tuple-element.193), channel_id=1, source_target_pairs={{1,0},{2,1},{3,2},{5,4},{6,5},{7,6},{9,8},{10,9},{11,10},{13,12},{... | collective-permute-start | bytes 6291464 | tf_op jit(solution)/shard_map/ppermute | solution.py:18
  223.9 57.4 %copy-start.1 = (f32[8,256,512]{1,2,0:T(8,128)S(1)}, f32[8,256,512]{1,2,0:T(8,128)}, u32[]{:S(2)}) copy-start(f32[8,256,512]{1,2,0:T(8,128)} %copy.375) | copy-start | bytes 12582916
  270.2 22.5 %slice-start = ((s8[8388608]{0:T(1024)(128)(4,1)}), s8[4194304]{0:T(1024)(128)(4,1)S(1)}, s32[]{:S(2)}) async-start(s8[8388608]{0:T(1024)(128)(4,1)} %bitcast.260), calls=%async_computation.6 | async-start | bytes 8388608
  276.6 45.3 %collective-permute-start.5 = (f32[8,4,64,256]{3,2,1,0:T(8,128)}, f32[8,4,64,256]{3,2,1,0:T(8,128)}, u32[]{:S(2)}, u32[]{:S(2)}) collective-permute-start(f32[8,4,64,256]{3,2,1,0:T(8,128)} %get-tuple-element.192), channel_id=1, source_target_pairs={{0,1},{1,2},{2,3},{4,5},{5,6},{6,7},{8,9},{9,10},{10,11},{12,13},{... | collective-permute-start | bytes 6291464 | tf_op jit(solution)/shard_map/ppermute | solution.py:18
  280.1 47.4 %collective-permute-start.6 = (f32[8,4,64,256]{3,2,1,0:T(8,128)}, f32[8,4,64,256]{3,2,1,0:T(8,128)}, u32[]{:S(2)}, u32[]{:S(2)}) collective-permute-start(f32[8,4,64,256]{3,2,1,0:T(8,128)} %get-tuple-element.191), channel_id=1, source_target_pairs={{1,0},{2,1},{3,2},{5,4},{6,5},{7,6},{9,8},{10,9},{11,10},{13,12},{... | collective-permute-start | bytes 6291464 | tf_op jit(solution)/shard_map/ppermute | solution.py:18
  281.4 11.3 %slice-start.1 = ((s8[8388608]{0:T(1024)(128)(4,1)}), s8[4194304]{0:T(1024)(128)(4,1)S(1)}, s32[]{:S(2)}) async-start(s8[8388608]{0:T(1024)(128)(4,1)} %bitcast.260), calls=%async_computation.7 | async-start | bytes 8388608
  327.4 8.2 %copy-start.20 = (f32[8,4,4,128,64]{3,4,2,1,0:T(8,128)S(1)}, f32[8,4,4,128,64]{3,4,2,1,0:T(8,128)}, u32[]{:S(2)}) copy-start(f32[8,4,4,128,64]{3,4,2,1,0:T(8,128)} %copy-done.19) | copy-start | bytes 12582916
  335.4 9.7 %copy-start.5 = (f32[8,4,4,64,256]{4,3,1,2,0:T(8,128)}, f32[8,4,4,64,256]{4,3,1,2,0:T(8,128)S(1)}, u32[]{:S(2)}) copy-start(f32[8,4,4,64,256]{4,3,1,2,0:T(8,128)S(1)} %get-tuple-element.149) | copy-start | bytes 25165828
  357.2 126.9 %reduce-scatter.5.cloned.1.call-start = ((), (), s32[]{:S(2)}) async-start(), calls=%async_computation.5 | async-start | bytes 4718592 | tf_op jit(solution)/shard_map/reduce_scatter | solution.py:275
  363.8 9.2 %copy-start.2 = (f32[8,256,512]{1,2,0:T(8,128)S(1)}, f32[8,256,512]{1,2,0:T(8,128)}, u32[]{:S(2)}) copy-start(f32[8,256,512]{1,2,0:T(8,128)} %copy.375) | copy-start | bytes 12582916
  372.8 8.7 %copy-start.7 = (f32[8,4,4,64,256]{4,3,1,2,0:T(8,128)}, f32[8,4,4,64,256]{4,3,1,2,0:T(8,128)S(1)}, u32[]{:S(2)}) copy-start(f32[8,4,4,64,256]{4,3,1,2,0:T(8,128)S(1)} %get-tuple-element.151) | copy-start | bytes 25165828
  373.0 8.5 %copy-start.11 = (f32[8,4,64,4,128]{4,3,2,1,0:T(4,128)S(1)}, f32[8,4,64,4,128]{4,3,2,1,0:T(4,128)}, u32[]{:S(2)}) copy-start(f32[8,4,64,4,128]{4,3,2,1,0:T(4,128)} %reshape.322) | copy-start | bytes 12582916
  373.0 8.5 %copy-start.26 = (f32[8,4,128,128]{2,3,1,0:T(8,128)S(1)}, f32[8,4,128,128]{2,3,1,0:T(8,128)}, u32[]{:S(2)}) copy-start(f32[8,4,128,128]{2,3,1,0:T(8,128)} %copy-done.25) | copy-start | bytes 6291460
  373.0 8.5 %copy-start.38 = (f32[8,4,4,128]{3,2,1,0:T(4,128)S(1)}, f32[8,4,4,128]{3,2,1,0:T(4,128)}, u32[]{:S(2)}) copy-start(f32[8,4,4,128]{3,2,1,0:T(4,128)} %copy.370) | copy-start | bytes 196612
  373.0 8.5 %copy-start.61 = (f32[8,4]{1,0:T(8,128)S(1)}, f32[8,4]{1,0:T(8,128)}, u32[]{:S(2)}) copy-start(f32[8,4]{1,0:T(8,128)} %get-tuple-element.206) | copy-start | bytes 388
  381.6 10.2 %copy-start.18 = (f32[8,4,4,64,128]{4,3,2,1,0:T(8,128)}, f32[8,4,4,64,128]{4,3,2,1,0:T(8,128)S(1)}, u32[]{:S(2)}) copy-start(f32[8,4,4,64,128]{4,3,2,1,0:T(8,128)S(1)} %fusion.16) | copy-start | bytes 12582916
  458.2 5.7 %copy-start.13 = (f32[8,256,512]{2,1,0:T(8,128)}, f32[8,256,512]{2,1,0:T(8,128)S(1)}, u32[]{:S(2)}) copy-start(f32[8,256,512]{2,1,0:T(8,128)S(1)} %get-tuple-element.140) | copy-start | bytes 12582916
  458.2 5.7 %copy-start.14 = (f32[8,256,512]{2,1,0:T(8,128)}, f32[8,256,512]{2,1,0:T(8,128)S(1)}, u32[]{:S(2)}) copy-start(f32[8,256,512]{2,1,0:T(8,128)S(1)} %get-tuple-element.141) | copy-start | bytes 12582916
  458.2 5.7 %copy-start.15 = (f32[8,256,512]{2,1,0:T(8,128)}, f32[8,256,512]{2,1,0:T(8,128)S(1)}, u32[]{:S(2)}) copy-start(f32[8,256,512]{2,1,0:T(8,128)S(1)} %get-tuple-element.142) | copy-start | bytes 12582916
  470.3 5.0 copy-start.35
  470.3 5.0 copy-start.52
  470.3 5.2 %copy-start.59 = (f32[4]{0:T(128)S(1)}, f32[4]{0:T(128)}, u32[]{:S(2)}) copy-start(f32[4]{0:T(128)} %copy-done.58) | copy-start | bytes 52
  480.1 5.4 %copy-start.24 = (f32[8,64,512]{2,1,0:T(8,128)S(1)}, f32[8,64,512]{2,1,0:T(8,128)}, u32[]{:S(2)}) copy-start(f32[8,64,512]{2,1,0:T(8,128)} %get-tuple-element.137) | copy-start | bytes 3145732
  480.1 5.4 %copy-start.41 = (f32[8,64]{1,0:T(8,128)S(1)}, f32[8,64]{1,0:T(8,128)}, u32[]{:S(2)}) copy-start(f32[8,64]{1,0:T(8,128)} %copy-done.40) | copy-start | bytes 6148
  489.4 7.7 %collective-permute-start.7 = (f32[8,320,3]{1,0,2:T(8,128)S(1)}, f32[8,320,3]{1,0,2:T(8,128)S(1)}, u32[]{:S(2)}, u32[]{:S(2)}) collective-permute-start(f32[8,320,3]{1,0,2:T(8,128)S(1)} %copy.434), channel_id=1, source_target_pairs={{1,0},{2,1},{3,2},{5,4},{6,5},{7,6},{9,8},{10,9},{11,10},{13,12},{... | collective-permute-start | bytes 92168 | tf_op jit(solution)/shard_map/ppermute | solution.py:18
  (21 other events, 62.2 us)
Sparse Core Ops, SparseCore 0:
  43.5 35.1 all-gather.3
  81.2 36.7 all-gather.5
  357.3 48.5 reduce-scatter.2
  424.3 48.8 reduce-scatter.4

commit v9 on v5

--- a/solution.py
+++ b/solution.py
@@ -180,7 +180,16 @@
         ],
         axis=1,
     )
-    packed_all = lax.all_gather(packed, "head", axis=0, tiled=True)
+    count, here = (lax.axis_size("head"), lax.axis_index("head"))
+    stacked = jnp.stack(
+        [packed]
+        + [
+            lax.ppermute(packed, "head", [(i, (i + k) % count) for i in range(count)])
+            for k in range(1, count)
+        ]
+    )
+    order = (here - jnp.arange(count)) % count
+    packed_all = jnp.take(stacked, order, axis=0).reshape((-1, packed.shape[1]))
     cuts = [conv_weight[0].size, conv_bias.shape[1], dt_bias.shape[1], a_log.shape[1]]
     bounds = [sum(cuts[:k]) for k in range(len(cuts) + 1)]
     weight_all = packed_all[:, : bounds[1]].reshape((-1,) + conv_weight.shape[1:])

time: 488 us -> 484 us (level)
  blocking collectives: 15.4 us -> 0 us
  waiting for transfers between devices: 101 us -> 106 us
    all_gather x1 -> x0, blocking collectives: 15.4 us -> none  [shards(): packed_all = lax.all_gather(packed, 'head', axis=0, tiled=True)]
    ppermute x0 -> x3, starting transfers between devices: none -> 7.01 us  [shards(): lax.ppermute(packed, 'head', [(i, (i + k) % count) for i in range(count)])]
    unnamed x219 -> x196, local copies, waits for them, and re-layouts: 16.5 us -> 16.8 us
  transfers between devices with their start and end apart: 12 -> 15, of which waited for: 8 -> 8; matrix products, arithmetic and copies ran while one was open for 51% -> 53% of each run, Pallas kernels for 0% -> 0%
where the time goes in v9:
time: 484 us; the launch traced here: 478 us
  matrix products  142 us (29%)
  waiting for transfers between devices  106 us (22%)
  other arithmetic  103 us (21%)
  local copies, waits for them, and re-layouts  84.6 us (17%)
  starting transfers between devices  27.7 us (6%)
  between operations  15.7 us (3%)
    ppermute x8, waiting for transfers between devices, passed_along(): lax.ppermute(value, axis, [(source, source + steps) for source in range(f...  81.9 us
    dot_general x3, matrix products, span_terms(): jnp.einsum('hcij,hpcj->hpci', decay * scores[None], weighted, precision=p...  41.3 us
    dot_general x3, matrix products, span_terms(): jnp.einsum('hpcj,hcj,ncj->hcpn', weighted, keep_end, b_three, precision=p...  41 us
    dot_general x3, matrix products, assemble(): jnp.einsum('nci,hci,chpn->hpci', c_three, entry, starts, precision=precise)  32.7 us
    reduce_sum x2, other arithmetic, weighted_sum(): return jnp.sum(weight[..., None, None] * stacked, axis=-3)  26.6 us
    ppermute x8, starting transfers between devices, passed_along(): lax.ppermute(value, axis, [(source, source + steps) for source in range(f...  19.9 us
    dot_general x3, matrix products, span_terms(): scores = jnp.einsum('nci,ncj->cij', c_three, b_three, precision=precise)  19.3 us
    all_gather x1, waiting for transfers between devices, shards(): c_conv = lax.all_gather(bc_conv[:, b_width:], 'seq', axis=1, tiled=True)  17.5 us
  transfers between devices with their start and end apart: 15, of which 8 were waited for; matrix products, arithmetic and copies ran while one was open for 53% of the time, Pallas kernels for 0%

profile of v9, /device:TPU:0, one launch (start us, length us, event | category | flops | bytes accessed | tf_op | source)
XLA Modules:
  0.0 478.3 jit_solution(7782935715409205419)
XLA Ops:
  9.1 3.1 collective-permute-start
  12.1 2.6 collective-permute-start.1
  16.1 3.3 copy.347
  19.4 1.7 copy.348
  21.2 1.7 copy.349
  22.8 1.4 pad_maximum_fusion.4
  24.2 2.6 collective-permute-start.3
  34.4 2.4 fusion.102
  39.6 2.6 convert_element_type.83
  42.1 2.6 reshape.358
  46.3 12.0 %fusion.50 = (f32[8,256,512]{2,1,0:T(8,128)}, f32[8,256,512]{2,1,0:T(8,128)}) fusion(f32[8,256,512]{2,1,0:T(8,128)} %convert_element_type.83, f32[8,256]{1,0:T(8,128)S(1)} %get-tuple-element.150, f32[512]{0:T(512)S(1)} %get-tuple-element.183, f32[8,256,3]{2,1,0:T(8,128)S(1)} %copy.350, f32[8,256]{1,0:T(8,128)S(1)} %get-tuple-element.148, ...), kind=kLoop, calls=%fused_computation.89 | loop fusion | flops 18874368 | bytes 12654592 | tf_op jit(solution)/shard_map/jvp(vmap(jit(silu)))/mul | solution.py:53
  58.4 5.3 %reshape.354 = f32[8,4,64,4,128]{4,3,2,1,0:T(4,128)} reshape(f32[8,256,512]{2,1,0:T(8,128)} %get-tuple-element.122) | data formatting | bytes 8388608 | tf_op jit(solution)/shard_map/jvp(vmap())/reshape | solution.py:59
  63.6 1.4 fusion.173
  66.9 6.3 %all-gather.5.cloned.1.call-done = f32[8,256,512]{2,0,1:T(8,128)} async-done(((f32[8,32,512]{2,0,1:T(8,128)}), f32[8,256,512]{2,0,1:T(8,128)}) %all-gather.5.cloned.1.call-update) | async-done | bytes 4194320 | tf_op jit(solution)/shard_map/all_gather | solution.py:239
  73.2 5.3 %copy.363 = f32[8,256,512]{1,2,0:T(8,128)} copy(f32[8,256,512]{2,0,1:T(8,128)} %all-gather.5.cloned.1.call-done) | data formatting | bytes 8388608 | tf_op jit(solution)/shard_map/all_gather | solution.py:239
  78.4 13.6 %multiply_reduce_fusion.5 = (f32[8,4,64,256]{3,2,1,0:T(8,128)S(1)}, f32[8,4,4,64,256]{4,3,1,2,0:T(8,128)}) fusion(f32[8,4,4]{1,2,0:T(4,128)S(1)} %copy.378, f32[8,256,4,128,1]{1,3,4,2,0:T(8,128)} %bitcast.244, f32[8,4,64,4,128]{4,3,2,1,0:T(4,128)} %reshape.354, f32[8,4,4,128]{3,2,1,0:T(4,128)S(1)} %copy.372, f32[8,4,4,128]{3,2,1,0:T(4,128)S(1)} %copy.353), kind=kOutput, calls=%fused_computation.26 | convolution fusion | flops 3226992640 | bytes 19005952 | tf_op jit(solution)/shard_map/jvp(vmap(hpcj,hcj,ncj->hcpn))/dot_general | solution.py:78
  93.3 1.5 broadcast_add_fusion
  94.9 17.5 %all-gather.3.cloned.1.call-done = f32[8,256,512]{2,0,1:T(8,128)} async-done(((f32[8,32,512]{2,0,1:T(8,128)}), f32[8,256,512]{2,0,1:T(8,128)}) %all-gather.3.cloned.1.call-update) | async-done | bytes 4194320 | tf_op jit(solution)/shard_map/all_gather | solution.py:240
  112.4 5.3 %copy.361 = f32[8,256,512]{1,2,0:T(8,128)} copy(f32[8,256,512]{2,0,1:T(8,128)} %all-gather.3.cloned.1.call-done) | data formatting | bytes 8388608 | tf_op jit(solution)/shard_map/all_gather | solution.py:240
  117.6 7.0 %fusion.82 = f32[8,4,64,256]{3,2,1,0:T(8,128)} fusion(f32[8,256,4,128,1]{1,3,2,4,0:T(8,128)} %bitcast.239, f32[8,4,4,128]{3,2,1,0:T(4,128)S(1)} %copy.382, bf16[8,4,64,4,128]{4,3,2,1,0:T(4,128)(2,1)S(1)} %reshape.358), kind=kOutput, calls=%fused_computation.114 | convolution fusion | flops 3223322624 | bytes 8454144 | tf_op jit(solution)/shard_map/ghpci,ghci,gnci->ghpn/dot_general | solution.py:261
  124.6 3.5 collective-permute-start.4
  134.6 39.0 %collective-permute-done.4 = f32[8,4,64,256]{3,2,1,0:T(8,128)S(1)} collective-permute-done((f32[8,4,64,256]{3,2,1,0:T(8,128)}, f32[8,4,64,256]{3,2,1,0:T(8,128)S(1)}, u32[]{:S(2)}, u32[]{:S(2)}) %collective-permute-start.4) | collective-permute-done | bytes 2097184 | tf_op jit(solution)/shard_map/ppermute | solution.py:18
  173.6 4.2 collective-permute-done.5
  177.9 5.7 %multiply_add_fusion.2 = (f32[8,4,64,256]{3,2,1,0:T(8,128)}, f32[8,4,64,256]{3,2,1,0:T(8,128)}) fusion(f32[8,4,64,256]{3,2,1,0:T(8,128)} %fusion.82, f32[8,4,64,256]{3,2,1,0:T(8,128)} %collective-permute-done.5, f32[8,4]{1,0:T(8,128)S(1)} %copy.377, f32[8,4,64,256]{3,2,1,0:T(8,128)S(1)} %collective-permute-done.4, f32[8,4,64,256]{3,2,1,0:T(8,128)} %copy-done.14, ...), kind=kLoop, calls=%fused_computation.104 | loop fusion | flops 2621440 | bytes 12583168 | tf_op jit(solution)/shard_map/add | solution.py:31
  183.6 4.6 collective-permute-start.6
  188.2 1.7 collective-permute-start.7
  190.0 5.8 %fusion.174 = f32[8,4,128,128]{2,3,1,0:T(8,128)} fusion(f32[8,256,4,128]{1,3,2,0:T(8,128)S(1)} %bitcast.241, f32[8,256,4,128]{1,3,2,0:T(8,128)S(1)} %bitcast.247), kind=kOutput, calls=%fused_computation.320 | convolution fusion | flops 1610612736 | bytes 10485760 | tf_op jit(solution)/shard_map/jvp(vmap(nci,ncj->cij))/dot_general | solution.py:72
  195.8 7.5 %fusion.60 = f32[8,4,4,64,256]{4,3,1,2,0:T(8,128)S(1)} fusion(f32[8,256,4,128,1]{1,3,4,2,0:T(8,128)S(1)} %bitcast.242, f32[8,4,4,128]{3,2,1,0:T(4,128)S(1)} %copy-done.30, bf16[8,4,64,4,128]{4,3,2,1,0:T(4,128)(2,1)S(1)} %copy-done.7), kind=kOutput, calls=%fused_computation.98 | convolution fusion | flops 3223322624 | bytes 14745600 | tf_op jit(solution)/shard_map/transpose(jvp(vmap(nci,hci,chpn->hpci)))/dot_general | solution.py:149
  203.4 17.9 %fusion.104 = (f32[8,4,4,128]{3,2,1,0:T(4,128)}, f32[8,4,4,128]{3,2,1,0:T(4,128)}, f32[8,4,128,128]{2,3,1,0:T(8,128)}) fusion(f32[8,4,4,128]{3,2,1,0:T(4,128)} %copy.356, f32[4,128,128]{1,2,0:T(8,128)} %compare_select_fusion, f32[8,4,128,128]{2,3,1,0:T(8,128)} %fusion.174, bf16[8,4,4,64,128]{4,2,3,1,0:T(4,128)(2,1)} %bitcast.250, ...), kind=kOutput, calls=%fused_computation.150 | convolution fusion | flops 1642561536 | bytes 11010048 | tf_op jit(solution)/shard_map/transpose(jvp(vmap(hcij,hpcj->hpci)))/dot_general | solution.py:74
  221.2 10.1 %collective-permute-done.6 = f32[8,4,64,256]{3,2,1,0:T(8,128)} collective-permute-done((f32[8,4,64,256]{3,2,1,0:T(8,128)}, f32[8,4,64,256]{3,2,1,0:T(8,128)}, u32[]{:S(2)}, u32[]{:S(2)}) %collective-permute-start.6) | collective-permute-done | bytes 2097184 | tf_op jit(solution)/shard_map/ppermute | solution.py:18
  231.4 5.4 %collective-permute-done.7 = f32[8,4,64,256]{3,2,1,0:T(8,128)} collective-permute-done((f32[8,4,64,256]{3,2,1,0:T(8,128)}, f32[8,4,64,256]{3,2,1,0:T(8,128)}, u32[]{:S(2)}, u32[]{:S(2)}) %collective-permute-start.7) | collective-permute-done | bytes 2097184 | tf_op jit(solution)/shard_map/ppermute | solution.py:18
  236.8 6.4 %multiply_add_fusion = (f32[8,4,64,256]{3,2,1,0:T(8,128)}, f32[8,4,64,256]{3,2,1,0:T(8,128)}) fusion(f32[8,4,64,256]{3,2,1,0:T(8,128)} %fusion.82, f32[8,4,64,256]{3,2,1,0:T(8,128)} %collective-permute-done.7, f32[8,4]{1,0:T(8,128)S(1)} %copy-done.60, f32[8,4,64,256]{3,2,1,0:T(8,128)} %collective-permute-done.6, f32[8,4,64,256]{3,2,1,0:T(8,128)} %copy-done.14, ...), kind=kLoop, calls=%fused_computation.102 | loop fusion | flops 2621440 | bytes 12583168 | tf_op jit(solution)/shard_map/add | solution.py:31
  243.2 3.4 collective-permute-start.8
  247.9 5.2 %fusion.175 = f32[8,4,128,256]{3,2,1,0:T(8,128)} fusion(f32[8,4,128,128]{2,3,1,0:T(8,128)S(1)} %copy-done.18, f32[8,256,4,128]{1,3,2,0:T(8,128)S(1)} %bitcast.243), kind=kOutput, calls=%fused_computation.321 | convolution fusion | flops 1610612736 | bytes 10485760 | tf_op jit(solution)/shard_map/transpose(jvp(vmap(nci,ncj->cij)))/dot_general | solution.py:72
  253.1 17.8 %multiply_reduce_fusion = (f32[8,4,4,4]{3,2,1,0:T(4,128)}, f32[8,4,4,64,256]{4,3,2,1,0:T(8,128)}, f32[8,4,4,64,256]{4,3,2,1,0:T(8,128)}) fusion(f32[8,4,4,4]{3,2,1,0:T(4,128)S(1)} %bitcast_multiply_fusion.8, f32[8,4,4,64,256]{4,3,1,2,0:T(8,128)S(1)} %bitcast.249, f32[8,4,4,64,256]{4,3,1,2,0:T(8,128)S(1)} %fusion.60), kind=kLoop, calls=%fused_computation.3 | loop fusion | flops 46136832 | bytes 33558528 | tf_op jit(solution)/shard_map/transpose(jvp(vmap()))/reduce_sum | solution.py:131
  270.9 17.7 %collective-permute-done.8 = f32[8,4,64,256]{3,2,1,0:T(8,128)} collective-permute-done((f32[8,4,64,256]{3,2,1,0:T(8,128)}, f32[8,4,64,256]{3,2,1,0:T(8,128)}, u32[]{:S(2)}, u32[]{:S(2)}) %collective-permute-start.8) | collective-permute-done | bytes 2097184 | tf_op jit(solution)/shard_map/ppermute | solution.py:18
  288.5 5.4 %collective-permute-done.9 = f32[8,4,64,256]{3,2,1,0:T(8,128)} collective-permute-done((f32[8,4,64,256]{3,2,1,0:T(8,128)}, f32[8,4,64,256]{3,2,1,0:T(8,128)}, u32[]{:S(2)}, u32[]{:S(2)}) %collective-permute-start.9) | collective-permute-done | bytes 2097184 | tf_op jit(solution)/shard_map/ppermute | solution.py:18
  293.9 8.8 %multiply_reduce_fusion.4 = (f32[8,4,4]{1,2,0:T(4,128)}, f32[8,4,4,64,256]{4,3,1,2,0:T(8,128)S(1)}) fusion(f32[8,4,4,64,256]{4,3,1,2,0:T(8,128)} %get-tuple-element.188, f32[8,4,64,256]{3,2,1,0:T(8,128)} %collective-permute-done.9, f32[8,4,4,64,256]{4,3,2,1,0:T(8,128)} %get-tuple-element.103, f32[8,4,4]{1,2,0:T(4,128)S(1)} %copy-done.48), kind=kLoop, calls=%fused_computation.25 | loop fusion | flops 8388480 | bytes 27264000 | tf_op jit(solution)/shard_map/transpose(jvp(vmap()))/reduce_sum | solution.py:131
  302.8 12.5 %bitcast_add_fusion.2 = f32[8,256,4,128]{1,3,2,0:T(8,128)} fusion(f32[8,4,128,256]{3,2,1,0:T(8,128)} %fusion.175, f32[8,4,4,64,256]{4,3,1,2,0:T(8,128)S(1)} %get-tuple-element.134, f32[8,4,64,4,128]{4,3,2,1,0:T(4,128)S(1)} %copy-done.4, f32[8,4,4,128]{3,2,1,0:T(4,128)} %copy-done.28, f32[8,4,4,128]{3,2,1,0:T(4,128)S(1)} %copy.353), kind=kOutput, calls=%fused_computation.60 | convolution fusion | flops 3224371200 | bytes 21102592 | tf_op jit(solution)/shard_map/transpose(jvp(vmap(hpcj,hcj,ncj->hcpn)))/dot_general | solution.py:78
  315.2 5.6 %copy.406 = f32[8,256,512]{2,0,1:T(8,128)} copy(f32[8,256,512]{1,2,0:T(8,128)} %bitcast.252) | data formatting | bytes 8388608 | tf_op jit(solution)/shard_map/transpose(jvp(vmap()))/reshape | solution.py:60
  322.5 8.3 %fusion.176 = f32[8,4,128,256]{3,2,1,0:T(8,128)} fusion(f32[8,4,128,128]{2,3,1,0:T(8,128)S(1)} %copy-done.19, f32[8,256,4,128]{1,3,2,0:T(8,128)} %bitcast.245), kind=kOutput, calls=%fused_computation.322 | convolution fusion | flops 1610612736 | bytes 10485760 | tf_op jit(solution)/shard_map/transpose(jvp(vmap(nci,ncj->cij)))/dot_general | solution.py:72
  330.8 2.7 multiply_reduce_fusion.6
  333.6 11.5 %multiply_reduce_fusion.3 = (f32[8,4,4]{1,2,0:T(4,128)S(1)}, f32[8,4,4,64,256]{4,3,1,2,0:T(8,128)}) fusion(f32[8,4,4,64,256]{4,3,1,2,0:T(8,128)} %copy-done.2, f32[8,4,64,256]{3,2,1,0:T(8,128)} %collective-permute-done.8, f32[8,4,4]{1,2,0:T(4,128)S(1)} %copy.376, f32[8,4,4,64,256]{4,3,2,1,0:T(8,128)} %get-tuple-element.102), kind=kLoop, calls=%fused_computation.24 | loop fusion | flops 8388480 | bytes 27264000 | tf_op jit(solution)/shard_map/transpose(jvp(vmap()))/reduce_sum | solution.py:142
  345.2 14.0 %bitcast_add_fusion.3 = f32[8,4,128,256]{3,2,1,0:T(8,128)} fusion(f32[8,4,128,256]{3,2,1,0:T(8,128)} %fusion.176, f32[8,4,4,64,256]{4,3,1,2,0:T(8,128)} %get-tuple-element.136, f32[8,4,4,128]{3,2,1,0:T(4,128)S(1)} %copy-done.31, bf16[8,4,64,4,128]{4,3,2,1,0:T(4,128)(2,1)S(1)} %copy-done.8), kind=kOutput, calls=%fused_computation.61 | convolution fusion | flops 3224371200 | bytes 18939904 | tf_op jit(solution)/shard_map/transpose(jvp(vmap(nci,hci,chpn->hpci)))/dot_general | solution.py:149
  359.2 5.6 %copy.411 = f32[8,256,512]{2,0,1:T(8,128)} copy(f32[8,256,512]{1,2,0:T(8,128)} %bitcast.253) | data formatting | bytes 8388608 | tf_op jit(solution)/shard_map/transpose(jvp(vmap()))/reshape | solution.py:61
  364.9 14.9 %fusion.38 = (f32[8,4,4,128]{3,2,1,0:T(4,128)S(1)}, f32[8,4,4,64,128]{4,3,1,2,0:T(8,128)}) fusion(f32[8,4,64,4,128]{4,3,2,1,0:T(4,128)} %reshape.354, f32[8,4,4,128]{3,2,1,0:T(4,128)S(1)} %copy.353, f32[8,4,4,64,256]{4,3,1,2,0:T(8,128)} %copy-done.3, f32[8,256,4,128,1]{1,3,2,4,0:T(8,128)} %bitcast.246), kind=kOutput, calls=%fused_computation.69 | convolution fusion | flops 3224354816 | bytes 21102592 | tf_op jit(solution)/shard_map/transpose(jvp(vmap(hpcj,hcj,ncj->hcpn)))/dot_general | solution.py:78
  380.9 13.7 %fusion.36 = (f32[8,4,4,128]{3,2,1,0:T(4,128)S(1)}, f32[8,4,64,4,128]{4,2,3,1,0:T(8,128)}) fusion(f32[8,4,64,4,128]{4,3,2,1,0:T(4,128)} %reshape.354, f32[8,4,4,128]{3,2,1,0:T(4,128)S(1)} %copy.353, bf16[8,4,64,4,128]{4,3,2,1,0:T(4,128)(2,1)S(1)} %copy-done.8, f32[8,4]{1,0:T(8,128)S(1)} %constant_dynamic-slice_fusion, ...), kind=kOutput, calls=%fused_computation.65 | convolution fusion | flops 1627373568 | bytes 19398784 | tf_op jit(solution)/shard_map/transpose(jvp(vmap(hcij,hpcj->hpci)))/dot_general | solution.py:74
  394.6 11.3 %fusion.16 = f32[8,4,4,64,128]{4,3,2,1,0:T(8,128)S(1)} fusion(f32[8,256,4,128,1]{1,3,4,2,0:T(8,128)} %bitcast.240, f32[8,4,4,64,256]{4,3,1,2,0:T(8,128)} %get-tuple-element.136), kind=kOutput, calls=%fused_computation.29 | convolution fusion | flops 3221225472 | bytes 16777216 | tf_op jit(solution)/shard_map/jvp(vmap(nci,hci,chpn->hpci))/dot_general | solution.py:149
  409.8 5.7 %copy.401 = f32[8,4,64,4,128]{4,3,2,1,0:T(4,128)} copy(f32[8,4,64,4,128]{4,2,3,1,0:T(8,128)S(1)} %copy-done.22) | data formatting | bytes 8388608 | tf_op jit(solution)/shard_map/transpose(jvp(vmap()))/add_any | solution.py:73
  415.4 5.5 %reshape.361 = f32[8,256,512]{2,1,0:T(8,128)} reshape(f32[8,4,64,4,128]{4,3,2,1,0:T(4,128)} %copy.401) | data formatting | bytes 8388608 | tf_op jit(solution)/shard_map/transpose(jvp(vmap()))/reshape | solution.py:59
  421.0 4.3 broadcast_multiply_fusion
  427.3 4.6 pad_add_fusion
  432.0 3.3 split.16
  435.3 1.7 copy-done.16
  437.0 9.7 %fusion.39 = bf16[8,4,64,4,128]{4,2,3,1,0:T(8,128)(2,1)S(1)} fusion(f32[8,4,4,64,128]{4,3,2,1,0:T(8,128)S(1)} %copy-done.16, f32[8,4,64,4,128]{4,3,2,1,0:T(4,128)S(1)} %copy-done.5, f32[8,4,128,128]{2,3,1,0:T(8,128)S(1)} %copy-done.23, f32[4,128,128]{1,2,0:T(8,128)S(1)} %copy-done.37, f32[8,4,4,128]{3,2,1,0:T(4,128)S(1)} %copy-done.50, ...), kind=kOutput, calls=%fused_computation.71 | convolution fusion | flops 1625292800 | bytes 13041792 | tf_op jit(solution)/shard_map/jvp(vmap(hcij,hpcj->hpci))/dot_general | solution.py:74
  446.7 2.0 copy.389
  448.7 2.2 convert_element_type.96
  450.9 2.6 pad_add_fusion.3
  455.0 1.4 copy_dynamic-update-slice_fusion
  460.3 1.6 collective-permute-start.10
  461.9 2.9 slice_maximum_fusion
  464.8 1.5 pad_maximum_fusion.1
  466.2 1.8 copy.415
  469.8 1.5 slice.269
  (335 shorter events, 41.4 us)
Async XLA Ops:
  7.2 14.0 %copy-start.27 = (bf16[8,32,512]{2,1,0:T(8,128)(2,1)S(1)}, bf16[8,32,512]{2,1,0:T(8,128)(2,1)}, u32[]{:S(2)}) copy-start(bf16[8,32,512]{2,1,0:T(8,128)(2,1)} %param.15) | copy-start | bytes 786436
  7.2 66.0 %all-gather.5.cloned.1.call-start = ((), (), s32[]{:S(2)}) async-start(), calls=%async_computation.3 | async-start | bytes 4718592 | tf_op jit(solution)/shard_map/all_gather | solution.py:239
  9.1 21.9 %collective-permute-start = (f32[2,12896]{1,0:T(2,128)S(1)}, f32[2,12896]{1,0:T(2,128)}, u32[]{:S(2)}, u32[]{:S(2)}) collective-permute-start(f32[2,12896]{1,0:T(2,128)S(1)} %concatenate.39), channel_id=1, source_target_pairs={{0,1},{1,2},{2,3},{3,0},{4,5},{5,6},{6,7},{7,4},{8,9},{9,10},{10,1... | collective-permute-start | bytes 309512 | tf_op jit(solution)/shard_map/ppermute | solution.py:187
  12.1 18.8 %collective-permute-start.1 = (f32[2,12896]{1,0:T(2,128)S(1)}, f32[2,12896]{1,0:T(2,128)}, u32[]{:S(2)}, u32[]{:S(2)}) collective-permute-start(f32[2,12896]{1,0:T(2,128)S(1)} %concatenate.39), channel_id=1, source_target_pairs={{0,2},{1,3},{2,0},{3,1},{4,6},{5,7},{6,4},{7,5},{8,10},{9,11},{10,... | collective-permute-start | bytes 309512 | tf_op jit(solution)/shard_map/ppermute | solution.py:187
  14.7 16.2 %collective-permute-start.2 = (f32[2,12896]{1,0:T(2,128)S(1)}, f32[2,12896]{1,0:T(2,128)}, u32[]{:S(2)}, u32[]{:S(2)}) collective-permute-start(f32[2,12896]{1,0:T(2,128)S(1)} %concatenate.39), channel_id=1, source_target_pairs={{0,3},{1,0},{2,1},{3,2},{4,7},{5,4},{6,5},{7,6},{8,11},{9,8},{10,9... | collective-permute-start | bytes 309512 | tf_op jit(solution)/shard_map/ppermute | solution.py:187
  19.4 7.4 %copy-start.90 = (s32[4]{0:T(128)S(1)}, s32[4]{0:T(128)}, u32[]{:S(2)}) copy-start(s32[4]{0:T(128)} %param.23) | copy-start | bytes 52
  24.2 6.5 %collective-permute-start.3 = (bf16[8,320,3]{1,0,2:T(8,128)(2,1)}, bf16[8,320,3]{1,0,2:T(8,128)(2,1)S(1)}, u32[]{:S(2)}, u32[]{:S(2)}) collective-permute-start(bf16[8,320,3]{1,0,2:T(8,128)(2,1)} %pad_maximum_fusion.4), channel_id=1, source_target_pairs={{0,1},{1,2},{2,3},{4,5},{5,6},{6,7},{8,9},{9,10},{10,11},{12,13},{... | collective-permute-start | bytes 46088 | tf_op jit(solution)/shard_map/ppermute | solution.py:18
  28.2 18.0 %copy-start.51 = (f32[512]{0:T(512)}, f32[512]{0:T(512)S(1)}, u32[]{:S(2)}) copy-start(f32[512]{0:T(512)S(1)} %get-tuple-element.182) | copy-start | bytes 6148
  28.2 18.1 %copy-start.53 = (f32[512]{0:T(512)}, f32[512]{0:T(512)S(1)}, u32[]{:S(2)}) copy-start(f32[512]{0:T(512)S(1)} %get-tuple-element.183) | copy-start | bytes 6148
  28.2 18.1 %copy-start.55 = (f32[512]{0:T(512)}, f32[512]{0:T(512)S(1)}, u32[]{:S(2)}) copy-start(f32[512]{0:T(512)S(1)} %get-tuple-element.184) | copy-start | bytes 6148
  33.8 5.4 %copy-start.57 = (f32[8,64]{1,0:T(8,128)}, f32[8,64]{1,0:T(8,128)S(1)}, u32[]{:S(2)}) copy-start(f32[8,64]{1,0:T(8,128)S(1)} %get-tuple-element.164) | copy-start | bytes 6148
  33.8 5.4 %copy-start.61 = (f32[8,64]{1,0:T(8,128)}, f32[8,64]{1,0:T(8,128)S(1)}, u32[]{:S(2)}) copy-start(f32[8,64]{1,0:T(8,128)S(1)} %get-tuple-element.162) | copy-start | bytes 6148
  38.1 74.3 %all-gather.3.cloned.1.call-start = ((), (), s32[]{:S(2)}) async-start(), calls=%async_computation.2 | async-start | bytes 4718592 | tf_op jit(solution)/shard_map/all_gather | solution.py:240
  39.3 5.6 %copy-start.82 = (s32[4]{0:T(128)S(1)}, s32[4]{0:T(128)}, u32[]{:S(2)}) copy-start(s32[4]{0:T(128)} %copy-done.81) | copy-start | bytes 52
  39.3 5.6 %copy-start.83 = (s32[4]{0:T(128)S(1)}, s32[4]{0:T(128)}, u32[]{:S(2)}) copy-start(s32[4]{0:T(128)} %get-tuple-element.121) | copy-start | bytes 52
  39.3 414.3 %reduce-scatter.3.cloned.1.call-start = ((), (), s32[]{:S(2)}) async-start(), calls=%async_computation.4 | async-start | bytes 4718592 | tf_op jit(solution)/shard_map/reduce_scatter | solution.py:277
  44.8 72.8 %copy-start.6 = (bf16[8,4,64,4,128]{4,3,2,1,0:T(4,128)(2,1)}, bf16[8,4,64,4,128]{4,3,2,1,0:T(4,128)(2,1)S(1)}, u32[]{:S(2)}) copy-start(bf16[8,4,64,4,128]{4,3,2,1,0:T(4,128)(2,1)S(1)} %reshape.358) | copy-start | bytes 6291460
  44.8 21.6 %copy-start.86 = (pred[4,4]{0,1:T(4,128)(4,1)}, pred[4,4]{0,1:T(4,128)(4,1)S(1)}, u32[]{:S(2)}) copy-start(pred[4,4]{0,1:T(4,128)(4,1)S(1)} %iota_compare_fusion.2) | copy-start | bytes 52
  44.9 21.3 %copy-start.69 = (f32[4,128]{1,0:T(4,128)}, f32[4,128]{1,0:T(4,128)S(1)}, u32[]{:S(2)}) copy-start(f32[4,128]{1,0:T(4,128)S(1)} %get-tuple-element.180) | copy-start | bytes 6148
  44.9 21.4 %copy-start.74 = (f32[4,128]{1,0:T(4,128)}, f32[4,128]{1,0:T(4,128)S(1)}, u32[]{:S(2)}) copy-start(f32[4,128]{1,0:T(4,128)S(1)} %get-tuple-element.181) | copy-start | bytes 6148
  46.2 12.1 %copy-start.38 = (f32[8,256]{1,0:T(8,128)}, f32[8,256]{1,0:T(8,128)S(1)}, u32[]{:S(2)}) copy-start(f32[8,256]{1,0:T(8,128)S(1)} %get-tuple-element.147) | copy-start | bytes 24580
  46.3 12.1 %copy-start.40 = (f32[8,256]{1,0:T(8,128)}, f32[8,256]{1,0:T(8,128)S(1)}, u32[]{:S(2)}) copy-start(f32[8,256]{1,0:T(8,128)S(1)} %get-tuple-element.148) | copy-start | bytes 24580
  46.3 12.1 %copy-start.42 = (f32[8,256]{1,0:T(8,128)}, f32[8,256]{1,0:T(8,128)S(1)}, u32[]{:S(2)}) copy-start(f32[8,256]{1,0:T(8,128)S(1)} %get-tuple-element.149) | copy-start | bytes 24580
  46.3 12.1 %copy-start.44 = (f32[8,256]{1,0:T(8,128)}, f32[8,256]{1,0:T(8,128)S(1)}, u32[]{:S(2)}) copy-start(f32[8,256]{1,0:T(8,128)S(1)} %get-tuple-element.150) | copy-start | bytes 24580
  58.4 7.0 %copy-start.67 = (bf16[8,4,512]{2,1,0:T(4,128)(2,1)S(1)}, bf16[8,4,512]{2,1,0:T(4,128)(2,1)}, u32[]{:S(2)}) copy-start(bf16[8,4,512]{2,1,0:T(4,128)(2,1)} %param.16) | copy-start | bytes 98308
  58.4 7.6 %copy-start.79 = (f32[4]{0:T(128)S(1)}, f32[4]{0:T(128)}, u32[]{:S(2)}) copy-start(f32[4]{0:T(128)} %get-tuple-element.120) | copy-start | bytes 52
  65.7 65.9 %copy-start.25 = (f32[8,4,4,128]{3,0,2,1:T(8,128)}, f32[8,4,4,128]{3,0,2,1:T(8,128)S(1)}, u32[]{:S(2)}) copy-start(f32[8,4,4,128]{3,0,2,1:T(8,128)S(1)} %fusion.108) | copy-start | bytes 196612
  66.4 12.0 %copy-start.28 = (f32[8,4,4,128]{3,2,1,0:T(4,128)}, f32[8,4,4,128]{3,2,1,0:T(4,128)S(1)}, u32[]{:S(2)}) copy-start(f32[8,4,4,128]{3,2,1,0:T(4,128)S(1)} %copy.372) | copy-start | bytes 196612
  66.9 111.0 %copy-start.46 = (f32[8,4]{1,0:T(8,128)}, f32[8,4]{1,0:T(8,128)S(1)}, u32[]{:S(2)}) copy-start(f32[8,4]{1,0:T(8,128)S(1)} %copy.380) | copy-start | bytes 388
  124.6 49.0 %collective-permute-start.4 = (f32[8,4,64,256]{3,2,1,0:T(8,128)}, f32[8,4,64,256]{3,2,1,0:T(8,128)S(1)}, u32[]{:S(2)}, u32[]{:S(2)}) collective-permute-start(f32[8,4,64,256]{3,2,1,0:T(8,128)} %broadcast_add_fusion), channel_id=1, source_target_pairs={{0,1},{1,2},{2,3},{4,5},{5,6},{6,7},{8,9},{9,10},{10,11},{12,13},{... | collective-permute-start | bytes 6291464 | tf_op jit(solution)/shard_map/ppermute | solution.py:18
  128.2 49.7 %collective-permute-start.5 = (f32[8,4,64,256]{3,2,1,0:T(8,128)}, f32[8,4,64,256]{3,2,1,0:T(8,128)}, u32[]{:S(2)}, u32[]{:S(2)}) collective-permute-start(f32[8,4,64,256]{3,2,1,0:T(8,128)} %fusion.82), channel_id=1, source_target_pairs={{1,0},{2,1},{3,2},{5,4},{6,5},{7,6},{9,8},{10,9},{11,10},{13,12},{... | collective-permute-start | bytes 6291464 | tf_op jit(solution)/shard_map/ppermute | solution.py:18
  129.7 53.9 %copy-start.88 = (pred[4,4]{0,1:T(4,128)(4,1)}, pred[4,4]{0,1:T(4,128)(4,1)S(1)}, u32[]{:S(2)}) copy-start(pred[4,4]{0,1:T(4,128)(4,1)S(1)} %copy.368) | copy-start | bytes 52
  130.6 53.0 %copy-start.71 = (f32[4,4]{1,0:T(4,128)}, f32[4,4]{1,0:T(4,128)S(1)}, u32[]{:S(2)}) copy-start(f32[4,4]{1,0:T(4,128)S(1)} %fusion.161) | copy-start | bytes 196
  132.3 51.3 %copy-start.59 = (f32[8,4]{1,0:T(8,128)}, f32[8,4]{1,0:T(8,128)S(1)}, u32[]{:S(2)}) copy-start(f32[8,4]{1,0:T(8,128)S(1)} %copy.377) | copy-start | bytes 388
  133.6 50.0 %copy-start.34 = (f32[4,8,4,4]{1,3,2,0:T(4,128)}, f32[4,8,4,4]{1,3,2,0:T(4,128)S(1)}, u32[]{:S(2)}) copy-start(f32[4,8,4,4]{1,3,2,0:T(4,128)S(1)} %get-tuple-element.172) | copy-start | bytes 6148
  134.6 55.4 %copy-start = (f32[8,256,512]{1,2,0:T(8,128)S(1)}, f32[8,256,512]{1,2,0:T(8,128)}, u32[]{:S(2)}) copy-start(f32[8,256,512]{1,2,0:T(8,128)} %copy.361) | copy-start | bytes 12582916
  134.6 55.4 %copy-start.1 = (f32[8,256,512]{1,2,0:T(8,128)S(1)}, f32[8,256,512]{1,2,0:T(8,128)}, u32[]{:S(2)}) copy-start(f32[8,256,512]{1,2,0:T(8,128)} %copy.363) | copy-start | bytes 12582916
  183.6 47.8 %collective-permute-start.6 = (f32[8,4,64,256]{3,2,1,0:T(8,128)}, f32[8,4,64,256]{3,2,1,0:T(8,128)}, u32[]{:S(2)}, u32[]{:S(2)}) collective-permute-start(f32[8,4,64,256]{3,2,1,0:T(8,128)} %get-tuple-element.179), channel_id=1, source_target_pairs={{0,1},{1,2},{2,3},{4,5},{5,6},{6,7},{8,9},{9,10},{10,11},{12,13},{... | collective-permute-start | bytes 6291464 | tf_op jit(solution)/shard_map/ppermute | solution.py:18
  188.2 48.6 %collective-permute-start.7 = (f32[8,4,64,256]{3,2,1,0:T(8,128)}, f32[8,4,64,256]{3,2,1,0:T(8,128)}, u32[]{:S(2)}, u32[]{:S(2)}) collective-permute-start(f32[8,4,64,256]{3,2,1,0:T(8,128)} %get-tuple-element.178), channel_id=1, source_target_pairs={{1,0},{2,1},{3,2},{5,4},{6,5},{7,6},{9,8},{10,9},{11,10},{13,12},{... | collective-permute-start | bytes 6291464 | tf_op jit(solution)/shard_map/ppermute | solution.py:18
  190.0 5.8 %copy-start.7 = (bf16[8,4,64,4,128]{4,3,2,1,0:T(4,128)(2,1)S(1)}, bf16[8,4,64,4,128]{4,3,2,1,0:T(4,128)(2,1)}, u32[]{:S(2)}) copy-start(bf16[8,4,64,4,128]{4,3,2,1,0:T(4,128)(2,1)} %copy-done.6) | copy-start | bytes 6291460
  190.0 5.8 %copy-start.30 = (f32[8,4,4,128]{3,2,1,0:T(4,128)S(1)}, f32[8,4,4,128]{3,2,1,0:T(4,128)}, u32[]{:S(2)}) copy-start(f32[8,4,4,128]{3,2,1,0:T(4,128)} %copy.388) | copy-start | bytes 196612
  195.8 7.5 %copy-start.4 = (f32[8,4,64,4,128]{4,3,2,1,0:T(4,128)S(1)}, f32[8,4,64,4,128]{4,3,2,1,0:T(4,128)}, u32[]{:S(2)}) copy-start(f32[8,4,64,4,128]{4,3,2,1,0:T(4,128)} %reshape.354) | copy-start | bytes 12582916
  195.8 57.2 %slice-start = ((s8[8388608]{0:T(1024)(128)(4,1)}), s8[4194304]{0:T(1024)(128)(4,1)S(1)}, s32[]{:S(2)}) async-start(s8[8388608]{0:T(1024)(128)(4,1)} %bitcast.248), calls=%async_computation.6 | async-start | bytes 8388608
  203.3 49.7 %copy-start.2 = (f32[8,4,4,64,256]{4,3,1,2,0:T(8,128)}, f32[8,4,4,64,256]{4,3,1,2,0:T(8,128)S(1)}, u32[]{:S(2)}) copy-start(f32[8,4,4,64,256]{4,3,1,2,0:T(8,128)S(1)} %fusion.60) | copy-start | bytes 25165828
  203.3 33.4 %copy-start.47 = (f32[8,4]{1,0:T(8,128)S(1)}, f32[8,4]{1,0:T(8,128)}, u32[]{:S(2)}) copy-start(f32[8,4]{1,0:T(8,128)} %copy-done.46) | copy-start | bytes 388
  203.4 33.4 %copy-start.60 = (f32[8,4]{1,0:T(8,128)S(1)}, f32[8,4]{1,0:T(8,128)}, u32[]{:S(2)}) copy-start(f32[8,4]{1,0:T(8,128)} %copy-done.59) | copy-start | bytes 388
  203.4 49.7 %slice-start.1 = ((s8[8388608]{0:T(1024)(128)(4,1)}), s8[4194304]{0:T(1024)(128)(4,1)S(1)}, s32[]{:S(2)}) async-start(s8[8388608]{0:T(1024)(128)(4,1)} %bitcast.248), calls=%async_computation.7 | async-start | bytes 8388608
  221.2 26.6 %copy-start.18 = (f32[8,4,128,128]{2,3,1,0:T(8,128)S(1)}, f32[8,4,128,128]{2,3,1,0:T(8,128)}, u32[]{:S(2)}) copy-start(f32[8,4,128,128]{2,3,1,0:T(8,128)} %get-tuple-element.100) | copy-start | bytes 6291460
  243.2 45.4 %collective-permute-start.8 = (f32[8,4,64,256]{3,2,1,0:T(8,128)}, f32[8,4,64,256]{3,2,1,0:T(8,128)}, u32[]{:S(2)}, u32[]{:S(2)}) collective-permute-start(f32[8,4,64,256]{3,2,1,0:T(8,128)} %get-tuple-element.177), channel_id=1, source_target_pairs={{0,1},{1,2},{2,3},{4,5},{5,6},{6,7},{8,9},{9,10},{10,11},{12,13},{... | collective-permute-start | bytes 6291464 | tf_op jit(solution)/shard_map/ppermute | solution.py:18
  246.6 47.4 %collective-permute-start.9 = (f32[8,4,64,256]{3,2,1,0:T(8,128)}, f32[8,4,64,256]{3,2,1,0:T(8,128)}, u32[]{:S(2)}, u32[]{:S(2)}) collective-permute-start(f32[8,4,64,256]{3,2,1,0:T(8,128)} %get-tuple-element.176), channel_id=1, source_target_pairs={{1,0},{2,1},{3,2},{5,4},{6,5},{7,6},{9,8},{10,9},{11,10},{13,12},{... | collective-permute-start | bytes 6291464 | tf_op jit(solution)/shard_map/ppermute | solution.py:18
  253.1 40.9 %copy-start.48 = (f32[8,4,4]{1,2,0:T(4,128)S(1)}, f32[8,4,4]{1,2,0:T(4,128)}, u32[]{:S(2)}) copy-start(f32[8,4,4]{1,2,0:T(4,128)} %copy.391) | copy-start | bytes 1540
  302.8 12.5 %copy-start.3 = (f32[8,4,4,64,256]{4,3,1,2,0:T(8,128)}, f32[8,4,4,64,256]{4,3,1,2,0:T(8,128)S(1)}, u32[]{:S(2)}) copy-start(f32[8,4,4,64,256]{4,3,1,2,0:T(8,128)S(1)} %get-tuple-element.134) | copy-start | bytes 25165828
  320.9 134.1 %reduce-scatter.5.cloned.1.call-start = ((), (), s32[]{:S(2)}) async-start(), calls=%async_computation.5 | async-start | bytes 4718592 | tf_op jit(solution)/shard_map/reduce_scatter | solution.py:278
  333.6 11.6 %copy-start.8 = (bf16[8,4,64,4,128]{4,3,2,1,0:T(4,128)(2,1)S(1)}, bf16[8,4,64,4,128]{4,3,2,1,0:T(4,128)(2,1)}, u32[]{:S(2)}) copy-start(bf16[8,4,64,4,128]{4,3,2,1,0:T(4,128)(2,1)} %copy-done.6) | copy-start | bytes 6291460
  333.6 11.6 %copy-start.31 = (f32[8,4,4,128]{3,2,1,0:T(4,128)S(1)}, f32[8,4,4,128]{3,2,1,0:T(4,128)}, u32[]{:S(2)}) copy-start(f32[8,4,4,128]{3,2,1,0:T(4,128)} %copy.388) | copy-start | bytes 196612
  359.2 5.6 %copy-start.35 = (f32[4,8,4,4]{1,3,2,0:T(4,128)S(1)}, f32[4,8,4,4]{1,3,2,0:T(4,128)}, u32[]{:S(2)}) copy-start(f32[4,8,4,4]{1,3,2,0:T(4,128)} %copy-done.34) | copy-start | bytes 6148
  359.2 5.6 %copy-start.87 = (pred[4,4]{0,1:T(4,128)(4,1)S(1)}, pred[4,4]{0,1:T(4,128)(4,1)}, u32[]{:S(2)}) copy-start(pred[4,4]{0,1:T(4,128)(4,1)} %copy-done.86) | copy-start | bytes 52
  364.9 15.0 %copy-start.26 = (f32[8,4,4,128]{3,0,2,1:T(8,128)S(1)}, f32[8,4,4,128]{3,0,2,1:T(8,128)}, u32[]{:S(2)}) copy-start(f32[8,4,4,128]{3,0,2,1:T(8,128)} %copy-done.25) | copy-start | bytes 196612
  364.9 15.0 %copy-start.70 = (f32[4,128]{1,0:T(4,128)S(1)}, f32[4,128]{1,0:T(4,128)}, u32[]{:S(2)}) copy-start(f32[4,128]{1,0:T(4,128)} %copy-done.69) | copy-start | bytes 6148
  415.4 5.5 %copy-start.45 = (f32[8,256]{1,0:T(8,128)S(1)}, f32[8,256]{1,0:T(8,128)}, u32[]{:S(2)}) copy-start(f32[8,256]{1,0:T(8,128)} %copy-done.44) | copy-start | bytes 24580
  427.3 8.0 %copy-start.23 = (f32[8,4,128,128]{2,3,1,0:T(8,128)S(1)}, f32[8,4,128,128]{2,3,1,0:T(8,128)}, u32[]{:S(2)}) copy-start(f32[8,4,128,128]{2,3,1,0:T(8,128)} %fusion.174) | copy-start | bytes 6291460
  450.9 5.4 %copy-start.21 = (f32[8,64,512]{2,1,0:T(8,128)S(1)}, f32[8,64,512]{2,1,0:T(8,128)}, u32[]{:S(2)}) copy-start(f32[8,64,512]{2,1,0:T(8,128)} %get-tuple-element.125) | copy-start | bytes 3145732
  450.9 5.4 %copy-start.58 = (f32[8,64]{1,0:T(8,128)S(1)}, f32[8,64]{1,0:T(8,128)}, u32[]{:S(2)}) copy-start(f32[8,64]{1,0:T(8,128)} %copy-done.57) | copy-start | bytes 6148
  460.3 7.7 %collective-permute-start.10 = (f32[8,320,3]{1,0,2:T(8,128)S(1)}, f32[8,320,3]{1,0,2:T(8,128)S(1)}, u32[]{:S(2)}, u32[]{:S(2)}) collective-permute-start(f32[8,320,3]{1,0,2:T(8,128)S(1)} %copy.414), channel_id=1, source_target_pairs={{1,0},{2,1},{3,2},{5,4},{6,5},{7,6},{9,8},{10,9},{11,10},{13,12},{... | collective-permute-start | bytes 92168 | tf_op jit(solution)/shard_map/ppermute | solution.py:18
  (46 other events, 121.5 us)
Sparse Core Ops, SparseCore 0:
  38.2 34.9 all-gather.4
  75.6 36.7 all-gather.2
  321.0 48.5 reduce-scatter.2
  380.3 48.6 reduce-scatter.4

commit v10 on v9

--- a/solution.py
+++ b/solution.py
@@ -236,8 +236,10 @@
         jnp.concatenate([b_in, c_in], axis=1).astype(jnp.float32),
         rim_chan.astype(jnp.float32),
     )
-    b_conv = lax.all_gather(bc_conv[:, :b_width], "seq", axis=1, tiled=True)
-    c_conv = lax.all_gather(bc_conv[:, b_width:], "seq", axis=1, tiled=True)
+    both_conv = lax.all_gather(
+        bc_conv.reshape(groups_here, 2, b_width, length), "seq", axis=2, tiled=True
+    )
+    b_conv, c_conv = (both_conv[:, 0], both_conv[:, 1])
 
     def local_terms(x_float, b_float, c_float, dt_float):
         return jax.vmap(scan_part, in_axes=(0, 0, 0, 0, 0, 0, 0, None))(

time: 484 us -> 498 us (1.029)
  local copies, waits for them, and re-layouts: 84.6 us -> 96.1 us
    slice x3, local copies, waits for them, and re-layouts: 2.31 us -> 18.9 us  [shards(): b_conv, c_conv = (both_conv[:, 0], both_conv[:, 1])]
    all_gather x2 -> x0, local copies, waits for them, and re-layouts: 10.5 us -> none  [the longest x1 5.26 us: shards(): c_conv = lax.all_gather(bc_conv[:, b_width:], 'seq', axis=1, tiled=True)]
    unnamed x196 -> x198, local copies, waits for them, and re-layouts: 16.8 us -> 18.6 us
    all_gather x2 -> x1, waiting for transfers between devices: 23.8 us -> 24.8 us  [shards(): lax.all_gather(bc_conv.reshape(groups_here, 2, b_width, length), 'seq', a...]
  transfers between devices with their start and end apart: 15 -> 14, of which waited for: 8 -> 7; matrix products, arithmetic and copies ran while one was open for 53% -> 47% of each run, Pallas kernels for 0% -> 0%
where the time goes in v10:
time: 498 us; the launch traced here: 493 us
  matrix products  141 us (28%)
  waiting for transfers between devices  107 us (21%)
  other arithmetic  106 us (21%)
  local copies, waits for them, and re-layouts  96.1 us (19%)
  starting transfers between devices  27.7 us (6%)
  between operations  15.6 us (3%)
    ppermute x8, waiting for transfers between devices, passed_along(): lax.ppermute(value, axis, [(source, source + steps) for source in range(f...  81.9 us
    dot_general x3, matrix products, span_terms(): jnp.einsum('hpcj,hcj,ncj->hcpn', weighted, keep_end, b_three, precision=p...  41.3 us
    dot_general x3, matrix products, span_terms(): jnp.einsum('hcij,hpcj->hpci', decay * scores[None], weighted, precision=p...  41.3 us
    dot_general x3, matrix products, assemble(): jnp.einsum('nci,hci,chpn->hpci', c_three, entry, starts, precision=precise)  32.7 us
    reduce_sum x2, other arithmetic, weighted_sum(): return jnp.sum(weight[..., None, None] * stacked, axis=-3)  26.7 us
    all_gather x1, waiting for transfers between devices, shards(): lax.all_gather(bc_conv.reshape(groups_here, 2, b_width, length), 'seq', a...  24.8 us
    ppermute x8, starting transfers between devices, passed_along(): lax.ppermute(value, axis, [(source, source + steps) for source in range(f...  19.9 us
    dot_general x3, matrix products, span_terms(): scores = jnp.einsum('nci,ncj->cij', c_three, b_three, precision=precise)  19.2 us
  transfers between devices with their start and end apart: 14, of which 7 were waited for; matrix products, arithmetic and copies ran while one was open for 47% of the time, Pallas kernels for 0%

profile of v10, /device:TPU:0, one launch (start us, length us, event | category | flops | bytes accessed | tf_op | source)
XLA Modules:
  0.0 492.7 jit_solution(4294659193348436283)
XLA Ops:
  9.1 3.1 collective-permute-start
  12.1 2.6 collective-permute-start.1
  16.1 3.3 copy.329
  19.4 1.7 copy.330
  21.2 1.7 copy.331
  24.2 2.6 collective-permute-start.3
  32.2 2.1 pad_maximum_fusion.3
  34.2 2.8 gather_fusion
  37.1 2.0 gather.7
  42.0 2.5 fusion.102
  44.9 2.7 convert_element_type.83
  47.6 2.6 reshape.354
  51.8 12.2 %fusion.50 = (f32[8,256,512]{2,1,0:T(8,128)}, f32[8,256,512]{2,1,0:T(8,128)}) fusion(f32[8,256,512]{2,1,0:T(8,128)} %convert_element_type.83, f32[8,256]{1,0:T(8,128)S(1)} %get-tuple-element.150, f32[512]{0:T(512)S(1)} %get-tuple-element.183, f32[8,256,3]{2,1,0:T(8,128)S(1)} %copy.332, f32[8,256]{1,0:T(8,128)S(1)} %get-tuple-element.148, ...), kind=kLoop, calls=%fused_computation.89 | loop fusion | flops 18874368 | bytes 12654592 | tf_op jit(solution)/shard_map/jvp(vmap(jit(silu)))/mul | solution.py:53
  64.0 5.3 %reshape.351 = f32[8,4,64,4,128]{4,3,2,1,0:T(4,128)} reshape(f32[8,256,512]{2,1,0:T(8,128)} %get-tuple-element.122) | data formatting | bytes 8388608 | tf_op jit(solution)/shard_map/jvp(vmap())/reshape | solution.py:59
  72.6 24.8 %all-gather.2.cloned.1.call-done = f32[8,2,256,512]{3,2,1,0:T(8,128)} async-done(((f32[8,2,32,512]{3,2,1,0:T(8,128)}), f32[8,2,256,512]{3,2,1,0:T(8,128)}) %all-gather.2.cloned.1.call-update) | async-done | bytes 8388624 | tf_op jit(solution)/shard_map/all_gather | solution.py:239
  97.3 8.2 %fusion.172 = (f32[8,1,256,512]{3,2,1,0:T(8,128)}, f32[8,1,256,512]{3,2,1,0:T(8,128)}) fusion(f32[8,2,256,512]{3,2,1,0:T(8,128)} %all-gather.2.cloned.1.call-done), kind=kLoop, calls=%fused_computation.318 | loop fusion | bytes 16777216 | tf_op jit(solution)/shard_map/slice | solution.py:242
  105.5 5.4 %copy.343 = f32[8,1,256,512]{2,3,0,1:T(8,128)} copy(f32[8,1,256,512]{3,2,1,0:T(8,128)} %get-tuple-element.126) | data formatting | bytes 8388608 | tf_op jit(solution)/shard_map/slice | solution.py:242
  110.9 5.4 %copy.342 = f32[8,1,256,512]{2,3,0,1:T(8,128)} copy(f32[8,1,256,512]{3,2,1,0:T(8,128)} %get-tuple-element.127) | data formatting | bytes 8388608 | tf_op jit(solution)/shard_map/slice | solution.py:242
  116.2 13.9 %multiply_reduce_fusion.5 = (f32[8,4,64,256]{3,2,1,0:T(8,128)S(1)}, f32[8,4,4,64,256]{4,3,1,2,0:T(8,128)}) fusion(f32[8,4,4]{1,2,0:T(4,128)S(1)} %copy.358, f32[8,256,4,128,1]{1,3,4,2,0:T(8,128)} %bitcast.245, f32[8,4,64,4,128]{4,3,2,1,0:T(4,128)} %reshape.351, f32[8,4,4,128]{3,2,1,0:T(4,128)S(1)} %copy.352, f32[8,4,4,128]{3,2,1,0:T(4,128)S(1)} %copy.335), kind=kOutput, calls=%fused_computation.26 | convolution fusion | flops 3226992640 | bytes 19005952 | tf_op jit(solution)/shard_map/jvp(vmap(hpcj,hcj,ncj->hcpn))/dot_general | solution.py:78
  130.2 1.7 broadcast_add_fusion
  131.9 2.0 copy-done
  133.9 5.6 %fusion.82 = f32[8,4,64,256]{3,2,1,0:T(8,128)} fusion(f32[8,256,4,128,1]{1,3,2,4,0:T(8,128)S(1)} %bitcast.241, f32[8,4,4,128]{3,2,1,0:T(4,128)S(1)} %copy.362, bf16[8,4,64,4,128]{4,3,2,1,0:T(4,128)(2,1)S(1)} %reshape.354), kind=kOutput, calls=%fused_computation.114 | convolution fusion | flops 3223322624 | bytes 8454144 | tf_op jit(solution)/shard_map/ghpci,ghci,gnci->ghpn/dot_general | solution.py:263
  139.5 3.5 collective-permute-start.4
  149.4 39.0 %collective-permute-done.4 = f32[8,4,64,256]{3,2,1,0:T(8,128)S(1)} collective-permute-done((f32[8,4,64,256]{3,2,1,0:T(8,128)}, f32[8,4,64,256]{3,2,1,0:T(8,128)S(1)}, u32[]{:S(2)}, u32[]{:S(2)}) %collective-permute-start.4) | collective-permute-done | bytes 2097184 | tf_op jit(solution)/shard_map/ppermute | solution.py:18
  188.4 4.2 collective-permute-done.5
  192.7 5.7 %multiply_add_fusion.2 = (f32[8,4,64,256]{3,2,1,0:T(8,128)}, f32[8,4,64,256]{3,2,1,0:T(8,128)}) fusion(f32[8,4,64,256]{3,2,1,0:T(8,128)} %fusion.82, f32[8,4,64,256]{3,2,1,0:T(8,128)} %collective-permute-done.5, f32[8,4]{1,0:T(8,128)S(1)} %copy.357, f32[8,4,64,256]{3,2,1,0:T(8,128)S(1)} %collective-permute-done.4, f32[8,4,64,256]{3,2,1,0:T(8,128)} %copy-done.15, ...), kind=kLoop, calls=%fused_computation.104 | loop fusion | flops 2621440 | bytes 12583168 | tf_op jit(solution)/shard_map/add | solution.py:31
  198.4 4.6 collective-permute-start.6
  203.0 1.7 collective-permute-start.7
  204.8 5.8 %fusion.174 = f32[8,4,128,128]{2,3,1,0:T(8,128)} fusion(f32[8,256,4,128]{1,3,2,0:T(8,128)S(1)} %bitcast.242, f32[8,256,4,128]{1,3,2,0:T(8,128)S(1)} %bitcast.248), kind=kOutput, calls=%fused_computation.320 | convolution fusion | flops 1610612736 | bytes 10485760 | tf_op jit(solution)/shard_map/jvp(vmap(nci,ncj->cij))/dot_general | solution.py:72
  210.6 7.5 %fusion.60 = f32[8,4,4,64,256]{4,3,1,2,0:T(8,128)S(1)} fusion(f32[8,256,4,128,1]{1,3,4,2,0:T(8,128)S(1)} %bitcast.243, f32[8,4,4,128]{3,2,1,0:T(4,128)S(1)} %copy-done.31, bf16[8,4,64,4,128]{4,3,2,1,0:T(4,128)(2,1)S(1)} %copy-done.8), kind=kOutput, calls=%fused_computation.98 | convolution fusion | flops 3223322624 | bytes 14745600 | tf_op jit(solution)/shard_map/transpose(jvp(vmap(nci,hci,chpn->hpci)))/dot_general | solution.py:149
  218.2 17.9 %fusion.104 = (f32[8,4,4,128]{3,2,1,0:T(4,128)}, f32[8,4,4,128]{3,2,1,0:T(4,128)}, f32[8,4,128,128]{2,3,1,0:T(8,128)}) fusion(f32[8,4,4,128]{3,2,1,0:T(4,128)} %copy.338, f32[4,128,128]{1,2,0:T(8,128)} %compare_select_fusion, f32[8,4,128,128]{2,3,1,0:T(8,128)} %fusion.174, bf16[8,4,4,64,128]{4,2,3,1,0:T(4,128)(2,1)} %bitcast.251, ...), kind=kOutput, calls=%fused_computation.150 | convolution fusion | flops 1642561536 | bytes 11010048 | tf_op jit(solution)/shard_map/transpose(jvp(vmap(hcij,hpcj->hpci)))/dot_general | solution.py:74
  236.0 10.1 %collective-permute-done.6 = f32[8,4,64,256]{3,2,1,0:T(8,128)} collective-permute-done((f32[8,4,64,256]{3,2,1,0:T(8,128)}, f32[8,4,64,256]{3,2,1,0:T(8,128)}, u32[]{:S(2)}, u32[]{:S(2)}) %collective-permute-start.6) | collective-permute-done | bytes 2097184 | tf_op jit(solution)/shard_map/ppermute | solution.py:18
  246.2 5.4 %collective-permute-done.7 = f32[8,4,64,256]{3,2,1,0:T(8,128)} collective-permute-done((f32[8,4,64,256]{3,2,1,0:T(8,128)}, f32[8,4,64,256]{3,2,1,0:T(8,128)}, u32[]{:S(2)}, u32[]{:S(2)}) %collective-permute-start.7) | collective-permute-done | bytes 2097184 | tf_op jit(solution)/shard_map/ppermute | solution.py:18
  251.6 6.4 %multiply_add_fusion = (f32[8,4,64,256]{3,2,1,0:T(8,128)}, f32[8,4,64,256]{3,2,1,0:T(8,128)}) fusion(f32[8,4,64,256]{3,2,1,0:T(8,128)} %fusion.82, f32[8,4,64,256]{3,2,1,0:T(8,128)} %collective-permute-done.7, f32[8,4]{1,0:T(8,128)S(1)} %copy-done.61, f32[8,4,64,256]{3,2,1,0:T(8,128)} %collective-permute-done.6, f32[8,4,64,256]{3,2,1,0:T(8,128)} %copy-done.15, ...), kind=kLoop, calls=%fused_computation.102 | loop fusion | flops 2621440 | bytes 12583168 | tf_op jit(solution)/shard_map/add | solution.py:31
  257.9 3.4 collective-permute-start.8
  262.6 5.2 %fusion.175 = f32[8,4,128,256]{3,2,1,0:T(8,128)} fusion(f32[8,4,128,128]{2,3,1,0:T(8,128)S(1)} %copy-done.19, f32[8,256,4,128]{1,3,2,0:T(8,128)S(1)} %bitcast.244), kind=kOutput, calls=%fused_computation.321 | convolution fusion | flops 1610612736 | bytes 10485760 | tf_op jit(solution)/shard_map/transpose(jvp(vmap(nci,ncj->cij)))/dot_general | solution.py:72
  267.8 17.8 %multiply_reduce_fusion = (f32[8,4,4,4]{3,2,1,0:T(4,128)}, f32[8,4,4,64,256]{4,3,2,1,0:T(8,128)}, f32[8,4,4,64,256]{4,3,2,1,0:T(8,128)}) fusion(f32[8,4,4,4]{3,2,1,0:T(4,128)S(1)} %bitcast_multiply_fusion.8, f32[8,4,4,64,256]{4,3,1,2,0:T(8,128)S(1)} %bitcast.250, f32[8,4,4,64,256]{4,3,1,2,0:T(8,128)S(1)} %fusion.60), kind=kLoop, calls=%fused_computation.3 | loop fusion | flops 46136832 | bytes 33558528 | tf_op jit(solution)/shard_map/transpose(jvp(vmap()))/reduce_sum | solution.py:131
  285.6 17.7 %collective-permute-done.8 = f32[8,4,64,256]{3,2,1,0:T(8,128)} collective-permute-done((f32[8,4,64,256]{3,2,1,0:T(8,128)}, f32[8,4,64,256]{3,2,1,0:T(8,128)}, u32[]{:S(2)}, u32[]{:S(2)}) %collective-permute-start.8) | collective-permute-done | bytes 2097184 | tf_op jit(solution)/shard_map/ppermute | solution.py:18
  303.3 5.4 %collective-permute-done.9 = f32[8,4,64,256]{3,2,1,0:T(8,128)} collective-permute-done((f32[8,4,64,256]{3,2,1,0:T(8,128)}, f32[8,4,64,256]{3,2,1,0:T(8,128)}, u32[]{:S(2)}, u32[]{:S(2)}) %collective-permute-start.9) | collective-permute-done | bytes 2097184 | tf_op jit(solution)/shard_map/ppermute | solution.py:18
  308.7 8.9 %multiply_reduce_fusion.4 = (f32[8,4,4]{1,2,0:T(4,128)}, f32[8,4,4,64,256]{4,3,1,2,0:T(8,128)S(1)}) fusion(f32[8,4,4,64,256]{4,3,1,2,0:T(8,128)} %get-tuple-element.188, f32[8,4,64,256]{3,2,1,0:T(8,128)} %collective-permute-done.9, f32[8,4,4,64,256]{4,3,2,1,0:T(8,128)} %get-tuple-element.103, f32[8,4,4]{1,2,0:T(4,128)S(1)} %copy-done.49), kind=kLoop, calls=%fused_computation.25 | loop fusion | flops 8388480 | bytes 27264000 | tf_op jit(solution)/shard_map/transpose(jvp(vmap()))/reduce_sum | solution.py:131
  317.6 12.4 %bitcast_add_fusion.2 = f32[8,256,4,128]{1,3,2,0:T(8,128)} fusion(f32[8,4,128,256]{3,2,1,0:T(8,128)} %fusion.175, f32[8,4,4,64,256]{4,3,1,2,0:T(8,128)S(1)} %get-tuple-element.136, f32[8,4,64,4,128]{4,3,2,1,0:T(4,128)S(1)} %copy-done.5, f32[8,4,4,128]{3,2,1,0:T(4,128)} %copy-done.29, f32[8,4,4,128]{3,2,1,0:T(4,128)S(1)} %copy.335), kind=kOutput, calls=%fused_computation.60 | convolution fusion | flops 3224371200 | bytes 21102592 | tf_op jit(solution)/shard_map/transpose(jvp(vmap(hpcj,hcj,ncj->hcpn)))/dot_general | solution.py:78
  330.1 5.4 %copy.386 = f32[8,256,512]{2,1,0:T(8,128)} copy(f32[8,256,512]{1,2,0:T(8,128)} %bitcast.253) | data formatting | bytes 8388608 | tf_op jit(solution)/shard_map/transpose(jvp(vmap()))/reshape | solution.py:60
  337.1 8.3 %fusion.176 = f32[8,4,128,256]{3,2,1,0:T(8,128)} fusion(f32[8,4,128,128]{2,3,1,0:T(8,128)S(1)} %copy-done.20, f32[8,256,4,128]{1,3,2,0:T(8,128)} %bitcast.246), kind=kOutput, calls=%fused_computation.322 | convolution fusion | flops 1610612736 | bytes 10485760 | tf_op jit(solution)/shard_map/transpose(jvp(vmap(nci,ncj->cij)))/dot_general | solution.py:72
  345.4 2.7 multiply_reduce_fusion.6
  348.2 11.5 %multiply_reduce_fusion.3 = (f32[8,4,4]{1,2,0:T(4,128)S(1)}, f32[8,4,4,64,256]{4,3,1,2,0:T(8,128)}) fusion(f32[8,4,4,64,256]{4,3,1,2,0:T(8,128)} %copy-done.3, f32[8,4,64,256]{3,2,1,0:T(8,128)} %collective-permute-done.8, f32[8,4,4]{1,2,0:T(4,128)S(1)} %copy.356, f32[8,4,4,64,256]{4,3,2,1,0:T(8,128)} %get-tuple-element.102), kind=kLoop, calls=%fused_computation.24 | loop fusion | flops 8388480 | bytes 27264000 | tf_op jit(solution)/shard_map/transpose(jvp(vmap()))/reduce_sum | solution.py:142
  359.9 14.0 %bitcast_add_fusion.3 = f32[8,4,128,256]{3,2,1,0:T(8,128)} fusion(f32[8,4,128,256]{3,2,1,0:T(8,128)} %fusion.176, f32[8,4,4,64,256]{4,3,1,2,0:T(8,128)} %get-tuple-element.138, f32[8,4,4,128]{3,2,1,0:T(4,128)S(1)} %copy-done.32, bf16[8,4,64,4,128]{4,3,2,1,0:T(4,128)(2,1)S(1)} %copy-done.9), kind=kOutput, calls=%fused_computation.61 | convolution fusion | flops 3224371200 | bytes 18939904 | tf_op jit(solution)/shard_map/transpose(jvp(vmap(nci,hci,chpn->hpci)))/dot_general | solution.py:149
  373.8 5.5 %copy.391 = f32[8,256,512]{2,1,0:T(8,128)} copy(f32[8,256,512]{1,2,0:T(8,128)} %bitcast.254) | data formatting | bytes 8388608 | tf_op jit(solution)/shard_map/transpose(jvp(vmap()))/reshape | solution.py:61
  379.5 15.0 %fusion.38 = (f32[8,4,4,128]{3,2,1,0:T(4,128)S(1)}, f32[8,4,4,64,128]{4,3,1,2,0:T(8,128)}) fusion(f32[8,4,64,4,128]{4,3,2,1,0:T(4,128)} %reshape.351, f32[8,4,4,128]{3,2,1,0:T(4,128)S(1)} %copy.335, f32[8,4,4,64,256]{4,3,1,2,0:T(8,128)} %copy-done.4, f32[8,256,4,128,1]{1,3,2,4,0:T(8,128)} %bitcast.247), kind=kOutput, calls=%fused_computation.69 | convolution fusion | flops 3224354816 | bytes 21102592 | tf_op jit(solution)/shard_map/transpose(jvp(vmap(hpcj,hcj,ncj->hcpn)))/dot_general | solution.py:78
  395.8 13.6 %fusion.36 = (f32[8,4,4,128]{3,2,1,0:T(4,128)S(1)}, f32[8,4,64,4,128]{4,2,3,1,0:T(8,128)}) fusion(f32[8,4,64,4,128]{4,3,2,1,0:T(4,128)} %reshape.351, f32[8,4,4,128]{3,2,1,0:T(4,128)S(1)} %copy.335, bf16[8,4,64,4,128]{4,3,2,1,0:T(4,128)(2,1)S(1)} %copy-done.9, f32[8,4]{1,0:T(8,128)S(1)} %constant_dynamic-slice_fusion, ...), kind=kOutput, calls=%fused_computation.65 | convolution fusion | flops 1627373568 | bytes 19398784 | tf_op jit(solution)/shard_map/transpose(jvp(vmap(hcij,hpcj->hpci)))/dot_general | solution.py:74
  409.5 11.3 %fusion.16 = f32[8,4,4,64,128]{4,3,2,1,0:T(8,128)S(1)} fusion(f32[8,256,4,128,1]{1,3,4,2,0:T(8,128)} %bitcast.240, f32[8,4,4,64,256]{4,3,1,2,0:T(8,128)} %get-tuple-element.138), kind=kOutput, calls=%fused_computation.29 | convolution fusion | flops 3221225472 | bytes 16777216 | tf_op jit(solution)/shard_map/jvp(vmap(nci,hci,chpn->hpci))/dot_general | solution.py:149
  424.7 5.7 %copy.381 = f32[8,4,64,4,128]{4,3,2,1,0:T(4,128)} copy(f32[8,4,64,4,128]{4,2,3,1,0:T(8,128)S(1)} %copy-done.23) | data formatting | bytes 8388608 | tf_op jit(solution)/shard_map/transpose(jvp(vmap()))/add_any | solution.py:73
  430.4 5.6 %reshape.357 = f32[8,256,512]{2,1,0:T(8,128)} reshape(f32[8,4,64,4,128]{4,3,2,1,0:T(4,128)} %copy.381) | data formatting | bytes 8388608 | tf_op jit(solution)/shard_map/transpose(jvp(vmap()))/reshape | solution.py:59
  436.0 4.3 broadcast_multiply_fusion
  442.3 4.6 pad_add_fusion
  447.0 3.3 split.16
  450.3 1.7 copy-done.17
  451.9 9.7 %fusion.39 = bf16[8,4,64,4,128]{4,2,3,1,0:T(8,128)(2,1)S(1)} fusion(f32[8,4,4,64,128]{4,3,2,1,0:T(8,128)S(1)} %copy-done.17, f32[8,4,64,4,128]{4,3,2,1,0:T(4,128)S(1)} %copy-done.6, f32[8,4,128,128]{2,3,1,0:T(8,128)S(1)} %copy-done.24, f32[4,128,128]{1,2,0:T(8,128)S(1)} %copy-done.38, f32[8,4,4,128]{3,2,1,0:T(4,128)S(1)} %copy-done.51, ...), kind=kOutput, calls=%fused_computation.71 | convolution fusion | flops 1625292800 | bytes 13041792 | tf_op jit(solution)/shard_map/jvp(vmap(hcij,hpcj->hpci))/dot_general | solution.py:74
  461.7 2.0 copy.369
  463.6 2.2 convert_element_type.96
  465.9 2.6 pad_add_fusion.3
  474.7 1.6 collective-permute-start.10
  476.3 2.9 slice_maximum_fusion
  480.6 1.8 copy.393
  484.2 1.5 slice.269
  (332 shorter events, 43.9 us)
Async XLA Ops:
  7.2 14.0 %copy-start.28 = (bf16[8,32,512]{2,1,0:T(8,128)(2,1)S(1)}, bf16[8,32,512]{2,1,0:T(8,128)(2,1)}, u32[]{:S(2)}) copy-start(bf16[8,32,512]{2,1,0:T(8,128)(2,1)} %param.15) | copy-start | bytes 786436
  7.2 90.2 %all-gather.2.cloned.1.call-start = ((), (), s32[]{:S(2)}) async-start(), calls=%async_computation.2 | async-start | bytes 9437184 | tf_op jit(solution)/shard_map/all_gather | solution.py:239
  9.1 23.1 %collective-permute-start = (f32[2,12896]{1,0:T(2,128)S(1)}, f32[2,12896]{1,0:T(2,128)}, u32[]{:S(2)}, u32[]{:S(2)}) collective-permute-start(f32[2,12896]{1,0:T(2,128)S(1)} %concatenate.39), channel_id=1, source_target_pairs={{0,1},{1,2},{2,3},{3,0},{4,5},{5,6},{6,7},{7,4},{8,9},{9,10},{10,1... | collective-permute-start | bytes 309512 | tf_op jit(solution)/shard_map/ppermute | solution.py:187
  12.1 20.0 %collective-permute-start.1 = (f32[2,12896]{1,0:T(2,128)S(1)}, f32[2,12896]{1,0:T(2,128)}, u32[]{:S(2)}, u32[]{:S(2)}) collective-permute-start(f32[2,12896]{1,0:T(2,128)S(1)} %concatenate.39), channel_id=1, source_target_pairs={{0,2},{1,3},{2,0},{3,1},{4,6},{5,7},{6,4},{7,5},{8,10},{9,11},{10,... | collective-permute-start | bytes 309512 | tf_op jit(solution)/shard_map/ppermute | solution.py:187
  14.7 17.4 %collective-permute-start.2 = (f32[2,12896]{1,0:T(2,128)S(1)}, f32[2,12896]{1,0:T(2,128)}, u32[]{:S(2)}, u32[]{:S(2)}) collective-permute-start(f32[2,12896]{1,0:T(2,128)S(1)} %concatenate.39), channel_id=1, source_target_pairs={{0,3},{1,0},{2,1},{3,2},{4,7},{5,4},{6,5},{7,6},{8,11},{9,8},{10,9... | collective-permute-start | bytes 309512 | tf_op jit(solution)/shard_map/ppermute | solution.py:187
  19.4 7.4 %copy-start.91 = (s32[4]{0:T(128)S(1)}, s32[4]{0:T(128)}, u32[]{:S(2)}) copy-start(s32[4]{0:T(128)} %param.23) | copy-start | bytes 52
  24.2 7.7 %collective-permute-start.3 = (bf16[8,320,3]{1,0,2:T(8,128)(2,1)}, bf16[8,320,3]{1,0,2:T(8,128)(2,1)S(1)}, u32[]{:S(2)}, u32[]{:S(2)}) collective-permute-start(bf16[8,320,3]{1,0,2:T(8,128)(2,1)} %pad_maximum_fusion.4), channel_id=1, source_target_pairs={{0,1},{1,2},{2,3},{4,5},{5,6},{6,7},{8,9},{9,10},{10,11},{12,13},{... | collective-permute-start | bytes 46088 | tf_op jit(solution)/shard_map/ppermute | solution.py:18
  28.2 23.5 %copy-start.52 = (f32[512]{0:T(512)}, f32[512]{0:T(512)S(1)}, u32[]{:S(2)}) copy-start(f32[512]{0:T(512)S(1)} %get-tuple-element.182) | copy-start | bytes 6148
  28.2 23.5 %copy-start.54 = (f32[512]{0:T(512)}, f32[512]{0:T(512)S(1)}, u32[]{:S(2)}) copy-start(f32[512]{0:T(512)S(1)} %get-tuple-element.183) | copy-start | bytes 6148
  28.2 23.5 %copy-start.56 = (f32[512]{0:T(512)}, f32[512]{0:T(512)S(1)}, u32[]{:S(2)}) copy-start(f32[512]{0:T(512)S(1)} %get-tuple-element.184) | copy-start | bytes 6148
  32.2 12.7 %copy-start.21 = (bf16[8,256,512]{2,1,0:T(8,128)(2,1)S(1)}, bf16[8,256,512]{2,1,0:T(8,128)(2,1)}, u32[]{:S(2)}) copy-start(bf16[8,256,512]{2,1,0:T(8,128)(2,1)} %param.13) | copy-start | bytes 6291460
  42.0 5.6 %copy-start.58 = (f32[8,64]{1,0:T(8,128)}, f32[8,64]{1,0:T(8,128)S(1)}, u32[]{:S(2)}) copy-start(f32[8,64]{1,0:T(8,128)S(1)} %get-tuple-element.164) | copy-start | bytes 6148
  42.0 5.6 %copy-start.62 = (f32[8,64]{1,0:T(8,128)}, f32[8,64]{1,0:T(8,128)S(1)}, u32[]{:S(2)}) copy-start(f32[8,64]{1,0:T(8,128)S(1)} %get-tuple-element.162) | copy-start | bytes 6148
  44.6 5.7 %copy-start.83 = (s32[4]{0:T(128)S(1)}, s32[4]{0:T(128)}, u32[]{:S(2)}) copy-start(s32[4]{0:T(128)} %copy-done.82) | copy-start | bytes 52
  44.6 5.7 %copy-start.84 = (s32[4]{0:T(128)S(1)}, s32[4]{0:T(128)}, u32[]{:S(2)}) copy-start(s32[4]{0:T(128)} %get-tuple-element.121) | copy-start | bytes 52
  44.6 423.9 %reduce-scatter.3.cloned.1.call-start = ((), (), s32[]{:S(2)}) async-start(), calls=%async_computation.3 | async-start | bytes 4718592 | tf_op jit(solution)/shard_map/reduce_scatter | solution.py:279
  50.2 81.6 %copy-start.7 = (bf16[8,4,64,4,128]{4,3,2,1,0:T(4,128)(2,1)}, bf16[8,4,64,4,128]{4,3,2,1,0:T(4,128)(2,1)S(1)}, u32[]{:S(2)}) copy-start(bf16[8,4,64,4,128]{4,3,2,1,0:T(4,128)(2,1)S(1)} %reshape.354) | copy-start | bytes 6291460
  50.2 21.9 %copy-start.87 = (pred[4,4]{0,1:T(4,128)(4,1)}, pred[4,4]{0,1:T(4,128)(4,1)S(1)}, u32[]{:S(2)}) copy-start(pred[4,4]{0,1:T(4,128)(4,1)S(1)} %iota_compare_fusion.2) | copy-start | bytes 52
  50.4 21.6 %copy-start.70 = (f32[4,128]{1,0:T(4,128)}, f32[4,128]{1,0:T(4,128)S(1)}, u32[]{:S(2)}) copy-start(f32[4,128]{1,0:T(4,128)S(1)} %get-tuple-element.180) | copy-start | bytes 6148
  50.4 21.6 %copy-start.75 = (f32[4,128]{1,0:T(4,128)}, f32[4,128]{1,0:T(4,128)S(1)}, u32[]{:S(2)}) copy-start(f32[4,128]{1,0:T(4,128)S(1)} %get-tuple-element.181) | copy-start | bytes 6148
  51.7 12.3 %copy-start.39 = (f32[8,256]{1,0:T(8,128)}, f32[8,256]{1,0:T(8,128)S(1)}, u32[]{:S(2)}) copy-start(f32[8,256]{1,0:T(8,128)S(1)} %get-tuple-element.147) | copy-start | bytes 24580
  51.7 12.3 %copy-start.41 = (f32[8,256]{1,0:T(8,128)}, f32[8,256]{1,0:T(8,128)S(1)}, u32[]{:S(2)}) copy-start(f32[8,256]{1,0:T(8,128)S(1)} %get-tuple-element.148) | copy-start | bytes 24580
  51.7 12.3 %copy-start.43 = (f32[8,256]{1,0:T(8,128)}, f32[8,256]{1,0:T(8,128)S(1)}, u32[]{:S(2)}) copy-start(f32[8,256]{1,0:T(8,128)S(1)} %get-tuple-element.149) | copy-start | bytes 24580
  51.7 12.3 %copy-start.45 = (f32[8,256]{1,0:T(8,128)}, f32[8,256]{1,0:T(8,128)S(1)}, u32[]{:S(2)}) copy-start(f32[8,256]{1,0:T(8,128)S(1)} %get-tuple-element.150) | copy-start | bytes 24580
  64.0 7.0 %copy-start.68 = (bf16[8,4,512]{2,1,0:T(4,128)(2,1)S(1)}, bf16[8,4,512]{2,1,0:T(4,128)(2,1)}, u32[]{:S(2)}) copy-start(bf16[8,4,512]{2,1,0:T(4,128)(2,1)} %param.16) | copy-start | bytes 98308
  64.0 7.6 %copy-start.80 = (f32[4]{0:T(128)S(1)}, f32[4]{0:T(128)}, u32[]{:S(2)}) copy-start(f32[4]{0:T(128)} %get-tuple-element.120) | copy-start | bytes 52
  71.4 75.0 %copy-start.26 = (f32[8,4,4,128]{3,0,2,1:T(8,128)}, f32[8,4,4,128]{3,0,2,1:T(8,128)S(1)}, u32[]{:S(2)}) copy-start(f32[8,4,4,128]{3,0,2,1:T(8,128)S(1)} %fusion.108) | copy-start | bytes 196612
  72.1 44.1 %copy-start.29 = (f32[8,4,4,128]{3,2,1,0:T(4,128)}, f32[8,4,4,128]{3,2,1,0:T(4,128)S(1)}, u32[]{:S(2)}) copy-start(f32[8,4,4,128]{3,2,1,0:T(4,128)S(1)} %copy.352) | copy-start | bytes 196612
  72.5 120.2 %copy-start.47 = (f32[8,4]{1,0:T(8,128)}, f32[8,4]{1,0:T(8,128)S(1)}, u32[]{:S(2)}) copy-start(f32[8,4]{1,0:T(8,128)S(1)} %copy.360) | copy-start | bytes 388
  130.2 9.3 %copy-start.15 = (f32[8,4,64,256]{3,2,1,0:T(8,128)}, f32[8,4,64,256]{3,2,1,0:T(8,128)S(1)}, u32[]{:S(2)}) copy-start(f32[8,4,64,256]{3,2,1,0:T(8,128)S(1)} %get-tuple-element.187) | copy-start | bytes 6291460
  139.5 49.0 %collective-permute-start.4 = (f32[8,4,64,256]{3,2,1,0:T(8,128)}, f32[8,4,64,256]{3,2,1,0:T(8,128)S(1)}, u32[]{:S(2)}, u32[]{:S(2)}) collective-permute-start(f32[8,4,64,256]{3,2,1,0:T(8,128)} %broadcast_add_fusion), channel_id=1, source_target_pairs={{0,1},{1,2},{2,3},{4,5},{5,6},{6,7},{8,9},{9,10},{10,11},{12,13},{... | collective-permute-start | bytes 6291464 | tf_op jit(solution)/shard_map/ppermute | solution.py:18
  143.0 49.7 %collective-permute-start.5 = (f32[8,4,64,256]{3,2,1,0:T(8,128)}, f32[8,4,64,256]{3,2,1,0:T(8,128)}, u32[]{:S(2)}, u32[]{:S(2)}) collective-permute-start(f32[8,4,64,256]{3,2,1,0:T(8,128)} %fusion.82), channel_id=1, source_target_pairs={{1,0},{2,1},{3,2},{5,4},{6,5},{7,6},{9,8},{10,9},{11,10},{13,12},{... | collective-permute-start | bytes 6291464 | tf_op jit(solution)/shard_map/ppermute | solution.py:18
  144.5 53.9 %copy-start.89 = (pred[4,4]{0,1:T(4,128)(4,1)}, pred[4,4]{0,1:T(4,128)(4,1)S(1)}, u32[]{:S(2)}) copy-start(pred[4,4]{0,1:T(4,128)(4,1)S(1)} %copy.348) | copy-start | bytes 52
  145.4 53.0 %copy-start.72 = (f32[4,4]{1,0:T(4,128)}, f32[4,4]{1,0:T(4,128)S(1)}, u32[]{:S(2)}) copy-start(f32[4,4]{1,0:T(4,128)S(1)} %fusion.161) | copy-start | bytes 196
  147.1 51.3 %copy-start.60 = (f32[8,4]{1,0:T(8,128)}, f32[8,4]{1,0:T(8,128)S(1)}, u32[]{:S(2)}) copy-start(f32[8,4]{1,0:T(8,128)S(1)} %copy.357) | copy-start | bytes 388
  148.4 50.0 %copy-start.35 = (f32[4,8,4,4]{1,3,2,0:T(4,128)}, f32[4,8,4,4]{1,3,2,0:T(4,128)S(1)}, u32[]{:S(2)}) copy-start(f32[4,8,4,4]{1,3,2,0:T(4,128)S(1)} %get-tuple-element.172) | copy-start | bytes 6148
  149.4 55.3 %copy-start.1 = (f32[8,1,256,512]{2,3,0,1:T(8,128)S(1)}, f32[8,1,256,512]{2,3,0,1:T(8,128)}, u32[]{:S(2)}) copy-start(f32[8,1,256,512]{2,3,0,1:T(8,128)} %copy.342) | copy-start | bytes 12582916
  149.4 55.3 %copy-start.2 = (f32[8,1,256,512]{2,3,0,1:T(8,128)S(1)}, f32[8,1,256,512]{2,3,0,1:T(8,128)}, u32[]{:S(2)}) copy-start(f32[8,1,256,512]{2,3,0,1:T(8,128)} %copy.343) | copy-start | bytes 12582916
  198.4 47.7 %collective-permute-start.6 = (f32[8,4,64,256]{3,2,1,0:T(8,128)}, f32[8,4,64,256]{3,2,1,0:T(8,128)}, u32[]{:S(2)}, u32[]{:S(2)}) collective-permute-start(f32[8,4,64,256]{3,2,1,0:T(8,128)} %get-tuple-element.179), channel_id=1, source_target_pairs={{0,1},{1,2},{2,3},{4,5},{5,6},{6,7},{8,9},{9,10},{10,11},{12,13},{... | collective-permute-start | bytes 6291464 | tf_op jit(solution)/shard_map/ppermute | solution.py:18
  203.0 48.6 %collective-permute-start.7 = (f32[8,4,64,256]{3,2,1,0:T(8,128)}, f32[8,4,64,256]{3,2,1,0:T(8,128)}, u32[]{:S(2)}, u32[]{:S(2)}) collective-permute-start(f32[8,4,64,256]{3,2,1,0:T(8,128)} %get-tuple-element.178), channel_id=1, source_target_pairs={{1,0},{2,1},{3,2},{5,4},{6,5},{7,6},{9,8},{10,9},{11,10},{13,12},{... | collective-permute-start | bytes 6291464 | tf_op jit(solution)/shard_map/ppermute | solution.py:18
  204.8 5.8 %copy-start.8 = (bf16[8,4,64,4,128]{4,3,2,1,0:T(4,128)(2,1)S(1)}, bf16[8,4,64,4,128]{4,3,2,1,0:T(4,128)(2,1)}, u32[]{:S(2)}) copy-start(bf16[8,4,64,4,128]{4,3,2,1,0:T(4,128)(2,1)} %copy-done.7) | copy-start | bytes 6291460
  204.8 5.8 %copy-start.31 = (f32[8,4,4,128]{3,2,1,0:T(4,128)S(1)}, f32[8,4,4,128]{3,2,1,0:T(4,128)}, u32[]{:S(2)}) copy-start(f32[8,4,4,128]{3,2,1,0:T(4,128)} %copy.368) | copy-start | bytes 196612
  210.6 7.5 %copy-start.5 = (f32[8,4,64,4,128]{4,3,2,1,0:T(4,128)S(1)}, f32[8,4,64,4,128]{4,3,2,1,0:T(4,128)}, u32[]{:S(2)}) copy-start(f32[8,4,64,4,128]{4,3,2,1,0:T(4,128)} %reshape.351) | copy-start | bytes 12582916
  210.6 57.2 %slice-start = ((s8[8388608]{0:T(1024)(128)(4,1)}), s8[4194304]{0:T(1024)(128)(4,1)S(1)}, s32[]{:S(2)}) async-start(s8[8388608]{0:T(1024)(128)(4,1)} %bitcast.249), calls=%async_computation.5 | async-start | bytes 8388608
  218.1 49.7 %copy-start.3 = (f32[8,4,4,64,256]{4,3,1,2,0:T(8,128)}, f32[8,4,4,64,256]{4,3,1,2,0:T(8,128)S(1)}, u32[]{:S(2)}) copy-start(f32[8,4,4,64,256]{4,3,1,2,0:T(8,128)S(1)} %fusion.60) | copy-start | bytes 25165828
  218.1 33.4 %copy-start.48 = (f32[8,4]{1,0:T(8,128)S(1)}, f32[8,4]{1,0:T(8,128)}, u32[]{:S(2)}) copy-start(f32[8,4]{1,0:T(8,128)} %copy-done.47) | copy-start | bytes 388
  218.1 33.4 %copy-start.61 = (f32[8,4]{1,0:T(8,128)S(1)}, f32[8,4]{1,0:T(8,128)}, u32[]{:S(2)}) copy-start(f32[8,4]{1,0:T(8,128)} %copy-done.60) | copy-start | bytes 388
  218.1 49.7 %slice-start.1 = ((s8[8388608]{0:T(1024)(128)(4,1)}), s8[4194304]{0:T(1024)(128)(4,1)S(1)}, s32[]{:S(2)}) async-start(s8[8388608]{0:T(1024)(128)(4,1)} %bitcast.249), calls=%async_computation.6 | async-start | bytes 8388608
  236.0 26.6 %copy-start.19 = (f32[8,4,128,128]{2,3,1,0:T(8,128)S(1)}, f32[8,4,128,128]{2,3,1,0:T(8,128)}, u32[]{:S(2)}) copy-start(f32[8,4,128,128]{2,3,1,0:T(8,128)} %get-tuple-element.100) | copy-start | bytes 6291460
  257.9 45.4 %collective-permute-start.8 = (f32[8,4,64,256]{3,2,1,0:T(8,128)}, f32[8,4,64,256]{3,2,1,0:T(8,128)}, u32[]{:S(2)}, u32[]{:S(2)}) collective-permute-start(f32[8,4,64,256]{3,2,1,0:T(8,128)} %get-tuple-element.177), channel_id=1, source_target_pairs={{0,1},{1,2},{2,3},{4,5},{5,6},{6,7},{8,9},{9,10},{10,11},{12,13},{... | collective-permute-start | bytes 6291464 | tf_op jit(solution)/shard_map/ppermute | solution.py:18
  261.3 47.4 %collective-permute-start.9 = (f32[8,4,64,256]{3,2,1,0:T(8,128)}, f32[8,4,64,256]{3,2,1,0:T(8,128)}, u32[]{:S(2)}, u32[]{:S(2)}) collective-permute-start(f32[8,4,64,256]{3,2,1,0:T(8,128)} %get-tuple-element.176), channel_id=1, source_target_pairs={{1,0},{2,1},{3,2},{5,4},{6,5},{7,6},{9,8},{10,9},{11,10},{13,12},{... | collective-permute-start | bytes 6291464 | tf_op jit(solution)/shard_map/ppermute | solution.py:18
  267.8 40.9 %copy-start.49 = (f32[8,4,4]{1,2,0:T(4,128)S(1)}, f32[8,4,4]{1,2,0:T(4,128)}, u32[]{:S(2)}) copy-start(f32[8,4,4]{1,2,0:T(4,128)} %copy.371) | copy-start | bytes 1540
  317.6 12.4 %copy-start.4 = (f32[8,4,4,64,256]{4,3,1,2,0:T(8,128)}, f32[8,4,4,64,256]{4,3,1,2,0:T(8,128)S(1)}, u32[]{:S(2)}) copy-start(f32[8,4,4,64,256]{4,3,1,2,0:T(8,128)S(1)} %get-tuple-element.136) | copy-start | bytes 25165828
  335.5 134.1 %reduce-scatter.5.cloned.1.call-start = ((), (), s32[]{:S(2)}) async-start(), calls=%async_computation.4 | async-start | bytes 4718592 | tf_op jit(solution)/shard_map/reduce_scatter | solution.py:280
  348.2 11.6 %copy-start.9 = (bf16[8,4,64,4,128]{4,3,2,1,0:T(4,128)(2,1)S(1)}, bf16[8,4,64,4,128]{4,3,2,1,0:T(4,128)(2,1)}, u32[]{:S(2)}) copy-start(bf16[8,4,64,4,128]{4,3,2,1,0:T(4,128)(2,1)} %copy-done.7) | copy-start | bytes 6291460
  348.2 11.6 %copy-start.32 = (f32[8,4,4,128]{3,2,1,0:T(4,128)S(1)}, f32[8,4,4,128]{3,2,1,0:T(4,128)}, u32[]{:S(2)}) copy-start(f32[8,4,4,128]{3,2,1,0:T(4,128)} %copy.368) | copy-start | bytes 196612
  373.8 5.5 %copy-start.36 = (f32[4,8,4,4]{1,3,2,0:T(4,128)S(1)}, f32[4,8,4,4]{1,3,2,0:T(4,128)}, u32[]{:S(2)}) copy-start(f32[4,8,4,4]{1,3,2,0:T(4,128)} %copy-done.35) | copy-start | bytes 6148
  373.8 5.5 %copy-start.88 = (pred[4,4]{0,1:T(4,128)(4,1)S(1)}, pred[4,4]{0,1:T(4,128)(4,1)}, u32[]{:S(2)}) copy-start(pred[4,4]{0,1:T(4,128)(4,1)} %copy-done.87) | copy-start | bytes 52
  430.3 5.6 %copy-start.46 = (f32[8,256]{1,0:T(8,128)S(1)}, f32[8,256]{1,0:T(8,128)}, u32[]{:S(2)}) copy-start(f32[8,256]{1,0:T(8,128)} %copy-done.45) | copy-start | bytes 24580
  441.6 5.4 %copy-start.12 = (f32[8,256,512]{2,1,0:T(8,128)}, f32[8,256,512]{2,1,0:T(8,128)S(1)}, u32[]{:S(2)}) copy-start(f32[8,256,512]{2,1,0:T(8,128)S(1)} %get-tuple-element.130) | copy-start | bytes 12582916
  441.6 5.4 %copy-start.13 = (f32[8,256,512]{2,1,0:T(8,128)}, f32[8,256,512]{2,1,0:T(8,128)S(1)}, u32[]{:S(2)}) copy-start(f32[8,256,512]{2,1,0:T(8,128)S(1)} %get-tuple-element.131) | copy-start | bytes 12582916
  441.6 5.4 %copy-start.14 = (f32[8,256,512]{2,1,0:T(8,128)}, f32[8,256,512]{2,1,0:T(8,128)S(1)}, u32[]{:S(2)}) copy-start(f32[8,256,512]{2,1,0:T(8,128)S(1)} %get-tuple-element.132) | copy-start | bytes 12582916
  442.3 8.0 %copy-start.24 = (f32[8,4,128,128]{2,3,1,0:T(8,128)S(1)}, f32[8,4,128,128]{2,3,1,0:T(8,128)}, u32[]{:S(2)}) copy-start(f32[8,4,128,128]{2,3,1,0:T(8,128)} %fusion.174) | copy-start | bytes 6291460
  474.7 7.7 %collective-permute-start.10 = (f32[8,320,3]{1,0,2:T(8,128)S(1)}, f32[8,320,3]{1,0,2:T(8,128)S(1)}, u32[]{:S(2)}, u32[]{:S(2)}) collective-permute-start(f32[8,320,3]{1,0,2:T(8,128)S(1)} %copy.392), channel_id=1, source_target_pairs={{1,0},{2,1},{3,2},{5,4},{6,5},{7,6},{9,8},{10,9},{11,10},{13,12},{... | collective-permute-start | bytes 92168 | tf_op jit(solution)/shard_map/ppermute | solution.py:18
  (46 other events, 112.7 us)
Sparse Core Ops, SparseCore 0:
  44.7 52.5 all-gather.1
  335.6 48.5 reduce-scatter.2
  394.7 48.5 reduce-scatter.4

commit v11 on v10

--- a/solution.py
+++ b/solution.py
@@ -236,10 +236,17 @@
         jnp.concatenate([b_in, c_in], axis=1).astype(jnp.float32),
         rim_chan.astype(jnp.float32),
     )
-    both_conv = lax.all_gather(
-        bc_conv.reshape(groups_here, 2, b_width, length), "seq", axis=2, tiled=True
-    )
-    b_conv, c_conv = (both_conv[:, 0], both_conv[:, 1])
+    lanes = lax.axis_size("seq")
+    spread = jnp.stack(
+        [bc_conv]
+        + [
+            lax.ppermute(bc_conv, "seq", [(i, (i + k) % lanes) for i in range(lanes)])
+            for k in range(1, lanes)
+        ]
+    )
+    spread = jnp.take(spread, (lane - jnp.arange(lanes)) % lanes, axis=0)
+    b_conv = jnp.moveaxis(spread[:, :, :b_width], 0, 1).reshape(groups_here, -1, length)
+    c_conv = jnp.moveaxis(spread[:, :, b_width:], 0, 1).reshape(groups_here, -1, length)
 
     def local_terms(x_float, b_float, c_float, dt_float):
         return jax.vmap(scan_part, in_axes=(0, 0, 0, 0, 0, 0, 0, None))(

time: 498 us -> 569 us (1.14)
  local copies, waits for them, and re-layouts: 96.1 us -> 118 us
  starting transfers between devices: 27.7 us -> 43.4 us
  other arithmetic: 106 us -> 120 us
  waiting for transfers between devices: 107 us -> 119 us
    ppermute x0 -> x7, waiting for transfers between devices: none -> 36.3 us  [shards(): lax.ppermute(bc_conv, 'seq', [(i, (i + k) % lanes) for i in range(lanes)])]
    all_gather x1 -> x0, waiting for transfers between devices: 24.8 us -> none  [shards(): lax.all_gather(bc_conv.reshape(groups_here, 2, b_width, length), 'seq', a...]
    ppermute x0 -> x7, starting transfers between devices: none -> 19 us  [shards(): lax.ppermute(bc_conv, 'seq', [(i, (i + k) % lanes) for i in range(lanes)])]
    slice x3 -> x0, local copies, waits for them, and re-layouts: 18.9 us -> none  [shards(): b_conv, c_conv = (both_conv[:, 0], both_conv[:, 1])]
    unnamed x198 -> x204, local copies, waits for them, and re-layouts: 18.6 us -> 31.4 us
    another operation x0 -> x3, local copies, waits for them, and re-layouts: none -> 11.6 us  [the longest x1 5.27 us: span_terms(): c_three = c_conv.reshape(STATE, blocks, SPAN)]
    transpose x0 -> x3, local copies, waits for them, and re-layouts: none -> 11 us  [the longest x2 6.03 us: shards(): jnp.moveaxis(spread[:, :, :b_width], 0, 1).reshape(groups_here, -1, length)]
    gather x0 -> x1, local copies, waits for them, and re-layouts: none -> 7.89 us  [shards(): spread = jnp.take(spread, (lane - jnp.arange(lanes)) % lanes, axis=0)]
  transfers between devices with their start and end apart: 14 -> 20, of which waited for: 7 -> 8; matrix products, arithmetic and copies ran while one was open for 47% -> 47% of each run, Pallas kernels for 0% -> 0%
where the time goes in v11:
time: 569 us; the launch traced here: 561 us
  matrix products  145 us (25%)
  other arithmetic  120 us (21%)
  waiting for transfers between devices  119 us (21%)
  local copies, waits for them, and re-layouts  118 us (21%)
  starting transfers between devices  43.4 us (8%)
  between operations  15.6 us (3%)
    ppermute x8, waiting for transfers between devices, passed_along(): lax.ppermute(value, axis, [(source, source + steps) for source in range(f...  83 us
    dot_general x3, matrix products, span_terms(): jnp.einsum('hpcj,hcj,ncj->hcpn', weighted, keep_end, b_three, precision=p...  41.6 us
    dot_general x3, matrix products, span_terms(): jnp.einsum('hcij,hpcj->hpci', decay * scores[None], weighted, precision=p...  41.2 us
    ppermute x7, waiting for transfers between devices, shards(): lax.ppermute(bc_conv, 'seq', [(i, (i + k) % lanes) for i in range(lanes)])  36.3 us
    dot_general x3, matrix products, assemble(): jnp.einsum('nci,hci,chpn->hpci', c_three, entry, starts, precision=precise)  33.2 us
    unnamed x204, local copies, waits for them, and re-layouts  31.4 us
    reduce_sum x2, other arithmetic, weighted_sum(): return jnp.sum(weight[..., None, None] * stacked, axis=-3)  26.7 us
    dot_general x3, matrix products, span_terms(): scores = jnp.einsum('nci,ncj->cij', c_three, b_three, precision=precise)  21.7 us
  transfers between devices with their start and end apart: 20, of which 8 were waited for; matrix products, arithmetic and copies ran while one was open for 47% of the time, Pallas kernels for 0%

profile of v11, /device:TPU:0, one launch (start us, length us, event | category | flops | bytes accessed | tf_op | source)
XLA Modules:
  0.0 560.6 jit_solution(13915643655052585100)
XLA Ops:
  9.1 3.1 collective-permute-start
  12.1 2.6 collective-permute-start.1
  16.1 4.5 copy.335
  25.5 2.6 collective-permute-start.3
  35.8 2.6 convert_element_type.83
  38.5 2.5 reshape.404
  46.2 4.8 fusion.121
  52.5 2.4 collective-permute-start.6
  59.0 2.4 while.13
  62.9 12.6 %fusion.55 = (f32[8,256,512]{2,1,0:T(8,128)}, f32[8,256,512]{2,1,0:T(8,128)}) fusion(f32[8,256,512]{2,1,0:T(8,128)} %convert_element_type.83, f32[8,256]{1,0:T(8,128)S(1)} %get-tuple-element.150, f32[512]{0:T(512)} %copy-done.54, f32[8,256,3]{2,1,0:T(8,128)} %copy.338, f32[8,256]{1,0:T(8,128)S(1)} %get-tuple-element.148, f32[512]{0:T(512)} %copy-done.56, ...), kind=kLoop, calls=%fused_computation.98 | loop fusion | flops 18874368 | bytes 12654592 | tf_op jit(solution)/shard_map/jvp(vmap(jit(silu)))/mul | solution.py:53
  76.4 5.3 reshape.402
  85.7 2.3 bitcast_dynamic-update-slice_fusion.7
  87.9 13.0 %collective-permute-start.10 = (f32[8,64,512]{2,1,0:T(8,128)}, f32[8,64,512]{2,1,0:T(8,128)S(1)}, u32[]{:S(2)}, u32[]{:S(2)}) collective-permute-start(f32[8,64,512]{2,1,0:T(8,128)} %get-tuple-element.124), channel_id=1, source_target_pairs={{0,28},{4,0},{8,4},{12,8},{16,12},{20,16},{24,20},{28,24},{1,29},{... | collective-permute-start | bytes 3145736 | tf_op jit(solution)/shard_map/ppermute | solution.py:243
  101.0 2.3 bitcast_dynamic-update-slice_fusion.6
  103.3 19.2 %collective-permute-done.6 = f32[8,64,512]{2,1,0:T(8,128)} collective-permute-done((f32[8,64,512]{2,1,0:T(8,128)}, f32[8,64,512]{2,1,0:T(8,128)}, u32[]{:S(2)}, u32[]{:S(2)}) %collective-permute-start.6) | collective-permute-done | bytes 1048608 | tf_op jit(solution)/shard_map/ppermute | solution.py:243
  122.5 2.3 bitcast_dynamic-update-slice_fusion.5
  124.8 2.3 bitcast_dynamic-update-slice_fusion.4
  127.1 17.0 %collective-permute-done.8 = f32[8,64,512]{2,1,0:T(8,128)} collective-permute-done((f32[8,64,512]{2,1,0:T(8,128)}, f32[8,64,512]{2,1,0:T(8,128)}, u32[]{:S(2)}, u32[]{:S(2)}) %collective-permute-start.8) | collective-permute-done | bytes 1048608 | tf_op jit(solution)/shard_map/ppermute | solution.py:243
  144.1 2.3 bitcast_dynamic-update-slice_fusion.3
  148.7 7.9 %gather_fusion.1 = f32[8,8,64,512]{3,2,1,0:T(8,128)} fusion(f32[8,8,64,512]{3,2,1,0:T(8,128)} %bitcast_dynamic-update-slice_fusion.1, s32[1024]{0:T(1024)} %pad_clamp_fusion), kind=kCustom, calls=%fused_computation.1 | custom fusion | bytes 16777248 | tf_op jit(solution)/shard_map/jit(_take)/gather | solution.py:247
  156.6 4.5 broadcast_select_fusion
  161.1 3.5 slice_bitcast_fusion
  164.6 2.5 copy.349
  167.1 5.2 reshape_reshape.7
  172.4 5.0 copy.348
  177.3 5.3 reshape_reshape.6
  182.6 14.0 %multiply_reduce_fusion.5 = (f32[8,4,64,256]{3,2,1,0:T(8,128)S(1)}, f32[8,4,4,64,256]{4,3,1,2,0:T(8,128)}) fusion(f32[8,4,4]{1,2,0:T(4,128)S(1)} %copy.365, f32[8,256,4,128,1]{3,2,1,0,4:T(4,128)} %bitcast.247, f32[8,4,64,4,128]{4,3,2,1,0:T(4,128)} %reshape.402, f32[8,4,4,128]{3,2,1,0:T(4,128)S(1)} %copy.359, f32[8,4,4,128]{3,2,1,0:T(4,128)S(1)} %copy.341), kind=kOutput, calls=%fused_computation.27 | convolution fusion | flops 3226992640 | bytes 19005952 | tf_op jit(solution)/shard_map/jvp(vmap(hpcj,hcj,ncj->hcpn))/dot_general | solution.py:78
  200.3 5.6 fusion.99
  205.9 2.3 collective-permute-start.11
  214.6 37.8 %collective-permute-done.11 = f32[8,4,64,256]{3,2,1,0:T(8,128)S(1)} collective-permute-done((f32[8,4,64,256]{3,2,1,0:T(8,128)}, f32[8,4,64,256]{3,2,1,0:T(8,128)S(1)}, u32[]{:S(2)}, u32[]{:S(2)}) %collective-permute-start.11) | collective-permute-done | bytes 2097184 | tf_op jit(solution)/shard_map/ppermute | solution.py:18
  252.4 4.8 collective-permute-done.12
  257.2 5.7 %multiply_add_fusion.2 = (f32[8,4,64,256]{3,2,1,0:T(8,128)}, f32[8,4,64,256]{3,2,1,0:T(8,128)}) fusion(f32[8,4,64,256]{3,2,1,0:T(8,128)} %fusion.99, f32[8,4,64,256]{3,2,1,0:T(8,128)} %collective-permute-done.12, f32[8,4]{1,0:T(8,128)S(1)} %copy.364, f32[8,4,64,256]{3,2,1,0:T(8,128)S(1)} %collective-permute-done.11, f32[8,4,64,256]{3,2,1,0:T(8,128)} %copy-done.15, ...), kind=kLoop, calls=%fused_computation.121 | loop fusion | flops 2621440 | bytes 12583168 | tf_op jit(solution)/shard_map/add | solution.py:31
  262.9 3.6 collective-permute-start.13
  268.2 8.1 %fusion.59 = f32[8,4,128,128]{2,3,1,0:T(8,128)} fusion(f32[8,256,4,128]{3,2,1,0:T(4,128)S(1)} %copy-done.1, f32[8,256,4,128]{3,2,1,0:T(4,128)S(1)} %copy-done.2), kind=kOutput, calls=%fused_computation.102 | convolution fusion | flops 1610612736 | bytes 10485760 | tf_op jit(solution)/shard_map/jvp(vmap(nci,ncj->cij))/dot_general | solution.py:72
  276.4 7.8 %fusion.70 = f32[8,4,4,64,256]{4,3,1,2,0:T(8,128)S(1)} fusion(f32[8,256,4,128,1]{3,2,1,0,4:T(4,128)S(1)} %bitcast.246, f32[8,4,4,128]{3,2,1,0:T(4,128)S(1)} %copy-done.31, bf16[8,4,64,4,128]{4,3,2,1,0:T(4,128)(2,1)S(1)} %copy-done.8), kind=kOutput, calls=%fused_computation.114 | convolution fusion | flops 3223322624 | bytes 14745600 | tf_op jit(solution)/shard_map/transpose(jvp(vmap(nci,hci,chpn->hpci)))/dot_general | solution.py:149
  284.2 17.8 %fusion.123 = (f32[8,4,4,128]{3,2,1,0:T(4,128)}, f32[8,4,4,128]{3,2,1,0:T(4,128)}, f32[8,4,128,128]{2,3,1,0:T(8,128)}) fusion(f32[8,4,4,128]{3,2,1,0:T(4,128)} %copy.344, f32[4,128,128]{1,2,0:T(8,128)} %compare_select_fusion, f32[8,4,128,128]{2,3,1,0:T(8,128)} %fusion.59, bf16[8,4,4,64,128]{4,2,3,1,0:T(4,128)(2,1)} %bitcast.251, ...), kind=kOutput, calls=%fused_computation.175 | convolution fusion | flops 1642561536 | bytes 11010048 | tf_op jit(solution)/shard_map/transpose(jvp(vmap(hcij,hpcj->hpci)))/dot_general | solution.py:74
  302.0 8.9 %collective-permute-done.13 = f32[8,4,64,256]{3,2,1,0:T(8,128)} collective-permute-done((f32[8,4,64,256]{3,2,1,0:T(8,128)}, f32[8,4,64,256]{3,2,1,0:T(8,128)}, u32[]{:S(2)}, u32[]{:S(2)}) %collective-permute-start.13) | collective-permute-done | bytes 2097184 | tf_op jit(solution)/shard_map/ppermute | solution.py:18
  311.0 6.1 %collective-permute-done.14 = f32[8,4,64,256]{3,2,1,0:T(8,128)} collective-permute-done((f32[8,4,64,256]{3,2,1,0:T(8,128)}, f32[8,4,64,256]{3,2,1,0:T(8,128)}, u32[]{:S(2)}, u32[]{:S(2)}) %collective-permute-start.14) | collective-permute-done | bytes 2097184 | tf_op jit(solution)/shard_map/ppermute | solution.py:18
  317.1 6.4 %multiply_add_fusion = (f32[8,4,64,256]{3,2,1,0:T(8,128)}, f32[8,4,64,256]{3,2,1,0:T(8,128)}) fusion(f32[8,4,64,256]{3,2,1,0:T(8,128)} %fusion.99, f32[8,4,64,256]{3,2,1,0:T(8,128)} %collective-permute-done.14, f32[8,4]{1,0:T(8,128)S(1)} %copy-done.61, f32[8,4,64,256]{3,2,1,0:T(8,128)} %collective-permute-done.13, f32[8,4,64,256]{3,2,1,0:T(8,128)} %copy-done.15, ...), kind=kLoop, calls=%fused_computation.119 | loop fusion | flops 2621440 | bytes 12583168 | tf_op jit(solution)/shard_map/add | solution.py:31
  323.5 2.7 collective-permute-start.15
  327.7 5.2 fusion.61
  332.9 17.8 %multiply_reduce_fusion = (f32[8,4,4,4]{3,2,1,0:T(4,128)}, f32[8,4,4,64,256]{4,3,2,1,0:T(8,128)}, f32[8,4,4,64,256]{4,3,2,1,0:T(8,128)}) fusion(f32[8,4,4,4]{3,2,1,0:T(4,128)S(1)} %bitcast_multiply_fusion.8, f32[8,4,4,64,256]{4,3,1,2,0:T(8,128)S(1)} %bitcast.250, f32[8,4,4,64,256]{4,3,1,2,0:T(8,128)S(1)} %fusion.70), kind=kLoop, calls=%fused_computation.4 | loop fusion | flops 46136832 | bytes 33558528 | tf_op jit(solution)/shard_map/transpose(jvp(vmap()))/reduce_sum | solution.py:131
  350.7 20.0 %collective-permute-done.15 = f32[8,4,64,256]{3,2,1,0:T(8,128)} collective-permute-done((f32[8,4,64,256]{3,2,1,0:T(8,128)}, f32[8,4,64,256]{3,2,1,0:T(8,128)}, u32[]{:S(2)}, u32[]{:S(2)}) %collective-permute-start.15) | collective-permute-done | bytes 2097184 | tf_op jit(solution)/shard_map/ppermute | solution.py:18
  370.7 5.4 collective-permute-done.16
  376.1 8.9 %multiply_reduce_fusion.4 = (f32[8,4,4]{1,2,0:T(4,128)}, f32[8,4,4,64,256]{4,3,1,2,0:T(8,128)S(1)}) fusion(f32[8,4,4,64,256]{4,3,1,2,0:T(8,128)} %get-tuple-element.188, f32[8,4,64,256]{3,2,1,0:T(8,128)} %collective-permute-done.16, f32[8,4,4,64,256]{4,3,2,1,0:T(8,128)} %get-tuple-element.103, f32[8,4,4]{1,2,0:T(4,128)S(1)} %copy-done.47), kind=kLoop, calls=%fused_computation.26 | loop fusion | flops 8388480 | bytes 27264000 | tf_op jit(solution)/shard_map/transpose(jvp(vmap()))/reduce_sum | solution.py:131
  385.0 12.4 %bitcast_add_fusion.2 = f32[8,256,4,128]{1,3,2,0:T(8,128)} fusion(f32[8,4,128,256]{3,2,1,0:T(8,128)} %fusion.61, f32[8,4,4,64,256]{4,3,1,2,0:T(8,128)S(1)} %get-tuple-element.136, f32[8,4,64,4,128]{4,3,2,1,0:T(4,128)S(1)} %copy-done.5, f32[8,4,4,128]{3,2,1,0:T(4,128)} %copy-done.29, f32[8,4,4,128]{3,2,1,0:T(4,128)S(1)} %copy.341), kind=kOutput, calls=%fused_computation.63 | convolution fusion | flops 3224371200 | bytes 21102592 | tf_op jit(solution)/shard_map/transpose(jvp(vmap(hpcj,hcj,ncj->hcpn)))/dot_general | solution.py:78
  397.4 5.4 copy.393
  404.5 8.3 %fusion.67 = f32[8,4,128,256]{3,2,1,0:T(8,128)} fusion(f32[8,4,128,128]{2,3,1,0:T(8,128)S(1)} %copy-done.22, f32[8,256,4,128]{3,2,1,0:T(4,128)} %reshape_reshape.7), kind=kOutput, calls=%fused_computation.110 | convolution fusion | flops 1610612736 | bytes 10485760 | tf_op jit(solution)/shard_map/transpose(jvp(vmap(nci,ncj->cij)))/dot_general | solution.py:72
  412.8 2.7 multiply_reduce_fusion.6
  415.6 11.5 %multiply_reduce_fusion.3 = (f32[8,4,4]{1,2,0:T(4,128)S(1)}, f32[8,4,4,64,256]{4,3,1,2,0:T(8,128)}) fusion(f32[8,4,4,64,256]{4,3,1,2,0:T(8,128)} %copy-done.3, f32[8,4,64,256]{3,2,1,0:T(8,128)} %collective-permute-done.15, f32[8,4,4]{1,2,0:T(4,128)S(1)} %copy.363, f32[8,4,4,64,256]{4,3,2,1,0:T(8,128)} %get-tuple-element.102), kind=kLoop, calls=%fused_computation.25 | loop fusion | flops 8388480 | bytes 27264000 | tf_op jit(solution)/shard_map/transpose(jvp(vmap()))/reduce_sum | solution.py:142
  427.3 14.0 %bitcast_add_fusion.3 = f32[8,4,128,256]{3,2,1,0:T(8,128)} fusion(f32[8,4,128,256]{3,2,1,0:T(8,128)} %fusion.67, f32[8,4,4,64,256]{4,3,1,2,0:T(8,128)} %get-tuple-element.138, f32[8,4,4,128]{3,2,1,0:T(4,128)S(1)} %copy-done.32, bf16[8,4,64,4,128]{4,3,2,1,0:T(4,128)(2,1)S(1)} %copy-done.9), kind=kOutput, calls=%fused_computation.64 | convolution fusion | flops 3224371200 | bytes 18939904 | tf_op jit(solution)/shard_map/transpose(jvp(vmap(nci,hci,chpn->hpci)))/dot_general | solution.py:149
  441.2 5.5 copy.398
  446.9 15.2 %fusion.38 = (f32[8,4,4,128]{3,2,1,0:T(4,128)S(1)}, f32[8,4,4,64,128]{4,3,1,2,0:T(8,128)}) fusion(f32[8,4,64,4,128]{4,3,2,1,0:T(4,128)} %reshape.402, f32[8,4,4,128]{3,2,1,0:T(4,128)S(1)} %copy.341, f32[8,4,4,64,256]{4,3,1,2,0:T(8,128)} %copy-done.4, f32[8,256,4,128,1]{3,2,1,0,4:T(4,128)} %bitcast.248), kind=kOutput, calls=%fused_computation.72 | convolution fusion | flops 3224354816 | bytes 21102592 | tf_op jit(solution)/shard_map/transpose(jvp(vmap(hpcj,hcj,ncj->hcpn)))/dot_general | solution.py:78
  463.5 13.7 %fusion.36 = (f32[8,4,4,128]{3,2,1,0:T(4,128)S(1)}, f32[8,4,64,4,128]{4,2,3,1,0:T(8,128)}) fusion(f32[8,4,64,4,128]{4,3,2,1,0:T(4,128)} %reshape.402, f32[8,4,4,128]{3,2,1,0:T(4,128)S(1)} %copy.341, bf16[8,4,64,4,128]{4,3,2,1,0:T(4,128)(2,1)S(1)} %copy-done.9, f32[8,4]{1,0:T(8,128)S(1)} %constant_dynamic-slice_fusion, ...), kind=kOutput, calls=%fused_computation.68 | convolution fusion | flops 1627373568 | bytes 19398784 | tf_op jit(solution)/shard_map/transpose(jvp(vmap(hcij,hpcj->hpci)))/dot_general | solution.py:74
  477.2 11.4 %fusion.16 = f32[8,4,4,64,128]{4,3,2,1,0:T(8,128)S(1)} fusion(f32[8,4,4,64,256]{4,3,1,2,0:T(8,128)} %get-tuple-element.138, f32[8,256,4,128,1]{3,2,1,0,4:T(4,128)} %bitcast.244), kind=kOutput, calls=%fused_computation.30 | convolution fusion | flops 3221225472 | bytes 16777216 | tf_op jit(solution)/shard_map/jvp(vmap(nci,hci,chpn->hpci))/dot_general | solution.py:149
  492.5 5.7 %copy.388 = f32[8,4,64,4,128]{4,3,2,1,0:T(4,128)} copy(f32[8,4,64,4,128]{4,2,3,1,0:T(8,128)S(1)} %copy-done.24) | data formatting | bytes 8388608 | tf_op jit(solution)/shard_map/transpose(jvp(vmap()))/add_any | solution.py:73
  498.2 5.6 reshape.407
  503.8 4.3 broadcast_multiply_fusion
  510.1 4.6 pad_add_fusion
  514.8 3.3 split.16
  519.8 9.7 %fusion.41 = bf16[8,4,64,4,128]{4,2,3,1,0:T(8,128)(2,1)S(1)} fusion(f32[8,4,4,64,128]{4,3,2,1,0:T(8,128)S(1)} %copy-done.17, f32[8,4,64,4,128]{4,3,2,1,0:T(4,128)S(1)} %copy-done.6, f32[8,4,128,128]{2,3,1,0:T(8,128)S(1)} %copy-done.25, f32[4,128,128]{1,2,0:T(8,128)S(1)} %copy-done.38, f32[8,4,4,128]{3,2,1,0:T(4,128)S(1)} %copy-done.49, ...), kind=kOutput, calls=%fused_computation.76 | convolution fusion | flops 1625292800 | bytes 13041792 | tf_op jit(solution)/shard_map/jvp(vmap(hcij,hpcj->hpci))/dot_general | solution.py:74
  531.4 2.2 convert_element_type.96
  533.6 2.6 pad_add_fusion.3
  544.1 2.9 slice_maximum_fusion
  (358 shorter events, 77.6 us)
Async XLA Ops:
  7.2 15.3 %copy-start.28 = (bf16[8,32,512]{2,1,0:T(8,128)(2,1)S(1)}, bf16[8,32,512]{2,1,0:T(8,128)(2,1)}, u32[]{:S(2)}) copy-start(bf16[8,32,512]{2,1,0:T(8,128)(2,1)} %param.15) | copy-start | bytes 786436
  7.2 529.1 %reduce-scatter.3.cloned.1.call-start = ((), (), s32[]{:S(2)}) async-start(), calls=%async_computation.2 | async-start | bytes 4718592 | tf_op jit(solution)/shard_map/reduce_scatter | solution.py:286
  9.1 33.8 %collective-permute-start = (f32[2,12896]{1,0:T(2,128)S(1)}, f32[2,12896]{1,0:T(2,128)}, u32[]{:S(2)}, u32[]{:S(2)}) collective-permute-start(f32[2,12896]{1,0:T(2,128)S(1)} %concatenate.39), channel_id=1, source_target_pairs={{0,1},{1,2},{2,3},{3,0},{4,5},{5,6},{6,7},{7,4},{8,9},{9,10},{10,1... | collective-permute-start | bytes 309512 | tf_op jit(solution)/shard_map/ppermute | solution.py:187
  12.1 30.7 %collective-permute-start.1 = (f32[2,12896]{1,0:T(2,128)S(1)}, f32[2,12896]{1,0:T(2,128)}, u32[]{:S(2)}, u32[]{:S(2)}) collective-permute-start(f32[2,12896]{1,0:T(2,128)S(1)} %concatenate.39), channel_id=1, source_target_pairs={{0,2},{1,3},{2,0},{3,1},{4,6},{5,7},{6,4},{7,5},{8,10},{9,11},{10,... | collective-permute-start | bytes 309512 | tf_op jit(solution)/shard_map/ppermute | solution.py:187
  14.7 28.1 %collective-permute-start.2 = (f32[2,12896]{1,0:T(2,128)S(1)}, f32[2,12896]{1,0:T(2,128)}, u32[]{:S(2)}, u32[]{:S(2)}) collective-permute-start(f32[2,12896]{1,0:T(2,128)S(1)} %concatenate.39), channel_id=1, source_target_pairs={{0,3},{1,0},{2,1},{3,2},{4,7},{5,4},{6,5},{7,6},{8,11},{9,8},{10,9... | collective-permute-start | bytes 309512 | tf_op jit(solution)/shard_map/ppermute | solution.py:187
  20.6 15.2 %copy-start.23 = (bf16[8,256,512]{2,1,0:T(8,128)(2,1)S(1)}, bf16[8,256,512]{2,1,0:T(8,128)(2,1)}, u32[]{:S(2)}) copy-start(bf16[8,256,512]{2,1,0:T(8,128)(2,1)} %param.13) | copy-start | bytes 6291460
  25.5 15.6 %collective-permute-start.3 = (bf16[8,320,3]{1,0,2:T(8,128)(2,1)}, bf16[8,320,3]{1,0,2:T(8,128)(2,1)S(1)}, u32[]{:S(2)}, u32[]{:S(2)}) collective-permute-start(bf16[8,320,3]{1,0,2:T(8,128)(2,1)} %pad_maximum_fusion.4), channel_id=1, source_target_pairs={{0,1},{1,2},{2,3},{4,5},{5,6},{6,7},{8,9},{9,10},{10,11},{12,13},{... | collective-permute-start | bytes 46088 | tf_op jit(solution)/shard_map/ppermute | solution.py:18
  28.5 12.6 %copy-start.50 = (s32[4,128]{1,0:T(4,128)}, s32[4,128]{1,0:T(4,128)S(1)}, u32[]{:S(2)}) copy-start(s32[4,128]{1,0:T(4,128)S(1)} %slice_bitcast_fusion.2) | copy-start | bytes 6148
  29.5 16.6 %copy-start.54 = (f32[512]{0:T(512)}, f32[512]{0:T(512)S(1)}, u32[]{:S(2)}) copy-start(f32[512]{0:T(512)S(1)} %get-tuple-element.183) | copy-start | bytes 6148
  29.5 16.6 %copy-start.56 = (f32[512]{0:T(512)}, f32[512]{0:T(512)S(1)}, u32[]{:S(2)}) copy-start(f32[512]{0:T(512)S(1)} %get-tuple-element.184) | copy-start | bytes 6148
  29.5 33.3 %copy-start.52 = (f32[512]{0:T(512)}, f32[512]{0:T(512)S(1)}, u32[]{:S(2)}) copy-start(f32[512]{0:T(512)S(1)} %get-tuple-element.182) | copy-start | bytes 6148
  41.1 157.2 %copy-start.7 = (bf16[8,4,64,4,128]{4,3,2,1,0:T(4,128)(2,1)}, bf16[8,4,64,4,128]{4,3,2,1,0:T(4,128)(2,1)S(1)}, u32[]{:S(2)}) copy-start(bf16[8,4,64,4,128]{4,3,2,1,0:T(4,128)(2,1)S(1)} %reshape.404) | copy-start | bytes 6291460
  45.7 10.8 %copy-start.58 = (f32[8,64]{1,0:T(8,128)}, f32[8,64]{1,0:T(8,128)S(1)}, u32[]{:S(2)}) copy-start(f32[8,64]{1,0:T(8,128)S(1)} %get-tuple-element.164) | copy-start | bytes 6148
  45.7 10.8 %copy-start.62 = (f32[8,64]{1,0:T(8,128)}, f32[8,64]{1,0:T(8,128)S(1)}, u32[]{:S(2)}) copy-start(f32[8,64]{1,0:T(8,128)S(1)} %get-tuple-element.162) | copy-start | bytes 6148
  45.7 15.7 %copy-start.64 = (f32[8,64]{1,0:T(8,128)}, f32[8,64]{1,0:T(8,128)S(1)}, u32[]{:S(2)}) copy-start(f32[8,64]{1,0:T(8,128)S(1)} %get-tuple-element.163) | copy-start | bytes 6148
  45.7 15.7 %copy-start.66 = (f32[8,64]{1,0:T(8,128)}, f32[8,64]{1,0:T(8,128)S(1)}, u32[]{:S(2)}) copy-start(f32[8,64]{1,0:T(8,128)S(1)} %get-tuple-element.165) | copy-start | bytes 6148
  51.0 32.0 %copy-start.18 = (f32[8,64,512]{2,1,0:T(8,128)}, f32[8,64,512]{2,1,0:T(8,128)S(1)}, u32[]{:S(2)}) copy-start(f32[8,64,512]{2,1,0:T(8,128)S(1)} %get-tuple-element.125) | copy-start | bytes 3145732
  51.0 33.2 %collective-permute-start.4 = (f32[8,64,512]{2,1,0:T(8,128)}, f32[8,64,512]{2,1,0:T(8,128)}, u32[]{:S(2)}, u32[]{:S(2)}) collective-permute-start(f32[8,64,512]{2,1,0:T(8,128)} %get-tuple-element.124), channel_id=1, source_target_pairs={{0,4},{4,8},{8,12},{12,16},{16,20},{20,24},{24,28},{28,0},{1,5},{5... | collective-permute-start | bytes 3145736 | tf_op jit(solution)/shard_map/ppermute | solution.py:243
  51.0 36.9 %collective-permute-start.5 = (f32[8,64,512]{2,1,0:T(8,128)}, f32[8,64,512]{2,1,0:T(8,128)}, u32[]{:S(2)}, u32[]{:S(2)}) collective-permute-start(f32[8,64,512]{2,1,0:T(8,128)} %get-tuple-element.124), channel_id=1, source_target_pairs={{0,8},{4,12},{8,16},{12,20},{16,24},{20,28},{24,0},{28,4},{1,9},{5... | collective-permute-start | bytes 3145736 | tf_op jit(solution)/shard_map/ppermute | solution.py:243
  52.5 70.0 %collective-permute-start.6 = (f32[8,64,512]{2,1,0:T(8,128)}, f32[8,64,512]{2,1,0:T(8,128)}, u32[]{:S(2)}, u32[]{:S(2)}) collective-permute-start(f32[8,64,512]{2,1,0:T(8,128)} %get-tuple-element.124), channel_id=1, source_target_pairs={{0,12},{4,16},{8,20},{12,24},{16,28},{20,0},{24,4},{28,8},{1,13},{... | collective-permute-start | bytes 3145736 | tf_op jit(solution)/shard_map/ppermute | solution.py:243
  54.9 69.9 %collective-permute-start.7 = (f32[8,64,512]{2,1,0:T(8,128)}, f32[8,64,512]{2,1,0:T(8,128)}, u32[]{:S(2)}, u32[]{:S(2)}) collective-permute-start(f32[8,64,512]{2,1,0:T(8,128)} %get-tuple-element.124), channel_id=1, source_target_pairs={{0,16},{4,20},{8,24},{12,28},{16,0},{20,4},{24,8},{28,12},{1,17},{... | collective-permute-start | bytes 3145736 | tf_op jit(solution)/shard_map/ppermute | solution.py:243
  55.4 88.7 %collective-permute-start.8 = (f32[8,64,512]{2,1,0:T(8,128)}, f32[8,64,512]{2,1,0:T(8,128)}, u32[]{:S(2)}, u32[]{:S(2)}) collective-permute-start(f32[8,64,512]{2,1,0:T(8,128)} %get-tuple-element.124), channel_id=1, source_target_pairs={{0,20},{4,24},{8,28},{12,0},{16,4},{20,8},{24,12},{28,16},{1,21},{... | collective-permute-start | bytes 3145736 | tf_op jit(solution)/shard_map/ppermute | solution.py:243
  56.3 25.5 %copy-start.78 = (f32[8,4]{0,1:T(4,128)}, f32[8,4]{0,1:T(4,128)S(1)}, u32[]{:S(2)}) copy-start(f32[8,4]{0,1:T(4,128)S(1)} %copy.340) | copy-start | bytes 388
  57.5 154.0 %copy-start.26 = (f32[8,4,4,128]{3,0,2,1:T(8,128)}, f32[8,4,4,128]{3,0,2,1:T(8,128)S(1)}, u32[]{:S(2)}) copy-start(f32[8,4,4,128]{3,0,2,1:T(8,128)S(1)} %fusion.127) | copy-start | bytes 196612
  62.9 12.7 %copy-start.41 = (f32[8,256]{1,0:T(8,128)}, f32[8,256]{1,0:T(8,128)S(1)}, u32[]{:S(2)}) copy-start(f32[8,256]{1,0:T(8,128)S(1)} %get-tuple-element.148) | copy-start | bytes 24580
  62.9 12.7 %copy-start.43 = (f32[8,256]{1,0:T(8,128)}, f32[8,256]{1,0:T(8,128)S(1)}, u32[]{:S(2)}) copy-start(f32[8,256]{1,0:T(8,128)S(1)} %get-tuple-element.149) | copy-start | bytes 24580
  62.9 12.7 %copy-start.45 = (f32[8,256]{1,0:T(8,128)}, f32[8,256]{1,0:T(8,128)S(1)}, u32[]{:S(2)}) copy-start(f32[8,256]{1,0:T(8,128)S(1)} %get-tuple-element.150) | copy-start | bytes 24580
  62.9 12.7 %copy-start.70 = (f32[4,128]{1,0:T(4,128)S(1)}, f32[4,128]{1,0:T(4,128)}, u32[]{:S(2)}) copy-start(f32[4,128]{1,0:T(4,128)} %get-tuple-element.180) | copy-start | bytes 6148
  62.9 12.7 %copy-start.75 = (f32[4,128]{1,0:T(4,128)S(1)}, f32[4,128]{1,0:T(4,128)}, u32[]{:S(2)}) copy-start(f32[4,128]{1,0:T(4,128)} %get-tuple-element.181) | copy-start | bytes 6148
  62.9 13.4 %copy-start.85 = (pred[4,4]{0,1:T(4,128)(4,1)S(1)}, pred[4,4]{0,1:T(4,128)(4,1)}, u32[]{:S(2)}) copy-start(pred[4,4]{0,1:T(4,128)(4,1)} %iota_compare_fusion.2) | copy-start | bytes 52
  81.7 100.9 %copy-start.29 = (f32[8,4,4,128]{3,2,1,0:T(4,128)}, f32[8,4,4,128]{3,2,1,0:T(4,128)S(1)}, u32[]{:S(2)}) copy-start(f32[8,4,4,128]{3,2,1,0:T(4,128)S(1)} %copy.359) | copy-start | bytes 196612
  84.2 62.2 %collective-permute-start.9 = (f32[8,64,512]{2,1,0:T(8,128)}, f32[8,64,512]{2,1,0:T(8,128)S(1)}, u32[]{:S(2)}, u32[]{:S(2)}) collective-permute-start(f32[8,64,512]{2,1,0:T(8,128)} %get-tuple-element.124), channel_id=1, source_target_pairs={{0,24},{4,28},{8,0},{12,4},{16,8},{20,12},{24,16},{28,20},{1,25},{... | collective-permute-start | bytes 3145736 | tf_op jit(solution)/shard_map/ppermute | solution.py:243
  87.9 59.6 %collective-permute-start.10 = (f32[8,64,512]{2,1,0:T(8,128)}, f32[8,64,512]{2,1,0:T(8,128)S(1)}, u32[]{:S(2)}, u32[]{:S(2)}) collective-permute-start(f32[8,64,512]{2,1,0:T(8,128)} %get-tuple-element.124), channel_id=1, source_target_pairs={{0,28},{4,0},{8,4},{12,8},{16,12},{20,16},{24,20},{28,24},{1,29},{... | collective-permute-start | bytes 3145736 | tf_op jit(solution)/shard_map/ppermute | solution.py:243
  148.7 7.9 %copy-start.89 = (pred[8]{0:T(512)(128)(4,1)S(1)}, pred[8]{0:T(512)(128)(4,1)}, u32[]{:S(2)}) copy-start(pred[8]{0:T(512)(128)(4,1)} %compare_and_fusion) | copy-start | bytes 28
  196.6 9.3 %copy-start.15 = (f32[8,4,64,256]{3,2,1,0:T(8,128)}, f32[8,4,64,256]{3,2,1,0:T(8,128)S(1)}, u32[]{:S(2)}) copy-start(f32[8,4,64,256]{3,2,1,0:T(8,128)S(1)} %get-tuple-element.187) | copy-start | bytes 6291460
  200.3 9.2 %copy-start.82 = (pred[4,4]{1,0:T(4,128)(4,1)S(1)}, pred[4,4]{1,0:T(4,128)(4,1)}, u32[]{:S(2)}) copy-start(pred[4,4]{1,0:T(4,128)(4,1)} %get-tuple-element.193) | copy-start | bytes 52
  200.3 10.3 %copy-start.51 = (s32[4,128]{1,0:T(4,128)S(1)}, s32[4,128]{1,0:T(4,128)}, u32[]{:S(2)}) copy-start(s32[4,128]{1,0:T(4,128)} %copy-done.50) | copy-start | bytes 6148
  200.3 12.6 %copy-start.90 = (pred[4,4]{1,0:T(4,128)(4,1)S(1)}, pred[4,4]{1,0:T(4,128)(4,1)}, u32[]{:S(2)}) copy-start(pred[4,4]{1,0:T(4,128)(4,1)} %get-tuple-element.192) | copy-start | bytes 52
  205.9 46.5 %collective-permute-start.11 = (f32[8,4,64,256]{3,2,1,0:T(8,128)}, f32[8,4,64,256]{3,2,1,0:T(8,128)S(1)}, u32[]{:S(2)}, u32[]{:S(2)}) collective-permute-start(f32[8,4,64,256]{3,2,1,0:T(8,128)} %broadcast_add_fusion), channel_id=1, source_target_pairs={{0,1},{1,2},{2,3},{4,5},{5,6},{6,7},{8,9},{9,10},{10,11},{12,13},{... | collective-permute-start | bytes 6291464 | tf_op jit(solution)/shard_map/ppermute | solution.py:18
  208.2 49.0 %collective-permute-start.12 = (f32[8,4,64,256]{3,2,1,0:T(8,128)}, f32[8,4,64,256]{3,2,1,0:T(8,128)}, u32[]{:S(2)}, u32[]{:S(2)}) collective-permute-start(f32[8,4,64,256]{3,2,1,0:T(8,128)} %fusion.99), channel_id=1, source_target_pairs={{1,0},{2,1},{3,2},{5,4},{6,5},{7,6},{9,8},{10,9},{11,10},{13,12},{... | collective-permute-start | bytes 6291464 | tf_op jit(solution)/shard_map/ppermute | solution.py:18
  210.6 52.3 %copy-start.72 = (f32[4,4]{1,0:T(4,128)}, f32[4,4]{1,0:T(4,128)S(1)}, u32[]{:S(2)}) copy-start(f32[4,4]{1,0:T(4,128)S(1)} %fusion.183) | copy-start | bytes 196
  212.3 50.6 %copy-start.60 = (f32[8,4]{1,0:T(8,128)}, f32[8,4]{1,0:T(8,128)S(1)}, u32[]{:S(2)}) copy-start(f32[8,4]{1,0:T(8,128)S(1)} %copy.364) | copy-start | bytes 388
  213.6 49.3 %copy-start.35 = (f32[4,8,4,4]{1,3,2,0:T(4,128)}, f32[4,8,4,4]{1,3,2,0:T(4,128)S(1)}, u32[]{:S(2)}) copy-start(f32[4,8,4,4]{1,3,2,0:T(4,128)S(1)} %get-tuple-element.172) | copy-start | bytes 6148
  213.6 49.3 %copy-start.39 = (f32[2,8,4,4]{1,3,2,0:T(4,128)}, f32[2,8,4,4]{1,3,2,0:T(4,128)S(1)}, u32[]{:S(2)}) copy-start(f32[2,8,4,4]{1,3,2,0:T(4,128)S(1)} %slice_multiply_fusion.4) | copy-start | bytes 3076
  214.6 53.6 %copy-start.1 = (f32[8,256,4,128]{3,2,1,0:T(4,128)S(1)}, f32[8,256,4,128]{3,2,1,0:T(4,128)}, u32[]{:S(2)}) copy-start(f32[8,256,4,128]{3,2,1,0:T(4,128)} %reshape_reshape.6) | copy-start | bytes 12582916
  214.6 53.6 %copy-start.2 = (f32[8,256,4,128]{3,2,1,0:T(4,128)S(1)}, f32[8,256,4,128]{3,2,1,0:T(4,128)}, u32[]{:S(2)}) copy-start(f32[8,256,4,128]{3,2,1,0:T(4,128)} %reshape_reshape.7) | copy-start | bytes 12582916
  262.9 48.0 %collective-permute-start.13 = (f32[8,4,64,256]{3,2,1,0:T(8,128)}, f32[8,4,64,256]{3,2,1,0:T(8,128)}, u32[]{:S(2)}, u32[]{:S(2)}) collective-permute-start(f32[8,4,64,256]{3,2,1,0:T(8,128)} %get-tuple-element.179), channel_id=1, source_target_pairs={{0,1},{1,2},{2,3},{4,5},{5,6},{6,7},{8,9},{9,10},{10,11},{12,13},{... | collective-permute-start | bytes 6291464 | tf_op jit(solution)/shard_map/ppermute | solution.py:18
  266.6 9.8 %copy-start.8 = (bf16[8,4,64,4,128]{4,3,2,1,0:T(4,128)(2,1)S(1)}, bf16[8,4,64,4,128]{4,3,2,1,0:T(4,128)(2,1)}, u32[]{:S(2)}) copy-start(bf16[8,4,64,4,128]{4,3,2,1,0:T(4,128)(2,1)} %copy-done.7) | copy-start | bytes 6291460
  266.6 9.8 %copy-start.31 = (f32[8,4,4,128]{3,2,1,0:T(4,128)S(1)}, f32[8,4,4,128]{3,2,1,0:T(4,128)}, u32[]{:S(2)}) copy-start(f32[8,4,4,128]{3,2,1,0:T(4,128)} %copy.375) | copy-start | bytes 196612
  266.6 50.5 %collective-permute-start.14 = (f32[8,4,64,256]{3,2,1,0:T(8,128)}, f32[8,4,64,256]{3,2,1,0:T(8,128)}, u32[]{:S(2)}, u32[]{:S(2)}) collective-permute-start(f32[8,4,64,256]{3,2,1,0:T(8,128)} %get-tuple-element.178), channel_id=1, source_target_pairs={{1,0},{2,1},{3,2},{5,4},{6,5},{7,6},{9,8},{10,9},{11,10},{13,12},{... | collective-permute-start | bytes 6291464 | tf_op jit(solution)/shard_map/ppermute | solution.py:18
  276.4 56.6 %slice-start = ((s8[8388608]{0:T(1024)(128)(4,1)}), s8[4194304]{0:T(1024)(128)(4,1)S(1)}, s32[]{:S(2)}) async-start(s8[8388608]{0:T(1024)(128)(4,1)} %bitcast.249), calls=%async_computation.4 | async-start | bytes 8388608
  284.2 48.8 %copy-start.3 = (f32[8,4,4,64,256]{4,3,1,2,0:T(8,128)}, f32[8,4,4,64,256]{4,3,1,2,0:T(8,128)S(1)}, u32[]{:S(2)}) copy-start(f32[8,4,4,64,256]{4,3,1,2,0:T(8,128)S(1)} %fusion.70) | copy-start | bytes 25165828
  284.2 32.9 %copy-start.61 = (f32[8,4]{1,0:T(8,128)S(1)}, f32[8,4]{1,0:T(8,128)}, u32[]{:S(2)}) copy-start(f32[8,4]{1,0:T(8,128)} %copy-done.60) | copy-start | bytes 388
  284.2 48.7 %slice-start.1 = ((s8[8388608]{0:T(1024)(128)(4,1)}), s8[4194304]{0:T(1024)(128)(4,1)S(1)}, s32[]{:S(2)}) async-start(s8[8388608]{0:T(1024)(128)(4,1)} %bitcast.249), calls=%async_computation.5 | async-start | bytes 8388608
  302.0 25.7 %copy-start.21 = (f32[8,4,128,128]{2,3,1,0:T(8,128)S(1)}, f32[8,4,128,128]{2,3,1,0:T(8,128)}, u32[]{:S(2)}) copy-start(f32[8,4,128,128]{2,3,1,0:T(8,128)} %get-tuple-element.100) | copy-start | bytes 6291460
  323.5 47.2 %collective-permute-start.15 = (f32[8,4,64,256]{3,2,1,0:T(8,128)}, f32[8,4,64,256]{3,2,1,0:T(8,128)}, u32[]{:S(2)}, u32[]{:S(2)}) collective-permute-start(f32[8,4,64,256]{3,2,1,0:T(8,128)} %get-tuple-element.177), channel_id=1, source_target_pairs={{0,1},{1,2},{2,3},{4,5},{5,6},{6,7},{8,9},{9,10},{10,11},{12,13},{... | collective-permute-start | bytes 6291464 | tf_op jit(solution)/shard_map/ppermute | solution.py:18
  326.2 49.9 %collective-permute-start.16 = (f32[8,4,64,256]{3,2,1,0:T(8,128)}, f32[8,4,64,256]{3,2,1,0:T(8,128)}, u32[]{:S(2)}, u32[]{:S(2)}) collective-permute-start(f32[8,4,64,256]{3,2,1,0:T(8,128)} %get-tuple-element.176), channel_id=1, source_target_pairs={{1,0},{2,1},{3,2},{5,4},{6,5},{7,6},{9,8},{10,9},{11,10},{13,12},{... | collective-permute-start | bytes 6291464 | tf_op jit(solution)/shard_map/ppermute | solution.py:18
  332.9 43.2 %copy-start.47 = (f32[8,4,4]{1,2,0:T(4,128)S(1)}, f32[8,4,4]{1,2,0:T(4,128)}, u32[]{:S(2)}) copy-start(f32[8,4,4]{1,2,0:T(4,128)} %copy.378) | copy-start | bytes 1540
  385.0 12.4 %copy-start.4 = (f32[8,4,4,64,256]{4,3,1,2,0:T(8,128)}, f32[8,4,4,64,256]{4,3,1,2,0:T(8,128)S(1)}, u32[]{:S(2)}) copy-start(f32[8,4,4,64,256]{4,3,1,2,0:T(8,128)S(1)} %get-tuple-element.136) | copy-start | bytes 25165828
  402.8 134.6 %reduce-scatter.5.cloned.1.call-start = ((), (), s32[]{:S(2)}) async-start(), calls=%async_computation.3 | async-start | bytes 4718592 | tf_op jit(solution)/shard_map/reduce_scatter | solution.py:287
  415.6 11.6 %copy-start.9 = (bf16[8,4,64,4,128]{4,3,2,1,0:T(4,128)(2,1)S(1)}, bf16[8,4,64,4,128]{4,3,2,1,0:T(4,128)(2,1)}, u32[]{:S(2)}) copy-start(bf16[8,4,64,4,128]{4,3,2,1,0:T(4,128)(2,1)} %copy-done.7) | copy-start | bytes 6291460
  415.6 11.6 %copy-start.32 = (f32[8,4,4,128]{3,2,1,0:T(4,128)S(1)}, f32[8,4,4,128]{3,2,1,0:T(4,128)}, u32[]{:S(2)}) copy-start(f32[8,4,4,128]{3,2,1,0:T(4,128)} %copy.375) | copy-start | bytes 196612
  510.1 8.0 %copy-start.25 = (f32[8,4,128,128]{2,3,1,0:T(8,128)S(1)}, f32[8,4,128,128]{2,3,1,0:T(8,128)}, u32[]{:S(2)}) copy-start(f32[8,4,128,128]{2,3,1,0:T(8,128)} %fusion.59) | copy-start | bytes 6291460
  542.5 7.7 %collective-permute-start.17 = (f32[8,320,3]{1,0,2:T(8,128)S(1)}, f32[8,320,3]{1,0,2:T(8,128)S(1)}, u32[]{:S(2)}, u32[]{:S(2)}) collective-permute-start(f32[8,320,3]{1,0,2:T(8,128)S(1)} %copy.399), channel_id=1, source_target_pairs={{1,0},{2,1},{3,2},{5,4},{6,5},{7,6},{9,8},{10,9},{11,10},{13,12},{... | collective-permute-start | bytes 92168 | tf_op jit(solution)/shard_map/ppermute | solution.py:18
  (52 other events, 168.6 us)
Sparse Core Ops, SparseCore 0:
  403.0 48.6 reduce-scatter.2
  462.4 48.7 reduce-scatter.4

commit v12 on v10

--- a/solution.py
+++ b/solution.py
@@ -236,10 +236,22 @@
         jnp.concatenate([b_in, c_in], axis=1).astype(jnp.float32),
         rim_chan.astype(jnp.float32),
     )
-    both_conv = lax.all_gather(
-        bc_conv.reshape(groups_here, 2, b_width, length), "seq", axis=2, tiled=True
-    )
-    b_conv, c_conv = (both_conv[:, 0], both_conv[:, 1])
+    bc_every = jnp.concatenate(
+        [
+            lax.all_gather(b_in, "seq", axis=1, tiled=True),
+            lax.all_gather(c_in, "seq", axis=1, tiled=True),
+        ],
+        axis=1,
+    )
+    rim_every = passed_along(bc_every[:, :, length - (TAPS - 1) :], "head", 1)
+    every_conv = jax.vmap(conv_part, in_axes=each_group)(
+        bc_every.astype(jnp.float32),
+        rim_every.astype(jnp.float32),
+        weight_all[:, :, x_total:],
+        bias_all[:, x_total:],
+        segment_extended,
+    )
+    b_conv, c_conv = (every_conv[:, :STATE], every_conv[:, STATE:])
 
     def local_terms(x_float, b_float, c_float, dt_float):
         return jax.vmap(scan_part, in_axes=(0, 0, 0, 0, 0, 0, 0, None))(

time: 498 us -> 474 us (0.952)
  waiting for transfers between devices: 107 us -> 75 us
  other arithmetic: 106 us -> 119 us
  matrix products: 141 us -> 130 us
  starting transfers between devices: 27.7 us -> 32.9 us
    all_gather x1 -> x2, waiting for transfers between devices: 24.8 us -> 0.02 us  [the longest x1 0.02 us: shards(): lax.all_gather(b_in, 'seq', axis=1, tiled=True)]
    slice x3, local copies, waits for them, and re-layouts: 18.9 us -> 4.17 us  [the longest x1 4.17 us: shards(): b_conv, c_conv = (every_conv[:, :STATE], every_conv[:, STATE:])]
    all_gather x0 -> x2, local copies, waits for them, and re-layouts: none -> 8.54 us  [the longest x1 4.27 us: shards(): lax.all_gather(b_in, 'seq', axis=1, tiled=True)]
    ppermute x8 -> x9, waiting for transfers between devices: 81.9 us -> 74.8 us  [passed_along(): lax.ppermute(value, axis, [(source, source + steps) for source in range(f...]
    ppermute x8 -> x9, starting transfers between devices: 19.9 us -> 25.5 us  [passed_along(): lax.ppermute(value, axis, [(source, source + steps) for source in range(f...]
    mul x2, other arithmetic: 14.7 us -> 20.1 us  [conv_silu(): return jax.nn.silu(total)]
    unnamed x198 -> x236, local copies, waits for them, and re-layouts: 18.6 us -> 21.7 us
  transfers between devices with their start and end apart: 14 -> 16, of which waited for: 7 -> 7; matrix products, arithmetic and copies ran while one was open for 47% -> 54% of each run, Pallas kernels for 0% -> 0%
where the time goes in v12:
time: 474 us; the launch traced here: 466 us
  matrix products  130 us (27%)
  other arithmetic  119 us (25%)
  local copies, waits for them, and re-layouts  94.1 us (20%)
  waiting for transfers between devices  75 us (16%)
  starting transfers between devices  32.9 us (7%)
  between operations  15.6 us (3%)
    ppermute x9, waiting for transfers between devices, passed_along(): lax.ppermute(value, axis, [(source, source + steps) for source in range(f...  74.8 us
    dot_general x3, matrix products, span_terms(): jnp.einsum('hcij,hpcj->hpci', decay * scores[None], weighted, precision=p...  41.3 us
    dot_general x3, matrix products, span_terms(): jnp.einsum('hpcj,hcj,ncj->hcpn', weighted, keep_end, b_three, precision=p...  37.3 us
    dot_general x3, matrix products, assemble(): jnp.einsum('nci,hci,chpn->hpci', c_three, entry, starts, precision=precise)  28.6 us
    reduce_sum x2, other arithmetic, weighted_sum(): return jnp.sum(weight[..., None, None] * stacked, axis=-3)  26.3 us
    ppermute x9, starting transfers between devices, passed_along(): lax.ppermute(value, axis, [(source, source + steps) for source in range(f...  25.5 us
    unnamed x236, local copies, waits for them, and re-layouts  21.7 us
    mul x2, other arithmetic, conv_silu(): return jax.nn.silu(total)  20.1 us
  transfers between devices with their start and end apart: 16, of which 7 were waited for; matrix products, arithmetic and copies ran while one was open for 54% of the time, Pallas kernels for 0%

profile of v12, /device:TPU:0, one launch (start us, length us, event | category | flops | bytes accessed | tf_op | source)
XLA Modules:
  0.0 466.1 jit_solution(14452912294817312281)
XLA Ops:
  7.2 1.8 copy.347
  10.9 3.1 collective-permute-start
  14.0 2.6 collective-permute-start.1
  17.9 1.7 copy.336
  19.7 4.5 copy.335
  24.2 1.7 copy.337
  26.7 2.6 collective-permute-start.3
  34.7 2.6 convert_element_type.93
  37.5 2.6 reshape.363
  41.2 1.9 pad_maximum_fusion.5
  43.1 2.7 gather_fusion
  45.8 2.0 gather.7
  49.8 11.9 %fusion.63 = (f32[8,256,512]{2,1,0:T(8,128)}, f32[8,256,512]{2,1,0:T(8,128)}) fusion(f32[8,256,512]{2,1,0:T(8,128)} %convert_element_type.93, f32[8,256]{1,0:T(8,128)S(1)} %get-tuple-element.150, f32[512]{0:T(512)S(1)} %get-tuple-element.185, f32[8,256,3]{2,1,0:T(8,128)S(1)} %copy.338, f32[8,256]{1,0:T(8,128)S(1)} %get-tuple-element.148, ...), kind=kLoop, calls=%fused_computation.109 | loop fusion | flops 18874368 | bytes 12654592 | tf_op jit(solution)/shard_map/jvp(vmap(jit(silu)))/mul | solution.py:53
  62.5 5.2 %reshape.359 = f32[8,4,64,4,128]{4,3,2,1,0:T(4,128)} reshape(f32[8,256,512]{2,1,0:T(8,128)} %get-tuple-element.122) | data formatting | bytes 8388608 | tf_op jit(solution)/shard_map/jvp(vmap())/reshape | solution.py:59
  69.7 4.3 copy.349
  74.0 4.3 copy.350
  79.2 2.3 collective-permute-start.4
  82.9 8.2 %divide_multiply_fusion = f32[8,512,512]{1,2,0:T(8,128)} fusion(f32[8,512,512]{1,2,0:T(8,128)S(1)} %fusion.30, f32[8,512,3]{1,2,0:T(4,128)S(1)} %convert_element_type.100, f32[8,512]{1,0:T(8,128)S(1)} %get-tuple-element.152, f32[512]{0:T(512)S(1)} %copy-done.69, f32[8,512]{1,0:T(8,128)S(1)} %get-tuple-element.153, f32[512]{0:T(512)S(1)} %copy-done.72, ...), kind=kLoop, calls=%fused_computation.42 | loop fusion | flops 37748736 | bytes 16914432 | tf_op jit(solution)/shard_map/vmap(jit(silu))/mul | solution.py:53
  91.1 4.2 fusion.180
  95.7 10.0 %multiply_reduce_fusion.5 = (f32[8,4,64,256]{3,2,1,0:T(8,128)S(1)}, f32[8,4,4,64,256]{4,3,1,2,0:T(8,128)}) fusion(f32[8,4,4]{1,2,0:T(4,128)S(1)} %copy.365, f32[8,256,4,128,1]{1,3,4,2,0:T(8,128)S(1)} %bitcast.252, f32[8,4,64,4,128]{4,3,2,1,0:T(4,128)S(1)} %copy-done.7, f32[8,4,4,128]{3,2,1,0:T(4,128)S(1)} %copy.359, f32[8,4,4,128]{3,2,1,0:T(4,128)S(1)} %copy.341), kind=kOutput, calls=%fused_computation.41 | convolution fusion | flops 3226992640 | bytes 19005952 | tf_op jit(solution)/shard_map/jvp(vmap(hpcj,hcj,ncj->hcpn))/dot_general | solution.py:78
  105.7 1.7 broadcast_add_fusion
  107.4 5.6 %fusion.91 = f32[8,4,64,256]{3,2,1,0:T(8,128)} fusion(f32[8,256,4,128,1]{1,3,2,4,0:T(8,128)S(1)} %bitcast.247, f32[8,4,4,128]{3,2,1,0:T(4,128)S(1)} %copy.369, bf16[8,4,64,4,128]{4,3,2,1,0:T(4,128)(2,1)S(1)} %reshape.363), kind=kOutput, calls=%fused_computation.134 | convolution fusion | flops 3223322624 | bytes 8454144 | tf_op jit(solution)/shard_map/ghpci,ghci,gnci->ghpn/dot_general | solution.py:275
  113.0 4.3 collective-permute-start.5
  122.7 38.1 %collective-permute-done.5 = f32[8,4,64,256]{3,2,1,0:T(8,128)S(1)} collective-permute-done((f32[8,4,64,256]{3,2,1,0:T(8,128)}, f32[8,4,64,256]{3,2,1,0:T(8,128)S(1)}, u32[]{:S(2)}, u32[]{:S(2)}) %collective-permute-start.5) | collective-permute-done | bytes 2097184 | tf_op jit(solution)/shard_map/ppermute | solution.py:18
  160.7 4.2 collective-permute-done.6
  165.0 5.7 %multiply_add_fusion.2 = (f32[8,4,64,256]{3,2,1,0:T(8,128)}, f32[8,4,64,256]{3,2,1,0:T(8,128)}) fusion(f32[8,4,64,256]{3,2,1,0:T(8,128)} %fusion.91, f32[8,4,64,256]{3,2,1,0:T(8,128)} %collective-permute-done.6, f32[8,4]{1,0:T(8,128)S(1)} %copy.364, f32[8,4,64,256]{3,2,1,0:T(8,128)S(1)} %collective-permute-done.5, f32[8,4,64,256]{3,2,1,0:T(8,128)} %copy-done.18, ...), kind=kLoop, calls=%fused_computation.124 | loop fusion | flops 2621440 | bytes 12583168 | tf_op jit(solution)/shard_map/add | solution.py:31
  170.7 4.6 collective-permute-start.7
  175.3 1.7 collective-permute-start.8
  177.0 5.8 %fusion.182 = f32[8,4,128,128]{2,3,1,0:T(8,128)} fusion(f32[8,256,4,128]{1,3,2,0:T(8,128)S(1)} %bitcast.249, f32[8,256,4,128]{1,3,2,0:T(8,128)S(1)} %bitcast.254), kind=kOutput, calls=%fused_computation.343 | convolution fusion | flops 1610612736 | bytes 10485760 | tf_op jit(solution)/shard_map/jvp(vmap(nci,ncj->cij))/dot_general | solution.py:72
  182.8 7.5 %fusion.73 = f32[8,4,4,64,256]{4,3,1,2,0:T(8,128)S(1)} fusion(f32[8,256,4,128,1]{1,3,4,2,0:T(8,128)S(1)} %bitcast.250, f32[8,4,4,128]{3,2,1,0:T(4,128)S(1)} %copy.375, bf16[8,4,64,4,128]{4,3,2,1,0:T(4,128)(2,1)S(1)} %copy-done.11), kind=kOutput, calls=%fused_computation.118 | convolution fusion | flops 3223322624 | bytes 14745600 | tf_op jit(solution)/shard_map/transpose(jvp(vmap(nci,hci,chpn->hpci)))/dot_general | solution.py:149
  190.4 17.1 %fusion.112 = (f32[8,4,4,128]{3,2,1,0:T(4,128)}, f32[8,4,4,128]{3,2,1,0:T(4,128)}, f32[8,4,128,128]{2,3,1,0:T(8,128)}) fusion(f32[8,4,4,128]{3,2,1,0:T(4,128)S(1)} %copy.344, f32[4,128,128]{1,2,0:T(8,128)} %compare_select_fusion, f32[8,4,128,128]{2,3,1,0:T(8,128)} %fusion.182, bf16[8,4,4,64,128]{4,2,3,1,0:T(4,128)(2,1)} %bitcast.258, ...), kind=kOutput, calls=%fused_computation.168 | convolution fusion | flops 1642561536 | bytes 11010048 | tf_op jit(solution)/shard_map/transpose(jvp(vmap(hcij,hpcj->hpci)))/dot_general | solution.py:74
  207.5 9.6 %collective-permute-done.7 = f32[8,4,64,256]{3,2,1,0:T(8,128)} collective-permute-done((f32[8,4,64,256]{3,2,1,0:T(8,128)}, f32[8,4,64,256]{3,2,1,0:T(8,128)}, u32[]{:S(2)}, u32[]{:S(2)}) %collective-permute-start.7) | collective-permute-done | bytes 2097184 | tf_op jit(solution)/shard_map/ppermute | solution.py:18
  217.0 5.4 %collective-permute-done.8 = f32[8,4,64,256]{3,2,1,0:T(8,128)} collective-permute-done((f32[8,4,64,256]{3,2,1,0:T(8,128)}, f32[8,4,64,256]{3,2,1,0:T(8,128)}, u32[]{:S(2)}, u32[]{:S(2)}) %collective-permute-start.8) | collective-permute-done | bytes 2097184 | tf_op jit(solution)/shard_map/ppermute | solution.py:18
  222.4 6.3 %multiply_add_fusion = (f32[8,4,64,256]{3,2,1,0:T(8,128)}, f32[8,4,64,256]{3,2,1,0:T(8,128)}) fusion(f32[8,4,64,256]{3,2,1,0:T(8,128)} %fusion.91, f32[8,4,64,256]{3,2,1,0:T(8,128)} %collective-permute-done.8, f32[8,4]{1,0:T(8,128)S(1)} %copy.364, f32[8,4,64,256]{3,2,1,0:T(8,128)} %collective-permute-done.7, f32[8,4,64,256]{3,2,1,0:T(8,128)} %copy-done.18, ...), kind=kLoop, calls=%fused_computation.122 | loop fusion | flops 2621440 | bytes 12583168 | tf_op jit(solution)/shard_map/add | solution.py:31
  230.0 5.9 %collective-permute-start.9 = (f32[8,4,64,256]{3,2,1,0:T(8,128)}, f32[8,4,64,256]{3,2,1,0:T(8,128)}, u32[]{:S(2)}, u32[]{:S(2)}) collective-permute-start(f32[8,4,64,256]{3,2,1,0:T(8,128)} %get-tuple-element.179), channel_id=1, source_target_pairs={{0,1},{1,2},{2,3},{4,5},{5,6},{6,7},{8,9},{9,10},{10,11},{12,13},{... | collective-permute-start | bytes 6291464 | tf_op jit(solution)/shard_map/ppermute | solution.py:18
  236.0 5.1 %fusion.183 = f32[8,4,128,256]{3,2,1,0:T(8,128)} fusion(f32[8,4,128,128]{2,3,1,0:T(8,128)S(1)} %copy-done.24, f32[8,256,4,128]{1,3,2,0:T(8,128)S(1)} %bitcast.251), kind=kOutput, calls=%fused_computation.344 | convolution fusion | flops 1610612736 | bytes 10485760 | tf_op jit(solution)/shard_map/transpose(jvp(vmap(nci,ncj->cij)))/dot_general | solution.py:72
  241.1 17.7 %multiply_reduce_fusion = (f32[8,4,4,4]{3,2,1,0:T(4,128)}, f32[8,4,4,64,256]{4,3,2,1,0:T(8,128)}, f32[8,4,4,64,256]{4,3,2,1,0:T(8,128)}) fusion(f32[8,4,4,4]{3,2,1,0:T(4,128)S(1)} %bitcast_multiply_fusion.8, f32[8,4,4,64,256]{4,3,1,2,0:T(8,128)S(1)} %bitcast.257, f32[8,4,4,64,256]{4,3,1,2,0:T(8,128)S(1)} %fusion.73), kind=kLoop, calls=%fused_computation.3 | loop fusion | flops 46136832 | bytes 33558528 | tf_op jit(solution)/shard_map/transpose(jvp(vmap()))/reduce_sum | solution.py:131
  258.8 16.2 %collective-permute-done.10 = f32[8,4,64,256]{3,2,1,0:T(8,128)} collective-permute-done((f32[8,4,64,256]{3,2,1,0:T(8,128)}, f32[8,4,64,256]{3,2,1,0:T(8,128)}, u32[]{:S(2)}, u32[]{:S(2)}) %collective-permute-start.10) | collective-permute-done | bytes 2097184 | tf_op jit(solution)/shard_map/ppermute | solution.py:18
  276.2 8.6 %multiply_reduce_fusion.4 = (f32[8,4,4]{1,2,0:T(4,128)}, f32[8,4,4,64,256]{4,3,1,2,0:T(8,128)S(1)}) fusion(f32[8,4,4,64,256]{4,3,1,2,0:T(8,128)} %get-tuple-element.190, f32[8,4,64,256]{3,2,1,0:T(8,128)} %collective-permute-done.10, f32[8,4,4,64,256]{4,3,2,1,0:T(8,128)} %get-tuple-element.103, f32[8,4,4]{1,2,0:T(4,128)S(1)} %copy.378), kind=kLoop, calls=%fused_computation.40 | loop fusion | flops 8388480 | bytes 27264000 | tf_op jit(solution)/shard_map/transpose(jvp(vmap()))/reduce_sum | solution.py:131
  284.8 12.4 %bitcast_add_fusion.2 = f32[8,256,4,128]{1,3,2,0:T(8,128)} fusion(f32[8,4,128,256]{3,2,1,0:T(8,128)} %fusion.183, f32[8,4,4,64,256]{4,3,1,2,0:T(8,128)S(1)} %get-tuple-element.134, f32[8,4,64,4,128]{4,3,2,1,0:T(4,128)S(1)} %copy-done.8, f32[8,4,4,128]{3,2,1,0:T(4,128)S(1)} %copy-done.42, f32[8,4,4,128]{3,2,1,0:T(4,128)S(1)} %copy.341), kind=kOutput, calls=%fused_computation.80 | convolution fusion | flops 3224371200 | bytes 21102592 | tf_op jit(solution)/shard_map/transpose(jvp(vmap(hpcj,hcj,ncj->hcpn)))/dot_general | solution.py:78
  297.1 5.3 %copy.393 = f32[8,256,512]{2,1,0:T(8,128)} copy(f32[8,256,512]{1,2,0:T(8,128)} %bitcast.261) | data formatting | bytes 8388608 | tf_op jit(solution)/shard_map/transpose(jvp(vmap()))/reshape | solution.py:60
  309.4 2.9 multiply_reduce_fusion.6
  313.1 12.2 %multiply_reduce_fusion.3 = (f32[8,4,4]{1,2,0:T(4,128)S(1)}, f32[8,4,4,64,256]{4,3,1,2,0:T(8,128)}) fusion(f32[8,4,4,64,256]{4,3,1,2,0:T(8,128)} %copy-done.5, f32[8,4,64,256]{3,2,1,0:T(8,128)} %collective-permute-done.9, f32[8,4,4]{1,2,0:T(4,128)S(1)} %copy.363, f32[8,4,4,64,256]{4,3,2,1,0:T(8,128)} %get-tuple-element.102), kind=kLoop, calls=%fused_computation.39 | loop fusion | flops 8388480 | bytes 27264000 | tf_op jit(solution)/shard_map/transpose(jvp(vmap()))/reduce_sum | solution.py:142
  325.4 9.9 %fusion.26 = f32[8,4,128,256,1]{3,2,4,1,0:T(8,128)S(1)} fusion(f32[8,4,4,64,256]{4,3,1,2,0:T(8,128)} %get-tuple-element.136, f32[8,4,4,128]{3,2,1,0:T(4,128)S(1)} %copy-done.45, bf16[8,4,64,4,128]{4,3,2,1,0:T(4,128)(2,1)S(1)} %copy-done.12), kind=kOutput, calls=%fused_computation.43 | convolution fusion | flops 3223322624 | bytes 14745600 | tf_op jit(solution)/shard_map/transpose(jvp(vmap(nci,hci,chpn->hpci)))/dot_general | solution.py:149
  335.3 5.3 %bitcast_add_fusion.3 = f32[8,4,128,256]{3,2,1,0:T(8,128)} fusion(f32[8,4,128,256,1]{3,2,4,1,0:T(8,128)S(1)} %fusion.26, f32[8,4,128,128]{2,3,1,0:T(8,128)S(1)} %copy-done.25, f32[8,256,4,128]{1,3,2,0:T(8,128)S(1)} %bitcast.255), kind=kOutput, calls=%fused_computation.81 | convolution fusion | flops 1611661312 | bytes 14680064 | tf_op jit(solution)/shard_map/transpose(jvp(vmap(nci,ncj->cij)))/dot_general | solution.py:72
  340.6 5.4 %copy.398 = f32[8,256,512]{2,1,0:T(8,128)} copy(f32[8,256,512]{1,2,0:T(8,128)} %bitcast.260) | data formatting | bytes 8388608 | tf_op jit(solution)/shard_map/transpose(jvp(vmap()))/reshape | solution.py:61
  346.3 15.0 %fusion.51 = (f32[8,4,4,128]{3,2,1,0:T(4,128)S(1)}, f32[8,4,4,64,128]{4,3,1,2,0:T(8,128)}) fusion(f32[8,4,64,4,128]{4,3,2,1,0:T(4,128)} %reshape.359, f32[8,4,4,128]{3,2,1,0:T(4,128)S(1)} %copy-done.36, f32[8,4,4,64,256]{4,3,1,2,0:T(8,128)} %copy-done.6, f32[8,256,4,128,1]{1,3,2,4,0:T(8,128)} %bitcast.253), kind=kOutput, calls=%fused_computation.89 | convolution fusion | flops 3224354816 | bytes 21102592 | tf_op jit(solution)/shard_map/transpose(jvp(vmap(hpcj,hcj,ncj->hcpn)))/dot_general | solution.py:78
  365.9 14.6 %fusion.49 = (f32[8,4,4,128]{3,2,1,0:T(4,128)}, f32[8,4,64,4,128]{4,2,3,1,0:T(8,128)}) fusion(f32[8,4,64,4,128]{4,3,2,1,0:T(4,128)} %reshape.359, f32[8,4,4,128]{3,2,1,0:T(4,128)S(1)} %copy-done.36, bf16[8,4,64,4,128]{4,3,2,1,0:T(4,128)(2,1)S(1)} %copy-done.12, f32[8,4]{1,0:T(8,128)} %constant_dynamic-slice_fusion.4, ...), kind=kOutput, calls=%fused_computation.85 | convolution fusion | flops 1627373568 | bytes 19398784 | tf_op jit(solution)/shard_map/transpose(jvp(vmap(hcij,hpcj->hpci)))/dot_general | solution.py:74
  382.0 11.2 %fusion.28 = f32[8,4,4,64,128]{4,3,2,1,0:T(8,128)S(1)} fusion(f32[8,256,4,128,1]{1,3,4,2,0:T(8,128)} %bitcast.248, f32[8,4,4,64,256]{4,3,1,2,0:T(8,128)} %get-tuple-element.136), kind=kOutput, calls=%fused_computation.45 | convolution fusion | flops 3221225472 | bytes 16777216 | tf_op jit(solution)/shard_map/jvp(vmap(nci,hci,chpn->hpci))/dot_general | solution.py:149
  397.1 5.7 %copy.388 = f32[8,4,64,4,128]{4,3,2,1,0:T(4,128)} copy(f32[8,4,64,4,128]{4,2,3,1,0:T(8,128)S(1)} %copy-done.27) | data formatting | bytes 8388608 | tf_op jit(solution)/shard_map/transpose(jvp(vmap()))/add_any | solution.py:73
  402.8 5.5 %reshape.366 = f32[8,256,512]{2,1,0:T(8,128)} reshape(f32[8,4,64,4,128]{4,3,2,1,0:T(4,128)} %copy.388) | data formatting | bytes 8388608 | tf_op jit(solution)/shard_map/transpose(jvp(vmap()))/reshape | solution.py:59
  408.3 4.4 broadcast_multiply_fusion
  414.8 4.7 %pad_add_fusion = f32[8,256,515]{2,1,0:T(8,128)S(1)} fusion(f32[8,256,512]{2,1,0:T(8,128)S(1)} %get-tuple-element.130, f32[8,256,512]{2,1,0:T(8,128)S(1)} %get-tuple-element.129, f32[8,256,512]{2,1,0:T(8,128)S(1)} %get-tuple-element.128, f32[8,256,512]{2,1,0:T(8,128)S(1)} %get-tuple-element.112), kind=kLoop, calls=%fused_computation.57 | loop fusion | flops 3164160 | bytes 20996096 | tf_op jit(solution)/shard_map/transpose(jvp(vmap()))/add_any | solution.py:51
  419.5 3.3 split.16
  422.8 1.7 copy-done.22
  424.4 9.6 %fusion.52 = bf16[8,4,64,4,128]{4,2,3,1,0:T(8,128)(2,1)S(1)} fusion(f32[8,4,4,64,128]{4,3,2,1,0:T(8,128)S(1)} %copy-done.22, f32[8,4,64,4,128]{4,3,2,1,0:T(4,128)S(1)} %copy-done.9, f32[8,4,128,128]{2,3,1,0:T(8,128)S(1)} %copy-done.33, f32[4,128,128]{1,2,0:T(8,128)S(1)} %copy-done.50, f32[8,4,4,128]{3,2,1,0:T(4,128)S(1)} %copy-done.78, ...), kind=kOutput, calls=%fused_computation.91 | convolution fusion | flops 1625292800 | bytes 13041792 | tf_op jit(solution)/shard_map/jvp(vmap(hcij,hpcj->hpci))/dot_general | solution.py:74
  434.1 2.0 copy.376
  436.1 2.2 convert_element_type.107
  438.3 2.5 pad_add_fusion.3
  443.1 1.6 broadcast_multiply_fusion.1
  448.3 1.6 collective-permute-start.11
  449.9 2.9 slice_maximum_fusion
  454.2 1.8 copy.401
  457.8 1.5 slice.330
  (381 shorter events, 54.1 us)
Async XLA Ops:
  7.2 17.0 %copy-start.29 = (bf16[8,32,512]{2,1,0:T(8,128)(2,1)S(1)}, bf16[8,32,512]{2,1,0:T(8,128)(2,1)}, u32[]{:S(2)}) copy-start(bf16[8,32,512]{2,1,0:T(8,128)(2,1)} %param.15) | copy-start | bytes 786436
  7.2 62.5 %all-gather.3.cloned.1.call-start = ((), (), s32[]{:S(2)}) async-start(), calls=%async_computation.2 | async-start | bytes 2359296 | tf_op jit(solution)/shard_map/all_gather | solution.py:241
  9.1 64.9 %all-gather.5.cloned.1.call-start = ((), (), s32[]{:S(2)}) async-start(), calls=%async_computation.3 | async-start | bytes 2359296 | tf_op jit(solution)/shard_map/all_gather | solution.py:242
  10.9 30.2 %collective-permute-start = (f32[2,12896]{1,0:T(2,128)S(1)}, f32[2,12896]{1,0:T(2,128)}, u32[]{:S(2)}, u32[]{:S(2)}) collective-permute-start(f32[2,12896]{1,0:T(2,128)S(1)} %concatenate.45), channel_id=1, source_target_pairs={{0,1},{1,2},{2,3},{3,0},{4,5},{5,6},{6,7},{7,4},{8,9},{9,10},{10,1... | collective-permute-start | bytes 309512 | tf_op jit(solution)/shard_map/ppermute | solution.py:187
  14.0 27.1 %collective-permute-start.1 = (f32[2,12896]{1,0:T(2,128)S(1)}, f32[2,12896]{1,0:T(2,128)}, u32[]{:S(2)}, u32[]{:S(2)}) collective-permute-start(f32[2,12896]{1,0:T(2,128)S(1)} %concatenate.45), channel_id=1, source_target_pairs={{0,2},{1,3},{2,0},{3,1},{4,6},{5,7},{6,4},{7,5},{8,10},{9,11},{10,... | collective-permute-start | bytes 309512 | tf_op jit(solution)/shard_map/ppermute | solution.py:187
  16.6 24.6 %collective-permute-start.2 = (f32[2,12896]{1,0:T(2,128)S(1)}, f32[2,12896]{1,0:T(2,128)}, u32[]{:S(2)}, u32[]{:S(2)}) collective-permute-start(f32[2,12896]{1,0:T(2,128)S(1)} %concatenate.45), channel_id=1, source_target_pairs={{0,3},{1,0},{2,1},{3,2},{4,7},{5,4},{6,5},{7,6},{8,11},{9,8},{10,9... | collective-permute-start | bytes 309512 | tf_op jit(solution)/shard_map/ppermute | solution.py:187
  24.2 10.5 %copy-start.26 = (bf16[8,256,512]{2,1,0:T(8,128)(2,1)S(1)}, bf16[8,256,512]{2,1,0:T(8,128)(2,1)}, u32[]{:S(2)}) copy-start(bf16[8,256,512]{2,1,0:T(8,128)(2,1)} %param.13) | copy-start | bytes 6291460
  26.7 13.4 %collective-permute-start.3 = (bf16[8,320,3]{1,0,2:T(8,128)(2,1)S(1)}, bf16[8,320,3]{1,0,2:T(8,128)(2,1)S(1)}, u32[]{:S(2)}, u32[]{:S(2)}) collective-permute-start(bf16[8,320,3]{1,0,2:T(8,128)(2,1)S(1)} %pad_maximum_fusion.6), channel_id=1, source_target_pairs={{0,1},{1,2},{2,3},{4,5},{5,6},{6,7},{8,9},{9,10},{10,11},{12,13},{... | collective-permute-start | bytes 46088 | tf_op jit(solution)/shard_map/ppermute | solution.py:18
  30.2 410.7 %reduce-scatter.3.cloned.1.call-start = ((), (), s32[]{:S(2)}) async-start(), calls=%async_computation.4 | async-start | bytes 4718592 | tf_op jit(solution)/shard_map/reduce_scatter | solution.py:291
  30.6 9.5 %copy-start.80 = (s32[4,128]{1,0:T(4,128)}, s32[4,128]{1,0:T(4,128)S(1)}, u32[]{:S(2)}) copy-start(s32[4,128]{1,0:T(4,128)S(1)} %slice_bitcast_fusion.4) | copy-start | bytes 6148
  31.7 18.1 %copy-start.68 = (f32[512]{0:T(512)}, f32[512]{0:T(512)S(1)}, u32[]{:S(2)}) copy-start(f32[512]{0:T(512)S(1)} %get-tuple-element.185) | copy-start | bytes 6148
  31.7 18.1 %copy-start.71 = (f32[512]{0:T(512)}, f32[512]{0:T(512)S(1)}, u32[]{:S(2)}) copy-start(f32[512]{0:T(512)S(1)} %get-tuple-element.186) | copy-start | bytes 6148
  40.1 67.3 %copy-start.10 = (bf16[8,4,64,4,128]{4,3,2,1,0:T(4,128)(2,1)}, bf16[8,4,64,4,128]{4,3,2,1,0:T(4,128)(2,1)S(1)}, u32[]{:S(2)}) copy-start(bf16[8,4,64,4,128]{4,3,2,1,0:T(4,128)(2,1)S(1)} %reshape.363) | copy-start | bytes 6291460
  48.9 13.5 %copy-start.34 = (f32[8,12896]{1,0:T(8,128)}, f32[8,12896]{1,0:T(8,128)S(1)}, u32[]{:S(2)}) copy-start(f32[8,12896]{1,0:T(8,128)S(1)} %broadcast_select_fusion) | copy-start | bytes 1238020
  49.0 20.6 %copy-start.40 = (f32[8,10240]{1,0:T(8,128)}, f32[8,10240]{1,0:T(8,128)S(1)}, u32[]{:S(2)}) copy-start(f32[8,10240]{1,0:T(8,128)S(1)} %slice.282) | copy-start | bytes 983044
  49.8 12.0 %copy-start.58 = (f32[8,256]{1,0:T(8,128)}, f32[8,256]{1,0:T(8,128)S(1)}, u32[]{:S(2)}) copy-start(f32[8,256]{1,0:T(8,128)S(1)} %get-tuple-element.147) | copy-start | bytes 24580
  49.8 12.0 %copy-start.60 = (f32[8,256]{1,0:T(8,128)}, f32[8,256]{1,0:T(8,128)S(1)}, u32[]{:S(2)}) copy-start(f32[8,256]{1,0:T(8,128)S(1)} %get-tuple-element.148) | copy-start | bytes 24580
  49.8 12.0 %copy-start.62 = (f32[8,256]{1,0:T(8,128)}, f32[8,256]{1,0:T(8,128)S(1)}, u32[]{:S(2)}) copy-start(f32[8,256]{1,0:T(8,128)S(1)} %get-tuple-element.149) | copy-start | bytes 24580
  49.8 12.0 %copy-start.64 = (f32[8,256]{1,0:T(8,128)}, f32[8,256]{1,0:T(8,128)S(1)}, u32[]{:S(2)}) copy-start(f32[8,256]{1,0:T(8,128)S(1)} %get-tuple-element.150) | copy-start | bytes 24580
  62.5 6.7 %copy-start.104 = (pred[4,4]{0,1:T(4,128)(4,1)S(1)}, pred[4,4]{0,1:T(4,128)(4,1)}, u32[]{:S(2)}) copy-start(pred[4,4]{0,1:T(4,128)(4,1)} %iota_compare_fusion.2) | copy-start | bytes 52
  67.9 10.3 %copy-start.96 = (f32[8,4]{0,1:T(4,128)}, f32[8,4]{0,1:T(4,128)S(1)}, u32[]{:S(2)}) copy-start(f32[8,4]{0,1:T(4,128)S(1)} %copy.340) | copy-start | bytes 388
  68.3 52.4 %copy-start.38 = (f32[8,4,4,128]{3,0,2,1:T(8,128)}, f32[8,4,4,128]{3,0,2,1:T(8,128)S(1)}, u32[]{:S(2)}) copy-start(f32[8,4,4,128]{3,0,2,1:T(8,128)S(1)} %fusion.116) | copy-start | bytes 196612
  69.2 26.1 %copy-start.41 = (f32[8,4,4,128]{3,2,1,0:T(4,128)}, f32[8,4,4,128]{3,2,1,0:T(4,128)S(1)}, u32[]{:S(2)}) copy-start(f32[8,4,4,128]{3,2,1,0:T(4,128)S(1)} %copy.359) | copy-start | bytes 196612
  69.5 215.3 %copy-start.35 = (f32[8,4,4,128]{3,2,1,0:T(4,128)}, f32[8,4,4,128]{3,2,1,0:T(4,128)S(1)}, u32[]{:S(2)}) copy-start(f32[8,4,4,128]{3,2,1,0:T(4,128)S(1)} %copy.341) | copy-start | bytes 196612
  69.6 95.4 %copy-start.74 = (f32[8,4]{1,0:T(8,128)}, f32[8,4]{1,0:T(8,128)S(1)}, u32[]{:S(2)}) copy-start(f32[8,4]{1,0:T(8,128)S(1)} %copy.367) | copy-start | bytes 388
  79.2 3.7 collective-permute-start.4
  95.3 10.4 %copy-start.2 = (f32[8,256,512]{1,2,0:T(8,128)}, f32[8,256,512]{1,2,0:T(8,128)S(1)}, u32[]{:S(2)}) copy-start(f32[8,256,512]{1,2,0:T(8,128)S(1)} %get-tuple-element.124) | copy-start | bytes 12582916
  95.3 12.1 %copy-start = (f32[8,256,512]{1,2,0:T(8,128)}, f32[8,256,512]{1,2,0:T(8,128)S(1)}, u32[]{:S(2)}) copy-start(f32[8,256,512]{1,2,0:T(8,128)S(1)} %get-tuple-element.125) | copy-start | bytes 12582916
  105.7 7.3 %copy-start.18 = (f32[8,4,64,256]{3,2,1,0:T(8,128)}, f32[8,4,64,256]{3,2,1,0:T(8,128)S(1)}, u32[]{:S(2)}) copy-start(f32[8,4,64,256]{3,2,1,0:T(8,128)S(1)} %get-tuple-element.189) | copy-start | bytes 6291460
  107.4 11.3 %copy-start.101 = (pred[4,4]{1,0:T(4,128)(4,1)S(1)}, pred[4,4]{1,0:T(4,128)(4,1)}, u32[]{:S(2)}) copy-start(pred[4,4]{1,0:T(4,128)(4,1)} %get-tuple-element.195) | copy-start | bytes 52
  107.4 12.4 %copy-start.81 = (s32[4,128]{1,0:T(4,128)S(1)}, s32[4,128]{1,0:T(4,128)}, u32[]{:S(2)}) copy-start(s32[4,128]{1,0:T(4,128)} %copy-done.80) | copy-start | bytes 6148
  107.4 13.5 %copy-start.108 = (pred[4,4]{1,0:T(4,128)(4,1)S(1)}, pred[4,4]{1,0:T(4,128)(4,1)}, u32[]{:S(2)}) copy-start(pred[4,4]{1,0:T(4,128)(4,1)} %get-tuple-element.194) | copy-start | bytes 52
  113.0 47.8 %collective-permute-start.5 = (f32[8,4,64,256]{3,2,1,0:T(8,128)}, f32[8,4,64,256]{3,2,1,0:T(8,128)S(1)}, u32[]{:S(2)}, u32[]{:S(2)}) collective-permute-start(f32[8,4,64,256]{3,2,1,0:T(8,128)} %broadcast_add_fusion), channel_id=1, source_target_pairs={{0,1},{1,2},{2,3},{4,5},{5,6},{6,7},{8,9},{9,10},{10,11},{12,13},{... | collective-permute-start | bytes 6291464 | tf_op jit(solution)/shard_map/ppermute | solution.py:18
  117.3 47.7 %collective-permute-start.6 = (f32[8,4,64,256]{3,2,1,0:T(8,128)}, f32[8,4,64,256]{3,2,1,0:T(8,128)}, u32[]{:S(2)}, u32[]{:S(2)}) collective-permute-start(f32[8,4,64,256]{3,2,1,0:T(8,128)} %fusion.91), channel_id=1, source_target_pairs={{1,0},{2,1},{3,2},{5,4},{6,5},{7,6},{9,8},{10,9},{11,10},{13,12},{... | collective-permute-start | bytes 6291464 | tf_op jit(solution)/shard_map/ppermute | solution.py:18
  119.8 50.9 %copy-start.88 = (f32[4,4]{1,0:T(4,128)}, f32[4,4]{1,0:T(4,128)S(1)}, u32[]{:S(2)}) copy-start(f32[4,4]{1,0:T(4,128)S(1)} %fusion.170) | copy-start | bytes 196
  120.8 69.6 %copy-start.77 = (f32[8,4,4,128]{3,2,1,0:T(4,128)}, f32[8,4,4,128]{3,2,1,0:T(4,128)S(1)}, u32[]{:S(2)}) copy-start(f32[8,4,4,128]{3,2,1,0:T(4,128)S(1)} %copy.344) | copy-start | bytes 196612
  120.9 62.0 %copy-start.44 = (f32[8,4,4,128]{3,2,1,0:T(4,128)}, f32[8,4,4,128]{3,2,1,0:T(4,128)S(1)}, u32[]{:S(2)}) copy-start(f32[8,4,4,128]{3,2,1,0:T(4,128)S(1)} %copy.375) | copy-start | bytes 196612
  121.6 49.1 %copy-start.47 = (f32[4,8,4,4]{1,3,2,0:T(4,128)}, f32[4,8,4,4]{1,3,2,0:T(4,128)S(1)}, u32[]{:S(2)}) copy-start(f32[4,8,4,4]{1,3,2,0:T(4,128)S(1)} %get-tuple-element.174) | copy-start | bytes 6148
  121.6 49.1 %copy-start.53 = (f32[2,8,4,4]{1,3,2,0:T(4,128)}, f32[2,8,4,4]{1,3,2,0:T(4,128)S(1)}, u32[]{:S(2)}) copy-start(f32[2,8,4,4]{1,3,2,0:T(4,128)S(1)} %slice_multiply_fusion.4) | copy-start | bytes 3076
  122.6 54.3 %copy-start.1 = (f32[8,256,512]{1,2,0:T(8,128)S(1)}, f32[8,256,512]{1,2,0:T(8,128)}, u32[]{:S(2)}) copy-start(f32[8,256,512]{1,2,0:T(8,128)} %copy-done) | copy-start | bytes 12582916
  122.6 54.3 %copy-start.3 = (f32[8,256,512]{1,2,0:T(8,128)S(1)}, f32[8,256,512]{1,2,0:T(8,128)}, u32[]{:S(2)}) copy-start(f32[8,256,512]{1,2,0:T(8,128)} %copy-done.2) | copy-start | bytes 12582916
  170.7 46.3 %collective-permute-start.7 = (f32[8,4,64,256]{3,2,1,0:T(8,128)}, f32[8,4,64,256]{3,2,1,0:T(8,128)}, u32[]{:S(2)}, u32[]{:S(2)}) collective-permute-start(f32[8,4,64,256]{3,2,1,0:T(8,128)} %get-tuple-element.181), channel_id=1, source_target_pairs={{0,1},{1,2},{2,3},{4,5},{5,6},{6,7},{8,9},{9,10},{10,11},{12,13},{... | collective-permute-start | bytes 6291464 | tf_op jit(solution)/shard_map/ppermute | solution.py:18
  175.3 47.1 %collective-permute-start.8 = (f32[8,4,64,256]{3,2,1,0:T(8,128)}, f32[8,4,64,256]{3,2,1,0:T(8,128)}, u32[]{:S(2)}, u32[]{:S(2)}) collective-permute-start(f32[8,4,64,256]{3,2,1,0:T(8,128)} %get-tuple-element.180), channel_id=1, source_target_pairs={{1,0},{2,1},{3,2},{5,4},{6,5},{7,6},{9,8},{10,9},{11,10},{13,12},{... | collective-permute-start | bytes 6291464 | tf_op jit(solution)/shard_map/ppermute | solution.py:18
  182.8 7.5 %copy-start.8 = (f32[8,4,64,4,128]{4,3,2,1,0:T(4,128)S(1)}, f32[8,4,64,4,128]{4,3,2,1,0:T(4,128)}, u32[]{:S(2)}) copy-start(f32[8,4,64,4,128]{4,3,2,1,0:T(4,128)} %reshape.359) | copy-start | bytes 12582916
  182.8 58.2 %slice-start = ((s8[8388608]{0:T(1024)(128)(4,1)}), s8[4194304]{0:T(1024)(128)(4,1)S(1)}, s32[]{:S(2)}) async-start(s8[8388608]{0:T(1024)(128)(4,1)} %bitcast.256), calls=%async_computation.6 | async-start | bytes 8388608
  190.3 50.7 %copy-start.5 = (f32[8,4,4,64,256]{4,3,1,2,0:T(8,128)}, f32[8,4,4,64,256]{4,3,1,2,0:T(8,128)S(1)}, u32[]{:S(2)}) copy-start(f32[8,4,4,64,256]{4,3,1,2,0:T(8,128)S(1)} %fusion.73) | copy-start | bytes 25165828
  190.4 32.0 %copy-start.75 = (f32[8,4]{1,0:T(8,128)S(1)}, f32[8,4]{1,0:T(8,128)}, u32[]{:S(2)}) copy-start(f32[8,4]{1,0:T(8,128)} %copy-done.74) | copy-start | bytes 388
  190.4 50.7 %slice-start.1 = ((s8[8388608]{0:T(1024)(128)(4,1)}), s8[4194304]{0:T(1024)(128)(4,1)S(1)}, s32[]{:S(2)}) async-start(s8[8388608]{0:T(1024)(128)(4,1)} %bitcast.256), calls=%async_computation.7 | async-start | bytes 8388608
  207.5 28.5 %copy-start.24 = (f32[8,4,128,128]{2,3,1,0:T(8,128)S(1)}, f32[8,4,128,128]{2,3,1,0:T(8,128)}, u32[]{:S(2)}) copy-start(f32[8,4,128,128]{2,3,1,0:T(8,128)} %get-tuple-element.100) | copy-start | bytes 6291460
  228.8 46.2 %collective-permute-start.10 = (f32[8,4,64,256]{3,2,1,0:T(8,128)}, f32[8,4,64,256]{3,2,1,0:T(8,128)}, u32[]{:S(2)}, u32[]{:S(2)}) collective-permute-start(f32[8,4,64,256]{3,2,1,0:T(8,128)} %get-tuple-element.178), channel_id=1, source_target_pairs={{1,0},{2,1},{3,2},{5,4},{6,5},{7,6},{9,8},{10,9},{11,10},{13,12},{... | collective-permute-start | bytes 6291464 | tf_op jit(solution)/shard_map/ppermute | solution.py:18
  230.0 46.1 %collective-permute-start.9 = (f32[8,4,64,256]{3,2,1,0:T(8,128)}, f32[8,4,64,256]{3,2,1,0:T(8,128)}, u32[]{:S(2)}, u32[]{:S(2)}) collective-permute-start(f32[8,4,64,256]{3,2,1,0:T(8,128)} %get-tuple-element.179), channel_id=1, source_target_pairs={{0,1},{1,2},{2,3},{4,5},{5,6},{6,7},{8,9},{9,10},{10,11},{12,13},{... | collective-permute-start | bytes 6291464 | tf_op jit(solution)/shard_map/ppermute | solution.py:18
  276.2 8.6 %copy-start.42 = (f32[8,4,4,128]{3,2,1,0:T(4,128)S(1)}, f32[8,4,4,128]{3,2,1,0:T(4,128)}, u32[]{:S(2)}) copy-start(f32[8,4,4,128]{3,2,1,0:T(4,128)} %copy-done.41) | copy-start | bytes 196612
  284.8 12.4 %copy-start.6 = (f32[8,4,4,64,256]{4,3,1,2,0:T(8,128)}, f32[8,4,4,64,256]{4,3,1,2,0:T(8,128)S(1)}, u32[]{:S(2)}) copy-start(f32[8,4,4,64,256]{4,3,1,2,0:T(8,128)S(1)} %get-tuple-element.134) | copy-start | bytes 25165828
  302.6 10.4 %copy-start.76 = (f32[8,4,4]{1,2,0:T(4,128)S(1)}, f32[8,4,4]{1,2,0:T(4,128)}, u32[]{:S(2)}) copy-start(f32[8,4,4]{1,2,0:T(4,128)} %get-tuple-element.133) | copy-start | bytes 1540
  302.6 139.4 %reduce-scatter.5.cloned.1.call-start = ((), (), s32[]{:S(2)}) async-start(), calls=%async_computation.5 | async-start | bytes 4718592 | tf_op jit(solution)/shard_map/reduce_scatter | solution.py:292
  313.1 12.3 %copy-start.12 = (bf16[8,4,64,4,128]{4,3,2,1,0:T(4,128)(2,1)S(1)}, bf16[8,4,64,4,128]{4,3,2,1,0:T(4,128)(2,1)}, u32[]{:S(2)}) copy-start(bf16[8,4,64,4,128]{4,3,2,1,0:T(4,128)(2,1)} %copy-done.10) | copy-start | bytes 6291460
  313.1 12.3 %copy-start.45 = (f32[8,4,4,128]{3,2,1,0:T(4,128)S(1)}, f32[8,4,4,128]{3,2,1,0:T(4,128)}, u32[]{:S(2)}) copy-start(f32[8,4,4,128]{3,2,1,0:T(4,128)} %copy-done.44) | copy-start | bytes 196612
  325.4 9.9 %copy-start.4 = (f32[8,256,512]{1,2,0:T(8,128)S(1)}, f32[8,256,512]{1,2,0:T(8,128)}, u32[]{:S(2)}) copy-start(f32[8,256,512]{1,2,0:T(8,128)} %copy-done.2) | copy-start | bytes 12582916
  325.4 9.9 %copy-start.25 = (f32[8,4,128,128]{2,3,1,0:T(8,128)S(1)}, f32[8,4,128,128]{2,3,1,0:T(8,128)}, u32[]{:S(2)}) copy-start(f32[8,4,128,128]{2,3,1,0:T(8,128)} %get-tuple-element.100) | copy-start | bytes 6291460
  414.8 8.0 %copy-start.33 = (f32[8,4,128,128]{2,3,1,0:T(8,128)S(1)}, f32[8,4,128,128]{2,3,1,0:T(8,128)}, u32[]{:S(2)}) copy-start(f32[8,4,128,128]{2,3,1,0:T(8,128)} %fusion.182) | copy-start | bytes 6291460
  414.8 8.0 %copy-start.50 = (f32[4,128,128]{1,2,0:T(8,128)S(1)}, f32[4,128,128]{1,2,0:T(8,128)}, u32[]{:S(2)}) copy-start(f32[4,128,128]{1,2,0:T(8,128)} %compare_select_fusion) | copy-start | bytes 786436
  414.8 8.0 %copy-start.78 = (f32[8,4,4,128]{3,2,1,0:T(4,128)S(1)}, f32[8,4,4,128]{3,2,1,0:T(4,128)}, u32[]{:S(2)}) copy-start(f32[8,4,4,128]{3,2,1,0:T(4,128)} %copy-done.77) | copy-start | bytes 196612
  414.8 8.0 %copy-start.100 = (f32[8,4]{1,0:T(8,128)S(1)}, f32[8,4]{1,0:T(8,128)}, u32[]{:S(2)}) copy-start(f32[8,4]{1,0:T(8,128)} %constant_dynamic-slice_fusion.4) | copy-start | bytes 388
  448.3 7.7 %collective-permute-start.11 = (f32[8,320,3]{1,0,2:T(8,128)S(1)}, f32[8,320,3]{1,0,2:T(8,128)S(1)}, u32[]{:S(2)}, u32[]{:S(2)}) collective-permute-start(f32[8,320,3]{1,0,2:T(8,128)S(1)} %copy.400), channel_id=1, source_target_pairs={{1,0},{2,1},{3,2},{5,4},{6,5},{7,6},{9,8},{10,9},{11,10},{13,12},{... | collective-permute-start | bytes 92168 | tf_op jit(solution)/shard_map/ppermute | solution.py:18
  (67 other events, 251.5 us)
Sparse Core Ops, SparseCore 0:
  10.5 30.7 all-gather.2
  43.7 27.8 all-gather.4
  302.7 51.8 reduce-scatter.2
  361.5 52.4 reduce-scatter.4
